TPU v7x, 256 devices: a whole 4x4x8 slice. The times are simulated.
256 devices in a mesh: ka: 64 (over z, y, core), pb: 4 (over x).
Axes of the slice: x: 4, y: 4, z: 8, core: 2. Of those that a mesh axis runs over, the one named last changes fastest.
Arguments:
- occupation: float32 [6, 262144], P(None, 'ka'), may hold values from 0 to 1
- gain_table: bfloat16 [64, 36, 262144], P('pb', None, 'ka'), may hold values from 0.0049743652 to 0.19921875
- loss_table: bfloat16 [64, 36, 262144], P('pb', None, 'ka'), may hold values from 0.0049743652 to 0.19921875
- owner: int32 [4, 64, 16, 32, 1], P('pb', 'ka'), may hold values from 0 to 63; in each aligned block of 512 rows (0 to 511, 512 to 1023, ..., all dimensions but the last counted through in order) at most 16 rows name the same one
- local_index: int32 [4, 64, 16, 32], P('pb', 'ka'), may hold values from 0 to 31
- pair_mask: int32 [64, 36], P('pb'), may hold values 0 or 1
- counts: int32 [4, 64], P('pb', 'ka'), may hold values from 1 to 16, as said below
Outputs:
- collision: float32 [6, 262144], P(None, ('ka', 'pb'))
- section_occupation: float32 [6, 262144], P(None, ('ka', 'pb'))
Inputs may be any that keep to these rules, and one draw needn't show every extreme that they name: Among the 16 x 32 entries of one q-shift group and one k-block, no owner is named more than 16 times. The active q-shifts of a group at a k-block are its first counts ones.
All inputs are finite; a program needn't handle non-finite values. No bound on the sum of `pair_mask` on one device may be relied on, other than what follows from the above.
Results may differ from a plain program's by a relative error of at most 0.0003.
Values sent between devices are 32-bit elements; how exact they have to be, the bound alone decides.
No kernel may reach another device: no remote copies, remote signals or barrier semaphores. Data moves between devices by JAX's collectives and lax.ppermute only.
A program may use at most 128 MiB of HBM per device.

v0:
```python
import jax
import jax.numpy as jnp
from jax import lax
from jax.sharding import PartitionSpec as P

half_step = 0.5


def body(occupation, gain_table, loss_table, owner, local_index, pair_mask, counts):
    bands, width = occupation.shape
    shifts = gain_table.shape[0]
    sub_count = local_index.shape[3]
    sub_width = width // sub_count
    ka_count = lax.axis_size("ka")
    total_requests = shifts * sub_count
    owners = owner.reshape(total_requests)
    sources = local_index.reshape(total_requests)
    whole = lax.all_gather(occupation, "ka", axis=1, tiled=True)
    pieces = whole.reshape(bands, ka_count * sub_count, sub_width)
    picked = jnp.take(pieces, owners * sub_count + sources, axis=1).transpose(1, 0, 2)
    shifted = (
        picked.reshape(shifts, sub_count, bands, sub_width)
        .transpose(0, 2, 1, 3)
        .reshape(shifts, bands, width)
    )
    active = (jnp.arange(shifts, dtype=jnp.int32) < counts.reshape(())).astype(jnp.float32)
    weight = pair_mask.astype(jnp.float32) * active[:, None]
    gain_four = (gain_table.astype(jnp.float32) * weight[:, :, None]).reshape(
        shifts, bands, bands, width
    )
    loss_four = (loss_table.astype(jnp.float32) * weight[:, :, None]).reshape(
        shifts, bands, bands, width
    )
    inflow = jnp.einsum("smnk,snk->mk", gain_four, shifted)
    outflow = jnp.einsum("smnk,snk->mk", loss_four, 1.0 - shifted)
    partial_terms = (1.0 - occupation) * inflow - occupation * outflow
    collision = lax.psum_scatter(partial_terms, "pb", scatter_dimension=1, tiled=True)
    share_width = collision.shape[1]
    own_share = lax.dynamic_slice_in_dim(
        occupation, lax.axis_index("pb") * share_width, share_width, 1
    )
    return (collision, own_share + half_step * collision)


def solution(mesh):
    return jax.shard_map(
        body,
        mesh=mesh,
        in_specs=(
            P(None, "ka"),
            P("pb", None, "ka"),
            P("pb", None, "ka"),
            P("pb", "ka", None, None, None),
            P("pb", "ka", None, None),
            P("pb", None),
            P("pb", "ka"),
        ),
        out_specs=(P(None, ("ka", "pb")), P(None, ("ka", "pb"))),
        check_vma=False,
    )
```

profile of v0, /device:TPU:24, one launch (start us, length us, event | category | flops | bytes accessed | tf_op | source)
XLA Modules:
  0.0 143.3 jit_solution(18443966641634054089)
XLA Ops:
  7.2 0.0 all-gather.2.cloned.1.call-start
  7.2 0.7 all-gather.2.cloned.1.call-update
  7.9 0.0 reduce-scatter.2.cloned.1.call-start
  7.9 0.8 reshape.77
  8.7 0.8 reshape.75
  9.5 0.7 fusion.1
  10.2 0.1 mul.61
  10.3 0.1 mul.60
  11.0 0.8 convert_multiply_fusion.2
  11.8 0.1 copy.10
  11.9 13.3 %convert_multiply_fusion.1 = (f32[16,36,4096]{2,0,1:T(8,128)}, f32[16,36,4096]{2,0,1:T(8,128)}) fusion(bf16[16,36,4096]{2,0,1:T(8,128)(2,1)} %param.8, f32[16,36]{0,1:T(8,128)S(1)} %copy.10, bf16[16,36,4096]{2,0,1:T(8,128)(2,1)} %param.9), kind=kLoop, calls=%fused_computation.4 | loop fusion | flops 9437184 | bytes 28313856 | tf_op jit(solution)/shard_map/mul | solution.py:28
  25.2 69.4 %all-gather.2.cloned.1.call-done = f32[6,262144]{1,0:T(8,128)} async-done(((f32[6,4096]{1,0:T(8,128)}), f32[6,262144]{1,0:T(8,128)}) %all-gather.2.cloned.1.call-update) | async-done | bytes 6291472 | tf_op jit(solution)/shard_map/all_gather | solution.py:18
  94.6 4.4 %gather_fusion = f32[512,6,128]{2,1,0:T(8,128)S(1)} fusion(f32[6,2048,128]{2,0,1:T(8,128)} %bitcast.36, s32[1024]{0:T(1024)S(1)} %pad_clamp_fusion), kind=kCustom, calls=%fused_computation | custom fusion | bytes 3147776 | tf_op jit(solution)/shard_map/jit(_take)/gather | solution.py:20
  99.0 1.7 %broadcast_select_fusion = f32[512,6,128]{2,1,0:T(8,128)S(1)} fusion(f32[512,6,128]{2,1,0:T(8,128)S(1)} %gather_fusion, pred[512]{0:T(512)(128)(4,1)S(1)} %compare_and_fusion), kind=kLoop, calls=%fused_computation.6 | loop fusion | flops 393216 | bytes 3146240 | tf_op jit(solution)/shard_map/jit(_take)/select_n | solution.py:20
  100.8 0.2 subtract_bitcast_fusion
  101.0 0.9 copy.24
  101.9 0.9 copy.23
  102.8 0.0 copy-start
  102.8 9.4 %multiply_reduce_fusion = (f32[4096,6]{0,1:T(8,128)S(1)}, f32[4096,6]{0,1:T(8,128)S(1)}) fusion(f32[4096,6,16,6]{0,2,1,3:T(8,128)} %bitcast.33, f32[4096,6,16]{0,2,1:T(8,128)S(1)} %copy.24, f32[4096,6,16,6]{0,2,1,3:T(8,128)} %bitcast.32, f32[4096,6,16]{0,2,1:T(8,128)S(1)} %copy.23), kind=kLoop, calls=%fused_computation.1 | loop fusion | flops 9388032 | bytes 22216704 | tf_op jit(solution)/shard_map/smnk,snk->mk/dot_general | solution.py:35
  112.2 0.0 copy-done
  112.3 0.7 fusion
  112.9 0.0 reduce-scatter.2.cloned.1.call-update
  112.9 22.1 %reduce-scatter.2.cloned.1.call-done = f32[6,1024]{1,0:T(8,128)} async-done(((f32[6,4096]{1,0:T(8,128)}), f32[6,1024]{1,0:T(8,128)}) %reduce-scatter.2.cloned.1.call-update) | async-done | bytes 24592 | tf_op jit(solution)/shard_map/reduce_scatter | solution.py:37
  135.1 1.4 multiply_add_fusion
  (4 shorter events, 0.0 us)
Async XLA Ops:
  7.2 87.5 %all-gather.2.cloned.1.call-start = ((), (), s32[]{:S(2)}) async-start(), calls=%async_computation.1 | async-start | bytes 8519680 | tf_op jit(solution)/shard_map/all_gather | solution.py:18
  7.9 127.2 %reduce-scatter.2.cloned.1.call-start = ((), (), s32[]{:S(2)}) async-start(), calls=%async_computation.2 | async-start | bytes 163840 | tf_op jit(solution)/shard_map/reduce_scatter | solution.py:37
  102.8 9.4 %copy-start = (f32[6,4096]{1,0:T(8,128)S(1)}, f32[6,4096]{1,0:T(8,128)}, u32[]{:S(2)}) copy-start(f32[6,4096]{1,0:T(8,128)} %param.7) | copy-start | bytes 294916
Sparse Core Ops, SparseCore 0:
  10.8 83.8 all-gather.1
  113.1 21.9 reduce-scatter.1
where the time goes:
time: 144 us; the launch traced here: 143 us
  waiting for transfers between devices  92.2 us (64%)
  other arithmetic  28.2 us (20%)
  between operations  14.8 us (10%)
  local copies, waits for them, and re-layouts  7.99 us (6%)
    all_gather x1, waiting for transfers between devices, body(): whole = lax.all_gather(occupation, 'ka', axis=1, tiled=True)  69.4 us
    reduce_scatter x1, waiting for transfers between devices, body(): lax.psum_scatter(partial_terms, 'pb', scatter_dimension=1, tiled=True)  22.1 us
    mul x1, other arithmetic, body(): gain_table.astype(jnp.float32) * weight[:, :, None]  13.3 us
    dot_general x1, other arithmetic, body(): outflow = jnp.einsum('smnk,snk->mk', loss_four, 1.0 - shifted)  9.4 us
    gather x1, local copies, waits for them, and re-layouts, body(): jnp.take(pieces, owners * sub_count + sources, axis=1).transpose(1, 0, 2)  4.36 us
  transfers between devices with their start and end apart: 2, of which 2 were waited for; matrix products, arithmetic and copies ran while one was open for 12% of the time, Pallas kernels for 0%

commit v1 on v0

--- a/solution.py
+++ b/solution.py
@@ -12,12 +12,30 @@
     sub_count = local_index.shape[3]
     sub_width = width // sub_count
     ka_count = lax.axis_size("ka")
+    pb_count = lax.axis_size("pb")
     total_requests = shifts * sub_count
+    cap = shifts
     owners = owner.reshape(total_requests)
     sources = local_index.reshape(total_requests)
-    whole = lax.all_gather(occupation, "ka", axis=1, tiled=True)
-    pieces = whole.reshape(bands, ka_count * sub_count, sub_width)
-    picked = jnp.take(pieces, owners * sub_count + sources, axis=1).transpose(1, 0, 2)
+
+    hits = (owners[:, None] == jnp.arange(ka_count, dtype=jnp.int32)[None, :]).astype(jnp.float32)
+    earlier = (
+        jnp.arange(total_requests, dtype=jnp.int32)[:, None]
+        > jnp.arange(total_requests, dtype=jnp.int32)[None, :]
+    ).astype(jnp.float32)
+    before = jnp.dot(earlier, hits, preferred_element_type=jnp.float32)
+    slot = jnp.sum(before * hits, axis=1).astype(jnp.int32)
+    place = owners * cap + slot
+
+    wanted = jnp.zeros((ka_count * cap,), jnp.int32).at[place].set(sources, unique_indices=True)
+    asked = lax.all_to_all(wanted.reshape(ka_count, cap), "ka", 0, 0, tiled=True)
+
+    blocks = occupation.reshape(bands, sub_count, sub_width).transpose(1, 0, 2)
+    outgoing = jnp.take(blocks, asked.reshape(ka_count * cap), axis=0)
+    incoming = lax.all_to_all(
+        outgoing.reshape(ka_count, cap * bands * sub_width), "ka", 0, 0, tiled=True
+    ).reshape(ka_count * cap, bands, sub_width)
+    picked = jnp.take(incoming, place, axis=0)
     shifted = (
         picked.reshape(shifts, sub_count, bands, sub_width)
         .transpose(0, 2, 1, 3)
@@ -34,8 +52,10 @@
     inflow = jnp.einsum("smnk,snk->mk", gain_four, shifted)
     outflow = jnp.einsum("smnk,snk->mk", loss_four, 1.0 - shifted)
     partial_terms = (1.0 - occupation) * inflow - occupation * outflow
-    collision = lax.psum_scatter(partial_terms, "pb", scatter_dimension=1, tiled=True)
-    share_width = collision.shape[1]
+    share_width = width // pb_count
+    parts = partial_terms.reshape(bands, pb_count, share_width).transpose(1, 0, 2)
+    gathered = lax.all_to_all(parts, "pb", 0, 0, tiled=True)
+    collision = jnp.sum(gathered, axis=0)
     own_share = lax.dynamic_slice_in_dim(
         occupation, lax.axis_index("pb") * share_width, share_width, 1
     )

time: 144 us -> 171 us (1.19)
  waiting for transfers between devices: 92.2 us -> 65.6 us
  blocking collectives: 0 us -> 19.5 us
  local copies, waits for them, and re-layouts: 7.99 us -> 27.3 us
  other arithmetic: 28.2 us -> 44.4 us
  between operations: 14.8 us -> 1.44 us
  starting transfers between devices: 0.08 us -> 11.6 us
    all_gather x1 -> x0, waiting for transfers between devices: 69.4 us -> none  [body(): whole = lax.all_gather(occupation, 'ka', axis=1, tiled=True)]
    all_to_all x0 -> x2, waiting for transfers between devices: none -> 65.6 us  [the longest x1 59.6 us: body(): lax.all_to_all(outgoing.reshape(ka_count, cap * bands * sub_width), 'ka',...]
    reduce_scatter x1 -> x0, waiting for transfers between devices: 22.1 us -> none  [body(): lax.psum_scatter(partial_terms, 'pb', scatter_dimension=1, tiled=True)]
    all_to_all x0 -> x1, blocking collectives: none -> 19.5 us  [body(): lax.all_to_all(wanted.reshape(ka_count, cap), 'ka', 0, 0, tiled=True)]
    all_to_all x0 -> x2, starting transfers between devices: none -> 11.6 us  [the longest x1 7.3 us: body(): lax.all_to_all(outgoing.reshape(ka_count, cap * bands * sub_width), 'ka',...]
    all_to_all x0 -> x2, other arithmetic: none -> 10.2 us  [the longest x1 9.42 us: body(): lax.all_to_all(outgoing.reshape(ka_count, cap * bands * sub_width), 'ka',...]
    gather x1 -> x2, local copies, waits for them, and re-layouts: 4.36 us -> 12.2 us  [the longest x1 9.06 us: body(): outgoing = jnp.take(blocks, asked.reshape(ka_count * cap), axis=0)]
    select_n x0 -> x1, local copies, waits for them, and re-layouts: none -> 6.02 us  [body(): outgoing = jnp.take(blocks, asked.reshape(ka_count * cap), axis=0)]
  transfers between devices with their start and end apart: 2 -> 2, of which waited for: 2 -> 2; matrix products, arithmetic and copies ran while one was open for 12% -> 8% of each run, Pallas kernels for 0% -> 0%
where the time goes in v1:
time: 171 us; the launch traced here: 170 us
  waiting for transfers between devices  65.6 us (38%)
  other arithmetic  44.4 us (26%)
  local copies, waits for them, and re-layouts  27.3 us (16%)
  blocking collectives  19.5 us (11%)
  starting transfers between devices  11.6 us (7%)
    all_to_all x1, waiting for transfers between devices, body(): lax.all_to_all(outgoing.reshape(ka_count, cap * bands * sub_width), 'ka',...  59.6 us
    all_to_all x1, blocking collectives, body(): lax.all_to_all(wanted.reshape(ka_count, cap), 'ka', 0, 0, tiled=True)  19.5 us
    mul x1, other arithmetic, body(): gain_table.astype(jnp.float32) * weight[:, :, None]  13.3 us
    all_to_all x1, other arithmetic, body(): lax.all_to_all(outgoing.reshape(ka_count, cap * bands * sub_width), 'ka',...  9.42 us
    dot_general x1, other arithmetic, body(): outflow = jnp.einsum('smnk,snk->mk', loss_four, 1.0 - shifted)  9.4 us
    gather x1, local copies, waits for them, and re-layouts, body(): outgoing = jnp.take(blocks, asked.reshape(ka_count * cap), axis=0)  9.06 us
    all_to_all x1, starting transfers between devices, body(): lax.all_to_all(outgoing.reshape(ka_count, cap * bands * sub_width), 'ka',...  7.3 us
    select_n x2, other arithmetic, body(): outgoing = jnp.take(blocks, asked.reshape(ka_count * cap), axis=0)  7.17 us
  transfers between devices with their start and end apart: 2, of which 2 were waited for; matrix products, arithmetic and copies ran while one was open for 8% of the time, Pallas kernels for 0%

profile of v1, /device:TPU:24, one launch (start us, length us, event | category | flops | bytes accessed | tf_op | source)
XLA Modules:
  0.0 170.2 jit_solution(10047257584456376707)
XLA Ops:
  0.6 0.5 broadcast.111
  1.1 1.4 fusion.7
  2.5 0.1 reshape.155
  2.6 0.3 fusion.1
  2.9 0.1 mul.66
  3.0 0.8 reshape.186
  3.8 2.4 %scatter_custom_fusion = s32[1024]{0:T(1024)S(1)} fusion(s32[512]{0:T(512)S(1)} %bitcast.53, s32[512]{0:T(512)S(1)} %reshape.186, s32[]{:T(128)} %constant.17.clone.1), kind=kCustom, calls=%fused_computation.30 | custom fusion | bytes 4100 | tf_op jit(solution)/shard_map/scatter | solution.py:30
  6.2 0.1 all_to_all.13
  6.3 19.5 %all_to_all.20 = s32[64,1,16]{2,1,0:T(1,128)S(1)} all-to-all(s32[64,1,16]{2,1,0:T(1,128)S(1)} %bitcast.49), channel_id=1, replica_groups=mesh['ka'=64,'pb'=4] {'ka'}, dimensions={0} | all-to-all | bytes 8192 | tf_op jit(solution)/shard_map/all_to_all | solution.py:31
  25.8 0.7 reduce.18
  26.6 0.1 reshape.157
  26.7 0.1 reshape.159
  26.8 9.1 %gather_fusion = f32[1024,6,128]{2,1,0:T(8,128)} fusion(f32[32,6,128]{2,1,0:T(8,128)} %bitcast.43, s32[1024]{0:T(1024)S(1)} %broadcast_clamp_fusion), kind=kCustom, calls=%fused_computation | custom fusion | bytes 6295552 | tf_op jit(solution)/shard_map/jit(_take)/gather | solution.py:34
  35.8 7.2 %broadcast_select_fusion = f32[1024,6,128]{2,1,0:T(8,128)} fusion(f32[1024,6,128]{2,1,0:T(8,128)} %gather_fusion, pred[1024]{0:T(1024)(128)(4,1)S(1)} %compare_and_fusion.1), kind=kLoop, calls=%fused_computation.9 | loop fusion | flops 786432 | bytes 6292480 | tf_op jit(solution)/shard_map/jit(_take)/select_n | solution.py:34
  43.0 6.0 %select_n.65 = f32[64,1,12288]{2,1,0:T(1,128)} reshape(f32[1024,6,128]{2,1,0:T(8,128)} %broadcast_select_fusion) | data formatting | bytes 6291456 | tf_op jit(solution)/shard_map/jit(_take)/select_n | solution.py:34
  49.0 0.0 copy-start.2
  49.0 7.3 %all-to-all-start.1 = ((f32[64,1,12288]{2,1,0:T(1,128)}), f32[64,1,12288]{2,1,0:T(1,128)}, u32[]{:S(2)}, u32[]{:S(2)}) async-start(f32[64,1,12288]{2,1,0:T(1,128)} %select_n.65), calls=%async_computation.1 | async-start | bytes 6291456 | tf_op jit(solution)/shard_map/all_to_all | solution.py:35
  56.3 0.1 convert_element_type.38
  57.1 0.0 copy-done.2
  57.1 0.1 convert_multiply_fusion.2
  57.2 0.1 copy.13
  57.3 13.3 %convert_multiply_fusion.1 = (f32[16,36,4096]{2,0,1:T(8,128)}, f32[16,36,4096]{2,0,1:T(8,128)}) fusion(bf16[16,36,4096]{2,0,1:T(8,128)(2,1)} %param.8, f32[16,36]{0,1:T(8,128)S(1)} %copy.13, bf16[16,36,4096]{2,0,1:T(8,128)(2,1)} %param.9), kind=kLoop, calls=%fused_computation.6 | loop fusion | flops 9437184 | bytes 28313856 | tf_op jit(solution)/shard_map/mul | solution.py:46
  70.5 59.6 %all-to-all-done.1 = f32[64,1,12288]{2,1,0:T(1,128)} async-done(((f32[64,1,12288]{2,1,0:T(1,128)}), f32[64,1,12288]{2,1,0:T(1,128)}, u32[]{:S(2)}, u32[]{:S(2)}) %all-to-all-start.1) | async-done | bytes 3145760 | tf_op jit(solution)/shard_map/all_to_all | solution.py:35
  130.1 9.4 %reduce.6 = f32[64,12288]{1,0:T(8,128)S(1)} reduce(f32[64,1,12288]{2,1,0:T(1,128)} %all-to-all-done.1, f32[]{:T(128)} %constant.60), dimensions={1}, to_apply=%all_to_all.15.reduce_sub_computation | reduce | bytes 6291460 | tf_op jit(solution)/shard_map/all_to_all | solution.py:35
  139.5 3.0 %reshape.160 = f32[1024,6,128]{2,1,0:T(8,128)} reshape(f32[64,12288]{1,0:T(8,128)S(1)} %reduce.6) | data formatting | bytes 6291456 | tf_op jit(solution)/shard_map/reshape | solution.py:37
  142.5 3.2 %gather_fusion.1 = f32[512,6,128]{2,1,0:T(8,128)S(1)} fusion(f32[1024,6,128]{2,1,0:T(8,128)} %reshape.160, s32[1024]{0:T(1024)S(1)} %pad_clamp_fusion), kind=kCustom, calls=%fused_computation.1 | custom fusion | bytes 3147776 | tf_op jit(solution)/shard_map/jit(_take)/gather | solution.py:38
  145.7 0.7 select_bitcast_fusion
  146.4 0.9 fusion
  147.3 0.9 copy.26
  148.3 0.9 copy.27
  149.2 0.0 copy-start
  149.2 9.4 %multiply_reduce_fusion = (f32[4096,6]{0,1:T(8,128)S(1)}, f32[4096,6]{0,1:T(8,128)S(1)}) fusion(f32[4096,6,16,6]{0,2,1,3:T(8,128)} %bitcast.45, f32[4096,6,16]{0,2,1:T(8,128)S(1)} %copy.27, f32[4096,6,16,6]{0,2,1,3:T(8,128)} %bitcast.44, f32[4096,6,16]{0,2,1:T(8,128)S(1)} %copy.26), kind=kLoop, calls=%fused_computation.3 | loop fusion | flops 9388032 | bytes 22216704 | tf_op jit(solution)/shard_map/smnk,snk->mk/dot_general | solution.py:53
  158.6 0.0 copy-done
  158.6 0.7 fusion.2
  159.3 4.3 %all-to-all-start.2 = ((f32[4,6,1024]{2,1,0:T(8,128)}), f32[4,6,1024]{2,1,0:T(8,128)S(1)}, u32[]{:S(2)}, u32[]{:S(2)}) async-start(f32[4,6,1024]{2,1,0:T(8,128)} %bitcast.24), calls=%async_computation.2 | async-start | bytes 262144 | tf_op jit(solution)/shard_map/all_to_all | solution.py:57
  163.6 6.0 %all-to-all-done.2 = f32[4,6,1024]{2,1,0:T(8,128)S(1)} async-done(((f32[4,6,1024]{2,1,0:T(8,128)}), f32[4,6,1024]{2,1,0:T(8,128)S(1)}, u32[]{:S(2)}, u32[]{:S(2)}) %all-to-all-start.2) | async-done | bytes 98336 | tf_op jit(solution)/shard_map/all_to_all | solution.py:57
  169.6 0.0 copy-start.1
  169.6 0.6 multiply_add_fusion
  170.2 0.0 copy-done.1
  (9 shorter events, 0.1 us)
Async XLA Ops:
  49.0 8.1 %copy-start.2 = (s32[16,36]{1,0:T(8,128)S(1)}, s32[16,36]{1,0:T(8,128)}, u32[]{:S(2)}) copy-start(s32[16,36]{1,0:T(8,128)} %param.12) | copy-start | bytes 6916
  49.0 81.1 %all-to-all-start.1 = ((f32[64,1,12288]{2,1,0:T(1,128)}), f32[64,1,12288]{2,1,0:T(1,128)}, u32[]{:S(2)}, u32[]{:S(2)}) async-start(f32[64,1,12288]{2,1,0:T(1,128)} %select_n.65), calls=%async_computation.1 | async-start | bytes 6291456 | tf_op jit(solution)/shard_map/all_to_all | solution.py:35
  149.2 9.4 %copy-start = (f32[6,4096]{1,0:T(8,128)S(1)}, f32[6,4096]{1,0:T(8,128)}, u32[]{:S(2)}) copy-start(f32[6,4096]{1,0:T(8,128)} %param.7) | copy-start | bytes 294916
  159.3 10.3 %all-to-all-start.2 = ((f32[4,6,1024]{2,1,0:T(8,128)}), f32[4,6,1024]{2,1,0:T(8,128)S(1)}, u32[]{:S(2)}, u32[]{:S(2)}) async-start(f32[4,6,1024]{2,1,0:T(8,128)} %bitcast.24), calls=%async_computation.2 | async-start | bytes 262144 | tf_op jit(solution)/shard_map/all_to_all | solution.py:57
  169.6 0.6 copy-start.1

commit v2 on v0

--- a/solution.py
+++ b/solution.py
@@ -6,18 +6,61 @@
 half_step = 0.5
 
 
+def ring_gather(block, y_count, z_count):
+    ka_count = 2 * y_count * z_count
+    per_z = 2 * y_count
+
+    def pairs(fn):
+        return [(j, fn(j)) for j in range(ka_count)]
+
+    def y_step(d):
+        return pairs(lambda j: (j // per_z) * per_z + ((j // 2 + d) % y_count) * 2 + j % 2)
+
+    def z_step(d):
+        return pairs(lambda j: ((j // per_z + d) % z_count) * per_z + j % per_z)
+
+    def ring(x, step, count):
+        ahead = {0: x}
+        fwd, back = x, x
+        for d in range(1, count // 2 + 1):
+            back = lax.ppermute(back, "ka", step(-1))
+            ahead[d] = back
+            if d < count - d:
+                fwd = lax.ppermute(fwd, "ka", step(1))
+                ahead[count - d] = fwd
+        return jnp.stack([ahead[d] for d in range(count)])
+
+    along_y = ring(block, y_step, y_count)
+    along_z = ring(along_y, z_step, z_count)
+    other = lax.ppermute(along_z, "ka", pairs(lambda j: j ^ 1))
+    return jnp.stack([along_z, other])
+
+
 def body(occupation, gain_table, loss_table, owner, local_index, pair_mask, counts):
     bands, width = occupation.shape
     shifts = gain_table.shape[0]
     sub_count = local_index.shape[3]
     sub_width = width // sub_count
     ka_count = lax.axis_size("ka")
+    pb_count = lax.axis_size("pb")
+    z_count = 8
+    y_count = ka_count // (2 * z_count)
     total_requests = shifts * sub_count
+
+    gathered = ring_gather(occupation, y_count, z_count).reshape(
+        ka_count, bands, sub_count, sub_width
+    )
+    me = lax.axis_index("ka")
+    my_z, my_y, my_c = me // (2 * y_count), (me // 2) % y_count, me % 2
     owners = owner.reshape(total_requests)
+    o_z, o_y, o_c = owners // (2 * y_count), (owners // 2) % y_count, owners % 2
+    where = (
+        (o_c ^ my_c) * (z_count * y_count)
+        + ((o_z - my_z) % z_count) * y_count
+        + (o_y - my_y) % y_count
+    )
     sources = local_index.reshape(total_requests)
-    whole = lax.all_gather(occupation, "ka", axis=1, tiled=True)
-    pieces = whole.reshape(bands, ka_count * sub_count, sub_width)
-    picked = jnp.take(pieces, owners * sub_count + sources, axis=1).transpose(1, 0, 2)
+    picked = gathered[where, :, sources, :]
     shifted = (
         picked.reshape(shifts, sub_count, bands, sub_width)
         .transpose(0, 2, 1, 3)
@@ -34,8 +77,9 @@
     inflow = jnp.einsum("smnk,snk->mk", gain_four, shifted)
     outflow = jnp.einsum("smnk,snk->mk", loss_four, 1.0 - shifted)
     partial_terms = (1.0 - occupation) * inflow - occupation * outflow
-    collision = lax.psum_scatter(partial_terms, "pb", scatter_dimension=1, tiled=True)
-    share_width = collision.shape[1]
+    share_width = width // pb_count
+    parts = partial_terms.reshape(bands, pb_count, share_width).transpose(1, 0, 2)
+    collision = jnp.sum(lax.all_to_all(parts, "pb", 0, 0, tiled=True), axis=0)
     own_share = lax.dynamic_slice_in_dim(
         occupation, lax.axis_index("pb") * share_width, share_width, 1
     )

time: 144 us -> 135 us (0.938)
  waiting for transfers between devices: 92.2 us -> 37.6 us
  local copies, waits for them, and re-layouts: 7.99 us -> 42.7 us
  starting transfers between devices: 0.08 us -> 24.6 us
  between operations: 14.8 us -> 1.5 us
    all_gather x1 -> x0, waiting for transfers between devices: 69.4 us -> none  [body(): whole = lax.all_gather(occupation, 'ka', axis=1, tiled=True)]
    ppermute x0 -> x11, waiting for transfers between devices: none -> 31.6 us  [the longest x6 31.6 us: ring(): back = lax.ppermute(back, 'ka', step(-1))]
    reduce_scatter x1 -> x0, waiting for transfers between devices: 22.1 us -> none  [body(): lax.psum_scatter(partial_terms, 'pb', scatter_dimension=1, tiled=True)]
    reshape x0 -> x3, local copies, waits for them, and re-layouts: none -> 20.7 us  [the longest x2 20.6 us: body(): ring_gather(occupation, y_count, z_count)]
    ppermute x0 -> x11, starting transfers between devices: none -> 20.3 us  [the longest x6 17.8 us: ring(): back = lax.ppermute(back, 'ka', step(-1))]
    another operation x0 -> x7, local copies, waits for them, and re-layouts: none -> 7.77 us  [the longest x6 4.75 us: ring(): return jnp.stack([ahead[d] for d in range(count)])]
    all_to_all x0 -> x1, waiting for transfers between devices: none -> 5.98 us  [body(): collision = jnp.sum(lax.all_to_all(parts, 'pb', 0, 0, tiled=True), axis=0)]
    all_to_all x0 -> x1, starting transfers between devices: none -> 4.29 us  [body(): collision = jnp.sum(lax.all_to_all(parts, 'pb', 0, 0, tiled=True), axis=0)]
  transfers between devices with their start and end apart: 2 -> 12, of which waited for: 2 -> 7; matrix products, arithmetic and copies ran while one was open for 12% -> 12% of each run, Pallas kernels for 0% -> 0%
where the time goes in v2:
time: 135 us; the launch traced here: 134 us
  local copies, waits for them, and re-layouts  42.7 us (32%)
  waiting for transfers between devices  37.6 us (28%)
  other arithmetic  28.1 us (21%)
  starting transfers between devices  24.6 us (18%)
  between operations  1.5 us (1%)
    ppermute x6, waiting for transfers between devices, ring(): back = lax.ppermute(back, 'ka', step(-1))  31.6 us
    reshape x2, local copies, waits for them, and re-layouts, body(): ring_gather(occupation, y_count, z_count)  20.6 us
    ppermute x6, starting transfers between devices, ring(): back = lax.ppermute(back, 'ka', step(-1))  17.8 us
    mul x1, other arithmetic, body(): gain_table.astype(jnp.float32) * weight[:, :, None]  13.3 us
    dot_general x1, other arithmetic, body(): outflow = jnp.einsum('smnk,snk->mk', loss_four, 1.0 - shifted)  9.4 us
    all_to_all x1, waiting for transfers between devices, body(): collision = jnp.sum(lax.all_to_all(parts, 'pb', 0, 0, tiled=True), axis=0)  5.98 us
    gather x1, local copies, waits for them, and re-layouts, body(): picked = gathered[where, :, sources, :]  5.85 us
    another operation x6, local copies, waits for them, and re-layouts, ring(): return jnp.stack([ahead[d] for d in range(count)])  4.75 us
  transfers between devices with their start and end apart: 12, of which 7 were waited for; matrix products, arithmetic and copies ran while one was open for 12% of the time, Pallas kernels for 0%

profile of v2, /device:TPU:24, one launch (start us, length us, event | category | flops | bytes accessed | tf_op | source)
XLA Modules:
  0.0 134.5 jit_solution(882098374407272236)
XLA Ops:
  0.6 0.8 collective-permute-start
  1.4 2.5 %collective-permute-start.2 = (f32[6,4096]{1,0:T(8,128)}, f32[6,4096]{1,0:T(8,128)S(1)}, u32[]{:S(2)}, u32[]{:S(2)}) collective-permute-start(f32[6,4096]{1,0:T(8,128)} %param.7), channel_id=1, source_target_pairs={{0,8},{4,12},{8,16},{12,20},{16,24},{20,28},{24,0},{28,4},{32,40},... | collective-permute-start | bytes 294920 | tf_op jit(solution)/shard_map/ppermute | solution.py:29
  3.9 3.4 %collective-permute-done = f32[6,4096]{1,0:T(8,128)S(1)} collective-permute-done((f32[6,4096]{1,0:T(8,128)}, f32[6,4096]{1,0:T(8,128)S(1)}, u32[]{:S(2)}, u32[]{:S(2)}) %collective-permute-start) | collective-permute-done | bytes 98336 | tf_op jit(solution)/shard_map/ppermute | solution.py:26
  7.4 0.0 collective-permute-start.1
  7.4 1.0 stack.51
  8.3 0.1 copy.23
  8.5 0.0 collective-permute-done.2
  8.5 0.1 stack.54
  8.5 5.0 %collective-permute-done.1 = f32[6,4096]{1,0:T(8,128)S(1)} collective-permute-done((f32[6,4096]{1,0:T(8,128)S(1)}, f32[6,4096]{1,0:T(8,128)S(1)}, u32[]{:S(2)}, u32[]{:S(2)}) %collective-permute-start.1) | collective-permute-done | bytes 98336 | tf_op jit(solution)/shard_map/ppermute | solution.py:26
  13.5 0.1 stack.53
  13.6 0.4 pad_maximum_fusion.1
  14.0 5.9 %collective-permute-start.3 = (f32[4,6,4096]{2,0,1:T(4,128)S(1)}, f32[4,6,4096]{2,0,1:T(4,128)S(1)}, u32[]{:S(2)}, u32[]{:S(2)}) collective-permute-start(f32[4,6,4096]{2,0,1:T(4,128)S(1)} %pad_maximum_fusion.1), channel_id=1, source_target_pairs={{0,224},{4,228},{8,232},{12,236},{16,240},{20,244},{24,248},{28,25... | collective-permute-start | bytes 1179656 | tf_op jit(solution)/shard_map/ppermute | solution.py:26
  19.9 0.0 collective-permute-start.7
  20.0 0.4 bitcast_dynamic-update-slice_fusion.7
  20.3 6.0 %collective-permute-done.3 = f32[4,6,4096]{2,0,1:T(4,128)S(1)} collective-permute-done((f32[4,6,4096]{2,0,1:T(4,128)S(1)}, f32[4,6,4096]{2,0,1:T(4,128)S(1)}, u32[]{:S(2)}, u32[]{:S(2)}) %collective-permute-start.3) | collective-permute-done | bytes 393248 | tf_op jit(solution)/shard_map/ppermute | solution.py:26
  26.3 3.7 %collective-permute-start.4 = (f32[4,6,4096]{2,0,1:T(4,128)S(1)}, f32[4,6,4096]{2,0,1:T(4,128)S(1)}, u32[]{:S(2)}, u32[]{:S(2)}) collective-permute-start(f32[4,6,4096]{2,0,1:T(4,128)S(1)} %collective-permute-done.3), channel_id=1, source_target_pairs={{0,224},{4,228},{8,232},{12,236},{16,240},{20,244},{24,248},{28,25... | collective-permute-start | bytes 1179656 | tf_op jit(solution)/shard_map/ppermute | solution.py:26
  30.0 0.0 collective-permute-done.7
  30.0 0.0 collective-permute-start.8
  30.0 0.1 bitcast_dynamic-update-slice_fusion.6
  30.1 5.5 %collective-permute-done.4 = f32[4,6,4096]{2,0,1:T(4,128)S(1)} collective-permute-done((f32[4,6,4096]{2,0,1:T(4,128)S(1)}, f32[4,6,4096]{2,0,1:T(4,128)S(1)}, u32[]{:S(2)}, u32[]{:S(2)}) %collective-permute-start.4) | collective-permute-done | bytes 393248 | tf_op jit(solution)/shard_map/ppermute | solution.py:26
  35.6 3.7 %collective-permute-start.5 = (f32[4,6,4096]{2,0,1:T(4,128)S(1)}, f32[4,6,4096]{2,0,1:T(4,128)S(1)}, u32[]{:S(2)}, u32[]{:S(2)}) collective-permute-start(f32[4,6,4096]{2,0,1:T(4,128)S(1)} %collective-permute-done.4), channel_id=1, source_target_pairs={{0,224},{4,228},{8,232},{12,236},{16,240},{20,244},{24,248},{28,25... | collective-permute-start | bytes 1179656 | tf_op jit(solution)/shard_map/ppermute | solution.py:26
  39.3 0.0 collective-permute-done.8
  39.3 0.0 collective-permute-start.9
  39.3 0.1 bitcast_dynamic-update-slice_fusion.5
  39.4 6.5 %collective-permute-done.5 = f32[4,6,4096]{2,0,1:T(4,128)S(1)} collective-permute-done((f32[4,6,4096]{2,0,1:T(4,128)S(1)}, f32[4,6,4096]{2,0,1:T(4,128)S(1)}, u32[]{:S(2)}, u32[]{:S(2)}) %collective-permute-start.5) | collective-permute-done | bytes 393248 | tf_op jit(solution)/shard_map/ppermute | solution.py:26
  45.8 3.7 %collective-permute-start.6 = (f32[4,6,4096]{2,0,1:T(4,128)S(1)}, f32[4,6,4096]{2,0,1:T(4,128)S(1)}, u32[]{:S(2)}, u32[]{:S(2)}) collective-permute-start(f32[4,6,4096]{2,0,1:T(4,128)S(1)} %collective-permute-done.5), channel_id=1, source_target_pairs={{0,224},{4,228},{8,232},{12,236},{16,240},{20,244},{24,248},{28,25... | collective-permute-start | bytes 1179656 | tf_op jit(solution)/shard_map/ppermute | solution.py:26
  49.5 0.1 bitcast_dynamic-update-slice_fusion.4
  49.6 5.2 %collective-permute-done.6 = f32[4,6,4096]{2,0,1:T(4,128)S(1)} collective-permute-done((f32[4,6,4096]{2,0,1:T(4,128)S(1)}, f32[4,6,4096]{2,0,1:T(4,128)S(1)}, u32[]{:S(2)}, u32[]{:S(2)}) %collective-permute-start.6) | collective-permute-done | bytes 393248 | tf_op jit(solution)/shard_map/ppermute | solution.py:26
  54.8 0.1 bitcast_dynamic-update-slice_fusion.3
  54.9 0.0 collective-permute-done.9
  54.9 0.1 bitcast_dynamic-update-slice_fusion.2
  54.9 0.1 bitcast_dynamic-update-slice_fusion.1
  55.0 0.1 bitcast_dynamic-update-slice_fusion
  55.0 0.0 copy-start.3
  55.1 0.0 copy-start.4
  55.1 0.0 copy-start.5
  55.1 3.5 %copy.24 = f32[8,4,6,4096]{3,0,2,1:T(8,128)} copy(f32[8,4,6,4096]{3,1,2,0:T(4,128)S(1)} %bitcast_dynamic-update-slice_fusion) | data formatting | bytes 6291456 | tf_op jit(solution)/shard_map/stack | solution.py:31
  58.6 0.0 collective-permute-start.10
  59.2 0.1 reshape.321
  59.3 0.5 broadcast.324
  59.8 0.7 reduce.7
  60.5 0.1 reshape.320
  60.6 0.1 convert_multiply_fusion.2
  60.7 0.1 copy.28
  60.7 0.1 fusion.12
  60.8 13.3 %convert_multiply_fusion.1 = (f32[16,36,4096]{2,0,1:T(8,128)}, f32[16,36,4096]{2,0,1:T(8,128)}) fusion(bf16[16,36,4096]{2,0,1:T(8,128)(2,1)} %param.8, f32[16,36]{0,1:T(8,128)S(1)} %copy.28, bf16[16,36,4096]{2,0,1:T(8,128)(2,1)} %param.9), kind=kLoop, calls=%fused_computation.4 | loop fusion | flops 9437184 | bytes 28313856 | tf_op jit(solution)/shard_map/mul | solution.py:71
  74.1 0.0 collective-permute-done.10
  74.1 3.9 %copy.44 = f32[8,4,6,4096]{3,1,2,0:T(4,128)S(1)} copy(f32[8,4,6,4096]{3,0,2,1:T(8,128)} %collective-permute-done.10) | data formatting | bytes 6291456 | tf_op jit(solution)/shard_map/ppermute | solution.py:35
  78.0 2.3 %pad_maximum_fusion = f32[2,8,4,6,4096]{4,2,3,1,0:T(4,128)S(1)} fusion(f32[1,8,4,6,4096]{4,2,3,1,0:T(4,128)S(1)} %bitcast.61, f32[1,8,4,6,4096]{4,2,3,1,0:T(4,128)S(1)} %bitcast.60), kind=kLoop, calls=%fused_computation.5 | loop fusion | flops 1572864 | bytes 12582912 | tf_op jit(solution)/shard_map/stack | solution.py:36
  80.3 3.0 %copy.26 = f32[2,8,4,6,4096]{4,2,1,0,3:T(4,128)} copy(f32[2,8,4,6,4096]{4,2,3,1,0:T(4,128)S(1)} %pad_maximum_fusion) | data formatting | bytes 12582912 | tf_op jit(solution)/shard_map/stack | solution.py:36
  83.3 8.4 %reshape.319 = f32[64,6,32,128]{3,2,0,1:T(8,128)} reshape(f32[2,8,4,6,4096]{4,2,1,0,3:T(4,128)} %copy.26) | data formatting | bytes 12582912 | tf_op jit(solution)/shard_map/reshape | solution.py:50
  91.8 12.1 %copy.27 = f32[64,6,32,128]{3,1,2,0:T(8,128)} copy(f32[64,6,32,128]{3,2,0,1:T(8,128)} %reshape.319) | data formatting | bytes 12582912 | tf_op jit(solution)/shard_map/reshape | solution.py:50
  103.9 5.9 %gather_fusion = f32[512,6,128]{2,1,0:T(8,128)S(1)} fusion(f32[64,6,32,128]{3,1,2,0:T(8,128)} %copy.27, s32[512]{0:T(512)S(1)} %bitcast.57), kind=kCustom, calls=%fused_computation | custom fusion | bytes 3149824 | tf_op jit(solution)/shard_map/gather | solution.py:63
  109.8 2.1 %copy.41 = f32[4096,6,16]{0,2,1:T(8,128)} copy(f32[4096,6,16]{0,1,2:T(8,128)S(1)} %bitcast.58) | data formatting | bytes 3145728
  111.9 0.2 subtract_bitcast_fusion
  112.1 0.9 copy.42
  113.0 0.5 copy-done
  113.5 9.4 %multiply_reduce_fusion = (f32[4096,6]{0,1:T(8,128)S(1)}, f32[4096,6]{0,1:T(8,128)S(1)}) fusion(f32[4096,6,16,6]{0,2,1,3:T(8,128)} %bitcast.56, f32[4096,6,16]{0,2,1:T(8,128)S(1)} %copy.42, f32[4096,6,16,6]{0,2,1,3:T(8,128)} %bitcast.55, f32[4096,6,16]{0,2,1:T(8,128)S(1)} %copy-done), kind=kLoop, calls=%fused_computation.1 | loop fusion | flops 9388032 | bytes 22216704 | tf_op jit(solution)/shard_map/smnk,snk->mk/dot_general | solution.py:78
  122.9 0.0 copy-done.1
  122.9 0.7 fusion
  123.6 4.3 %all-to-all-start = ((f32[4,6,1024]{2,1,0:T(8,128)}), f32[4,6,1024]{2,1,0:T(8,128)S(1)}, u32[]{:S(2)}, u32[]{:S(2)}) async-start(f32[4,6,1024]{2,1,0:T(8,128)} %bitcast.30), calls=%async_computation | async-start | bytes 262144 | tf_op jit(solution)/shard_map/all_to_all | solution.py:82
  127.8 6.0 %all-to-all-done = f32[4,6,1024]{2,1,0:T(8,128)S(1)} async-done(((f32[4,6,1024]{2,1,0:T(8,128)}), f32[4,6,1024]{2,1,0:T(8,128)S(1)}, u32[]{:S(2)}, u32[]{:S(2)}) %all-to-all-start) | async-done | bytes 98336 | tf_op jit(solution)/shard_map/all_to_all | solution.py:82
  133.8 0.0 copy-start.2
  133.9 0.6 multiply_add_fusion
  (8 shorter events, 0.0 us)
Async XLA Ops:
  0.6 6.7 %collective-permute-start = (f32[6,4096]{1,0:T(8,128)}, f32[6,4096]{1,0:T(8,128)S(1)}, u32[]{:S(2)}, u32[]{:S(2)}) collective-permute-start(f32[6,4096]{1,0:T(8,128)} %param.7), channel_id=1, source_target_pairs={{0,24},{4,28},{8,0},{12,4},{16,8},{20,12},{24,16},{28,20},{32,56},... | collective-permute-start | bytes 294920 | tf_op jit(solution)/shard_map/ppermute | solution.py:26
  1.4 7.0 %collective-permute-start.2 = (f32[6,4096]{1,0:T(8,128)}, f32[6,4096]{1,0:T(8,128)S(1)}, u32[]{:S(2)}, u32[]{:S(2)}) collective-permute-start(f32[6,4096]{1,0:T(8,128)} %param.7), channel_id=1, source_target_pairs={{0,8},{4,12},{8,16},{12,20},{16,24},{20,28},{24,0},{28,4},{32,40},... | collective-permute-start | bytes 294920 | tf_op jit(solution)/shard_map/ppermute | solution.py:29
  7.4 6.2 %collective-permute-start.1 = (f32[6,4096]{1,0:T(8,128)S(1)}, f32[6,4096]{1,0:T(8,128)S(1)}, u32[]{:S(2)}, u32[]{:S(2)}) collective-permute-start(f32[6,4096]{1,0:T(8,128)S(1)} %collective-permute-done), channel_id=1, source_target_pairs={{0,24},{4,28},{8,0},{12,4},{16,8},{20,12},{24,16},{28,20},{32,56},... | collective-permute-start | bytes 294920 | tf_op jit(solution)/shard_map/ppermute | solution.py:26
  14.0 12.3 %collective-permute-start.3 = (f32[4,6,4096]{2,0,1:T(4,128)S(1)}, f32[4,6,4096]{2,0,1:T(4,128)S(1)}, u32[]{:S(2)}, u32[]{:S(2)}) collective-permute-start(f32[4,6,4096]{2,0,1:T(4,128)S(1)} %pad_maximum_fusion.1), channel_id=1, source_target_pairs={{0,224},{4,228},{8,232},{12,236},{16,240},{20,244},{24,248},{28,25... | collective-permute-start | bytes 1179656 | tf_op jit(solution)/shard_map/ppermute | solution.py:26
  19.9 10.0 %collective-permute-start.7 = (f32[4,6,4096]{2,0,1:T(4,128)S(1)}, f32[4,6,4096]{2,0,1:T(4,128)S(1)}, u32[]{:S(2)}, u32[]{:S(2)}) collective-permute-start(f32[4,6,4096]{2,0,1:T(4,128)S(1)} %pad_maximum_fusion.1), channel_id=1, source_target_pairs={{0,32},{4,36},{8,40},{12,44},{16,48},{20,52},{24,56},{28,60},{32,6... | collective-permute-start | bytes 1179656 | tf_op jit(solution)/shard_map/ppermute | solution.py:29
  26.3 9.3 %collective-permute-start.4 = (f32[4,6,4096]{2,0,1:T(4,128)S(1)}, f32[4,6,4096]{2,0,1:T(4,128)S(1)}, u32[]{:S(2)}, u32[]{:S(2)}) collective-permute-start(f32[4,6,4096]{2,0,1:T(4,128)S(1)} %collective-permute-done.3), channel_id=1, source_target_pairs={{0,224},{4,228},{8,232},{12,236},{16,240},{20,244},{24,248},{28,25... | collective-permute-start | bytes 1179656 | tf_op jit(solution)/shard_map/ppermute | solution.py:26
  30.0 9.3 %collective-permute-start.8 = (f32[4,6,4096]{2,0,1:T(4,128)S(1)}, f32[4,6,4096]{2,0,1:T(4,128)S(1)}, u32[]{:S(2)}, u32[]{:S(2)}) collective-permute-start(f32[4,6,4096]{2,0,1:T(4,128)S(1)} %collective-permute-done.7), channel_id=1, source_target_pairs={{0,32},{4,36},{8,40},{12,44},{16,48},{20,52},{24,56},{28,60},{32,6... | collective-permute-start | bytes 1179656 | tf_op jit(solution)/shard_map/ppermute | solution.py:29
  35.6 10.2 %collective-permute-start.5 = (f32[4,6,4096]{2,0,1:T(4,128)S(1)}, f32[4,6,4096]{2,0,1:T(4,128)S(1)}, u32[]{:S(2)}, u32[]{:S(2)}) collective-permute-start(f32[4,6,4096]{2,0,1:T(4,128)S(1)} %collective-permute-done.4), channel_id=1, source_target_pairs={{0,224},{4,228},{8,232},{12,236},{16,240},{20,244},{24,248},{28,25... | collective-permute-start | bytes 1179656 | tf_op jit(solution)/shard_map/ppermute | solution.py:26
  39.3 15.6 %collective-permute-start.9 = (f32[4,6,4096]{2,0,1:T(4,128)S(1)}, f32[4,6,4096]{2,0,1:T(4,128)S(1)}, u32[]{:S(2)}, u32[]{:S(2)}) collective-permute-start(f32[4,6,4096]{2,0,1:T(4,128)S(1)} %collective-permute-done.8), channel_id=1, source_target_pairs={{0,32},{4,36},{8,40},{12,44},{16,48},{20,52},{24,56},{28,60},{32,6... | collective-permute-start | bytes 1179656 | tf_op jit(solution)/shard_map/ppermute | solution.py:29
  45.8 9.0 %collective-permute-start.6 = (f32[4,6,4096]{2,0,1:T(4,128)S(1)}, f32[4,6,4096]{2,0,1:T(4,128)S(1)}, u32[]{:S(2)}, u32[]{:S(2)}) collective-permute-start(f32[4,6,4096]{2,0,1:T(4,128)S(1)} %collective-permute-done.5), channel_id=1, source_target_pairs={{0,224},{4,228},{8,232},{12,236},{16,240},{20,244},{24,248},{28,25... | collective-permute-start | bytes 1179656 | tf_op jit(solution)/shard_map/ppermute | solution.py:26
  55.0 4.2 %copy-start.3 = (s32[1,1,16,32]{3,2,1,0:T(8,128)S(1)}, s32[1,1,16,32]{3,2,1,0:T(8,128)}, u32[]{:S(2)}) copy-start(s32[1,1,16,32]{3,2,1,0:T(8,128)} %param.11) | copy-start | bytes 6148
  55.1 4.8 %copy-start.4 = (s32[1,1,16,32,1]{3,4,2,1,0:T(1,128)S(1)}, s32[1,1,16,32,1]{3,4,2,1,0:T(1,128)}, u32[]{:S(2)}) copy-start(s32[1,1,16,32,1]{3,4,2,1,0:T(1,128)} %param.10) | copy-start | bytes 6148
  55.1 5.5 %copy-start.5 = (s32[16,36]{1,0:T(8,128)S(1)}, s32[16,36]{1,0:T(8,128)}, u32[]{:S(2)}) copy-start(s32[16,36]{1,0:T(8,128)} %param.12) | copy-start | bytes 6916
  58.6 15.5 %collective-permute-start.10 = (f32[8,4,6,4096]{3,0,2,1:T(8,128)}, f32[8,4,6,4096]{3,0,2,1:T(8,128)}, u32[]{:S(2)}, u32[]{:S(2)}) collective-permute-start(f32[8,4,6,4096]{3,0,2,1:T(8,128)} %copy.24), channel_id=1, source_target_pairs={{0,4},{4,0},{8,12},{12,8},{16,20},{20,16},{24,28},{28,24},{32,36},... | collective-permute-start | bytes 9437192 | tf_op jit(solution)/shard_map/ppermute | solution.py:35
  112.1 1.4 %copy-start = (f32[4096,6,16]{0,2,1:T(8,128)S(1)}, f32[4096,6,16]{0,2,1:T(8,128)}, u32[]{:S(2)}) copy-start(f32[4096,6,16]{0,2,1:T(8,128)} %copy.41) | copy-start | bytes 4718596
  113.5 9.4 %copy-start.1 = (f32[6,4096]{1,0:T(8,128)S(1)}, f32[6,4096]{1,0:T(8,128)}, u32[]{:S(2)}) copy-start(f32[6,4096]{1,0:T(8,128)} %param.7) | copy-start | bytes 294916
  123.6 10.3 %all-to-all-start = ((f32[4,6,1024]{2,1,0:T(8,128)}), f32[4,6,1024]{2,1,0:T(8,128)S(1)}, u32[]{:S(2)}, u32[]{:S(2)}) async-start(f32[4,6,1024]{2,1,0:T(8,128)} %bitcast.30), calls=%async_computation | async-start | bytes 262144 | tf_op jit(solution)/shard_map/all_to_all | solution.py:82
  133.8 0.6 copy-start.2

commit v3 on v2

--- a/solution.py
+++ b/solution.py
@@ -1,9 +1,63 @@
+import functools
+
 import jax
 import jax.numpy as jnp
+import numpy as np
 from jax import lax
+from jax.experimental import pallas as pl
+from jax.experimental.pallas import tpu as pltpu
 from jax.sharding import PartitionSpec as P
 
 half_step = 0.5
+HI = lax.Precision.HIGHEST
+
+
+def collide_kernel(idx_ref, g_ref, e_ref, f_ref, gain_ref, loss_ref, occ_ref, out_ref, *, shifts, nsub, sub_count, lanes):
+    t = pl.program_id(0)
+    pairs = gain_ref.shape[1]
+
+    def step(s, carry):
+        acc_i, acc_o = carry
+        base = s * sub_count + t * nsub
+        sh = jnp.concatenate([g_ref[idx_ref[base + jj]] for jj in range(nsub)], axis=1)
+        both = jnp.concatenate([sh, 1.0 - sh], axis=1)
+        spread = jnp.dot(e_ref[s], both, precision=HI, preferred_element_type=jnp.float32)
+        acc_i = acc_i + gain_ref[s].astype(jnp.float32) * spread[:, :lanes]
+        acc_o = acc_o + loss_ref[s].astype(jnp.float32) * spread[:, lanes:]
+        return acc_i, acc_o
+
+    zero = jnp.zeros((pairs, lanes), jnp.float32)
+    acc_i, acc_o = lax.fori_loop(0, shifts, step, (zero, zero))
+    inflow = jnp.dot(f_ref[...], acc_i, precision=HI, preferred_element_type=jnp.float32)
+    outflow = jnp.dot(f_ref[...], acc_o, precision=HI, preferred_element_type=jnp.float32)
+    occ = occ_ref[...]
+    out_ref[...] = (1.0 - occ) * inflow - occ * outflow
+
+
+def collide(idx, blocks, spread_w, fold, gain, loss, occ, lanes=512):
+    shifts, pairs, width = gain.shape
+    bands = occ.shape[0]
+    sub_width = blocks.shape[2]
+    sub_count = width // sub_width
+    nsub = lanes // sub_width
+    kern = functools.partial(collide_kernel, shifts=shifts, nsub=nsub, sub_count=sub_count, lanes=lanes)
+    return pl.pallas_call(
+        kern,
+        out_shape=jax.ShapeDtypeStruct((bands, width), jnp.float32),
+        grid_spec=pltpu.PrefetchScalarGridSpec(
+            num_scalar_prefetch=1,
+            grid=(width // lanes,),
+            in_specs=[
+                pl.BlockSpec(blocks.shape, lambda t, i: (0, 0, 0)),
+                pl.BlockSpec(spread_w.shape, lambda t, i: (0, 0, 0)),
+                pl.BlockSpec(fold.shape, lambda t, i: (0, 0)),
+                pl.BlockSpec((shifts, pairs, lanes), lambda t, i: (0, 0, t)),
+                pl.BlockSpec((shifts, pairs, lanes), lambda t, i: (0, 0, t)),
+                pl.BlockSpec((bands, lanes), lambda t, i: (0, t)),
+            ],
+            out_specs=pl.BlockSpec((bands, lanes), lambda t, i: (0, t)),
+        ),
+    )(idx, blocks, spread_w, fold, gain, loss, occ)
 
 
 def ring_gather(block, y_count, z_count):
@@ -60,23 +114,19 @@
         + (o_y - my_y) % y_count
     )
     sources = local_index.reshape(total_requests)
-    picked = gathered[where, :, sources, :]
-    shifted = (
-        picked.reshape(shifts, sub_count, bands, sub_width)
-        .transpose(0, 2, 1, 3)
-        .reshape(shifts, bands, width)
+    blocks = (
+        gathered.transpose(0, 2, 1, 3).reshape(ka_count * sub_count, bands, sub_width)
     )
+    picks = where * sub_count + sources
     active = (jnp.arange(shifts, dtype=jnp.int32) < counts.reshape(())).astype(jnp.float32)
     weight = pair_mask.astype(jnp.float32) * active[:, None]
-    gain_four = (gain_table.astype(jnp.float32) * weight[:, :, None]).reshape(
-        shifts, bands, bands, width
+    pair = np.arange(bands * bands)
+    spread = (pair[:, None] % bands == np.arange(bands)[None, :]).astype(np.float32)
+    fold = (pair[None, :] // bands == np.arange(bands)[:, None]).astype(np.float32)
+    spread_w = jnp.asarray(spread)[None] * weight[:, :, None]
+    partial_terms = collide(
+        picks, blocks, spread_w, jnp.asarray(fold), gain_table, loss_table, occupation
     )
-    loss_four = (loss_table.astype(jnp.float32) * weight[:, :, None]).reshape(
-        shifts, bands, bands, width
-    )
-    inflow = jnp.einsum("smnk,snk->mk", gain_four, shifted)
-    outflow = jnp.einsum("smnk,snk->mk", loss_four, 1.0 - shifted)
-    partial_terms = (1.0 - occupation) * inflow - occupation * outflow
     share_width = width // pb_count
     parts = partial_terms.reshape(bands, pb_count, share_width).transpose(1, 0, 2)
     collision = jnp.sum(lax.all_to_all(parts, "pb", 0, 0, tiled=True), axis=0)

time: 135 us -> 161 us (1.19)
  Pallas kernels: 0 us -> 42.7 us
  other arithmetic: 28.1 us -> 6.72 us
  local copies, waits for them, and re-layouts: 42.7 us -> 47.6 us
    pallas_call x0 -> x1, Pallas kernels: none -> 42.7 us  [collide(): pl.pallas_call(kern, out_shape=jax.ShapeDtypeStruct((bands, width), jnp.f...]
    mul x1, other arithmetic: 13.3 us -> 0.88 us  [body(): spread_w = jnp.asarray(spread)[None] * weight[:, :, None]]
    reshape x2 -> x1, local copies, waits for them, and re-layouts: 20.6 us -> 8.44 us  [body(): ring_gather(occupation, y_count, z_count)]
    transpose x0 -> x1, local copies, waits for them, and re-layouts: none -> 12 us  [body(): gathered.transpose(0, 2, 1, 3)]
    unnamed x21 -> x19, local copies, waits for them, and re-layouts: 4.33 us -> 15.3 us
    dot_general x1 -> x0, other arithmetic: 9.4 us -> none  [body(): outflow = jnp.einsum('smnk,snk->mk', loss_four, 1.0 - shifted)]
    gather x1 -> x0, local copies, waits for them, and re-layouts: 5.85 us -> none  [body(): picked = gathered[where, :, sources, :]]
where the time goes in v3:
time: 161 us
  local copies, waits for them, and re-layouts  47.6 us (30%)
  Pallas kernels  42.7 us (27%)
  waiting for transfers between devices  37.6 us (23%)
  starting transfers between devices  24.6 us (15%)
  other arithmetic  6.72 us (4%)
    pallas_call x1, Pallas kernels, collide(): pl.pallas_call(kern, out_shape=jax.ShapeDtypeStruct((bands, width), jnp.f...  42.7 us
    ppermute x6, waiting for transfers between devices, ring(): back = lax.ppermute(back, 'ka', step(-1))  31.6 us
    ppermute x6, starting transfers between devices, ring(): back = lax.ppermute(back, 'ka', step(-1))  17.8 us
    unnamed x19, local copies, waits for them, and re-layouts  15.3 us
    transpose x1, local copies, waits for them, and re-layouts, body(): gathered.transpose(0, 2, 1, 3)  12 us
    reshape x1, local copies, waits for them, and re-layouts, body(): ring_gather(occupation, y_count, z_count)  8.44 us
    all_to_all x1, waiting for transfers between devices, body(): collision = jnp.sum(lax.all_to_all(parts, 'pb', 0, 0, tiled=True), axis=0)  5.98 us
    another operation x6, local copies, waits for them, and re-layouts, ring(): return jnp.stack([ahead[d] for d in range(count)])  4.72 us
  transfers between devices with their start and end apart: 12, of which 7 were waited for; matrix products, arithmetic and copies ran while one was open for 12% of the time, Pallas kernels for 0%

profile of v3, /device:TPU:24, one launch (start us, length us, event | category | flops | bytes accessed | tf_op | source)
XLA Modules:
  0.0 160.7 jit_solution(11136454715444401260)
XLA Ops:
  0.6 0.8 collective-permute-start
  1.4 2.5 %collective-permute-start.2 = (f32[6,4096]{1,0:T(8,128)}, f32[6,4096]{1,0:T(8,128)S(1)}, u32[]{:S(2)}, u32[]{:S(2)}) collective-permute-start(f32[6,4096]{1,0:T(8,128)} %occ_ref.1), channel_id=1, source_target_pairs={{0,8},{4,12},{8,16},{12,20},{16,24},{20,28},{24,0},{28,4},{32,40},... | collective-permute-start | bytes 294920 | tf_op jit(solution)/shard_map/ppermute | solution.py:83
  3.9 3.4 %collective-permute-done = f32[6,4096]{1,0:T(8,128)S(1)} collective-permute-done((f32[6,4096]{1,0:T(8,128)}, f32[6,4096]{1,0:T(8,128)S(1)}, u32[]{:S(2)}, u32[]{:S(2)}) %collective-permute-start) | collective-permute-done | bytes 98336 | tf_op jit(solution)/shard_map/ppermute | solution.py:80
  7.4 0.0 collective-permute-start.1
  7.4 1.0 stack.51
  8.3 0.1 copy.30
  8.5 0.0 collective-permute-done.2
  8.5 0.1 stack.54
  8.5 5.0 %collective-permute-done.1 = f32[6,4096]{1,0:T(8,128)S(1)} collective-permute-done((f32[6,4096]{1,0:T(8,128)S(1)}, f32[6,4096]{1,0:T(8,128)S(1)}, u32[]{:S(2)}, u32[]{:S(2)}) %collective-permute-start.1) | collective-permute-done | bytes 98336 | tf_op jit(solution)/shard_map/ppermute | solution.py:80
  13.5 0.1 stack.53
  13.6 0.4 pad_maximum_fusion.1
  14.0 5.9 %collective-permute-start.3 = (f32[4,6,4096]{2,0,1:T(4,128)S(1)}, f32[4,6,4096]{2,0,1:T(4,128)S(1)}, u32[]{:S(2)}, u32[]{:S(2)}) collective-permute-start(f32[4,6,4096]{2,0,1:T(4,128)S(1)} %pad_maximum_fusion.1), channel_id=1, source_target_pairs={{0,224},{4,228},{8,232},{12,236},{16,240},{20,244},{24,248},{28,25... | collective-permute-start | bytes 1179656 | tf_op jit(solution)/shard_map/ppermute | solution.py:80
  19.9 0.0 collective-permute-start.7
  20.0 0.4 bitcast_dynamic-update-slice_fusion.7
  20.3 6.0 %collective-permute-done.3 = f32[4,6,4096]{2,0,1:T(4,128)S(1)} collective-permute-done((f32[4,6,4096]{2,0,1:T(4,128)S(1)}, f32[4,6,4096]{2,0,1:T(4,128)S(1)}, u32[]{:S(2)}, u32[]{:S(2)}) %collective-permute-start.3) | collective-permute-done | bytes 393248 | tf_op jit(solution)/shard_map/ppermute | solution.py:80
  26.3 3.7 %collective-permute-start.4 = (f32[4,6,4096]{2,0,1:T(4,128)S(1)}, f32[4,6,4096]{2,0,1:T(4,128)S(1)}, u32[]{:S(2)}, u32[]{:S(2)}) collective-permute-start(f32[4,6,4096]{2,0,1:T(4,128)S(1)} %collective-permute-done.3), channel_id=1, source_target_pairs={{0,224},{4,228},{8,232},{12,236},{16,240},{20,244},{24,248},{28,25... | collective-permute-start | bytes 1179656 | tf_op jit(solution)/shard_map/ppermute | solution.py:80
  30.0 0.0 collective-permute-done.7
  30.0 0.0 collective-permute-start.8
  30.0 0.1 bitcast_dynamic-update-slice_fusion.6
  30.1 5.5 %collective-permute-done.4 = f32[4,6,4096]{2,0,1:T(4,128)S(1)} collective-permute-done((f32[4,6,4096]{2,0,1:T(4,128)S(1)}, f32[4,6,4096]{2,0,1:T(4,128)S(1)}, u32[]{:S(2)}, u32[]{:S(2)}) %collective-permute-start.4) | collective-permute-done | bytes 393248 | tf_op jit(solution)/shard_map/ppermute | solution.py:80
  35.6 3.7 %collective-permute-start.5 = (f32[4,6,4096]{2,0,1:T(4,128)S(1)}, f32[4,6,4096]{2,0,1:T(4,128)S(1)}, u32[]{:S(2)}, u32[]{:S(2)}) collective-permute-start(f32[4,6,4096]{2,0,1:T(4,128)S(1)} %collective-permute-done.4), channel_id=1, source_target_pairs={{0,224},{4,228},{8,232},{12,236},{16,240},{20,244},{24,248},{28,25... | collective-permute-start | bytes 1179656 | tf_op jit(solution)/shard_map/ppermute | solution.py:80
  39.3 0.0 collective-permute-done.8
  39.3 0.0 collective-permute-start.9
  39.3 0.1 bitcast_dynamic-update-slice_fusion.5
  39.4 6.5 %collective-permute-done.5 = f32[4,6,4096]{2,0,1:T(4,128)S(1)} collective-permute-done((f32[4,6,4096]{2,0,1:T(4,128)S(1)}, f32[4,6,4096]{2,0,1:T(4,128)S(1)}, u32[]{:S(2)}, u32[]{:S(2)}) %collective-permute-start.5) | collective-permute-done | bytes 393248 | tf_op jit(solution)/shard_map/ppermute | solution.py:80
  45.8 3.7 %collective-permute-start.6 = (f32[4,6,4096]{2,0,1:T(4,128)S(1)}, f32[4,6,4096]{2,0,1:T(4,128)S(1)}, u32[]{:S(2)}, u32[]{:S(2)}) collective-permute-start(f32[4,6,4096]{2,0,1:T(4,128)S(1)} %collective-permute-done.5), channel_id=1, source_target_pairs={{0,224},{4,228},{8,232},{12,236},{16,240},{20,244},{24,248},{28,25... | collective-permute-start | bytes 1179656 | tf_op jit(solution)/shard_map/ppermute | solution.py:80
  49.5 0.1 bitcast_dynamic-update-slice_fusion.4
  49.6 5.2 %collective-permute-done.6 = f32[4,6,4096]{2,0,1:T(4,128)S(1)} collective-permute-done((f32[4,6,4096]{2,0,1:T(4,128)S(1)}, f32[4,6,4096]{2,0,1:T(4,128)S(1)}, u32[]{:S(2)}, u32[]{:S(2)}) %collective-permute-start.6) | collective-permute-done | bytes 393248 | tf_op jit(solution)/shard_map/ppermute | solution.py:80
  54.8 0.1 bitcast_dynamic-update-slice_fusion.3
  54.9 0.0 collective-permute-done.9
  54.9 0.1 bitcast_dynamic-update-slice_fusion.2
  54.9 0.1 bitcast_dynamic-update-slice_fusion.1
  55.0 0.1 bitcast_dynamic-update-slice_fusion
  55.0 0.0 copy-start.2
  55.1 0.0 copy-start.3
  55.1 3.4 %copy.31 = f32[8,4,6,4096]{3,0,2,1:T(8,128)} copy(f32[8,4,6,4096]{3,1,2,0:T(4,128)S(1)} %bitcast_dynamic-update-slice_fusion) | data formatting | bytes 6291456 | tf_op jit(solution)/shard_map/stack | solution.py:85
  58.5 0.0 collective-permute-start.10
  59.2 0.0 copy-done.2
  59.2 0.1 reshape.30
  59.3 0.5 broadcast.45
  59.8 0.0 copy-done.3
  59.8 0.7 reduce.3
  60.5 0.1 reshape.29
  60.5 7.2 %copy.35.gain_ref = bf16[16,36,4096]{2,1,0:T(8,128)(2,1)} copy(bf16[16,36,4096]{2,0,1:T(8,128)(2,1)} %param.10) | data formatting | bytes 9437184 | tf_op args[1]
  67.8 0.0 copy-start.4
  67.8 0.0 copy-start.1
  67.8 7.3 %copy.36.loss_ref = bf16[16,36,4096]{2,1,0:T(8,128)(2,1)} copy(bf16[16,36,4096]{2,0,1:T(8,128)(2,1)} %param.11) | data formatting | bytes 9437184 | tf_op args[2]
  75.0 0.6 fusion.5.idx_ref
  75.6 0.0 copy-done.4
  75.6 0.1 convert_multiply_fusion
  75.7 0.0 copy-done.1
  75.7 0.9 broadcast_multiply_fusion.e_ref
  76.6 0.0 collective-permute-done.10
  76.6 3.9 %copy.39 = f32[8,4,6,4096]{3,1,2,0:T(4,128)S(1)} copy(f32[8,4,6,4096]{3,0,2,1:T(8,128)} %collective-permute-done.10) | data formatting | bytes 6291456 | tf_op jit(solution)/shard_map/ppermute | solution.py:89
  80.5 2.3 %pad_maximum_fusion = f32[2,8,4,6,4096]{4,2,3,1,0:T(4,128)S(1)} fusion(f32[1,8,4,6,4096]{4,2,3,1,0:T(4,128)S(1)} %bitcast.36, f32[1,8,4,6,4096]{4,2,3,1,0:T(4,128)S(1)} %bitcast.35), kind=kLoop, calls=%fused_computation | loop fusion | flops 1572864 | bytes 12582912 | tf_op jit(solution)/shard_map/stack | solution.py:90
  82.8 3.1 %copy.33 = f32[2,8,4,6,4096]{4,2,1,0,3:T(4,128)} copy(f32[2,8,4,6,4096]{4,2,3,1,0:T(4,128)S(1)} %pad_maximum_fusion) | data formatting | bytes 12582912 | tf_op jit(solution)/shard_map/stack | solution.py:90
  85.9 8.4 %reshape.31 = f32[64,6,32,128]{3,2,0,1:T(8,128)} reshape(f32[2,8,4,6,4096]{4,2,1,0,3:T(4,128)} %copy.33) | data formatting | bytes 12582912 | tf_op jit(solution)/shard_map/reshape | solution.py:104
  94.3 12.0 %copy.34 = f32[64,32,6,128]{3,2,1,0:T(8,128)} copy(f32[64,32,6,128]{3,1,0,2:T(8,128)} %bitcast.34) | data formatting | bytes 12582912 | tf_op jit(solution)/shard_map/transpose | solution.py:118
  106.3 42.7 %shard_map.104 = f32[6,4096]{1,0:T(8,128)} custom-call(s32[512]{0:T(512)} %fusion.5.idx_ref, f32[2048,6,128]{2,1,0:T(8,128)} %bitcast.33, f32[16,36,6]{2,1,0:T(8,128)} %broadcast_multiply_fusion.e_ref, f32[6,36]{1,0:T(8,128)} %constant.113.clone.f_ref, bf16[16,36,4096]{2,1,0:T(8,128)(2,1)} %copy.35.gain_ref, bf16[16,36,4096]{2,1,0:T(8,128)(2,1)} %copy.36.loss_ref, ...), custom_call_target="tpu_custom_call" | custom-call | tf_op jit(solution)/shard_map/pallas_call | solution.py:44
  149.0 4.3 %all-to-all-start = ((f32[4,6,1024]{2,1,0:T(8,128)}), f32[4,6,1024]{2,1,0:T(8,128)S(1)}, u32[]{:S(2)}, u32[]{:S(2)}) async-start(f32[4,6,1024]{2,1,0:T(8,128)} %bitcast.37), calls=%async_computation | async-start | bytes 262144 | tf_op jit(solution)/shard_map/all_to_all | solution.py:132
  153.3 6.0 %all-to-all-done = f32[4,6,1024]{2,1,0:T(8,128)S(1)} async-done(((f32[4,6,1024]{2,1,0:T(8,128)}), f32[4,6,1024]{2,1,0:T(8,128)S(1)}, u32[]{:S(2)}, u32[]{:S(2)}) %all-to-all-start) | async-done | bytes 98336 | tf_op jit(solution)/shard_map/all_to_all | solution.py:132
  159.3 0.0 copy-start
  159.3 1.4 multiply_add_fusion
  160.7 0.0 copy-done
  (2 shorter events, 0.0 us)
Async XLA Ops:
  0.6 6.7 %collective-permute-start = (f32[6,4096]{1,0:T(8,128)}, f32[6,4096]{1,0:T(8,128)S(1)}, u32[]{:S(2)}, u32[]{:S(2)}) collective-permute-start(f32[6,4096]{1,0:T(8,128)} %occ_ref.1), channel_id=1, source_target_pairs={{0,24},{4,28},{8,0},{12,4},{16,8},{20,12},{24,16},{28,20},{32,56},... | collective-permute-start | bytes 294920 | tf_op jit(solution)/shard_map/ppermute | solution.py:80
  1.4 7.0 %collective-permute-start.2 = (f32[6,4096]{1,0:T(8,128)}, f32[6,4096]{1,0:T(8,128)S(1)}, u32[]{:S(2)}, u32[]{:S(2)}) collective-permute-start(f32[6,4096]{1,0:T(8,128)} %occ_ref.1), channel_id=1, source_target_pairs={{0,8},{4,12},{8,16},{12,20},{16,24},{20,28},{24,0},{28,4},{32,40},... | collective-permute-start | bytes 294920 | tf_op jit(solution)/shard_map/ppermute | solution.py:83
  7.4 6.2 %collective-permute-start.1 = (f32[6,4096]{1,0:T(8,128)S(1)}, f32[6,4096]{1,0:T(8,128)S(1)}, u32[]{:S(2)}, u32[]{:S(2)}) collective-permute-start(f32[6,4096]{1,0:T(8,128)S(1)} %collective-permute-done), channel_id=1, source_target_pairs={{0,24},{4,28},{8,0},{12,4},{16,8},{20,12},{24,16},{28,20},{32,56},... | collective-permute-start | bytes 294920 | tf_op jit(solution)/shard_map/ppermute | solution.py:80
  14.0 12.3 %collective-permute-start.3 = (f32[4,6,4096]{2,0,1:T(4,128)S(1)}, f32[4,6,4096]{2,0,1:T(4,128)S(1)}, u32[]{:S(2)}, u32[]{:S(2)}) collective-permute-start(f32[4,6,4096]{2,0,1:T(4,128)S(1)} %pad_maximum_fusion.1), channel_id=1, source_target_pairs={{0,224},{4,228},{8,232},{12,236},{16,240},{20,244},{24,248},{28,25... | collective-permute-start | bytes 1179656 | tf_op jit(solution)/shard_map/ppermute | solution.py:80
  19.9 10.0 %collective-permute-start.7 = (f32[4,6,4096]{2,0,1:T(4,128)S(1)}, f32[4,6,4096]{2,0,1:T(4,128)S(1)}, u32[]{:S(2)}, u32[]{:S(2)}) collective-permute-start(f32[4,6,4096]{2,0,1:T(4,128)S(1)} %pad_maximum_fusion.1), channel_id=1, source_target_pairs={{0,32},{4,36},{8,40},{12,44},{16,48},{20,52},{24,56},{28,60},{32,6... | collective-permute-start | bytes 1179656 | tf_op jit(solution)/shard_map/ppermute | solution.py:83
  26.3 9.3 %collective-permute-start.4 = (f32[4,6,4096]{2,0,1:T(4,128)S(1)}, f32[4,6,4096]{2,0,1:T(4,128)S(1)}, u32[]{:S(2)}, u32[]{:S(2)}) collective-permute-start(f32[4,6,4096]{2,0,1:T(4,128)S(1)} %collective-permute-done.3), channel_id=1, source_target_pairs={{0,224},{4,228},{8,232},{12,236},{16,240},{20,244},{24,248},{28,25... | collective-permute-start | bytes 1179656 | tf_op jit(solution)/shard_map/ppermute | solution.py:80
  30.0 9.3 %collective-permute-start.8 = (f32[4,6,4096]{2,0,1:T(4,128)S(1)}, f32[4,6,4096]{2,0,1:T(4,128)S(1)}, u32[]{:S(2)}, u32[]{:S(2)}) collective-permute-start(f32[4,6,4096]{2,0,1:T(4,128)S(1)} %collective-permute-done.7), channel_id=1, source_target_pairs={{0,32},{4,36},{8,40},{12,44},{16,48},{20,52},{24,56},{28,60},{32,6... | collective-permute-start | bytes 1179656 | tf_op jit(solution)/shard_map/ppermute | solution.py:83
  35.6 10.2 %collective-permute-start.5 = (f32[4,6,4096]{2,0,1:T(4,128)S(1)}, f32[4,6,4096]{2,0,1:T(4,128)S(1)}, u32[]{:S(2)}, u32[]{:S(2)}) collective-permute-start(f32[4,6,4096]{2,0,1:T(4,128)S(1)} %collective-permute-done.4), channel_id=1, source_target_pairs={{0,224},{4,228},{8,232},{12,236},{16,240},{20,244},{24,248},{28,25... | collective-permute-start | bytes 1179656 | tf_op jit(solution)/shard_map/ppermute | solution.py:80
  39.3 15.6 %collective-permute-start.9 = (f32[4,6,4096]{2,0,1:T(4,128)S(1)}, f32[4,6,4096]{2,0,1:T(4,128)S(1)}, u32[]{:S(2)}, u32[]{:S(2)}) collective-permute-start(f32[4,6,4096]{2,0,1:T(4,128)S(1)} %collective-permute-done.8), channel_id=1, source_target_pairs={{0,32},{4,36},{8,40},{12,44},{16,48},{20,52},{24,56},{28,60},{32,6... | collective-permute-start | bytes 1179656 | tf_op jit(solution)/shard_map/ppermute | solution.py:83
  45.8 9.0 %collective-permute-start.6 = (f32[4,6,4096]{2,0,1:T(4,128)S(1)}, f32[4,6,4096]{2,0,1:T(4,128)S(1)}, u32[]{:S(2)}, u32[]{:S(2)}) collective-permute-start(f32[4,6,4096]{2,0,1:T(4,128)S(1)} %collective-permute-done.5), channel_id=1, source_target_pairs={{0,224},{4,228},{8,232},{12,236},{16,240},{20,244},{24,248},{28,25... | collective-permute-start | bytes 1179656 | tf_op jit(solution)/shard_map/ppermute | solution.py:80
  55.0 4.1 %copy-start.2 = (s32[1,1,16,32]{3,2,1,0:T(8,128)S(1)}, s32[1,1,16,32]{3,2,1,0:T(8,128)}, u32[]{:S(2)}) copy-start(s32[1,1,16,32]{3,2,1,0:T(8,128)} %param.13) | copy-start | bytes 6148
  55.1 4.7 %copy-start.3 = (s32[1,1,16,32,1]{3,4,2,1,0:T(1,128)S(1)}, s32[1,1,16,32,1]{3,4,2,1,0:T(1,128)}, u32[]{:S(2)}) copy-start(s32[1,1,16,32,1]{3,4,2,1,0:T(1,128)} %param.12) | copy-start | bytes 6148
  58.5 18.1 %collective-permute-start.10 = (f32[8,4,6,4096]{3,0,2,1:T(8,128)}, f32[8,4,6,4096]{3,0,2,1:T(8,128)}, u32[]{:S(2)}, u32[]{:S(2)}) collective-permute-start(f32[8,4,6,4096]{3,0,2,1:T(8,128)} %copy.31), channel_id=1, source_target_pairs={{0,4},{4,0},{8,12},{12,8},{16,20},{20,16},{24,28},{28,24},{32,36},... | collective-permute-start | bytes 9437192 | tf_op jit(solution)/shard_map/ppermute | solution.py:89
  67.8 7.9 %copy-start.4 = (s32[16,36]{1,0:T(8,128)S(1)}, s32[16,36]{1,0:T(8,128)}, u32[]{:S(2)}) copy-start(s32[16,36]{1,0:T(8,128)} %param.14) | copy-start | bytes 6916
  67.8 7.9 %copy-start.1 = (f32[36,6]{1,0:T(8,128)S(1)}, f32[36,6]{1,0:T(8,128)}, u32[]{:S(2)}) copy-start(f32[36,6]{1,0:T(8,128)} %constant.112.clone) | copy-start | bytes 2596
  149.0 10.3 %all-to-all-start = ((f32[4,6,1024]{2,1,0:T(8,128)}), f32[4,6,1024]{2,1,0:T(8,128)S(1)}, u32[]{:S(2)}, u32[]{:S(2)}) async-start(f32[4,6,1024]{2,1,0:T(8,128)} %bitcast.37), calls=%async_computation | async-start | bytes 262144 | tf_op jit(solution)/shard_map/all_to_all | solution.py:132
  159.3 1.4 copy-start

commit v4 on v2

--- a/solution.py
+++ b/solution.py
@@ -1,9 +1,68 @@
+import functools
+
 import jax
 import jax.numpy as jnp
 from jax import lax
+from jax.experimental import pallas as pl
+from jax.experimental.pallas import tpu as pltpu
 from jax.sharding import PartitionSpec as P
 
 half_step = 0.5
+
+
+def collide_kernel(idx_ref, g_ref, w_ref, gain_ref, loss_ref, occ_ref, out_ref, sh_ref, rest_ref,
+                   *, shifts, nsub, sub_count, sub_width, bands):
+    t = pl.program_id(0)
+    for s in range(shifts):
+        for jj in range(nsub):
+            row = g_ref[pl.ds(idx_ref[s * sub_count + t * nsub + jj], 1), :]
+            for n in range(bands):
+                piece = row[:, n * sub_width:(n + 1) * sub_width]
+                sh_ref[n, pl.ds(s, 1), pl.ds(jj * sub_width, sub_width)] = piece
+                rest_ref[n, pl.ds(s, 1), pl.ds(jj * sub_width, sub_width)] = 1.0 - piece
+    occ = occ_ref[...]
+    for m in range(bands):
+        acc_i = None
+        acc_o = None
+        for n in range(bands):
+            p = m * bands + n
+            w = w_ref[p]
+            term_i = gain_ref[p].astype(jnp.float32) * w * sh_ref[n]
+            term_o = loss_ref[p].astype(jnp.float32) * w * rest_ref[n]
+            acc_i = term_i if acc_i is None else acc_i + term_i
+            acc_o = term_o if acc_o is None else acc_o + term_o
+        inflow = jnp.sum(acc_i, axis=0, keepdims=True)
+        outflow = jnp.sum(acc_o, axis=0, keepdims=True)
+        out_ref[pl.ds(m, 1), :] = (1.0 - occ[m:m + 1]) * inflow - occ[m:m + 1] * outflow
+
+
+def collide(idx, rows, weight_t, gain_t, loss_t, occ, sub_width, lanes=512):
+    pairs, shifts, width = gain_t.shape
+    bands = occ.shape[0]
+    sub_count = width // sub_width
+    nsub = lanes // sub_width
+    kern = functools.partial(collide_kernel, shifts=shifts, nsub=nsub, sub_count=sub_count,
+                             sub_width=sub_width, bands=bands)
+    return pl.pallas_call(
+        kern,
+        out_shape=jax.ShapeDtypeStruct((bands, width), jnp.float32),
+        grid_spec=pltpu.PrefetchScalarGridSpec(
+            num_scalar_prefetch=1,
+            grid=(width // lanes,),
+            in_specs=[
+                pl.BlockSpec(rows.shape, lambda t, i: (0, 0)),
+                pl.BlockSpec(weight_t.shape, lambda t, i: (0, 0, 0)),
+                pl.BlockSpec((pairs, shifts, lanes), lambda t, i: (0, 0, t)),
+                pl.BlockSpec((pairs, shifts, lanes), lambda t, i: (0, 0, t)),
+                pl.BlockSpec((bands, lanes), lambda t, i: (0, t)),
+            ],
+            out_specs=pl.BlockSpec((bands, lanes), lambda t, i: (0, t)),
+            scratch_shapes=[
+                pltpu.VMEM((bands, shifts, lanes), jnp.float32),
+                pltpu.VMEM((bands, shifts, lanes), jnp.float32),
+            ],
+        ),
+    )(idx, rows, weight_t, gain_t, loss_t, occ)
 
 
 def ring_gather(block, y_count, z_count):
@@ -47,8 +106,13 @@
     y_count = ka_count // (2 * z_count)
     total_requests = shifts * sub_count
 
-    gathered = ring_gather(occupation, y_count, z_count).reshape(
-        ka_count, bands, sub_count, sub_width
+    local_rows = (
+        occupation.reshape(bands, sub_count, sub_width)
+        .transpose(1, 0, 2)
+        .reshape(sub_count, bands * sub_width)
+    )
+    rows = ring_gather(local_rows, y_count, z_count).reshape(
+        ka_count * sub_count, bands * sub_width
     )
     me = lax.axis_index("ka")
     my_z, my_y, my_c = me // (2 * y_count), (me // 2) % y_count, me % 2
@@ -60,23 +124,18 @@
         + (o_y - my_y) % y_count
     )
     sources = local_index.reshape(total_requests)
-    picked = gathered[where, :, sources, :]
-    shifted = (
-        picked.reshape(shifts, sub_count, bands, sub_width)
-        .transpose(0, 2, 1, 3)
-        .reshape(shifts, bands, width)
-    )
+    picks = where * sub_count + sources
     active = (jnp.arange(shifts, dtype=jnp.int32) < counts.reshape(())).astype(jnp.float32)
     weight = pair_mask.astype(jnp.float32) * active[:, None]
-    gain_four = (gain_table.astype(jnp.float32) * weight[:, :, None]).reshape(
-        shifts, bands, bands, width
+    partial_terms = collide(
+        picks,
+        rows,
+        weight.T[:, :, None],
+        gain_table.transpose(1, 0, 2),
+        loss_table.transpose(1, 0, 2),
+        occupation,
+        sub_width,
     )
-    loss_four = (loss_table.astype(jnp.float32) * weight[:, :, None]).reshape(
-        shifts, bands, bands, width
-    )
-    inflow = jnp.einsum("smnk,snk->mk", gain_four, shifted)
-    outflow = jnp.einsum("smnk,snk->mk", loss_four, 1.0 - shifted)
-    partial_terms = (1.0 - occupation) * inflow - occupation * outflow
     share_width = width // pb_count
     parts = partial_terms.reshape(bands, pb_count, share_width).transpose(1, 0, 2)
     collision = jnp.sum(lax.all_to_all(parts, "pb", 0, 0, tiled=True), axis=0)

time: 135 us -> 90.7 us (0.67)
  local copies, waits for them, and re-layouts: 42.7 us -> 3.69 us
  other arithmetic: 28.1 us -> 9.14 us
  Pallas kernels: 0 us -> 12 us
  waiting for transfers between devices: 37.6 us -> 39 us
    reshape x2 -> x0, local copies, waits for them, and re-layouts: 20.6 us -> none  [body(): ring_gather(occupation, y_count, z_count)]
    mul x2 -> x0, other arithmetic: 13.3 us -> none  [the longest x1 13.3 us: body(): gain_table.astype(jnp.float32) * weight[:, :, None]]
    pallas_call x0 -> x1, Pallas kernels: none -> 12 us  [collide(): pl.pallas_call(kern, out_shape=jax.ShapeDtypeStruct((bands, width), jnp.f...]
    dot_general x1 -> x0, other arithmetic: 9.4 us -> none  [body(): outflow = jnp.einsum('smnk,snk->mk', loss_four, 1.0 - shifted)]
    gather x1 -> x0, local copies, waits for them, and re-layouts: 5.85 us -> none  [body(): picked = gathered[where, :, sources, :]]
    ppermute x1 -> x0, local copies, waits for them, and re-layouts: 3.91 us -> none  [ring_gather(): other = lax.ppermute(along_z, 'ka', pairs(lambda j: j ^ 1))]
    another operation x6 -> x2, local copies, waits for them, and re-layouts: 4.75 us -> 0.96 us  [ring(): return jnp.stack([ahead[d] for d in range(count)])]
    another operation x1, other arithmetic: 2.3 us -> 5.64 us  [ring_gather(): return jnp.stack([along_z, other])]
  transfers between devices with their start and end apart: 12 -> 12, of which waited for: 7 -> 9; matrix products, arithmetic and copies ran while one was open for 12% -> 5% of each run, Pallas kernels for 0% -> 0%
where the time goes in v4:
time: 90.7 us; the launch traced here: 90.1 us
  waiting for transfers between devices  39 us (43%)
  starting transfers between devices  24.7 us (27%)
  Pallas kernels  12 us (13%)
  other arithmetic  9.14 us (10%)
  local copies, waits for them, and re-layouts  3.69 us (4%)
  between operations  1.47 us (2%)
    ppermute x6, waiting for transfers between devices, ring(): back = lax.ppermute(back, 'ka', step(-1))  31.6 us
    ppermute x6, starting transfers between devices, ring(): back = lax.ppermute(back, 'ka', step(-1))  17.8 us
    pallas_call x1, Pallas kernels, collide(): pl.pallas_call(kern, out_shape=jax.ShapeDtypeStruct((bands, width), jnp.f...  12 us
    all_to_all x1, waiting for transfers between devices, body(): collision = jnp.sum(lax.all_to_all(parts, 'pb', 0, 0, tiled=True), axis=0)  5.98 us
    another operation x1, other arithmetic, ring_gather(): return jnp.stack([along_z, other])  5.64 us
    all_to_all x1, starting transfers between devices, body(): collision = jnp.sum(lax.all_to_all(parts, 'pb', 0, 0, tiled=True), axis=0)  4.29 us
    ppermute x4, starting transfers between devices, ring(): fwd = lax.ppermute(fwd, 'ka', step(1))  2.52 us
  transfers between devices with their start and end apart: 12, of which 9 were waited for; matrix products, arithmetic and copies ran while one was open for 5% of the time, Pallas kernels for 0%

profile of v4, /device:TPU:24, one launch (start us, length us, event | category | flops | bytes accessed | tf_op | source)
XLA Modules:
  0.0 90.1 jit_solution(13979183891581390480)
XLA Ops:
  0.6 0.9 %copy.19 = f32[4,8,6,128]{3,1,2,0:T(8,128)S(1)} copy(f32[4,8,6,128]{3,2,1,0:T(8,128)} %bitcast.47) | data formatting | bytes 196608
  1.6 0.8 collective-permute-start
  2.4 2.5 %collective-permute-start.2 = (f32[32,768]{1,0:T(8,128)S(1)}, f32[32,768]{1,0:T(8,128)S(1)}, u32[]{:S(2)}, u32[]{:S(2)}) collective-permute-start(f32[32,768]{1,0:T(8,128)S(1)} %bitcast.57), channel_id=1, source_target_pairs={{0,8},{4,12},{8,16},{12,20},{16,24},{20,28},{24,0},{28,4},{32,40},... | collective-permute-start | bytes 294920 | tf_op jit(solution)/shard_map/ppermute | solution.py:88
  4.9 2.6 %collective-permute-done = f32[32,768]{1,0:T(8,128)S(1)} collective-permute-done((f32[32,768]{1,0:T(8,128)S(1)}, f32[32,768]{1,0:T(8,128)S(1)}, u32[]{:S(2)}, u32[]{:S(2)}) %collective-permute-start) | collective-permute-done | bytes 98336 | tf_op jit(solution)/shard_map/ppermute | solution.py:85
  7.5 0.0 collective-permute-start.1
  7.5 0.9 %stack_reshape.3 = f32[1,32,768]{2,1,0:T(8,128)S(1)} reshape(f32[32,6,128]{2,1,0:T(8,128)} %bitcast.48) | data formatting | bytes 196608 | tf_op jit(solution)/shard_map/stack;reshape | solution.py:90
  8.4 0.0 collective-permute-done.2
  8.4 4.9 %collective-permute-done.1 = f32[32,768]{1,0:T(8,128)S(1)} collective-permute-done((f32[32,768]{1,0:T(8,128)S(1)}, f32[32,768]{1,0:T(8,128)S(1)}, u32[]{:S(2)}, u32[]{:S(2)}) %collective-permute-start.1) | collective-permute-done | bytes 98336 | tf_op jit(solution)/shard_map/ppermute | solution.py:85
  13.3 0.0 copy-start.2
  13.3 0.0 copy-start.1
  13.3 5.9 %collective-permute-start.3 = (f32[4,32,768]{2,1,0:T(8,128)S(1)}, f32[4,32,768]{2,1,0:T(8,128)S(1)}, u32[]{:S(2)}, u32[]{:S(2)}) collective-permute-start(f32[4,32,768]{2,1,0:T(8,128)S(1)} %pad_maximum_fusion.1), channel_id=1, source_target_pairs={{0,224},{4,228},{8,232},{12,236},{16,240},{20,244},{24,248},{28,25... | collective-permute-start | bytes 1179656 | tf_op jit(solution)/shard_map/ppermute | solution.py:85
  19.3 0.0 collective-permute-start.7
  19.3 6.1 %collective-permute-done.3 = f32[4,32,768]{2,1,0:T(8,128)S(1)} collective-permute-done((f32[4,32,768]{2,1,0:T(8,128)S(1)}, f32[4,32,768]{2,1,0:T(8,128)S(1)}, u32[]{:S(2)}, u32[]{:S(2)}) %collective-permute-start.3) | collective-permute-done | bytes 393248 | tf_op jit(solution)/shard_map/ppermute | solution.py:85
  25.4 3.7 %collective-permute-start.4 = (f32[4,32,768]{2,1,0:T(8,128)S(1)}, f32[4,32,768]{2,1,0:T(8,128)S(1)}, u32[]{:S(2)}, u32[]{:S(2)}) collective-permute-start(f32[4,32,768]{2,1,0:T(8,128)S(1)} %collective-permute-done.3), channel_id=1, source_target_pairs={{0,224},{4,228},{8,232},{12,236},{16,240},{20,244},{24,248},{28,25... | collective-permute-start | bytes 1179656 | tf_op jit(solution)/shard_map/ppermute | solution.py:85
  29.0 0.0 collective-permute-done.7
  29.0 0.0 collective-permute-start.8
  29.0 5.9 %collective-permute-done.4 = f32[4,32,768]{2,1,0:T(8,128)S(1)} collective-permute-done((f32[4,32,768]{2,1,0:T(8,128)S(1)}, f32[4,32,768]{2,1,0:T(8,128)S(1)}, u32[]{:S(2)}, u32[]{:S(2)}) %collective-permute-start.4) | collective-permute-done | bytes 393248 | tf_op jit(solution)/shard_map/ppermute | solution.py:85
  35.0 3.7 %collective-permute-start.5 = (f32[4,32,768]{2,1,0:T(8,128)S(1)}, f32[4,32,768]{2,1,0:T(8,128)S(1)}, u32[]{:S(2)}, u32[]{:S(2)}) collective-permute-start(f32[4,32,768]{2,1,0:T(8,128)S(1)} %collective-permute-done.4), channel_id=1, source_target_pairs={{0,224},{4,228},{8,232},{12,236},{16,240},{20,244},{24,248},{28,25... | collective-permute-start | bytes 1179656 | tf_op jit(solution)/shard_map/ppermute | solution.py:85
  38.8 0.1 collective-permute-done.8
  38.8 0.0 collective-permute-start.9
  38.9 6.9 %collective-permute-done.5 = f32[4,32,768]{2,1,0:T(8,128)S(1)} collective-permute-done((f32[4,32,768]{2,1,0:T(8,128)S(1)}, f32[4,32,768]{2,1,0:T(8,128)S(1)}, u32[]{:S(2)}, u32[]{:S(2)}) %collective-permute-start.5) | collective-permute-done | bytes 393248 | tf_op jit(solution)/shard_map/ppermute | solution.py:85
  45.7 3.7 %collective-permute-start.6 = (f32[4,32,768]{2,1,0:T(8,128)S(1)}, f32[4,32,768]{2,1,0:T(8,128)S(1)}, u32[]{:S(2)}, u32[]{:S(2)}) collective-permute-start(f32[4,32,768]{2,1,0:T(8,128)S(1)} %collective-permute-done.5), channel_id=1, source_target_pairs={{0,224},{4,228},{8,232},{12,236},{16,240},{20,244},{24,248},{28,25... | collective-permute-start | bytes 1179656 | tf_op jit(solution)/shard_map/ppermute | solution.py:85
  49.5 5.2 %collective-permute-done.6 = f32[4,32,768]{2,1,0:T(8,128)S(1)} collective-permute-done((f32[4,32,768]{2,1,0:T(8,128)S(1)}, f32[4,32,768]{2,1,0:T(8,128)S(1)}, u32[]{:S(2)}, u32[]{:S(2)}) %collective-permute-start.6) | collective-permute-done | bytes 393248 | tf_op jit(solution)/shard_map/ppermute | solution.py:85
  54.7 0.0 collective-permute-done.9
  54.9 0.1 collective-permute-start.10
  55.0 0.5 broadcast.43
  55.5 0.0 copy-done.2
  55.5 0.7 reduce.3
  56.2 0.1 reshape.30
  56.3 0.0 copy-done.1
  56.3 0.1 reshape.31
  57.0 0.8 multiply_bitcast_fusion
  57.8 0.9 %copy.15.w_ref = f32[36,16,1]{2,1,0:T(8,128)} copy(f32[36,16,1]{0,1,2:T(8,128)S(1)} %multiply_bitcast_fusion) | data formatting | bytes 4608 | tf_op jit(solution)/shard_map/broadcast_in_dim | solution.py:133
  58.7 0.6 fusion.5.idx_ref
  59.3 1.4 %collective-permute-done.10 = f32[8,4,32,768]{3,2,1,0:T(8,128)} collective-permute-done((f32[8,4,32,768]{3,2,1,0:T(8,128)S(1)}, f32[8,4,32,768]{3,2,1,0:T(8,128)}, u32[]{:S(2)}, u32[]{:S(2)}) %collective-permute-start.10) | collective-permute-done | bytes 3145760 | tf_op jit(solution)/shard_map/ppermute | solution.py:94
  60.7 5.6 %pad_maximum_fusion = f32[2,8,4,32,768]{4,3,2,1,0:T(8,128)} fusion(f32[1,8,4,32,768]{4,3,2,1,0:T(8,128)} %bitcast.15, f32[1,8,4,32,768]{4,3,2,1,0:T(8,128)S(1)} %bitcast.46), kind=kLoop, calls=%fused_computation | loop fusion | flops 1572864 | bytes 12582912 | tf_op jit(solution)/shard_map/stack | solution.py:95
  66.4 12.0 %shard_map.86 = f32[6,4096]{1,0:T(8,128)} custom-call(s32[512]{0:T(512)} %fusion.5.idx_ref, f32[2048,768]{1,0:T(8,128)} %bitcast.43, f32[36,16,1]{2,1,0:T(8,128)} %copy.15.w_ref, bf16[36,16,4096]{2,1,0:T(8,128)(2,1)} %bitcast.44, bf16[36,16,4096]{2,1,0:T(8,128)(2,1)} %bitcast.45, f32[6,4096]{1,0:T(8,128)} %occ_ref.1), custom_call_target="tpu_custom_call" | custom-call | tf_op jit(solution)/shard_map/pallas_call | solution.py:46
  78.4 4.3 %all-to-all-start = ((f32[4,6,1024]{2,1,0:T(8,128)}), f32[4,6,1024]{2,1,0:T(8,128)S(1)}, u32[]{:S(2)}, u32[]{:S(2)}) async-start(f32[4,6,1024]{2,1,0:T(8,128)} %bitcast.49), calls=%async_computation | async-start | bytes 262144 | tf_op jit(solution)/shard_map/all_to_all | solution.py:141
  82.7 6.0 %all-to-all-done = f32[4,6,1024]{2,1,0:T(8,128)S(1)} async-done(((f32[4,6,1024]{2,1,0:T(8,128)}), f32[4,6,1024]{2,1,0:T(8,128)S(1)}, u32[]{:S(2)}, u32[]{:S(2)}) %all-to-all-start) | async-done | bytes 98336 | tf_op jit(solution)/shard_map/all_to_all | solution.py:141
  88.7 0.0 copy-start
  88.7 1.4 %multiply_add_fusion = f32[6,1024]{1,0:T(8,128)} fusion(f32[6,1024]{1,0:T(8,128)S(1)} %reduce_sum.9, f32[6,4096]{1,0:T(8,128)} %occ_ref.1, s32[]{:T(128)S(6)} %select_n.57), kind=kLoop, calls=%fused_computation.11 | loop fusion | flops 12288 | bytes 73732 | tf_op jit(solution)/shard_map/add | solution.py:145
  90.1 0.0 copy-done
  (11 shorter events, 0.3 us)
Async XLA Ops:
  1.6 5.9 %collective-permute-start = (f32[32,768]{1,0:T(8,128)S(1)}, f32[32,768]{1,0:T(8,128)S(1)}, u32[]{:S(2)}, u32[]{:S(2)}) collective-permute-start(f32[32,768]{1,0:T(8,128)S(1)} %bitcast.56), channel_id=1, source_target_pairs={{0,24},{4,28},{8,0},{12,4},{16,8},{20,12},{24,16},{28,20},{32,56},... | collective-permute-start | bytes 294920 | tf_op jit(solution)/shard_map/ppermute | solution.py:85
  2.4 6.0 %collective-permute-start.2 = (f32[32,768]{1,0:T(8,128)S(1)}, f32[32,768]{1,0:T(8,128)S(1)}, u32[]{:S(2)}, u32[]{:S(2)}) collective-permute-start(f32[32,768]{1,0:T(8,128)S(1)} %bitcast.57), channel_id=1, source_target_pairs={{0,8},{4,12},{8,16},{12,20},{16,24},{20,28},{24,0},{28,4},{32,40},... | collective-permute-start | bytes 294920 | tf_op jit(solution)/shard_map/ppermute | solution.py:88
  7.5 5.8 %collective-permute-start.1 = (f32[32,768]{1,0:T(8,128)S(1)}, f32[32,768]{1,0:T(8,128)S(1)}, u32[]{:S(2)}, u32[]{:S(2)}) collective-permute-start(f32[32,768]{1,0:T(8,128)S(1)} %collective-permute-done), channel_id=1, source_target_pairs={{0,24},{4,28},{8,0},{12,4},{16,8},{20,12},{24,16},{28,20},{32,56},... | collective-permute-start | bytes 294920 | tf_op jit(solution)/shard_map/ppermute | solution.py:85
  13.3 42.2 %copy-start.2 = (s32[1,1,16,32,1]{3,4,2,1,0:T(1,128)S(1)}, s32[1,1,16,32,1]{3,4,2,1,0:T(1,128)}, u32[]{:S(2)}) copy-start(s32[1,1,16,32,1]{3,4,2,1,0:T(1,128)} %param.10) | copy-start | bytes 6148
  13.3 42.9 %copy-start.1 = (s32[1,1,16,32]{3,2,1,0:T(8,128)S(1)}, s32[1,1,16,32]{3,2,1,0:T(8,128)}, u32[]{:S(2)}) copy-start(s32[1,1,16,32]{3,2,1,0:T(8,128)} %param.11) | copy-start | bytes 6148
  13.3 12.0 %collective-permute-start.3 = (f32[4,32,768]{2,1,0:T(8,128)S(1)}, f32[4,32,768]{2,1,0:T(8,128)S(1)}, u32[]{:S(2)}, u32[]{:S(2)}) collective-permute-start(f32[4,32,768]{2,1,0:T(8,128)S(1)} %pad_maximum_fusion.1), channel_id=1, source_target_pairs={{0,224},{4,228},{8,232},{12,236},{16,240},{20,244},{24,248},{28,25... | collective-permute-start | bytes 1179656 | tf_op jit(solution)/shard_map/ppermute | solution.py:85
  19.3 9.8 %collective-permute-start.7 = (f32[4,32,768]{2,1,0:T(8,128)S(1)}, f32[4,32,768]{2,1,0:T(8,128)S(1)}, u32[]{:S(2)}, u32[]{:S(2)}) collective-permute-start(f32[4,32,768]{2,1,0:T(8,128)S(1)} %pad_maximum_fusion.1), channel_id=1, source_target_pairs={{0,32},{4,36},{8,40},{12,44},{16,48},{20,52},{24,56},{28,60},{32,6... | collective-permute-start | bytes 1179656 | tf_op jit(solution)/shard_map/ppermute | solution.py:88
  25.4 9.6 %collective-permute-start.4 = (f32[4,32,768]{2,1,0:T(8,128)S(1)}, f32[4,32,768]{2,1,0:T(8,128)S(1)}, u32[]{:S(2)}, u32[]{:S(2)}) collective-permute-start(f32[4,32,768]{2,1,0:T(8,128)S(1)} %collective-permute-done.3), channel_id=1, source_target_pairs={{0,224},{4,228},{8,232},{12,236},{16,240},{20,244},{24,248},{28,25... | collective-permute-start | bytes 1179656 | tf_op jit(solution)/shard_map/ppermute | solution.py:85
  29.0 9.8 %collective-permute-start.8 = (f32[4,32,768]{2,1,0:T(8,128)S(1)}, f32[4,32,768]{2,1,0:T(8,128)S(1)}, u32[]{:S(2)}, u32[]{:S(2)}) collective-permute-start(f32[4,32,768]{2,1,0:T(8,128)S(1)} %collective-permute-done.7), channel_id=1, source_target_pairs={{0,32},{4,36},{8,40},{12,44},{16,48},{20,52},{24,56},{28,60},{32,6... | collective-permute-start | bytes 1179656 | tf_op jit(solution)/shard_map/ppermute | solution.py:88
  35.0 10.7 %collective-permute-start.5 = (f32[4,32,768]{2,1,0:T(8,128)S(1)}, f32[4,32,768]{2,1,0:T(8,128)S(1)}, u32[]{:S(2)}, u32[]{:S(2)}) collective-permute-start(f32[4,32,768]{2,1,0:T(8,128)S(1)} %collective-permute-done.4), channel_id=1, source_target_pairs={{0,224},{4,228},{8,232},{12,236},{16,240},{20,244},{24,248},{28,25... | collective-permute-start | bytes 1179656 | tf_op jit(solution)/shard_map/ppermute | solution.py:85
  38.8 15.9 %collective-permute-start.9 = (f32[4,32,768]{2,1,0:T(8,128)S(1)}, f32[4,32,768]{2,1,0:T(8,128)S(1)}, u32[]{:S(2)}, u32[]{:S(2)}) collective-permute-start(f32[4,32,768]{2,1,0:T(8,128)S(1)} %collective-permute-done.8), channel_id=1, source_target_pairs={{0,32},{4,36},{8,40},{12,44},{16,48},{20,52},{24,56},{28,60},{32,6... | collective-permute-start | bytes 1179656 | tf_op jit(solution)/shard_map/ppermute | solution.py:88
  45.7 9.0 %collective-permute-start.6 = (f32[4,32,768]{2,1,0:T(8,128)S(1)}, f32[4,32,768]{2,1,0:T(8,128)S(1)}, u32[]{:S(2)}, u32[]{:S(2)}) collective-permute-start(f32[4,32,768]{2,1,0:T(8,128)S(1)} %collective-permute-done.5), channel_id=1, source_target_pairs={{0,224},{4,228},{8,232},{12,236},{16,240},{20,244},{24,248},{28,25... | collective-permute-start | bytes 1179656 | tf_op jit(solution)/shard_map/ppermute | solution.py:85
  54.9 5.9 %collective-permute-start.10 = (f32[8,4,32,768]{3,2,1,0:T(8,128)S(1)}, f32[8,4,32,768]{3,2,1,0:T(8,128)}, u32[]{:S(2)}, u32[]{:S(2)}) collective-permute-start(f32[8,4,32,768]{3,2,1,0:T(8,128)S(1)} %bitcast_dynamic-update-slice_fusion), channel_id=1, source_target_pairs={{0,4},{4,0},{8,12},{12,8},{16,20},{20,16},{24,28},{28,24},{32,36},... | collective-permute-start | bytes 9437192 | tf_op jit(solution)/shard_map/ppermute | solution.py:94
  78.4 10.3 %all-to-all-start = ((f32[4,6,1024]{2,1,0:T(8,128)}), f32[4,6,1024]{2,1,0:T(8,128)S(1)}, u32[]{:S(2)}, u32[]{:S(2)}) async-start(f32[4,6,1024]{2,1,0:T(8,128)} %bitcast.49), calls=%async_computation | async-start | bytes 262144 | tf_op jit(solution)/shard_map/all_to_all | solution.py:141
  88.7 1.4 %copy-start = (f32[6,1024]{1,0:T(8,128)}, f32[6,1024]{1,0:T(8,128)S(1)}, u32[]{:S(2)}) copy-start(f32[6,1024]{1,0:T(8,128)S(1)} %reduce_sum.9) | copy-start | bytes 73732

commit v5 on v4

--- a/solution.py
+++ b/solution.py
@@ -10,12 +10,16 @@
 half_step = 0.5
 
 
-def collide_kernel(idx_ref, g_ref, w_ref, gain_ref, loss_ref, occ_ref, out_ref, sh_ref, rest_ref,
+def collide_kernel(idx_ref, near_ref, far_ref, w_ref, gain_ref, loss_ref, occ_ref, out_ref, sh_ref, rest_ref,
                    *, shifts, nsub, sub_count, sub_width, bands):
     t = pl.program_id(0)
+    half = near_ref.shape[0]
     for s in range(shifts):
         for jj in range(nsub):
-            row = g_ref[pl.ds(idx_ref[s * sub_count + t * nsub + jj], 1), :]
+            at = idx_ref[s * sub_count + t * nsub + jj]
+            near = near_ref[pl.ds(jnp.minimum(at, half - 1), 1), :]
+            far = far_ref[pl.ds(jnp.maximum(at - half, 0), 1), :]
+            row = jnp.where(at < half, near, far)
             for n in range(bands):
                 piece = row[:, n * sub_width:(n + 1) * sub_width]
                 sh_ref[n, pl.ds(s, 1), pl.ds(jj * sub_width, sub_width)] = piece
@@ -36,7 +40,7 @@
         out_ref[pl.ds(m, 1), :] = (1.0 - occ[m:m + 1]) * inflow - occ[m:m + 1] * outflow
 
 
-def collide(idx, rows, weight_t, gain_t, loss_t, occ, sub_width, lanes=512):
+def collide(idx, near, far, weight_t, gain_t, loss_t, occ, sub_width, lanes=512):
     pairs, shifts, width = gain_t.shape
     bands = occ.shape[0]
     sub_count = width // sub_width
@@ -50,7 +54,8 @@
             num_scalar_prefetch=1,
             grid=(width // lanes,),
             in_specs=[
-                pl.BlockSpec(rows.shape, lambda t, i: (0, 0)),
+                pl.BlockSpec(near.shape, lambda t, i: (0, 0)),
+                pl.BlockSpec(far.shape, lambda t, i: (0, 0)),
                 pl.BlockSpec(weight_t.shape, lambda t, i: (0, 0, 0)),
                 pl.BlockSpec((pairs, shifts, lanes), lambda t, i: (0, 0, t)),
                 pl.BlockSpec((pairs, shifts, lanes), lambda t, i: (0, 0, t)),
@@ -62,7 +67,7 @@
                 pltpu.VMEM((bands, shifts, lanes), jnp.float32),
             ],
         ),
-    )(idx, rows, weight_t, gain_t, loss_t, occ)
+    )(idx, near, far, weight_t, gain_t, loss_t, occ)
 
 
 def ring_gather(block, y_count, z_count):
@@ -92,7 +97,7 @@
     along_y = ring(block, y_step, y_count)
     along_z = ring(along_y, z_step, z_count)
     other = lax.ppermute(along_z, "ka", pairs(lambda j: j ^ 1))
-    return jnp.stack([along_z, other])
+    return along_z, other
 
 
 def body(occupation, gain_table, loss_table, owner, local_index, pair_mask, counts):
@@ -111,9 +116,9 @@
         .transpose(1, 0, 2)
         .reshape(sub_count, bands * sub_width)
     )
-    rows = ring_gather(local_rows, y_count, z_count).reshape(
-        ka_count * sub_count, bands * sub_width
-    )
+    near, far = ring_gather(local_rows, y_count, z_count)
+    near = near.reshape(ka_count * sub_count // 2, bands * sub_width)
+    far = far.reshape(ka_count * sub_count // 2, bands * sub_width)
     me = lax.axis_index("ka")
     my_z, my_y, my_c = me // (2 * y_count), (me // 2) % y_count, me % 2
     owners = owner.reshape(total_requests)
@@ -129,7 +134,8 @@
     weight = pair_mask.astype(jnp.float32) * active[:, None]
     partial_terms = collide(
         picks,
-        rows,
+        near,
+        far,
         weight.T[:, :, None],
         gain_table.transpose(1, 0, 2),
         loss_table.transpose(1, 0, 2),

time: 90.7 us -> 86.2 us (0.950)
  other arithmetic: 9.14 us -> 3.55 us
  Pallas kernels: 12 us -> 13.2 us
    another operation x1 -> x0, other arithmetic: 5.64 us -> none  [ring_gather(): return jnp.stack([along_z, other])]
    pallas_call x1, Pallas kernels: 12 us -> 13.2 us  [collide(): pl.pallas_call(kern, out_shape=jax.ShapeDtypeStruct((bands, width), jnp.f...]
  transfers between devices with their start and end apart: 12 -> 12, of which waited for: 9 -> 9; matrix products, arithmetic and copies ran while one was open for 5% -> 6% of each run, Pallas kernels for 0% -> 0%
where the time goes in v5:
time: 86.2 us; the launch traced here: 85.6 us
  waiting for transfers between devices  38.9 us (45%)
  starting transfers between devices  24.7 us (29%)
  Pallas kernels  13.2 us (15%)
  local copies, waits for them, and re-layouts  3.81 us (4%)
  other arithmetic  3.55 us (4%)
  between operations  1.48 us (2%)
    ppermute x6, waiting for transfers between devices, ring(): back = lax.ppermute(back, 'ka', step(-1))  31.6 us
    ppermute x6, starting transfers between devices, ring(): back = lax.ppermute(back, 'ka', step(-1))  17.8 us
    pallas_call x1, Pallas kernels, collide(): pl.pallas_call(kern, out_shape=jax.ShapeDtypeStruct((bands, width), jnp.f...  13.2 us
    all_to_all x1, waiting for transfers between devices, body(): collision = jnp.sum(lax.all_to_all(parts, 'pb', 0, 0, tiled=True), axis=0)  5.98 us
    all_to_all x1, starting transfers between devices, body(): collision = jnp.sum(lax.all_to_all(parts, 'pb', 0, 0, tiled=True), axis=0)  4.29 us
    ppermute x4, starting transfers between devices, ring(): fwd = lax.ppermute(fwd, 'ka', step(1))  2.52 us
    unnamed x16, local copies, waits for them, and re-layouts  1.77 us
  transfers between devices with their start and end apart: 12, of which 9 were waited for; matrix products, arithmetic and copies ran while one was open for 6% of the time, Pallas kernels for 0%

profile of v5, /device:TPU:24, one launch (start us, length us, event | category | flops | bytes accessed | tf_op | source)
XLA Modules:
  0.0 85.6 jit_solution(17457593646686376855)
XLA Ops:
  0.6 0.9 %copy.19 = f32[4,8,6,128]{3,1,2,0:T(8,128)S(1)} copy(f32[4,8,6,128]{3,2,1,0:T(8,128)} %bitcast.45) | data formatting | bytes 196608
  1.6 0.8 collective-permute-start
  2.4 2.5 %collective-permute-start.2 = (f32[32,768]{1,0:T(8,128)S(1)}, f32[32,768]{1,0:T(8,128)S(1)}, u32[]{:S(2)}, u32[]{:S(2)}) collective-permute-start(f32[32,768]{1,0:T(8,128)S(1)} %bitcast.55), channel_id=1, source_target_pairs={{0,8},{4,12},{8,16},{12,20},{16,24},{20,28},{24,0},{28,4},{32,40},... | collective-permute-start | bytes 294920 | tf_op jit(solution)/shard_map/ppermute | solution.py:93
  4.9 2.6 %collective-permute-done = f32[32,768]{1,0:T(8,128)S(1)} collective-permute-done((f32[32,768]{1,0:T(8,128)S(1)}, f32[32,768]{1,0:T(8,128)S(1)}, u32[]{:S(2)}, u32[]{:S(2)}) %collective-permute-start) | collective-permute-done | bytes 98336 | tf_op jit(solution)/shard_map/ppermute | solution.py:90
  7.5 0.0 collective-permute-start.1
  7.5 0.9 %stack_reshape.3 = f32[1,32,768]{2,1,0:T(8,128)S(1)} reshape(f32[32,6,128]{2,1,0:T(8,128)} %bitcast.46) | data formatting | bytes 196608 | tf_op jit(solution)/shard_map/stack;reshape | solution.py:95
  8.4 0.0 collective-permute-done.2
  8.4 4.9 %collective-permute-done.1 = f32[32,768]{1,0:T(8,128)S(1)} collective-permute-done((f32[32,768]{1,0:T(8,128)S(1)}, f32[32,768]{1,0:T(8,128)S(1)}, u32[]{:S(2)}, u32[]{:S(2)}) %collective-permute-start.1) | collective-permute-done | bytes 98336 | tf_op jit(solution)/shard_map/ppermute | solution.py:90
  13.3 0.0 copy-start.3
  13.3 0.0 copy-start.2
  13.3 5.9 %collective-permute-start.3 = (f32[4,32,768]{2,1,0:T(8,128)S(1)}, f32[4,32,768]{2,1,0:T(8,128)S(1)}, u32[]{:S(2)}, u32[]{:S(2)}) collective-permute-start(f32[4,32,768]{2,1,0:T(8,128)S(1)} %pad_maximum_fusion), channel_id=1, source_target_pairs={{0,224},{4,228},{8,232},{12,236},{16,240},{20,244},{24,248},{28,25... | collective-permute-start | bytes 1179656 | tf_op jit(solution)/shard_map/ppermute | solution.py:90
  19.3 0.0 collective-permute-start.7
  19.3 6.1 %collective-permute-done.3 = f32[4,32,768]{2,1,0:T(8,128)S(1)} collective-permute-done((f32[4,32,768]{2,1,0:T(8,128)S(1)}, f32[4,32,768]{2,1,0:T(8,128)S(1)}, u32[]{:S(2)}, u32[]{:S(2)}) %collective-permute-start.3) | collective-permute-done | bytes 393248 | tf_op jit(solution)/shard_map/ppermute | solution.py:90
  25.4 3.7 %collective-permute-start.4 = (f32[4,32,768]{2,1,0:T(8,128)S(1)}, f32[4,32,768]{2,1,0:T(8,128)S(1)}, u32[]{:S(2)}, u32[]{:S(2)}) collective-permute-start(f32[4,32,768]{2,1,0:T(8,128)S(1)} %collective-permute-done.3), channel_id=1, source_target_pairs={{0,224},{4,228},{8,232},{12,236},{16,240},{20,244},{24,248},{28,25... | collective-permute-start | bytes 1179656 | tf_op jit(solution)/shard_map/ppermute | solution.py:90
  29.0 0.0 collective-permute-done.7
  29.0 0.0 collective-permute-start.8
  29.0 5.9 %collective-permute-done.4 = f32[4,32,768]{2,1,0:T(8,128)S(1)} collective-permute-done((f32[4,32,768]{2,1,0:T(8,128)S(1)}, f32[4,32,768]{2,1,0:T(8,128)S(1)}, u32[]{:S(2)}, u32[]{:S(2)}) %collective-permute-start.4) | collective-permute-done | bytes 393248 | tf_op jit(solution)/shard_map/ppermute | solution.py:90
  35.0 3.7 %collective-permute-start.5 = (f32[4,32,768]{2,1,0:T(8,128)S(1)}, f32[4,32,768]{2,1,0:T(8,128)S(1)}, u32[]{:S(2)}, u32[]{:S(2)}) collective-permute-start(f32[4,32,768]{2,1,0:T(8,128)S(1)} %collective-permute-done.4), channel_id=1, source_target_pairs={{0,224},{4,228},{8,232},{12,236},{16,240},{20,244},{24,248},{28,25... | collective-permute-start | bytes 1179656 | tf_op jit(solution)/shard_map/ppermute | solution.py:90
  38.8 0.1 collective-permute-done.8
  38.8 0.0 collective-permute-start.9
  38.9 6.9 %collective-permute-done.5 = f32[4,32,768]{2,1,0:T(8,128)S(1)} collective-permute-done((f32[4,32,768]{2,1,0:T(8,128)S(1)}, f32[4,32,768]{2,1,0:T(8,128)S(1)}, u32[]{:S(2)}, u32[]{:S(2)}) %collective-permute-start.5) | collective-permute-done | bytes 393248 | tf_op jit(solution)/shard_map/ppermute | solution.py:90
  45.7 3.7 %collective-permute-start.6 = (f32[4,32,768]{2,1,0:T(8,128)S(1)}, f32[4,32,768]{2,1,0:T(8,128)S(1)}, u32[]{:S(2)}, u32[]{:S(2)}) collective-permute-start(f32[4,32,768]{2,1,0:T(8,128)S(1)} %collective-permute-done.5), channel_id=1, source_target_pairs={{0,224},{4,228},{8,232},{12,236},{16,240},{20,244},{24,248},{28,25... | collective-permute-start | bytes 1179656 | tf_op jit(solution)/shard_map/ppermute | solution.py:90
  49.5 5.2 %collective-permute-done.6 = f32[4,32,768]{2,1,0:T(8,128)S(1)} collective-permute-done((f32[4,32,768]{2,1,0:T(8,128)S(1)}, f32[4,32,768]{2,1,0:T(8,128)S(1)}, u32[]{:S(2)}, u32[]{:S(2)}) %collective-permute-start.6) | collective-permute-done | bytes 393248 | tf_op jit(solution)/shard_map/ppermute | solution.py:90
  54.7 0.0 collective-permute-done.9
  54.9 0.0 copy-start
  54.9 0.1 collective-permute-start.10
  55.0 0.6 broadcast.43
  55.7 0.0 copy-done.3
  55.7 0.7 reduce.3
  56.4 0.1 reshape.33
  56.5 0.0 copy-done.2
  56.5 0.1 reshape.34
  57.2 0.8 multiply_bitcast_fusion
  58.0 0.9 %copy.15.w_ref = f32[36,16,1]{2,1,0:T(8,128)} copy(f32[36,16,1]{0,1,2:T(8,128)S(1)} %multiply_bitcast_fusion) | data formatting | bytes 4608 | tf_op jit(solution)/shard_map/broadcast_in_dim | solution.py:139
  58.9 0.6 fusion.5.idx_ref
  59.5 1.2 %collective-permute-done.10 = f32[8,4,32,768]{3,2,1,0:T(8,128)} collective-permute-done((f32[8,4,32,768]{3,2,1,0:T(8,128)S(1)}, f32[8,4,32,768]{3,2,1,0:T(8,128)}, u32[]{:S(2)}, u32[]{:S(2)}) %collective-permute-start.10) | collective-permute-done | bytes 3145760 | tf_op jit(solution)/shard_map/ppermute | solution.py:99
  60.8 0.0 copy-done
  60.8 13.2 %shard_map.86 = f32[6,4096]{1,0:T(8,128)} custom-call(s32[512]{0:T(512)} %fusion.5.idx_ref, f32[1024,768]{1,0:T(8,128)} %bitcast.44, f32[1024,768]{1,0:T(8,128)} %bitcast.15.far_ref, f32[36,16,1]{2,1,0:T(8,128)} %copy.15.w_ref, bf16[36,16,4096]{2,1,0:T(8,128)(2,1)} %bitcast.42, bf16[36,16,4096]{2,1,0:T(8,128)(2,1)} %bitcast.43, f32[6,4096]{1,0:T(8,128)} %occ_ref.1), custom_call_target="tpu_custom_call" | custom-call | tf_op jit(solution)/shard_map/pallas_call | solution.py:50
  74.0 4.3 %all-to-all-start = ((f32[4,6,1024]{2,1,0:T(8,128)}), f32[4,6,1024]{2,1,0:T(8,128)S(1)}, u32[]{:S(2)}, u32[]{:S(2)}) async-start(f32[4,6,1024]{2,1,0:T(8,128)} %bitcast.47), calls=%async_computation | async-start | bytes 262144 | tf_op jit(solution)/shard_map/all_to_all | solution.py:147
  78.2 6.0 %all-to-all-done = f32[4,6,1024]{2,1,0:T(8,128)S(1)} async-done(((f32[4,6,1024]{2,1,0:T(8,128)}), f32[4,6,1024]{2,1,0:T(8,128)S(1)}, u32[]{:S(2)}, u32[]{:S(2)}) %all-to-all-start) | async-done | bytes 98336 | tf_op jit(solution)/shard_map/all_to_all | solution.py:147
  84.2 0.0 copy-start.1
  84.2 1.4 %multiply_add_fusion = f32[6,1024]{1,0:T(8,128)} fusion(f32[6,1024]{1,0:T(8,128)S(1)} %reduce_sum.9, f32[6,4096]{1,0:T(8,128)} %occ_ref.1, s32[]{:T(128)S(6)} %select_n.57), kind=kLoop, calls=%fused_computation.10 | loop fusion | flops 12288 | bytes 73732 | tf_op jit(solution)/shard_map/add | solution.py:151
  85.6 0.0 copy-done.1
  (11 shorter events, 0.3 us)
Async XLA Ops:
  1.6 5.9 %collective-permute-start = (f32[32,768]{1,0:T(8,128)S(1)}, f32[32,768]{1,0:T(8,128)S(1)}, u32[]{:S(2)}, u32[]{:S(2)}) collective-permute-start(f32[32,768]{1,0:T(8,128)S(1)} %bitcast.54), channel_id=1, source_target_pairs={{0,24},{4,28},{8,0},{12,4},{16,8},{20,12},{24,16},{28,20},{32,56},... | collective-permute-start | bytes 294920 | tf_op jit(solution)/shard_map/ppermute | solution.py:90
  2.4 6.0 %collective-permute-start.2 = (f32[32,768]{1,0:T(8,128)S(1)}, f32[32,768]{1,0:T(8,128)S(1)}, u32[]{:S(2)}, u32[]{:S(2)}) collective-permute-start(f32[32,768]{1,0:T(8,128)S(1)} %bitcast.55), channel_id=1, source_target_pairs={{0,8},{4,12},{8,16},{12,20},{16,24},{20,28},{24,0},{28,4},{32,40},... | collective-permute-start | bytes 294920 | tf_op jit(solution)/shard_map/ppermute | solution.py:93
  7.5 5.8 %collective-permute-start.1 = (f32[32,768]{1,0:T(8,128)S(1)}, f32[32,768]{1,0:T(8,128)S(1)}, u32[]{:S(2)}, u32[]{:S(2)}) collective-permute-start(f32[32,768]{1,0:T(8,128)S(1)} %collective-permute-done), channel_id=1, source_target_pairs={{0,24},{4,28},{8,0},{12,4},{16,8},{20,12},{24,16},{28,20},{32,56},... | collective-permute-start | bytes 294920 | tf_op jit(solution)/shard_map/ppermute | solution.py:90
  13.3 42.3 %copy-start.3 = (s32[1,1,16,32,1]{3,4,2,1,0:T(1,128)S(1)}, s32[1,1,16,32,1]{3,4,2,1,0:T(1,128)}, u32[]{:S(2)}) copy-start(s32[1,1,16,32,1]{3,4,2,1,0:T(1,128)} %param.10) | copy-start | bytes 6148
  13.3 43.1 %copy-start.2 = (s32[1,1,16,32]{3,2,1,0:T(8,128)S(1)}, s32[1,1,16,32]{3,2,1,0:T(8,128)}, u32[]{:S(2)}) copy-start(s32[1,1,16,32]{3,2,1,0:T(8,128)} %param.11) | copy-start | bytes 6148
  13.3 12.0 %collective-permute-start.3 = (f32[4,32,768]{2,1,0:T(8,128)S(1)}, f32[4,32,768]{2,1,0:T(8,128)S(1)}, u32[]{:S(2)}, u32[]{:S(2)}) collective-permute-start(f32[4,32,768]{2,1,0:T(8,128)S(1)} %pad_maximum_fusion), channel_id=1, source_target_pairs={{0,224},{4,228},{8,232},{12,236},{16,240},{20,244},{24,248},{28,25... | collective-permute-start | bytes 1179656 | tf_op jit(solution)/shard_map/ppermute | solution.py:90
  19.3 9.8 %collective-permute-start.7 = (f32[4,32,768]{2,1,0:T(8,128)S(1)}, f32[4,32,768]{2,1,0:T(8,128)S(1)}, u32[]{:S(2)}, u32[]{:S(2)}) collective-permute-start(f32[4,32,768]{2,1,0:T(8,128)S(1)} %pad_maximum_fusion), channel_id=1, source_target_pairs={{0,32},{4,36},{8,40},{12,44},{16,48},{20,52},{24,56},{28,60},{32,6... | collective-permute-start | bytes 1179656 | tf_op jit(solution)/shard_map/ppermute | solution.py:93
  25.4 9.6 %collective-permute-start.4 = (f32[4,32,768]{2,1,0:T(8,128)S(1)}, f32[4,32,768]{2,1,0:T(8,128)S(1)}, u32[]{:S(2)}, u32[]{:S(2)}) collective-permute-start(f32[4,32,768]{2,1,0:T(8,128)S(1)} %collective-permute-done.3), channel_id=1, source_target_pairs={{0,224},{4,228},{8,232},{12,236},{16,240},{20,244},{24,248},{28,25... | collective-permute-start | bytes 1179656 | tf_op jit(solution)/shard_map/ppermute | solution.py:90
  29.0 9.8 %collective-permute-start.8 = (f32[4,32,768]{2,1,0:T(8,128)S(1)}, f32[4,32,768]{2,1,0:T(8,128)S(1)}, u32[]{:S(2)}, u32[]{:S(2)}) collective-permute-start(f32[4,32,768]{2,1,0:T(8,128)S(1)} %collective-permute-done.7), channel_id=1, source_target_pairs={{0,32},{4,36},{8,40},{12,44},{16,48},{20,52},{24,56},{28,60},{32,6... | collective-permute-start | bytes 1179656 | tf_op jit(solution)/shard_map/ppermute | solution.py:93
  35.0 10.7 %collective-permute-start.5 = (f32[4,32,768]{2,1,0:T(8,128)S(1)}, f32[4,32,768]{2,1,0:T(8,128)S(1)}, u32[]{:S(2)}, u32[]{:S(2)}) collective-permute-start(f32[4,32,768]{2,1,0:T(8,128)S(1)} %collective-permute-done.4), channel_id=1, source_target_pairs={{0,224},{4,228},{8,232},{12,236},{16,240},{20,244},{24,248},{28,25... | collective-permute-start | bytes 1179656 | tf_op jit(solution)/shard_map/ppermute | solution.py:90
  38.8 15.9 %collective-permute-start.9 = (f32[4,32,768]{2,1,0:T(8,128)S(1)}, f32[4,32,768]{2,1,0:T(8,128)S(1)}, u32[]{:S(2)}, u32[]{:S(2)}) collective-permute-start(f32[4,32,768]{2,1,0:T(8,128)S(1)} %collective-permute-done.8), channel_id=1, source_target_pairs={{0,32},{4,36},{8,40},{12,44},{16,48},{20,52},{24,56},{28,60},{32,6... | collective-permute-start | bytes 1179656 | tf_op jit(solution)/shard_map/ppermute | solution.py:93
  45.7 9.0 %collective-permute-start.6 = (f32[4,32,768]{2,1,0:T(8,128)S(1)}, f32[4,32,768]{2,1,0:T(8,128)S(1)}, u32[]{:S(2)}, u32[]{:S(2)}) collective-permute-start(f32[4,32,768]{2,1,0:T(8,128)S(1)} %collective-permute-done.5), channel_id=1, source_target_pairs={{0,224},{4,228},{8,232},{12,236},{16,240},{20,244},{24,248},{28,25... | collective-permute-start | bytes 1179656 | tf_op jit(solution)/shard_map/ppermute | solution.py:90
  54.9 5.9 %copy-start = (f32[8,4,32,768]{3,2,1,0:T(8,128)}, f32[8,4,32,768]{3,2,1,0:T(8,128)S(1)}, u32[]{:S(2)}) copy-start(f32[8,4,32,768]{3,2,1,0:T(8,128)S(1)} %bitcast_dynamic-update-slice_fusion) | copy-start | bytes 9437188
  54.9 5.9 %collective-permute-start.10 = (f32[8,4,32,768]{3,2,1,0:T(8,128)S(1)}, f32[8,4,32,768]{3,2,1,0:T(8,128)}, u32[]{:S(2)}, u32[]{:S(2)}) collective-permute-start(f32[8,4,32,768]{3,2,1,0:T(8,128)S(1)} %bitcast_dynamic-update-slice_fusion), channel_id=1, source_target_pairs={{0,4},{4,0},{8,12},{12,8},{16,20},{20,16},{24,28},{28,24},{32,36},... | collective-permute-start | bytes 9437192 | tf_op jit(solution)/shard_map/ppermute | solution.py:99
  74.0 10.3 %all-to-all-start = ((f32[4,6,1024]{2,1,0:T(8,128)}), f32[4,6,1024]{2,1,0:T(8,128)S(1)}, u32[]{:S(2)}, u32[]{:S(2)}) async-start(f32[4,6,1024]{2,1,0:T(8,128)} %bitcast.47), calls=%async_computation | async-start | bytes 262144 | tf_op jit(solution)/shard_map/all_to_all | solution.py:147
  84.2 1.4 %copy-start.1 = (f32[6,1024]{1,0:T(8,128)}, f32[6,1024]{1,0:T(8,128)S(1)}, u32[]{:S(2)}) copy-start(f32[6,1024]{1,0:T(8,128)S(1)} %reduce_sum.9) | copy-start | bytes 73732

commit v6 on v5

--- a/solution.py
+++ b/solution.py
@@ -10,7 +10,7 @@
 half_step = 0.5
 
 
-def collide_kernel(idx_ref, near_ref, far_ref, w_ref, gain_ref, loss_ref, occ_ref, out_ref, sh_ref, rest_ref,
+def collide_kernel(idx_ref, near_ref, far_ref, gain_ref, loss_ref, occ_ref, out_ref, sh_ref, rest_ref,
                    *, shifts, nsub, sub_count, sub_width, bands):
     t = pl.program_id(0)
     half = near_ref.shape[0]
@@ -30,9 +30,8 @@
         acc_o = None
         for n in range(bands):
             p = m * bands + n
-            w = w_ref[p]
-            term_i = gain_ref[p].astype(jnp.float32) * w * sh_ref[n]
-            term_o = loss_ref[p].astype(jnp.float32) * w * rest_ref[n]
+            term_i = gain_ref[p] * sh_ref[n]
+            term_o = loss_ref[p] * rest_ref[n]
             acc_i = term_i if acc_i is None else acc_i + term_i
             acc_o = term_o if acc_o is None else acc_o + term_o
         inflow = jnp.sum(acc_i, axis=0, keepdims=True)
@@ -40,7 +39,7 @@
         out_ref[pl.ds(m, 1), :] = (1.0 - occ[m:m + 1]) * inflow - occ[m:m + 1] * outflow
 
 
-def collide(idx, near, far, weight_t, gain_t, loss_t, occ, sub_width, lanes=512):
+def collide(idx, near, far, gain_t, loss_t, occ, sub_width, lanes=512):
     pairs, shifts, width = gain_t.shape
     bands = occ.shape[0]
     sub_count = width // sub_width
@@ -56,7 +55,6 @@
             in_specs=[
                 pl.BlockSpec(near.shape, lambda t, i: (0, 0)),
                 pl.BlockSpec(far.shape, lambda t, i: (0, 0)),
-                pl.BlockSpec(weight_t.shape, lambda t, i: (0, 0, 0)),
                 pl.BlockSpec((pairs, shifts, lanes), lambda t, i: (0, 0, t)),
                 pl.BlockSpec((pairs, shifts, lanes), lambda t, i: (0, 0, t)),
                 pl.BlockSpec((bands, lanes), lambda t, i: (0, t)),
@@ -67,10 +65,10 @@
                 pltpu.VMEM((bands, shifts, lanes), jnp.float32),
             ],
         ),
-    )(idx, near, far, weight_t, gain_t, loss_t, occ)
+    )(idx, near, far, gain_t, loss_t, occ)
 
 
-def ring_gather(block, y_count, z_count):
+def ring_gather(block, y_count, z_count, riders):
     ka_count = 2 * y_count * z_count
     per_z = 2 * y_count
 
@@ -95,9 +93,10 @@
         return jnp.stack([ahead[d] for d in range(count)])
 
     along_y = ring(block, y_step, y_count)
+    along_y, riders = lax.optimization_barrier((along_y, riders))
     along_z = ring(along_y, z_step, z_count)
     other = lax.ppermute(along_z, "ka", pairs(lambda j: j ^ 1))
-    return along_z, other
+    return along_z, other, riders
 
 
 def body(occupation, gain_table, loss_table, owner, local_index, pair_mask, counts):
@@ -116,7 +115,11 @@
         .transpose(1, 0, 2)
         .reshape(sub_count, bands * sub_width)
     )
-    near, far = ring_gather(local_rows, y_count, z_count)
+    active = (jnp.arange(shifts, dtype=jnp.int32) < counts.reshape(())).astype(jnp.float32)
+    weight_t = (pair_mask.astype(jnp.float32) * active[:, None]).T[:, :, None]
+    gain_w = gain_table.transpose(1, 0, 2).astype(jnp.float32) * weight_t
+    loss_w = loss_table.transpose(1, 0, 2).astype(jnp.float32) * weight_t
+    near, far, (gain_w, loss_w) = ring_gather(local_rows, y_count, z_count, (gain_w, loss_w))
     near = near.reshape(ka_count * sub_count // 2, bands * sub_width)
     far = far.reshape(ka_count * sub_count // 2, bands * sub_width)
     me = lax.axis_index("ka")
@@ -130,15 +133,12 @@
     )
     sources = local_index.reshape(total_requests)
     picks = where * sub_count + sources
-    active = (jnp.arange(shifts, dtype=jnp.int32) < counts.reshape(())).astype(jnp.float32)
-    weight = pair_mask.astype(jnp.float32) * active[:, None]
     partial_terms = collide(
         picks,
         near,
         far,
-        weight.T[:, :, None],
-        gain_table.transpose(1, 0, 2),
-        loss_table.transpose(1, 0, 2),
+        gain_w,
+        loss_w,
         occupation,
         sub_width,
     )

time: 86.2 us -> 97.7 us (1.13)
  the two profiles are of different devices: /device:TPU:24 before, /device:TPU:1 now
where the time goes in v6:
time: 97.7 us; the launch traced here: 97.2 us
  starting transfers between devices  32.3 us (33%)
  waiting for transfers between devices  30.1 us (31%)
  other arithmetic  16.7 us (17%)
  Pallas kernels  14.6 us (15%)
  local copies, waits for them, and re-layouts  1.95 us (2%)
  between operations  1.45 us (1%)
    ppermute x6, starting transfers between devices, ring(): back = lax.ppermute(back, 'ka', step(-1))  22.3 us
    ppermute x6, waiting for transfers between devices, ring(): back = lax.ppermute(back, 'ka', step(-1))  21.8 us
    pallas_call x1, Pallas kernels, collide(): pl.pallas_call(kern, out_shape=jax.ShapeDtypeStruct((bands, width), jnp.f...  14.6 us
    mul x1, other arithmetic, body(): loss_w = loss_table.transpose(1, 0, 2).astype(jnp.float32) * weight_t  13.2 us
    ppermute x1, starting transfers between devices, ring_gather(): other = lax.ppermute(along_z, 'ka', pairs(lambda j: j ^ 1))  5.97 us
    all_to_all x1, waiting for transfers between devices, body(): collision = jnp.sum(lax.all_to_all(parts, 'pb', 0, 0, tiled=True), axis=0)  4.83 us
    all_to_all x1, starting transfers between devices, body(): collision = jnp.sum(lax.all_to_all(parts, 'pb', 0, 0, tiled=True), axis=0)  4.01 us
    ppermute x1, waiting for transfers between devices, ring_gather(): other = lax.ppermute(along_z, 'ka', pairs(lambda j: j ^ 1))  3.46 us
  transfers between devices with their start and end apart: 12, of which 7 were waited for; matrix products, arithmetic and copies ran while one was open for 17% of the time, Pallas kernels for 0%

profile of v6, /device:TPU:1, one launch (start us, length us, event | category | flops | bytes accessed | tf_op | source)
XLA Modules:
  0.0 97.2 jit_solution(4097163242298460084)
XLA Ops:
  0.6 0.9 copy.19
  1.6 3.6 %collective-permute-start = (f32[32,768]{1,0:T(8,128)S(1)}, f32[32,768]{1,0:T(8,128)S(1)}, u32[]{:S(2)}, u32[]{:S(2)}) collective-permute-start(f32[32,768]{1,0:T(8,128)S(1)} %bitcast.48), channel_id=1, source_target_pairs={{0,24},{4,28},{8,0},{12,4},{16,8},{20,12},{24,16},{28,20},{32,56},... | collective-permute-start | bytes 294920 | tf_op jit(solution)/shard_map/ppermute | solution.py:88
  5.2 0.0 collective-permute-start.2
  5.9 0.8 multiply_bitcast_fusion
  6.6 0.1 copy.15
  6.7 0.0 copy-start.1
  6.7 0.1 collective-permute-done
  6.8 3.0 %collective-permute-start.1 = (f32[32,768]{1,0:T(8,128)S(1)}, f32[32,768]{1,0:T(8,128)S(1)}, u32[]{:S(2)}, u32[]{:S(2)}) collective-permute-start(f32[32,768]{1,0:T(8,128)S(1)} %collective-permute-done), channel_id=1, source_target_pairs={{0,24},{4,28},{8,0},{12,4},{16,8},{20,12},{24,16},{28,20},{32,56},... | collective-permute-start | bytes 294920 | tf_op jit(solution)/shard_map/ppermute | solution.py:88
  9.9 13.2 %bitcast_multiply_fusion = (f32[36,16,4096]{2,1,0:T(8,128)}, f32[36,16,4096]{2,1,0:T(8,128)}) fusion(bf16[16,36,4096]{2,0,1:T(8,128)(2,1)} %param.9, f32[36,16]{1,0:T(8,128)S(1)} %copy.15, bf16[16,36,4096]{2,0,1:T(8,128)(2,1)} %param.8), kind=kLoop, calls=%fused_computation | loop fusion | flops 9437184 | bytes 28313856 | tf_op jit(solution)/shard_map/mul | solution.py:121
  23.1 0.0 copy-done.1
  23.1 0.0 collective-permute-done.2
  23.2 0.0 collective-permute-done.1
  23.2 0.0 copy-start.4
  23.2 0.0 copy-start.3
  23.2 5.7 %collective-permute-start.3 = (f32[4,32,768]{2,1,0:T(8,128)S(1)}, f32[4,32,768]{2,1,0:T(8,128)S(1)}, u32[]{:S(2)}, u32[]{:S(2)}) collective-permute-start(f32[4,32,768]{2,1,0:T(8,128)S(1)} %pad_maximum_fusion), channel_id=1, source_target_pairs={{0,224},{4,228},{8,232},{12,236},{16,240},{20,244},{24,248},{28,25... | collective-permute-start | bytes 1179656 | tf_op jit(solution)/shard_map/ppermute | solution.py:88
  28.9 0.0 collective-permute-start.7
  28.9 6.3 %collective-permute-done.3 = f32[4,32,768]{2,1,0:T(8,128)S(1)} collective-permute-done((f32[4,32,768]{2,1,0:T(8,128)S(1)}, f32[4,32,768]{2,1,0:T(8,128)S(1)}, u32[]{:S(2)}, u32[]{:S(2)}) %collective-permute-start.3) | collective-permute-done | bytes 393248 | tf_op jit(solution)/shard_map/ppermute | solution.py:88
  35.2 3.4 %collective-permute-start.4 = (f32[4,32,768]{2,1,0:T(8,128)S(1)}, f32[4,32,768]{2,1,0:T(8,128)S(1)}, u32[]{:S(2)}, u32[]{:S(2)}) collective-permute-start(f32[4,32,768]{2,1,0:T(8,128)S(1)} %collective-permute-done.3), channel_id=1, source_target_pairs={{0,224},{4,228},{8,232},{12,236},{16,240},{20,244},{24,248},{28,25... | collective-permute-start | bytes 1179656 | tf_op jit(solution)/shard_map/ppermute | solution.py:88
  38.6 0.0 collective-permute-done.7
  38.6 0.0 collective-permute-start.8
  38.6 5.4 %collective-permute-done.4 = f32[4,32,768]{2,1,0:T(8,128)S(1)} collective-permute-done((f32[4,32,768]{2,1,0:T(8,128)S(1)}, f32[4,32,768]{2,1,0:T(8,128)S(1)}, u32[]{:S(2)}, u32[]{:S(2)}) %collective-permute-start.4) | collective-permute-done | bytes 393248 | tf_op jit(solution)/shard_map/ppermute | solution.py:88
  44.0 3.4 %collective-permute-start.5 = (f32[4,32,768]{2,1,0:T(8,128)S(1)}, f32[4,32,768]{2,1,0:T(8,128)S(1)}, u32[]{:S(2)}, u32[]{:S(2)}) collective-permute-start(f32[4,32,768]{2,1,0:T(8,128)S(1)} %collective-permute-done.4), channel_id=1, source_target_pairs={{0,224},{4,228},{8,232},{12,236},{16,240},{20,244},{24,248},{28,25... | collective-permute-start | bytes 1179656 | tf_op jit(solution)/shard_map/ppermute | solution.py:88
  47.5 0.0 collective-permute-done.8
  47.5 0.1 collective-permute-start.9
  47.6 4.6 %collective-permute-done.5 = f32[4,32,768]{2,1,0:T(8,128)S(1)} collective-permute-done((f32[4,32,768]{2,1,0:T(8,128)S(1)}, f32[4,32,768]{2,1,0:T(8,128)S(1)}, u32[]{:S(2)}, u32[]{:S(2)}) %collective-permute-start.5) | collective-permute-done | bytes 393248 | tf_op jit(solution)/shard_map/ppermute | solution.py:88
  52.1 3.1 %collective-permute-start.6 = (f32[4,32,768]{2,1,0:T(8,128)S(1)}, f32[4,32,768]{2,1,0:T(8,128)S(1)}, u32[]{:S(2)}, u32[]{:S(2)}) collective-permute-start(f32[4,32,768]{2,1,0:T(8,128)S(1)} %collective-permute-done.5), channel_id=1, source_target_pairs={{0,224},{4,228},{8,232},{12,236},{16,240},{20,244},{24,248},{28,25... | collective-permute-start | bytes 1179656 | tf_op jit(solution)/shard_map/ppermute | solution.py:88
  55.3 5.4 %collective-permute-done.6 = f32[4,32,768]{2,1,0:T(8,128)S(1)} collective-permute-done((f32[4,32,768]{2,1,0:T(8,128)S(1)}, f32[4,32,768]{2,1,0:T(8,128)S(1)}, u32[]{:S(2)}, u32[]{:S(2)}) %collective-permute-start.6) | collective-permute-done | bytes 393248 | tf_op jit(solution)/shard_map/ppermute | solution.py:88
  60.8 0.0 collective-permute-done.9
  60.9 0.0 copy-start
  60.9 6.0 %collective-permute-start.10 = (f32[8,4,32,768]{3,2,1,0:T(8,128)S(1)}, f32[8,4,32,768]{3,2,1,0:T(8,128)}, u32[]{:S(2)}, u32[]{:S(2)}) collective-permute-start(f32[8,4,32,768]{3,2,1,0:T(8,128)S(1)} %bitcast_dynamic-update-slice_fusion), channel_id=1, source_target_pairs={{0,4},{4,0},{8,12},{12,8},{16,20},{20,16},{24,28},{28,24},{32,36},... | collective-permute-start | bytes 9437192 | tf_op jit(solution)/shard_map/ppermute | solution.py:98
  66.9 0.5 broadcast.44
  67.4 0.0 copy-done.4
  67.4 0.7 reduce.3
  68.0 0.1 reshape.34
  68.1 0.0 copy-done.3
  68.1 0.1 reshape.35
  68.2 0.6 fusion.5.idx_ref
  68.8 3.5 %collective-permute-done.10 = f32[8,4,32,768]{3,2,1,0:T(8,128)} collective-permute-done((f32[8,4,32,768]{3,2,1,0:T(8,128)S(1)}, f32[8,4,32,768]{3,2,1,0:T(8,128)}, u32[]{:S(2)}, u32[]{:S(2)}) %collective-permute-start.10) | collective-permute-done | bytes 3145760 | tf_op jit(solution)/shard_map/ppermute | solution.py:98
  72.3 0.0 copy-done
  72.3 14.6 %shard_map.86 = f32[6,4096]{1,0:T(8,128)} custom-call(s32[512]{0:T(512)} %fusion.5.idx_ref, f32[1024,768]{1,0:T(8,128)} %bitcast.42, f32[1024,768]{1,0:T(8,128)} %bitcast.19.far_ref, f32[36,16,4096]{2,1,0:T(8,128)} %get-tuple-element.6.gain_ref, f32[36,16,4096]{2,1,0:T(8,128)} %get-tuple-element.7.loss_ref, f32[6,4096]{1,0:T(8,128)} %occ_ref.1), custom_call_target="tpu_custom_call" | custom-call | tf_op jit(solution)/shard_map/pallas_call | solution.py:49
  86.9 4.0 %all-to-all-start = ((f32[4,6,1024]{2,1,0:T(8,128)}), f32[4,6,1024]{2,1,0:T(8,128)S(1)}, u32[]{:S(2)}, u32[]{:S(2)}) async-start(f32[4,6,1024]{2,1,0:T(8,128)} %bitcast.45), calls=%async_computation | async-start | bytes 262144 | tf_op jit(solution)/shard_map/all_to_all | solution.py:147
  90.9 4.8 %all-to-all-done = f32[4,6,1024]{2,1,0:T(8,128)S(1)} async-done(((f32[4,6,1024]{2,1,0:T(8,128)}), f32[4,6,1024]{2,1,0:T(8,128)S(1)}, u32[]{:S(2)}, u32[]{:S(2)}) %all-to-all-start) | async-done | bytes 98336 | tf_op jit(solution)/shard_map/all_to_all | solution.py:147
  95.8 0.0 copy-start.2
  95.8 1.4 %multiply_add_fusion = f32[6,1024]{1,0:T(8,128)} fusion(f32[6,1024]{1,0:T(8,128)S(1)} %reduce_sum.9, f32[6,4096]{1,0:T(8,128)} %occ_ref.1, s32[]{:T(128)S(6)} %select_n.57), kind=kLoop, calls=%fused_computation.12 | loop fusion | flops 12288 | bytes 73732 | tf_op jit(solution)/shard_map/add | solution.py:151
  97.2 0.0 copy-done.2
  (12 shorter events, 0.3 us)
Async XLA Ops:
  1.6 5.3 %collective-permute-start = (f32[32,768]{1,0:T(8,128)S(1)}, f32[32,768]{1,0:T(8,128)S(1)}, u32[]{:S(2)}, u32[]{:S(2)}) collective-permute-start(f32[32,768]{1,0:T(8,128)S(1)} %bitcast.48), channel_id=1, source_target_pairs={{0,24},{4,28},{8,0},{12,4},{16,8},{20,12},{24,16},{28,20},{32,56},... | collective-permute-start | bytes 294920 | tf_op jit(solution)/shard_map/ppermute | solution.py:88
  5.2 18.0 %collective-permute-start.2 = (f32[32,768]{1,0:T(8,128)S(1)}, f32[32,768]{1,0:T(8,128)S(1)}, u32[]{:S(2)}, u32[]{:S(2)}) collective-permute-start(f32[32,768]{1,0:T(8,128)S(1)} %bitcast.49), channel_id=1, source_target_pairs={{0,8},{4,12},{8,16},{12,20},{16,24},{20,28},{24,0},{28,4},{32,40},... | collective-permute-start | bytes 294920 | tf_op jit(solution)/shard_map/ppermute | solution.py:91
  6.7 16.4 %copy-start.1 = (f32[6,4096]{1,0:T(8,128)S(1)}, f32[6,4096]{1,0:T(8,128)}, u32[]{:S(2)}) copy-start(f32[6,4096]{1,0:T(8,128)} %occ_ref.1) | copy-start | bytes 294916
  6.8 16.3 %collective-permute-start.1 = (f32[32,768]{1,0:T(8,128)S(1)}, f32[32,768]{1,0:T(8,128)S(1)}, u32[]{:S(2)}, u32[]{:S(2)}) collective-permute-start(f32[32,768]{1,0:T(8,128)S(1)} %collective-permute-done), channel_id=1, source_target_pairs={{0,24},{4,28},{8,0},{12,4},{16,8},{20,12},{24,16},{28,20},{32,56},... | collective-permute-start | bytes 294920 | tf_op jit(solution)/shard_map/ppermute | solution.py:88
  23.2 44.2 %copy-start.4 = (s32[1,1,16,32,1]{3,4,2,1,0:T(1,128)S(1)}, s32[1,1,16,32,1]{3,4,2,1,0:T(1,128)}, u32[]{:S(2)}) copy-start(s32[1,1,16,32,1]{3,4,2,1,0:T(1,128)} %param.10) | copy-start | bytes 6148
  23.2 44.9 %copy-start.3 = (s32[1,1,16,32]{3,2,1,0:T(8,128)S(1)}, s32[1,1,16,32]{3,2,1,0:T(8,128)}, u32[]{:S(2)}) copy-start(s32[1,1,16,32]{3,2,1,0:T(8,128)} %param.11) | copy-start | bytes 6148
  23.2 12.0 %collective-permute-start.3 = (f32[4,32,768]{2,1,0:T(8,128)S(1)}, f32[4,32,768]{2,1,0:T(8,128)S(1)}, u32[]{:S(2)}, u32[]{:S(2)}) collective-permute-start(f32[4,32,768]{2,1,0:T(8,128)S(1)} %pad_maximum_fusion), channel_id=1, source_target_pairs={{0,224},{4,228},{8,232},{12,236},{16,240},{20,244},{24,248},{28,25... | collective-permute-start | bytes 1179656 | tf_op jit(solution)/shard_map/ppermute | solution.py:88
  28.9 9.7 %collective-permute-start.7 = (f32[4,32,768]{2,1,0:T(8,128)S(1)}, f32[4,32,768]{2,1,0:T(8,128)S(1)}, u32[]{:S(2)}, u32[]{:S(2)}) collective-permute-start(f32[4,32,768]{2,1,0:T(8,128)S(1)} %pad_maximum_fusion), channel_id=1, source_target_pairs={{0,32},{4,36},{8,40},{12,44},{16,48},{20,52},{24,56},{28,60},{32,6... | collective-permute-start | bytes 1179656 | tf_op jit(solution)/shard_map/ppermute | solution.py:91
  35.2 8.8 %collective-permute-start.4 = (f32[4,32,768]{2,1,0:T(8,128)S(1)}, f32[4,32,768]{2,1,0:T(8,128)S(1)}, u32[]{:S(2)}, u32[]{:S(2)}) collective-permute-start(f32[4,32,768]{2,1,0:T(8,128)S(1)} %collective-permute-done.3), channel_id=1, source_target_pairs={{0,224},{4,228},{8,232},{12,236},{16,240},{20,244},{24,248},{28,25... | collective-permute-start | bytes 1179656 | tf_op jit(solution)/shard_map/ppermute | solution.py:88
  38.6 8.9 %collective-permute-start.8 = (f32[4,32,768]{2,1,0:T(8,128)S(1)}, f32[4,32,768]{2,1,0:T(8,128)S(1)}, u32[]{:S(2)}, u32[]{:S(2)}) collective-permute-start(f32[4,32,768]{2,1,0:T(8,128)S(1)} %collective-permute-done.7), channel_id=1, source_target_pairs={{0,32},{4,36},{8,40},{12,44},{16,48},{20,52},{24,56},{28,60},{32,6... | collective-permute-start | bytes 1179656 | tf_op jit(solution)/shard_map/ppermute | solution.py:91
  44.0 8.1 %collective-permute-start.5 = (f32[4,32,768]{2,1,0:T(8,128)S(1)}, f32[4,32,768]{2,1,0:T(8,128)S(1)}, u32[]{:S(2)}, u32[]{:S(2)}) collective-permute-start(f32[4,32,768]{2,1,0:T(8,128)S(1)} %collective-permute-done.4), channel_id=1, source_target_pairs={{0,224},{4,228},{8,232},{12,236},{16,240},{20,244},{24,248},{28,25... | collective-permute-start | bytes 1179656 | tf_op jit(solution)/shard_map/ppermute | solution.py:88
  47.5 13.3 %collective-permute-start.9 = (f32[4,32,768]{2,1,0:T(8,128)S(1)}, f32[4,32,768]{2,1,0:T(8,128)S(1)}, u32[]{:S(2)}, u32[]{:S(2)}) collective-permute-start(f32[4,32,768]{2,1,0:T(8,128)S(1)} %collective-permute-done.8), channel_id=1, source_target_pairs={{0,32},{4,36},{8,40},{12,44},{16,48},{20,52},{24,56},{28,60},{32,6... | collective-permute-start | bytes 1179656 | tf_op jit(solution)/shard_map/ppermute | solution.py:91
  52.1 8.6 %collective-permute-start.6 = (f32[4,32,768]{2,1,0:T(8,128)S(1)}, f32[4,32,768]{2,1,0:T(8,128)S(1)}, u32[]{:S(2)}, u32[]{:S(2)}) collective-permute-start(f32[4,32,768]{2,1,0:T(8,128)S(1)} %collective-permute-done.5), channel_id=1, source_target_pairs={{0,224},{4,228},{8,232},{12,236},{16,240},{20,244},{24,248},{28,25... | collective-permute-start | bytes 1179656 | tf_op jit(solution)/shard_map/ppermute | solution.py:88
  60.9 11.4 %copy-start = (f32[8,4,32,768]{3,2,1,0:T(8,128)}, f32[8,4,32,768]{3,2,1,0:T(8,128)S(1)}, u32[]{:S(2)}) copy-start(f32[8,4,32,768]{3,2,1,0:T(8,128)S(1)} %bitcast_dynamic-update-slice_fusion) | copy-start | bytes 9437188
  60.9 11.4 %collective-permute-start.10 = (f32[8,4,32,768]{3,2,1,0:T(8,128)S(1)}, f32[8,4,32,768]{3,2,1,0:T(8,128)}, u32[]{:S(2)}, u32[]{:S(2)}) collective-permute-start(f32[8,4,32,768]{3,2,1,0:T(8,128)S(1)} %bitcast_dynamic-update-slice_fusion), channel_id=1, source_target_pairs={{0,4},{4,0},{8,12},{12,8},{16,20},{20,16},{24,28},{28,24},{32,36},... | collective-permute-start | bytes 9437192 | tf_op jit(solution)/shard_map/ppermute | solution.py:98
  86.9 8.8 %all-to-all-start = ((f32[4,6,1024]{2,1,0:T(8,128)}), f32[4,6,1024]{2,1,0:T(8,128)S(1)}, u32[]{:S(2)}, u32[]{:S(2)}) async-start(f32[4,6,1024]{2,1,0:T(8,128)} %bitcast.45), calls=%async_computation | async-start | bytes 262144 | tf_op jit(solution)/shard_map/all_to_all | solution.py:147
  95.8 1.4 %copy-start.2 = (f32[6,1024]{1,0:T(8,128)}, f32[6,1024]{1,0:T(8,128)S(1)}, u32[]{:S(2)}) copy-start(f32[6,1024]{1,0:T(8,128)S(1)} %reduce_sum.9) | copy-start | bytes 73732

commit v7 on v4

--- a/solution.py
+++ b/solution.py
@@ -10,12 +10,20 @@
 half_step = 0.5
 
 
-def collide_kernel(idx_ref, g_ref, w_ref, gain_ref, loss_ref, occ_ref, out_ref, sh_ref, rest_ref,
+def collide_kernel(idx_ref, a_ref, b_ref, c_ref, d_ref, w_ref, gain_ref, loss_ref, occ_ref, out_ref, sh_ref, rest_ref,
                    *, shifts, nsub, sub_count, sub_width, bands):
     t = pl.program_id(0)
+    quarter = a_ref.shape[0]
     for s in range(shifts):
         for jj in range(nsub):
-            row = g_ref[pl.ds(idx_ref[s * sub_count + t * nsub + jj], 1), :]
+            at = idx_ref[s * sub_count + t * nsub + jj]
+            part = at // quarter
+            off = at % quarter
+            row = jnp.where(
+                part < 2,
+                jnp.where(part == 0, a_ref[pl.ds(off, 1), :], b_ref[pl.ds(off, 1), :]),
+                jnp.where(part == 2, c_ref[pl.ds(off, 1), :], d_ref[pl.ds(off, 1), :]),
+            )
             for n in range(bands):
                 piece = row[:, n * sub_width:(n + 1) * sub_width]
                 sh_ref[n, pl.ds(s, 1), pl.ds(jj * sub_width, sub_width)] = piece
@@ -36,7 +44,7 @@
         out_ref[pl.ds(m, 1), :] = (1.0 - occ[m:m + 1]) * inflow - occ[m:m + 1] * outflow
 
 
-def collide(idx, rows, weight_t, gain_t, loss_t, occ, sub_width, lanes=512):
+def collide(idx, quads, weight_t, gain_t, loss_t, occ, sub_width, lanes=512):
     pairs, shifts, width = gain_t.shape
     bands = occ.shape[0]
     sub_count = width // sub_width
@@ -50,7 +58,7 @@
             num_scalar_prefetch=1,
             grid=(width // lanes,),
             in_specs=[
-                pl.BlockSpec(rows.shape, lambda t, i: (0, 0)),
+                *[pl.BlockSpec(q.shape, lambda t, i: (0, 0)) for q in quads],
                 pl.BlockSpec(weight_t.shape, lambda t, i: (0, 0, 0)),
                 pl.BlockSpec((pairs, shifts, lanes), lambda t, i: (0, 0, t)),
                 pl.BlockSpec((pairs, shifts, lanes), lambda t, i: (0, 0, t)),
@@ -62,7 +70,7 @@
                 pltpu.VMEM((bands, shifts, lanes), jnp.float32),
             ],
         ),
-    )(idx, rows, weight_t, gain_t, loss_t, occ)
+    )(idx, *quads, weight_t, gain_t, loss_t, occ)
 
 
 def ring_gather(block, y_count, z_count):
@@ -89,10 +97,19 @@
                 ahead[count - d] = fwd
         return jnp.stack([ahead[d] for d in range(count)])
 
-    along_y = ring(block, y_step, y_count)
-    along_z = ring(along_y, z_step, z_count)
-    other = lax.ppermute(along_z, "ka", pairs(lambda j: j ^ 1))
-    return jnp.stack([along_z, other])
+    half = block.shape[0] // 2
+    first, second = block[:half], block[half:]
+    first_y = ring(first, y_step, y_count)
+    second_z = ring(second, z_step, z_count)
+    first_yz = ring(first_y, z_step, z_count)
+    second_zy = ring(second_z, y_step, y_count)
+    swap = pairs(lambda j: j ^ 1)
+    return (
+        first_yz,
+        lax.ppermute(first_yz, "ka", swap),
+        second_zy,
+        lax.ppermute(second_zy, "ka", swap),
+    )
 
 
 def body(occupation, gain_table, loss_table, owner, local_index, pair_mask, counts):
@@ -111,25 +128,33 @@
         .transpose(1, 0, 2)
         .reshape(sub_count, bands * sub_width)
     )
-    rows = ring_gather(local_rows, y_count, z_count).reshape(
-        ka_count * sub_count, bands * sub_width
-    )
+    quads = [
+        q.reshape(ka_count * sub_count // 4, bands * sub_width)
+        for q in ring_gather(local_rows, y_count, z_count)
+    ]
     me = lax.axis_index("ka")
     my_z, my_y, my_c = me // (2 * y_count), (me // 2) % y_count, me % 2
     owners = owner.reshape(total_requests)
     o_z, o_y, o_c = owners // (2 * y_count), (owners // 2) % y_count, owners % 2
-    where = (
-        (o_c ^ my_c) * (z_count * y_count)
-        + ((o_z - my_z) % z_count) * y_count
-        + (o_y - my_y) % y_count
+    sources = local_index.reshape(total_requests)
+    half_sub = sub_count // 2
+    core_off = o_c ^ my_c
+    dz = (o_z - my_z) % z_count
+    dy = (o_y - my_y) % y_count
+    low = sources < half_sub
+    picks = jnp.where(
+        low,
+        ((core_off * z_count + dz) * y_count + dy) * half_sub + sources,
+        ka_count * half_sub
+        + ((core_off * y_count + dy) * z_count + dz) * half_sub
+        + sources
+        - half_sub,
     )
-    sources = local_index.reshape(total_requests)
-    picks = where * sub_count + sources
     active = (jnp.arange(shifts, dtype=jnp.int32) < counts.reshape(())).astype(jnp.float32)
     weight = pair_mask.astype(jnp.float32) * active[:, None]
     partial_terms = collide(
         picks,
-        rows,
+        quads,
         weight.T[:, :, None],
         gain_table.transpose(1, 0, 2),
         loss_table.transpose(1, 0, 2),

time: 90.7 us -> 90.6 us (level)
  the two profiles are of different devices: /device:TPU:24 before, /device:TPU:96 now
where the time goes in v7:
time: 90.6 us; the launch traced here: 90 us
  waiting for transfers between devices  33.7 us (37%)
  starting transfers between devices  33.3 us (37%)
  Pallas kernels  14.3 us (16%)
  local copies, waits for them, and re-layouts  3.61 us (4%)
  other arithmetic  3.59 us (4%)
  between operations  1.55 us (2%)
    ppermute x12, waiting for transfers between devices, ring(): back = lax.ppermute(back, 'ka', step(-1))  27.3 us
    ppermute x8, starting transfers between devices, ring(): fwd = lax.ppermute(fwd, 'ka', step(1))  20.5 us
    pallas_call x1, Pallas kernels, collide(): pl.pallas_call(kern, out_shape=jax.ShapeDtypeStruct((bands, width), jnp.f...  14.3 us
    ppermute x12, starting transfers between devices, ring(): back = lax.ppermute(back, 'ka', step(-1))  8.41 us
    all_to_all x1, waiting for transfers between devices, body(): collision = jnp.sum(lax.all_to_all(parts, 'pb', 0, 0, tiled=True), axis=0)  5.98 us
    all_to_all x1, starting transfers between devices, body(): collision = jnp.sum(lax.all_to_all(parts, 'pb', 0, 0, tiled=True), axis=0)  4.29 us
  transfers between devices with their start and end apart: 23, of which 8 were waited for; matrix products, arithmetic and copies ran while one was open for 4% of the time, Pallas kernels for 0%

profile of v7, /device:TPU:96, one launch (start us, length us, event | category | flops | bytes accessed | tf_op | source)
XLA Modules:
  0.0 90.0 jit_solution(4043564852113857196)
XLA Ops:
  0.6 0.9 fusion.8
  1.5 3.2 %collective-permute-start.15 = (f32[16,768]{1,0:T(8,128)S(1)}, f32[16,768]{1,0:T(8,128)S(1)}, u32[]{:S(2)}, u32[]{:S(2)}) collective-permute-start(f32[16,768]{1,0:T(8,128)S(1)} %bitcast.86), channel_id=1, source_target_pairs={{0,32},{4,36},{8,40},{12,44},{16,48},{20,52},{24,56},{28,60},{32,6... | collective-permute-start | bytes 147464 | tf_op jit(solution)/shard_map/ppermute | solution.py:96
  4.7 0.0 collective-permute-start.11
  4.8 1.7 %collective-permute-start.2 = (f32[16,768]{1,0:T(8,128)S(1)}, f32[16,768]{1,0:T(8,128)S(1)}, u32[]{:S(2)}, u32[]{:S(2)}) collective-permute-start(f32[16,768]{1,0:T(8,128)S(1)} %bitcast.84), channel_id=1, source_target_pairs={{0,8},{4,12},{8,16},{12,20},{16,24},{20,28},{24,0},{28,4},{32,40},... | collective-permute-start | bytes 147464 | tf_op jit(solution)/shard_map/ppermute | solution.py:96
  6.4 1.7 %collective-permute-start = (f32[16,768]{1,0:T(8,128)S(1)}, f32[16,768]{1,0:T(8,128)S(1)}, u32[]{:S(2)}, u32[]{:S(2)}) collective-permute-start(f32[16,768]{1,0:T(8,128)S(1)} %bitcast.85), channel_id=1, source_target_pairs={{0,24},{4,28},{8,0},{12,4},{16,8},{20,12},{24,16},{28,20},{32,56},... | collective-permute-start | bytes 147464 | tf_op jit(solution)/shard_map/ppermute | solution.py:93
  8.1 0.0 collective-permute-done.15
  8.1 3.3 %collective-permute-start.16 = (f32[16,768]{1,0:T(8,128)S(1)}, f32[16,768]{1,0:T(8,128)S(1)}, u32[]{:S(2)}, u32[]{:S(2)}) collective-permute-start(f32[16,768]{1,0:T(8,128)S(1)} %collective-permute-done.15), channel_id=1, source_target_pairs={{0,32},{4,36},{8,40},{12,44},{16,48},{20,52},{24,56},{28,60},{32,6... | collective-permute-start | bytes 147464 | tf_op jit(solution)/shard_map/ppermute | solution.py:96
  11.4 0.0 collective-permute-done.11
  11.4 0.0 collective-permute-start.12
  11.5 0.0 collective-permute-done
  11.5 1.9 %collective-permute-start.1 = (f32[16,768]{1,0:T(8,128)S(1)}, f32[16,768]{1,0:T(8,128)S(1)}, u32[]{:S(2)}, u32[]{:S(2)}) collective-permute-start(f32[16,768]{1,0:T(8,128)S(1)} %collective-permute-done), channel_id=1, source_target_pairs={{0,24},{4,28},{8,0},{12,4},{16,8},{20,12},{24,16},{28,20},{32,56},... | collective-permute-start | bytes 147464 | tf_op jit(solution)/shard_map/ppermute | solution.py:93
  13.4 0.0 collective-permute-done.2
  13.4 2.2 %collective-permute-done.1 = f32[16,768]{1,0:T(8,128)S(1)} collective-permute-done((f32[16,768]{1,0:T(8,128)S(1)}, f32[16,768]{1,0:T(8,128)S(1)}, u32[]{:S(2)}, u32[]{:S(2)}) %collective-permute-start.1) | collective-permute-done | bytes 49184 | tf_op jit(solution)/shard_map/ppermute | solution.py:93
  15.6 0.1 collective-permute-start.3
  15.7 3.2 %collective-permute-start.7 = (f32[4,16,768]{2,1,0:T(8,128)S(1)}, f32[4,16,768]{2,1,0:T(8,128)S(1)}, u32[]{:S(2)}, u32[]{:S(2)}) collective-permute-start(f32[4,16,768]{2,1,0:T(8,128)S(1)} %pad_maximum_fusion.1), channel_id=1, source_target_pairs={{0,32},{4,36},{8,40},{12,44},{16,48},{20,52},{24,56},{28,60},{32,6... | collective-permute-start | bytes 589832 | tf_op jit(solution)/shard_map/ppermute | solution.py:96
  19.0 0.0 collective-permute-done.16
  19.0 2.0 %collective-permute-start.17 = (f32[16,768]{1,0:T(8,128)S(1)}, f32[16,768]{1,0:T(8,128)S(1)}, u32[]{:S(2)}, u32[]{:S(2)}) collective-permute-start(f32[16,768]{1,0:T(8,128)S(1)} %collective-permute-done.16), channel_id=1, source_target_pairs={{0,32},{4,36},{8,40},{12,44},{16,48},{20,52},{24,56},{28,60},{32,6... | collective-permute-start | bytes 147464 | tf_op jit(solution)/shard_map/ppermute | solution.py:96
  21.0 0.0 collective-permute-done.12
  21.0 0.1 collective-permute-start.13
  21.1 5.5 %collective-permute-done.13 = f32[16,768]{1,0:T(8,128)S(1)} collective-permute-done((f32[16,768]{1,0:T(8,128)S(1)}, f32[16,768]{1,0:T(8,128)S(1)}, u32[]{:S(2)}, u32[]{:S(2)}) %collective-permute-start.13) | collective-permute-done | bytes 49184 | tf_op jit(solution)/shard_map/ppermute | solution.py:93
  26.6 0.0 collective-permute-start.14
  26.6 5.3 %collective-permute-done.14 = f32[16,768]{1,0:T(8,128)S(1)} collective-permute-done((f32[16,768]{1,0:T(8,128)S(1)}, f32[16,768]{1,0:T(8,128)S(1)}, u32[]{:S(2)}, u32[]{:S(2)}) %collective-permute-start.14) | collective-permute-done | bytes 49184 | tf_op jit(solution)/shard_map/ppermute | solution.py:93
  31.9 0.0 collective-permute-done.17
  31.9 0.6 collective-permute-start.20
  32.5 2.9 %collective-permute-start.18 = (f32[8,16,768]{2,1,0:T(8,128)S(1)}, f32[8,16,768]{2,1,0:T(8,128)S(1)}, u32[]{:S(2)}, u32[]{:S(2)}) collective-permute-start(f32[8,16,768]{2,1,0:T(8,128)S(1)} %bitcast_dynamic-update-slice_fusion.8), channel_id=1, source_target_pairs={{0,24},{4,28},{8,0},{12,4},{16,8},{20,12},{24,16},{28,20},{32,56},... | collective-permute-start | bytes 1179656 | tf_op jit(solution)/shard_map/ppermute | solution.py:93
  35.5 0.0 collective-permute-done.3
  35.5 0.0 collective-permute-start.4
  35.5 0.0 collective-permute-done.7
  35.5 3.2 %collective-permute-start.8 = (f32[4,16,768]{2,1,0:T(8,128)S(1)}, f32[4,16,768]{2,1,0:T(8,128)S(1)}, u32[]{:S(2)}, u32[]{:S(2)}) collective-permute-start(f32[4,16,768]{2,1,0:T(8,128)S(1)} %collective-permute-done.7), channel_id=1, source_target_pairs={{0,32},{4,36},{8,40},{12,44},{16,48},{20,52},{24,56},{28,60},{32,6... | collective-permute-start | bytes 589832 | tf_op jit(solution)/shard_map/ppermute | solution.py:96
  38.7 5.0 %collective-permute-done.4 = f32[4,16,768]{2,1,0:T(8,128)S(1)} collective-permute-done((f32[4,16,768]{2,1,0:T(8,128)S(1)}, f32[4,16,768]{2,1,0:T(8,128)S(1)}, u32[]{:S(2)}, u32[]{:S(2)}) %collective-permute-start.4) | collective-permute-done | bytes 196640 | tf_op jit(solution)/shard_map/ppermute | solution.py:93
  43.7 0.0 collective-permute-start.5
  43.7 0.0 collective-permute-done.8
  43.7 3.2 %collective-permute-start.9 = (f32[4,16,768]{2,1,0:T(8,128)S(1)}, f32[4,16,768]{2,1,0:T(8,128)S(1)}, u32[]{:S(2)}, u32[]{:S(2)}) collective-permute-start(f32[4,16,768]{2,1,0:T(8,128)S(1)} %collective-permute-done.8), channel_id=1, source_target_pairs={{0,32},{4,36},{8,40},{12,44},{16,48},{20,52},{24,56},{28,60},{32,6... | collective-permute-start | bytes 589832 | tf_op jit(solution)/shard_map/ppermute | solution.py:96
  47.0 0.0 collective-permute-done.18
  47.0 1.7 %collective-permute-start.19 = (f32[8,16,768]{2,1,0:T(8,128)S(1)}, f32[8,16,768]{2,1,0:T(8,128)S(1)}, u32[]{:S(2)}, u32[]{:S(2)}) collective-permute-start(f32[8,16,768]{2,1,0:T(8,128)S(1)} %collective-permute-done.18), channel_id=1, source_target_pairs={{0,24},{4,28},{8,0},{12,4},{16,8},{20,12},{24,16},{28,20},{32,56},... | collective-permute-start | bytes 1179656 | tf_op jit(solution)/shard_map/ppermute | solution.py:93
  48.7 2.4 %collective-permute-done.5 = f32[4,16,768]{2,1,0:T(8,128)S(1)} collective-permute-done((f32[4,16,768]{2,1,0:T(8,128)S(1)}, f32[4,16,768]{2,1,0:T(8,128)S(1)}, u32[]{:S(2)}, u32[]{:S(2)}) %collective-permute-start.5) | collective-permute-done | bytes 196640 | tf_op jit(solution)/shard_map/ppermute | solution.py:93
  51.1 0.0 collective-permute-start.6
  51.2 6.9 %collective-permute-done.6 = f32[4,16,768]{2,1,0:T(8,128)S(1)} collective-permute-done((f32[4,16,768]{2,1,0:T(8,128)S(1)}, f32[4,16,768]{2,1,0:T(8,128)S(1)}, u32[]{:S(2)}, u32[]{:S(2)}) %collective-permute-start.6) | collective-permute-done | bytes 196640 | tf_op jit(solution)/shard_map/ppermute | solution.py:93
  58.0 0.0 collective-permute-done.9
  58.1 0.0 copy-start.1
  58.1 0.1 collective-permute-start.10
  58.2 0.0 collective-permute-done.20
  58.2 0.0 collective-permute-done.19
  58.3 0.0 copy-start.3
  58.3 0.0 copy-start.4
  58.3 0.1 pad_maximum_fusion
  58.4 0.9 copy-done.1
  59.3 0.0 collective-permute-start.21
  59.9 0.0 copy-done.3
  59.9 0.1 reshape.41
  60.0 0.5 broadcast.58
  60.5 0.0 copy-done.4
  60.5 0.7 reduce.3
  61.2 0.1 reshape.42
  61.3 0.8 multiply_bitcast_fusion
  62.1 0.9 %copy.17.w_ref = f32[36,16,1]{2,1,0:T(8,128)} copy(f32[36,16,1]{0,1,2:T(8,128)S(1)} %multiply_bitcast_fusion) | data formatting | bytes 4608 | tf_op jit(solution)/shard_map/broadcast_in_dim | solution.py:158
  63.0 0.6 add_select_fusion.6.idx_ref
  63.6 0.0 collective-permute-done.10
  63.6 0.4 collective-permute-done.21
  64.0 14.3 %shard_map.86 = f32[6,4096]{1,0:T(8,128)} custom-call(s32[512]{0:T(512)} %add_select_fusion.6.idx_ref, f32[512,768]{1,0:T(8,128)} %bitcast.69, f32[512,768]{1,0:T(8,128)} %bitcast.14.b_ref, f32[512,768]{1,0:T(8,128)} %bitcast.66, f32[512,768]{1,0:T(8,128)} %bitcast.28.d_ref, f32[36,16,1]{2,1,0:T(8,128)} %copy.17.w_ref, bf16[36,16,4096]{2,1,0:T(8,128)(2,1)} %bitcast.67, ...), custom_call_target="tpu_custom_call" | custom-call | tf_op jit(solution)/shard_map/pallas_call | solution.py:54
  78.3 4.3 %all-to-all-start = ((f32[4,6,1024]{2,1,0:T(8,128)}), f32[4,6,1024]{2,1,0:T(8,128)S(1)}, u32[]{:S(2)}, u32[]{:S(2)}) async-start(f32[4,6,1024]{2,1,0:T(8,128)} %bitcast.73), calls=%async_computation | async-start | bytes 262144 | tf_op jit(solution)/shard_map/all_to_all | solution.py:166
  82.6 6.0 %all-to-all-done = f32[4,6,1024]{2,1,0:T(8,128)S(1)} async-done(((f32[4,6,1024]{2,1,0:T(8,128)}), f32[4,6,1024]{2,1,0:T(8,128)S(1)}, u32[]{:S(2)}, u32[]{:S(2)}) %all-to-all-start) | async-done | bytes 98336 | tf_op jit(solution)/shard_map/all_to_all | solution.py:166
  88.6 0.0 copy-start.2
  88.6 1.4 %multiply_add_fusion = f32[6,1024]{1,0:T(8,128)} fusion(f32[6,1024]{1,0:T(8,128)S(1)} %reduce_sum.9, f32[6,4096]{1,0:T(8,128)} %occ_ref.1, s32[]{:T(128)S(6)} %select_n.61), kind=kLoop, calls=%fused_computation.20 | loop fusion | flops 12288 | bytes 73732 | tf_op jit(solution)/shard_map/add | solution.py:170
  (26 shorter events, 0.2 us)
Async XLA Ops:
  1.5 6.6 %collective-permute-start.15 = (f32[16,768]{1,0:T(8,128)S(1)}, f32[16,768]{1,0:T(8,128)S(1)}, u32[]{:S(2)}, u32[]{:S(2)}) collective-permute-start(f32[16,768]{1,0:T(8,128)S(1)} %bitcast.86), channel_id=1, source_target_pairs={{0,32},{4,36},{8,40},{12,44},{16,48},{20,52},{24,56},{28,60},{32,6... | collective-permute-start | bytes 147464 | tf_op jit(solution)/shard_map/ppermute | solution.py:96
  4.7 6.7 %collective-permute-start.11 = (f32[16,768]{1,0:T(8,128)S(1)}, f32[16,768]{1,0:T(8,128)S(1)}, u32[]{:S(2)}, u32[]{:S(2)}) collective-permute-start(f32[16,768]{1,0:T(8,128)S(1)} %bitcast.87), channel_id=1, source_target_pairs={{0,224},{4,228},{8,232},{12,236},{16,240},{20,244},{24,248},{28,25... | collective-permute-start | bytes 147464 | tf_op jit(solution)/shard_map/ppermute | solution.py:93
  4.8 8.6 %collective-permute-start.2 = (f32[16,768]{1,0:T(8,128)S(1)}, f32[16,768]{1,0:T(8,128)S(1)}, u32[]{:S(2)}, u32[]{:S(2)}) collective-permute-start(f32[16,768]{1,0:T(8,128)S(1)} %bitcast.84), channel_id=1, source_target_pairs={{0,8},{4,12},{8,16},{12,20},{16,24},{20,28},{24,0},{28,4},{32,40},... | collective-permute-start | bytes 147464 | tf_op jit(solution)/shard_map/ppermute | solution.py:96
  6.4 5.0 %collective-permute-start = (f32[16,768]{1,0:T(8,128)S(1)}, f32[16,768]{1,0:T(8,128)S(1)}, u32[]{:S(2)}, u32[]{:S(2)}) collective-permute-start(f32[16,768]{1,0:T(8,128)S(1)} %bitcast.85), channel_id=1, source_target_pairs={{0,24},{4,28},{8,0},{12,4},{16,8},{20,12},{24,16},{28,20},{32,56},... | collective-permute-start | bytes 147464 | tf_op jit(solution)/shard_map/ppermute | solution.py:93
  8.1 10.9 %collective-permute-start.16 = (f32[16,768]{1,0:T(8,128)S(1)}, f32[16,768]{1,0:T(8,128)S(1)}, u32[]{:S(2)}, u32[]{:S(2)}) collective-permute-start(f32[16,768]{1,0:T(8,128)S(1)} %collective-permute-done.15), channel_id=1, source_target_pairs={{0,32},{4,36},{8,40},{12,44},{16,48},{20,52},{24,56},{28,60},{32,6... | collective-permute-start | bytes 147464 | tf_op jit(solution)/shard_map/ppermute | solution.py:96
  11.4 9.6 %collective-permute-start.12 = (f32[16,768]{1,0:T(8,128)S(1)}, f32[16,768]{1,0:T(8,128)S(1)}, u32[]{:S(2)}, u32[]{:S(2)}) collective-permute-start(f32[16,768]{1,0:T(8,128)S(1)} %collective-permute-done.11), channel_id=1, source_target_pairs={{0,224},{4,228},{8,232},{12,236},{16,240},{20,244},{24,248},{28,25... | collective-permute-start | bytes 147464 | tf_op jit(solution)/shard_map/ppermute | solution.py:93
  11.5 4.2 %collective-permute-start.1 = (f32[16,768]{1,0:T(8,128)S(1)}, f32[16,768]{1,0:T(8,128)S(1)}, u32[]{:S(2)}, u32[]{:S(2)}) collective-permute-start(f32[16,768]{1,0:T(8,128)S(1)} %collective-permute-done), channel_id=1, source_target_pairs={{0,24},{4,28},{8,0},{12,4},{16,8},{20,12},{24,16},{28,20},{32,56},... | collective-permute-start | bytes 147464 | tf_op jit(solution)/shard_map/ppermute | solution.py:93
  15.6 19.8 %collective-permute-start.3 = (f32[4,16,768]{2,1,0:T(8,128)S(1)}, f32[4,16,768]{2,1,0:T(8,128)S(1)}, u32[]{:S(2)}, u32[]{:S(2)}) collective-permute-start(f32[4,16,768]{2,1,0:T(8,128)S(1)} %pad_maximum_fusion.1), channel_id=1, source_target_pairs={{0,224},{4,228},{8,232},{12,236},{16,240},{20,244},{24,248},{28,25... | collective-permute-start | bytes 589832 | tf_op jit(solution)/shard_map/ppermute | solution.py:93
  15.7 19.7 %collective-permute-start.7 = (f32[4,16,768]{2,1,0:T(8,128)S(1)}, f32[4,16,768]{2,1,0:T(8,128)S(1)}, u32[]{:S(2)}, u32[]{:S(2)}) collective-permute-start(f32[4,16,768]{2,1,0:T(8,128)S(1)} %pad_maximum_fusion.1), channel_id=1, source_target_pairs={{0,32},{4,36},{8,40},{12,44},{16,48},{20,52},{24,56},{28,60},{32,6... | collective-permute-start | bytes 589832 | tf_op jit(solution)/shard_map/ppermute | solution.py:96
  19.0 12.9 %collective-permute-start.17 = (f32[16,768]{1,0:T(8,128)S(1)}, f32[16,768]{1,0:T(8,128)S(1)}, u32[]{:S(2)}, u32[]{:S(2)}) collective-permute-start(f32[16,768]{1,0:T(8,128)S(1)} %collective-permute-done.16), channel_id=1, source_target_pairs={{0,32},{4,36},{8,40},{12,44},{16,48},{20,52},{24,56},{28,60},{32,6... | collective-permute-start | bytes 147464 | tf_op jit(solution)/shard_map/ppermute | solution.py:96
  21.0 5.6 %collective-permute-start.13 = (f32[16,768]{1,0:T(8,128)S(1)}, f32[16,768]{1,0:T(8,128)S(1)}, u32[]{:S(2)}, u32[]{:S(2)}) collective-permute-start(f32[16,768]{1,0:T(8,128)S(1)} %collective-permute-done.12), channel_id=1, source_target_pairs={{0,224},{4,228},{8,232},{12,236},{16,240},{20,244},{24,248},{28,25... | collective-permute-start | bytes 147464 | tf_op jit(solution)/shard_map/ppermute | solution.py:93
  26.6 5.3 %collective-permute-start.14 = (f32[16,768]{1,0:T(8,128)S(1)}, f32[16,768]{1,0:T(8,128)S(1)}, u32[]{:S(2)}, u32[]{:S(2)}) collective-permute-start(f32[16,768]{1,0:T(8,128)S(1)} %collective-permute-done.13), channel_id=1, source_target_pairs={{0,224},{4,228},{8,232},{12,236},{16,240},{20,244},{24,248},{28,25... | collective-permute-start | bytes 147464 | tf_op jit(solution)/shard_map/ppermute | solution.py:93
  31.9 26.3 %collective-permute-start.20 = (f32[8,16,768]{2,1,0:T(8,128)S(1)}, f32[8,16,768]{2,1,0:T(8,128)S(1)}, u32[]{:S(2)}, u32[]{:S(2)}) collective-permute-start(f32[8,16,768]{2,1,0:T(8,128)S(1)} %bitcast_dynamic-update-slice_fusion.8), channel_id=1, source_target_pairs={{0,8},{4,12},{8,16},{12,20},{16,24},{20,28},{24,0},{28,4},{32,40},... | collective-permute-start | bytes 1179656 | tf_op jit(solution)/shard_map/ppermute | solution.py:96
  32.5 14.4 %collective-permute-start.18 = (f32[8,16,768]{2,1,0:T(8,128)S(1)}, f32[8,16,768]{2,1,0:T(8,128)S(1)}, u32[]{:S(2)}, u32[]{:S(2)}) collective-permute-start(f32[8,16,768]{2,1,0:T(8,128)S(1)} %bitcast_dynamic-update-slice_fusion.8), channel_id=1, source_target_pairs={{0,24},{4,28},{8,0},{12,4},{16,8},{20,12},{24,16},{28,20},{32,56},... | collective-permute-start | bytes 1179656 | tf_op jit(solution)/shard_map/ppermute | solution.py:93
  35.5 8.3 %collective-permute-start.4 = (f32[4,16,768]{2,1,0:T(8,128)S(1)}, f32[4,16,768]{2,1,0:T(8,128)S(1)}, u32[]{:S(2)}, u32[]{:S(2)}) collective-permute-start(f32[4,16,768]{2,1,0:T(8,128)S(1)} %collective-permute-done.3), channel_id=1, source_target_pairs={{0,224},{4,228},{8,232},{12,236},{16,240},{20,244},{24,248},{28,25... | collective-permute-start | bytes 589832 | tf_op jit(solution)/shard_map/ppermute | solution.py:93
  35.5 8.2 %collective-permute-start.8 = (f32[4,16,768]{2,1,0:T(8,128)S(1)}, f32[4,16,768]{2,1,0:T(8,128)S(1)}, u32[]{:S(2)}, u32[]{:S(2)}) collective-permute-start(f32[4,16,768]{2,1,0:T(8,128)S(1)} %collective-permute-done.7), channel_id=1, source_target_pairs={{0,32},{4,36},{8,40},{12,44},{16,48},{20,52},{24,56},{28,60},{32,6... | collective-permute-start | bytes 589832 | tf_op jit(solution)/shard_map/ppermute | solution.py:96
  43.7 7.4 %collective-permute-start.5 = (f32[4,16,768]{2,1,0:T(8,128)S(1)}, f32[4,16,768]{2,1,0:T(8,128)S(1)}, u32[]{:S(2)}, u32[]{:S(2)}) collective-permute-start(f32[4,16,768]{2,1,0:T(8,128)S(1)} %collective-permute-done.4), channel_id=1, source_target_pairs={{0,224},{4,228},{8,232},{12,236},{16,240},{20,244},{24,248},{28,25... | collective-permute-start | bytes 589832 | tf_op jit(solution)/shard_map/ppermute | solution.py:93
  43.7 14.3 %collective-permute-start.9 = (f32[4,16,768]{2,1,0:T(8,128)S(1)}, f32[4,16,768]{2,1,0:T(8,128)S(1)}, u32[]{:S(2)}, u32[]{:S(2)}) collective-permute-start(f32[4,16,768]{2,1,0:T(8,128)S(1)} %collective-permute-done.8), channel_id=1, source_target_pairs={{0,32},{4,36},{8,40},{12,44},{16,48},{20,52},{24,56},{28,60},{32,6... | collective-permute-start | bytes 589832 | tf_op jit(solution)/shard_map/ppermute | solution.py:96
  47.0 11.3 %collective-permute-start.19 = (f32[8,16,768]{2,1,0:T(8,128)S(1)}, f32[8,16,768]{2,1,0:T(8,128)S(1)}, u32[]{:S(2)}, u32[]{:S(2)}) collective-permute-start(f32[8,16,768]{2,1,0:T(8,128)S(1)} %collective-permute-done.18), channel_id=1, source_target_pairs={{0,24},{4,28},{8,0},{12,4},{16,8},{20,12},{24,16},{28,20},{32,56},... | collective-permute-start | bytes 1179656 | tf_op jit(solution)/shard_map/ppermute | solution.py:93
  51.1 6.9 %collective-permute-start.6 = (f32[4,16,768]{2,1,0:T(8,128)S(1)}, f32[4,16,768]{2,1,0:T(8,128)S(1)}, u32[]{:S(2)}, u32[]{:S(2)}) collective-permute-start(f32[4,16,768]{2,1,0:T(8,128)S(1)} %collective-permute-done.5), channel_id=1, source_target_pairs={{0,224},{4,228},{8,232},{12,236},{16,240},{20,244},{24,248},{28,25... | collective-permute-start | bytes 589832 | tf_op jit(solution)/shard_map/ppermute | solution.py:93
  58.1 1.2 %copy-start.1 = (f32[8,4,16,768]{3,2,1,0:T(8,128)}, f32[8,4,16,768]{3,2,1,0:T(8,128)S(1)}, u32[]{:S(2)}) copy-start(f32[8,4,16,768]{3,2,1,0:T(8,128)S(1)} %bitcast_dynamic-update-slice_fusion) | copy-start | bytes 4718596
  58.1 5.5 %collective-permute-start.10 = (f32[8,4,16,768]{3,2,1,0:T(8,128)S(1)}, f32[8,4,16,768]{3,2,1,0:T(8,128)}, u32[]{:S(2)}, u32[]{:S(2)}) collective-permute-start(f32[8,4,16,768]{3,2,1,0:T(8,128)S(1)} %bitcast_dynamic-update-slice_fusion), channel_id=1, source_target_pairs={{0,4},{4,0},{8,12},{12,8},{16,20},{20,16},{24,28},{28,24},{32,36},... | collective-permute-start | bytes 4718600 | tf_op jit(solution)/shard_map/ppermute | solution.py:109
  58.3 1.7 %copy-start.3 = (s32[1,1,16,32]{3,2,1,0:T(8,128)S(1)}, s32[1,1,16,32]{3,2,1,0:T(8,128)}, u32[]{:S(2)}) copy-start(s32[1,1,16,32]{3,2,1,0:T(8,128)} %param.11) | copy-start | bytes 6148
  58.3 2.3 %copy-start.4 = (s32[1,1,16,32,1]{3,4,2,1,0:T(1,128)S(1)}, s32[1,1,16,32,1]{3,4,2,1,0:T(1,128)}, u32[]{:S(2)}) copy-start(s32[1,1,16,32,1]{3,4,2,1,0:T(1,128)} %param.10) | copy-start | bytes 6148
  59.3 4.7 %copy-start = (f32[4,8,16,768]{3,2,1,0:T(8,128)}, f32[4,8,16,768]{3,2,1,0:T(8,128)S(1)}, u32[]{:S(2)}) copy-start(f32[4,8,16,768]{3,2,1,0:T(8,128)S(1)} %pad_maximum_fusion) | copy-start | bytes 4718596
  59.3 4.7 %collective-permute-start.21 = (f32[4,8,16,768]{3,2,1,0:T(8,128)S(1)}, f32[4,8,16,768]{3,2,1,0:T(8,128)}, u32[]{:S(2)}, u32[]{:S(2)}) collective-permute-start(f32[4,8,16,768]{3,2,1,0:T(8,128)S(1)} %pad_maximum_fusion), channel_id=1, source_target_pairs={{0,4},{4,0},{8,12},{12,8},{16,20},{20,16},{24,28},{28,24},{32,36},... | collective-permute-start | bytes 4718600 | tf_op jit(solution)/shard_map/ppermute | solution.py:111
  78.3 10.3 %all-to-all-start = ((f32[4,6,1024]{2,1,0:T(8,128)}), f32[4,6,1024]{2,1,0:T(8,128)S(1)}, u32[]{:S(2)}, u32[]{:S(2)}) async-start(f32[4,6,1024]{2,1,0:T(8,128)} %bitcast.73), calls=%async_computation | async-start | bytes 262144 | tf_op jit(solution)/shard_map/all_to_all | solution.py:166
  88.6 1.4 %copy-start.2 = (f32[6,1024]{1,0:T(8,128)}, f32[6,1024]{1,0:T(8,128)S(1)}, u32[]{:S(2)}) copy-start(f32[6,1024]{1,0:T(8,128)S(1)} %reduce_sum.9) | copy-start | bytes 73732

commit v8 on v5

--- a/solution.py
+++ b/solution.py
@@ -10,13 +10,13 @@
 half_step = 0.5
 
 
-def collide_kernel(idx_ref, near_ref, far_ref, w_ref, gain_ref, loss_ref, occ_ref, out_ref, sh_ref, rest_ref,
+def collide_kernel(idx_ref, tiles_ref, near_ref, far_ref, w_ref, gain_ref, loss_ref, occ_ref, out_ref, sh_ref, rest_ref,
                    *, shifts, nsub, sub_count, sub_width, bands):
-    t = pl.program_id(0)
+    tile = tiles_ref[pl.program_id(0)]
     half = near_ref.shape[0]
     for s in range(shifts):
         for jj in range(nsub):
-            at = idx_ref[s * sub_count + t * nsub + jj]
+            at = idx_ref[s * sub_count + tile * nsub + jj]
             near = near_ref[pl.ds(jnp.minimum(at, half - 1), 1), :]
             far = far_ref[pl.ds(jnp.maximum(at - half, 0), 1), :]
             row = jnp.where(at < half, near, far)
@@ -40,8 +40,9 @@
         out_ref[pl.ds(m, 1), :] = (1.0 - occ[m:m + 1]) * inflow - occ[m:m + 1] * outflow
 
 
-def collide(idx, near, far, weight_t, gain_t, loss_t, occ, sub_width, lanes=512):
+def collide(idx, tiles, near, far, weight_t, gain_t, loss_t, occ, sub_width, lanes):
     pairs, shifts, width = gain_t.shape
+    count = tiles.shape[0]
     bands = occ.shape[0]
     sub_count = width // sub_width
     nsub = lanes // sub_width
@@ -49,25 +50,25 @@
                              sub_width=sub_width, bands=bands)
     return pl.pallas_call(
         kern,
-        out_shape=jax.ShapeDtypeStruct((bands, width), jnp.float32),
+        out_shape=jax.ShapeDtypeStruct((bands, count * lanes), jnp.float32),
         grid_spec=pltpu.PrefetchScalarGridSpec(
-            num_scalar_prefetch=1,
-            grid=(width // lanes,),
+            num_scalar_prefetch=2,
+            grid=(count,),
             in_specs=[
-                pl.BlockSpec(near.shape, lambda t, i: (0, 0)),
-                pl.BlockSpec(far.shape, lambda t, i: (0, 0)),
-                pl.BlockSpec(weight_t.shape, lambda t, i: (0, 0, 0)),
-                pl.BlockSpec((pairs, shifts, lanes), lambda t, i: (0, 0, t)),
-                pl.BlockSpec((pairs, shifts, lanes), lambda t, i: (0, 0, t)),
-                pl.BlockSpec((bands, lanes), lambda t, i: (0, t)),
+                pl.BlockSpec(near.shape, lambda t, i, c: (0, 0)),
+                pl.BlockSpec(far.shape, lambda t, i, c: (0, 0)),
+                pl.BlockSpec(weight_t.shape, lambda t, i, c: (0, 0, 0)),
+                pl.BlockSpec((pairs, shifts, lanes), lambda t, i, c: (0, 0, c[t])),
+                pl.BlockSpec((pairs, shifts, lanes), lambda t, i, c: (0, 0, c[t])),
+                pl.BlockSpec((bands, lanes), lambda t, i, c: (0, c[t])),
             ],
-            out_specs=pl.BlockSpec((bands, lanes), lambda t, i: (0, t)),
+            out_specs=pl.BlockSpec((bands, lanes), lambda t, i, c: (0, t)),
             scratch_shapes=[
                 pltpu.VMEM((bands, shifts, lanes), jnp.float32),
                 pltpu.VMEM((bands, shifts, lanes), jnp.float32),
             ],
         ),
-    )(idx, near, far, weight_t, gain_t, loss_t, occ)
+    )(idx, tiles, near, far, weight_t, gain_t, loss_t, occ)
 
 
 def ring_gather(block, y_count, z_count):
@@ -132,19 +133,26 @@
     picks = where * sub_count + sources
     active = (jnp.arange(shifts, dtype=jnp.int32) < counts.reshape(())).astype(jnp.float32)
     weight = pair_mask.astype(jnp.float32) * active[:, None]
-    partial_terms = collide(
-        picks,
-        near,
-        far,
-        weight.T[:, :, None],
-        gain_table.transpose(1, 0, 2),
-        loss_table.transpose(1, 0, 2),
-        occupation,
-        sub_width,
+    lanes = 512
+    share_width = width // pb_count
+    per_share = share_width // lanes
+    me_pb = lax.axis_index("pb")
+    step = jnp.arange(per_share, dtype=jnp.int32)
+    remote = jnp.concatenate(
+        [((me_pb + d) % pb_count) * per_share + step for d in range(1, pb_count)]
     )
-    share_width = width // pb_count
-    parts = partial_terms.reshape(bands, pb_count, share_width).transpose(1, 0, 2)
-    collision = jnp.sum(lax.all_to_all(parts, "pb", 0, 0, tiled=True), axis=0)
+    own = me_pb * per_share + step
+    tables = (picks, near, far, weight.T[:, :, None],
+              gain_table.transpose(1, 0, 2), loss_table.transpose(1, 0, 2), occupation)
+    sent = collide(tables[0], remote, *tables[1:], sub_width, lanes)
+    slots = jnp.concatenate([jnp.zeros((bands, share_width), jnp.float32), sent], axis=1)
+    slots = slots.reshape(bands, pb_count, share_width).transpose(1, 0, 2)
+    by_target = lax.dynamic_slice_in_dim(
+        jnp.concatenate([slots, slots]), (pb_count - me_pb) % pb_count, pb_count, 0
+    )
+    received = lax.all_to_all(by_target, "pb", 0, 0, tiled=True)
+    kept = collide(tables[0], own, *tables[1:], sub_width, lanes)
+    collision = kept + jnp.sum(received, axis=0)
     own_share = lax.dynamic_slice_in_dim(
         occupation, lax.axis_index("pb") * share_width, share_width, 1
     )

time: 86.2 us -> 87 us (level)
  waiting for transfers between devices: 38.9 us -> 32.3 us
  Pallas kernels: 13.2 us -> 17.3 us
  other arithmetic: 3.55 us -> 5.39 us
  local copies, waits for them, and re-layouts: 3.81 us -> 4.72 us
    all_to_all x1, waiting for transfers between devices: 5.98 us -> 0.01 us  [body(): received = lax.all_to_all(by_target, 'pb', 0, 0, tiled=True)]
    pallas_call x1 -> x2, Pallas kernels: 13.2 us -> 17.3 us  [collide(): pl.pallas_call(kern, out_shape=jax.ShapeDtypeStruct((bands, count * lanes...]
    concatenate x0 -> x2, other arithmetic: none -> 1.28 us  [the longest x1 0.7 us: body(): jnp.concatenate([slots, slots])]
    concatenate x0 -> x1, local copies, waits for them, and re-layouts: none -> 0.9 us  [body(): jnp.concatenate([jnp.zeros((bands, share_width), jnp.float32), sent], axi...]
    unnamed x16 -> x14, local copies, waits for them, and re-layouts: 1.77 us -> 1.77 us
  transfers between devices with their start and end apart: 12 -> 12, of which waited for: 9 -> 8; matrix products, arithmetic and copies ran while one was open for 6% -> 7% of each run, Pallas kernels for 0% -> 8%
where the time goes in v8:
time: 87 us; the launch traced here: 85.9 us
  waiting for transfers between devices  32.3 us (37%)
  starting transfers between devices  24.7 us (28%)
  Pallas kernels  17.3 us (20%)
  other arithmetic  5.39 us (6%)
  local copies, waits for them, and re-layouts  4.72 us (5%)
  between operations  1.52 us (2%)
    ppermute x6, waiting for transfers between devices, ring(): back = lax.ppermute(back, 'ka', step(-1))  31.6 us
    ppermute x6, starting transfers between devices, ring(): back = lax.ppermute(back, 'ka', step(-1))  17.8 us
    pallas_call x2, Pallas kernels, collide(): pl.pallas_call(kern, out_shape=jax.ShapeDtypeStruct((bands, count * lanes...  17.3 us
    all_to_all x1, starting transfers between devices, body(): received = lax.all_to_all(by_target, 'pb', 0, 0, tiled=True)  4.3 us
    ppermute x4, starting transfers between devices, ring(): fwd = lax.ppermute(fwd, 'ka', step(1))  2.52 us
    unnamed x14, local copies, waits for them, and re-layouts  1.77 us
  transfers between devices with their start and end apart: 12, of which 8 were waited for; matrix products, arithmetic and copies ran while one was open for 7% of the time, Pallas kernels for 8%

profile of v8, /device:TPU:24, one launch (start us, length us, event | category | flops | bytes accessed | tf_op | source)
XLA Modules:
  0.0 85.9 jit_solution(14742775782065680073)
XLA Ops:
  0.6 0.9 %copy.21 = f32[4,8,6,128]{3,1,2,0:T(8,128)S(1)} copy(f32[4,8,6,128]{3,2,1,0:T(8,128)} %bitcast.48) | data formatting | bytes 196608
  1.6 0.8 collective-permute-start
  2.4 2.5 %collective-permute-start.2 = (f32[32,768]{1,0:T(8,128)S(1)}, f32[32,768]{1,0:T(8,128)S(1)}, u32[]{:S(2)}, u32[]{:S(2)}) collective-permute-start(f32[32,768]{1,0:T(8,128)S(1)} %bitcast.58), channel_id=1, source_target_pairs={{0,8},{4,12},{8,16},{12,20},{16,24},{20,28},{24,0},{28,4},{32,40},... | collective-permute-start | bytes 294920 | tf_op jit(solution)/shard_map/ppermute | solution.py:94
  4.9 2.6 %collective-permute-done = f32[32,768]{1,0:T(8,128)S(1)} collective-permute-done((f32[32,768]{1,0:T(8,128)S(1)}, f32[32,768]{1,0:T(8,128)S(1)}, u32[]{:S(2)}, u32[]{:S(2)}) %collective-permute-start) | collective-permute-done | bytes 98336 | tf_op jit(solution)/shard_map/ppermute | solution.py:91
  7.5 0.0 collective-permute-start.1
  7.5 0.9 %stack_reshape.3 = f32[1,32,768]{2,1,0:T(8,128)S(1)} reshape(f32[32,6,128]{2,1,0:T(8,128)} %bitcast.49) | data formatting | bytes 196608 | tf_op jit(solution)/shard_map/stack;reshape | solution.py:96
  8.4 0.0 collective-permute-done.2
  8.4 4.9 %collective-permute-done.1 = f32[32,768]{1,0:T(8,128)S(1)} collective-permute-done((f32[32,768]{1,0:T(8,128)S(1)}, f32[32,768]{1,0:T(8,128)S(1)}, u32[]{:S(2)}, u32[]{:S(2)}) %collective-permute-start.1) | collective-permute-done | bytes 98336 | tf_op jit(solution)/shard_map/ppermute | solution.py:91
  13.3 0.0 copy-start.2
  13.3 0.0 copy-start.1
  13.3 5.9 %collective-permute-start.3 = (f32[4,32,768]{2,1,0:T(8,128)S(1)}, f32[4,32,768]{2,1,0:T(8,128)S(1)}, u32[]{:S(2)}, u32[]{:S(2)}) collective-permute-start(f32[4,32,768]{2,1,0:T(8,128)S(1)} %pad_maximum_fusion), channel_id=1, source_target_pairs={{0,224},{4,228},{8,232},{12,236},{16,240},{20,244},{24,248},{28,25... | collective-permute-start | bytes 1179656 | tf_op jit(solution)/shard_map/ppermute | solution.py:91
  19.3 0.0 collective-permute-start.7
  19.3 6.1 %collective-permute-done.3 = f32[4,32,768]{2,1,0:T(8,128)S(1)} collective-permute-done((f32[4,32,768]{2,1,0:T(8,128)S(1)}, f32[4,32,768]{2,1,0:T(8,128)S(1)}, u32[]{:S(2)}, u32[]{:S(2)}) %collective-permute-start.3) | collective-permute-done | bytes 393248 | tf_op jit(solution)/shard_map/ppermute | solution.py:91
  25.4 3.7 %collective-permute-start.4 = (f32[4,32,768]{2,1,0:T(8,128)S(1)}, f32[4,32,768]{2,1,0:T(8,128)S(1)}, u32[]{:S(2)}, u32[]{:S(2)}) collective-permute-start(f32[4,32,768]{2,1,0:T(8,128)S(1)} %collective-permute-done.3), channel_id=1, source_target_pairs={{0,224},{4,228},{8,232},{12,236},{16,240},{20,244},{24,248},{28,25... | collective-permute-start | bytes 1179656 | tf_op jit(solution)/shard_map/ppermute | solution.py:91
  29.0 0.0 collective-permute-done.7
  29.0 0.0 collective-permute-start.8
  29.0 5.9 %collective-permute-done.4 = f32[4,32,768]{2,1,0:T(8,128)S(1)} collective-permute-done((f32[4,32,768]{2,1,0:T(8,128)S(1)}, f32[4,32,768]{2,1,0:T(8,128)S(1)}, u32[]{:S(2)}, u32[]{:S(2)}) %collective-permute-start.4) | collective-permute-done | bytes 393248 | tf_op jit(solution)/shard_map/ppermute | solution.py:91
  35.0 3.7 %collective-permute-start.5 = (f32[4,32,768]{2,1,0:T(8,128)S(1)}, f32[4,32,768]{2,1,0:T(8,128)S(1)}, u32[]{:S(2)}, u32[]{:S(2)}) collective-permute-start(f32[4,32,768]{2,1,0:T(8,128)S(1)} %collective-permute-done.4), channel_id=1, source_target_pairs={{0,224},{4,228},{8,232},{12,236},{16,240},{20,244},{24,248},{28,25... | collective-permute-start | bytes 1179656 | tf_op jit(solution)/shard_map/ppermute | solution.py:91
  38.8 0.1 collective-permute-done.8
  38.8 0.0 collective-permute-start.9
  38.9 6.9 %collective-permute-done.5 = f32[4,32,768]{2,1,0:T(8,128)S(1)} collective-permute-done((f32[4,32,768]{2,1,0:T(8,128)S(1)}, f32[4,32,768]{2,1,0:T(8,128)S(1)}, u32[]{:S(2)}, u32[]{:S(2)}) %collective-permute-start.5) | collective-permute-done | bytes 393248 | tf_op jit(solution)/shard_map/ppermute | solution.py:91
  45.7 3.7 %collective-permute-start.6 = (f32[4,32,768]{2,1,0:T(8,128)S(1)}, f32[4,32,768]{2,1,0:T(8,128)S(1)}, u32[]{:S(2)}, u32[]{:S(2)}) collective-permute-start(f32[4,32,768]{2,1,0:T(8,128)S(1)} %collective-permute-done.5), channel_id=1, source_target_pairs={{0,224},{4,228},{8,232},{12,236},{16,240},{20,244},{24,248},{28,25... | collective-permute-start | bytes 1179656 | tf_op jit(solution)/shard_map/ppermute | solution.py:91
  49.5 5.2 %collective-permute-done.6 = f32[4,32,768]{2,1,0:T(8,128)S(1)} collective-permute-done((f32[4,32,768]{2,1,0:T(8,128)S(1)}, f32[4,32,768]{2,1,0:T(8,128)S(1)}, u32[]{:S(2)}, u32[]{:S(2)}) %collective-permute-start.6) | collective-permute-done | bytes 393248 | tf_op jit(solution)/shard_map/ppermute | solution.py:91
  54.7 0.0 collective-permute-done.9
  54.9 0.0 copy-start
  54.9 0.1 collective-permute-start.10
  55.1 0.7 broadcast.53
  55.7 0.0 copy-done.2
  55.7 0.7 reduce.3
  56.4 0.1 reshape.33
  56.5 0.0 copy-done.1
  56.5 0.1 reshape.34
  57.3 0.8 multiply_bitcast_fusion
  58.0 0.9 %copy.16.w_ref = f32[36,16,1]{2,1,0:T(8,128)} copy(f32[36,16,1]{0,1,2:T(8,128)S(1)} %multiply_bitcast_fusion) | data formatting | bytes 4608 | tf_op jit(solution)/shard_map/broadcast_in_dim | solution.py:145
  59.0 0.6 pad_add_fusion.tiles_ref
  59.6 0.6 fusion.6.idx_ref
  60.2 0.6 collective-permute-done.10
  60.8 0.0 copy-done
  60.8 10.8 %shard_map.87 = f32[6,3072]{1,0:T(8,128)} custom-call(s32[512]{0:T(512)} %fusion.6.idx_ref, s32[6]{0:T(128)} %pad_add_fusion.tiles_ref, f32[1024,768]{1,0:T(8,128)} %bitcast.46, f32[1024,768]{1,0:T(8,128)} %bitcast.15.far_ref, f32[36,16,1]{2,1,0:T(8,128)} %copy.16.w_ref, bf16[36,16,4096]{2,1,0:T(8,128)(2,1)} %bitcast.42, bf16[36,16,4096]{2,1,0:T(8,128)(2,1)} %bitcast.44, ...), custom_call_target="tpu_custom_call" | custom-call | tf_op jit(solution)/shard_map/pallas_call | solution.py:51
  71.5 0.9 %concatenate.10 = f32[6,4096]{1,0:T(8,128)S(1)} pad(f32[6,3072]{1,0:T(8,128)} %shard_map.87, f32[]{:T(128)} %constant.123.clone.1), padding=0_0x1024_0 | pad | bytes 172036 | tf_op jit(solution)/shard_map/concatenate | solution.py:148
  72.4 0.7 fusion
  73.1 4.3 %all-to-all-start = ((f32[4,6,1024]{2,1,0:T(8,128)}), f32[4,6,1024]{2,1,0:T(8,128)S(1)}, u32[]{:S(2)}, u32[]{:S(2)}) async-start(f32[4,6,1024]{2,1,0:T(8,128)} %fusion), calls=%async_computation | async-start | bytes 262144 | tf_op jit(solution)/shard_map/all_to_all | solution.py:153
  77.4 0.5 iota_add_fusion.3.tiles_ref
  78.0 6.5 %shard_map.86 = f32[6,1024]{1,0:T(8,128)} custom-call(s32[512]{0:T(512)} %fusion.6.idx_ref, s32[2]{0:T(128)} %iota_add_fusion.3.tiles_ref, f32[1024,768]{1,0:T(8,128)} %bitcast.47, f32[1024,768]{1,0:T(8,128)} %bitcast.15.far_ref, f32[36,16,1]{2,1,0:T(8,128)} %copy.16.w_ref, bf16[36,16,4096]{2,1,0:T(8,128)(2,1)} %bitcast.43, bf16[36,16,4096]{2,1,0:T(8,128)(2,1)} %bitcast.45, ...), custom_call_target="tpu_custom_call" | custom-call | tf_op jit(solution)/shard_map/pallas_call | solution.py:51
  84.5 0.0 all-to-all-done
  84.5 1.4 %multiply_add_fusion = (f32[6,1024]{1,0:T(8,128)}, f32[6,1024]{1,0:T(8,128)}) fusion(f32[6,4096]{1,0:T(8,128)} %occ_ref.3, s32[]{:T(128)S(6)} %select_n.81, f32[6,1024]{1,0:T(8,128)} %shard_map.86, f32[6,1024]{1,0:T(8,128)S(1)} %reduce_sum.9), kind=kLoop, calls=%fused_computation.13 | loop fusion | flops 18432 | bytes 122884 | tf_op jit(solution)/shard_map/add | solution.py:159
  (13 shorter events, 0.3 us)
Async XLA Ops:
  1.6 5.9 %collective-permute-start = (f32[32,768]{1,0:T(8,128)S(1)}, f32[32,768]{1,0:T(8,128)S(1)}, u32[]{:S(2)}, u32[]{:S(2)}) collective-permute-start(f32[32,768]{1,0:T(8,128)S(1)} %bitcast.57), channel_id=1, source_target_pairs={{0,24},{4,28},{8,0},{12,4},{16,8},{20,12},{24,16},{28,20},{32,56},... | collective-permute-start | bytes 294920 | tf_op jit(solution)/shard_map/ppermute | solution.py:91
  2.4 6.0 %collective-permute-start.2 = (f32[32,768]{1,0:T(8,128)S(1)}, f32[32,768]{1,0:T(8,128)S(1)}, u32[]{:S(2)}, u32[]{:S(2)}) collective-permute-start(f32[32,768]{1,0:T(8,128)S(1)} %bitcast.58), channel_id=1, source_target_pairs={{0,8},{4,12},{8,16},{12,20},{16,24},{20,28},{24,0},{28,4},{32,40},... | collective-permute-start | bytes 294920 | tf_op jit(solution)/shard_map/ppermute | solution.py:94
  7.5 5.8 %collective-permute-start.1 = (f32[32,768]{1,0:T(8,128)S(1)}, f32[32,768]{1,0:T(8,128)S(1)}, u32[]{:S(2)}, u32[]{:S(2)}) collective-permute-start(f32[32,768]{1,0:T(8,128)S(1)} %collective-permute-done), channel_id=1, source_target_pairs={{0,24},{4,28},{8,0},{12,4},{16,8},{20,12},{24,16},{28,20},{32,56},... | collective-permute-start | bytes 294920 | tf_op jit(solution)/shard_map/ppermute | solution.py:91
  13.3 42.4 %copy-start.2 = (s32[1,1,16,32,1]{3,4,2,1,0:T(1,128)S(1)}, s32[1,1,16,32,1]{3,4,2,1,0:T(1,128)}, u32[]{:S(2)}) copy-start(s32[1,1,16,32,1]{3,4,2,1,0:T(1,128)} %param.10) | copy-start | bytes 6148
  13.3 43.2 %copy-start.1 = (s32[1,1,16,32]{3,2,1,0:T(8,128)S(1)}, s32[1,1,16,32]{3,2,1,0:T(8,128)}, u32[]{:S(2)}) copy-start(s32[1,1,16,32]{3,2,1,0:T(8,128)} %param.11) | copy-start | bytes 6148
  13.3 12.0 %collective-permute-start.3 = (f32[4,32,768]{2,1,0:T(8,128)S(1)}, f32[4,32,768]{2,1,0:T(8,128)S(1)}, u32[]{:S(2)}, u32[]{:S(2)}) collective-permute-start(f32[4,32,768]{2,1,0:T(8,128)S(1)} %pad_maximum_fusion), channel_id=1, source_target_pairs={{0,224},{4,228},{8,232},{12,236},{16,240},{20,244},{24,248},{28,25... | collective-permute-start | bytes 1179656 | tf_op jit(solution)/shard_map/ppermute | solution.py:91
  19.3 9.8 %collective-permute-start.7 = (f32[4,32,768]{2,1,0:T(8,128)S(1)}, f32[4,32,768]{2,1,0:T(8,128)S(1)}, u32[]{:S(2)}, u32[]{:S(2)}) collective-permute-start(f32[4,32,768]{2,1,0:T(8,128)S(1)} %pad_maximum_fusion), channel_id=1, source_target_pairs={{0,32},{4,36},{8,40},{12,44},{16,48},{20,52},{24,56},{28,60},{32,6... | collective-permute-start | bytes 1179656 | tf_op jit(solution)/shard_map/ppermute | solution.py:94
  25.4 9.6 %collective-permute-start.4 = (f32[4,32,768]{2,1,0:T(8,128)S(1)}, f32[4,32,768]{2,1,0:T(8,128)S(1)}, u32[]{:S(2)}, u32[]{:S(2)}) collective-permute-start(f32[4,32,768]{2,1,0:T(8,128)S(1)} %collective-permute-done.3), channel_id=1, source_target_pairs={{0,224},{4,228},{8,232},{12,236},{16,240},{20,244},{24,248},{28,25... | collective-permute-start | bytes 1179656 | tf_op jit(solution)/shard_map/ppermute | solution.py:91
  29.0 9.8 %collective-permute-start.8 = (f32[4,32,768]{2,1,0:T(8,128)S(1)}, f32[4,32,768]{2,1,0:T(8,128)S(1)}, u32[]{:S(2)}, u32[]{:S(2)}) collective-permute-start(f32[4,32,768]{2,1,0:T(8,128)S(1)} %collective-permute-done.7), channel_id=1, source_target_pairs={{0,32},{4,36},{8,40},{12,44},{16,48},{20,52},{24,56},{28,60},{32,6... | collective-permute-start | bytes 1179656 | tf_op jit(solution)/shard_map/ppermute | solution.py:94
  35.0 10.7 %collective-permute-start.5 = (f32[4,32,768]{2,1,0:T(8,128)S(1)}, f32[4,32,768]{2,1,0:T(8,128)S(1)}, u32[]{:S(2)}, u32[]{:S(2)}) collective-permute-start(f32[4,32,768]{2,1,0:T(8,128)S(1)} %collective-permute-done.4), channel_id=1, source_target_pairs={{0,224},{4,228},{8,232},{12,236},{16,240},{20,244},{24,248},{28,25... | collective-permute-start | bytes 1179656 | tf_op jit(solution)/shard_map/ppermute | solution.py:91
  38.8 15.9 %collective-permute-start.9 = (f32[4,32,768]{2,1,0:T(8,128)S(1)}, f32[4,32,768]{2,1,0:T(8,128)S(1)}, u32[]{:S(2)}, u32[]{:S(2)}) collective-permute-start(f32[4,32,768]{2,1,0:T(8,128)S(1)} %collective-permute-done.8), channel_id=1, source_target_pairs={{0,32},{4,36},{8,40},{12,44},{16,48},{20,52},{24,56},{28,60},{32,6... | collective-permute-start | bytes 1179656 | tf_op jit(solution)/shard_map/ppermute | solution.py:94
  45.7 9.0 %collective-permute-start.6 = (f32[4,32,768]{2,1,0:T(8,128)S(1)}, f32[4,32,768]{2,1,0:T(8,128)S(1)}, u32[]{:S(2)}, u32[]{:S(2)}) collective-permute-start(f32[4,32,768]{2,1,0:T(8,128)S(1)} %collective-permute-done.5), channel_id=1, source_target_pairs={{0,224},{4,228},{8,232},{12,236},{16,240},{20,244},{24,248},{28,25... | collective-permute-start | bytes 1179656 | tf_op jit(solution)/shard_map/ppermute | solution.py:91
  54.9 5.9 %copy-start = (f32[8,4,32,768]{3,2,1,0:T(8,128)}, f32[8,4,32,768]{3,2,1,0:T(8,128)S(1)}, u32[]{:S(2)}) copy-start(f32[8,4,32,768]{3,2,1,0:T(8,128)S(1)} %bitcast_dynamic-update-slice_fusion) | copy-start | bytes 9437188
  54.9 5.9 %collective-permute-start.10 = (f32[8,4,32,768]{3,2,1,0:T(8,128)S(1)}, f32[8,4,32,768]{3,2,1,0:T(8,128)}, u32[]{:S(2)}, u32[]{:S(2)}) collective-permute-start(f32[8,4,32,768]{3,2,1,0:T(8,128)S(1)} %bitcast_dynamic-update-slice_fusion), channel_id=1, source_target_pairs={{0,4},{4,0},{8,12},{12,8},{16,20},{20,16},{24,28},{28,24},{32,36},... | collective-permute-start | bytes 9437192 | tf_op jit(solution)/shard_map/ppermute | solution.py:100
  73.1 11.3 %all-to-all-start = ((f32[4,6,1024]{2,1,0:T(8,128)}), f32[4,6,1024]{2,1,0:T(8,128)S(1)}, u32[]{:S(2)}, u32[]{:S(2)}) async-start(f32[4,6,1024]{2,1,0:T(8,128)} %fusion), calls=%async_computation | async-start | bytes 262144 | tf_op jit(solution)/shard_map/all_to_all | solution.py:153

commit v9 on v5

--- a/solution.py
+++ b/solution.py
@@ -23,14 +23,15 @@
             for n in range(bands):
                 piece = row[:, n * sub_width:(n + 1) * sub_width]
                 sh_ref[n, pl.ds(s, 1), pl.ds(jj * sub_width, sub_width)] = piece
-                rest_ref[n, pl.ds(s, 1), pl.ds(jj * sub_width, sub_width)] = 1.0 - piece
+    for n in range(bands):
+        rest_ref[n] = 1.0 - sh_ref[n]
     occ = occ_ref[...]
     for m in range(bands):
         acc_i = None
         acc_o = None
         for n in range(bands):
             p = m * bands + n
-            w = w_ref[p]
+            w = jnp.tile(w_ref[p], (1, gain_ref.shape[2] // w_ref.shape[2]))
             term_i = gain_ref[p].astype(jnp.float32) * w * sh_ref[n]
             term_o = loss_ref[p].astype(jnp.float32) * w * rest_ref[n]
             acc_i = term_i if acc_i is None else acc_i + term_i
@@ -40,7 +41,7 @@
         out_ref[pl.ds(m, 1), :] = (1.0 - occ[m:m + 1]) * inflow - occ[m:m + 1] * outflow
 
 
-def collide(idx, near, far, weight_t, gain_t, loss_t, occ, sub_width, lanes=512):
+def collide(idx, near, far, weight_t, gain_t, loss_t, occ, sub_width, lanes=1024):
     pairs, shifts, width = gain_t.shape
     bands = occ.shape[0]
     sub_count = width // sub_width
@@ -136,7 +137,7 @@
         picks,
         near,
         far,
-        weight.T[:, :, None],
+        jnp.broadcast_to(weight.T[:, :, None], (bands * bands, shifts, sub_width)),
         gain_table.transpose(1, 0, 2),
         loss_table.transpose(1, 0, 2),
         occupation,

time: 86.2 us -> 85.3 us (0.990)
  Pallas kernels: 13.2 us -> 11.5 us
    pallas_call x1, Pallas kernels: 13.2 us -> 11.5 us  [collide(): pl.pallas_call(kern, out_shape=jax.ShapeDtypeStruct((bands, width), jnp.f...]
  transfers between devices with their start and end apart: 12 -> 12, of which waited for: 9 -> 9; matrix products, arithmetic and copies ran while one was open for 6% -> 5% of each run, Pallas kernels for 0% -> 0%
where the time goes in v9:
time: 85.3 us; the launch traced here: 84.8 us
  waiting for transfers between devices  39.7 us (47%)
  starting transfers between devices  24.7 us (29%)
  Pallas kernels  11.5 us (13%)
  local copies, waits for them, and re-layouts  3.82 us (4%)
  other arithmetic  3.55 us (4%)
  between operations  1.48 us (2%)
    ppermute x6, waiting for transfers between devices, ring(): back = lax.ppermute(back, 'ka', step(-1))  31.6 us
    ppermute x6, starting transfers between devices, ring(): back = lax.ppermute(back, 'ka', step(-1))  17.8 us
    pallas_call x1, Pallas kernels, collide(): pl.pallas_call(kern, out_shape=jax.ShapeDtypeStruct((bands, width), jnp.f...  11.5 us
    all_to_all x1, waiting for transfers between devices, body(): collision = jnp.sum(lax.all_to_all(parts, 'pb', 0, 0, tiled=True), axis=0)  5.98 us
    all_to_all x1, starting transfers between devices, body(): collision = jnp.sum(lax.all_to_all(parts, 'pb', 0, 0, tiled=True), axis=0)  4.29 us
    ppermute x4, starting transfers between devices, ring(): fwd = lax.ppermute(fwd, 'ka', step(1))  2.52 us
    ppermute x1, waiting for transfers between devices, ring_gather(): other = lax.ppermute(along_z, 'ka', pairs(lambda j: j ^ 1))  2.07 us
    unnamed x16, local copies, waits for them, and re-layouts  1.77 us
  transfers between devices with their start and end apart: 12, of which 9 were waited for; matrix products, arithmetic and copies ran while one was open for 5% of the time, Pallas kernels for 0%

profile of v9, /device:TPU:24, one launch (start us, length us, event | category | flops | bytes accessed | tf_op | source)
XLA Modules:
  0.0 84.8 jit_solution(9924096694317677611)
XLA Ops:
  0.6 0.9 %copy.19 = f32[4,8,6,128]{3,1,2,0:T(8,128)S(1)} copy(f32[4,8,6,128]{3,2,1,0:T(8,128)} %bitcast.43) | data formatting | bytes 196608
  1.6 0.8 collective-permute-start
  2.4 2.5 %collective-permute-start.2 = (f32[32,768]{1,0:T(8,128)S(1)}, f32[32,768]{1,0:T(8,128)S(1)}, u32[]{:S(2)}, u32[]{:S(2)}) collective-permute-start(f32[32,768]{1,0:T(8,128)S(1)} %bitcast.53), channel_id=1, source_target_pairs={{0,8},{4,12},{8,16},{12,20},{16,24},{20,28},{24,0},{28,4},{32,40},... | collective-permute-start | bytes 294920 | tf_op jit(solution)/shard_map/ppermute | solution.py:94
  4.9 2.6 %collective-permute-done = f32[32,768]{1,0:T(8,128)S(1)} collective-permute-done((f32[32,768]{1,0:T(8,128)S(1)}, f32[32,768]{1,0:T(8,128)S(1)}, u32[]{:S(2)}, u32[]{:S(2)}) %collective-permute-start) | collective-permute-done | bytes 98336 | tf_op jit(solution)/shard_map/ppermute | solution.py:91
  7.5 0.0 collective-permute-start.1
  7.5 0.9 %stack_reshape.3 = f32[1,32,768]{2,1,0:T(8,128)S(1)} reshape(f32[32,6,128]{2,1,0:T(8,128)} %bitcast.44) | data formatting | bytes 196608 | tf_op jit(solution)/shard_map/stack;reshape | solution.py:96
  8.4 0.0 collective-permute-done.2
  8.4 4.9 %collective-permute-done.1 = f32[32,768]{1,0:T(8,128)S(1)} collective-permute-done((f32[32,768]{1,0:T(8,128)S(1)}, f32[32,768]{1,0:T(8,128)S(1)}, u32[]{:S(2)}, u32[]{:S(2)}) %collective-permute-start.1) | collective-permute-done | bytes 98336 | tf_op jit(solution)/shard_map/ppermute | solution.py:91
  13.3 0.0 copy-start.3
  13.3 0.0 copy-start.2
  13.3 5.9 %collective-permute-start.3 = (f32[4,32,768]{2,1,0:T(8,128)S(1)}, f32[4,32,768]{2,1,0:T(8,128)S(1)}, u32[]{:S(2)}, u32[]{:S(2)}) collective-permute-start(f32[4,32,768]{2,1,0:T(8,128)S(1)} %pad_maximum_fusion), channel_id=1, source_target_pairs={{0,224},{4,228},{8,232},{12,236},{16,240},{20,244},{24,248},{28,25... | collective-permute-start | bytes 1179656 | tf_op jit(solution)/shard_map/ppermute | solution.py:91
  19.3 0.0 collective-permute-start.7
  19.3 6.1 %collective-permute-done.3 = f32[4,32,768]{2,1,0:T(8,128)S(1)} collective-permute-done((f32[4,32,768]{2,1,0:T(8,128)S(1)}, f32[4,32,768]{2,1,0:T(8,128)S(1)}, u32[]{:S(2)}, u32[]{:S(2)}) %collective-permute-start.3) | collective-permute-done | bytes 393248 | tf_op jit(solution)/shard_map/ppermute | solution.py:91
  25.4 3.7 %collective-permute-start.4 = (f32[4,32,768]{2,1,0:T(8,128)S(1)}, f32[4,32,768]{2,1,0:T(8,128)S(1)}, u32[]{:S(2)}, u32[]{:S(2)}) collective-permute-start(f32[4,32,768]{2,1,0:T(8,128)S(1)} %collective-permute-done.3), channel_id=1, source_target_pairs={{0,224},{4,228},{8,232},{12,236},{16,240},{20,244},{24,248},{28,25... | collective-permute-start | bytes 1179656 | tf_op jit(solution)/shard_map/ppermute | solution.py:91
  29.0 0.0 collective-permute-done.7
  29.0 0.0 collective-permute-start.8
  29.0 5.9 %collective-permute-done.4 = f32[4,32,768]{2,1,0:T(8,128)S(1)} collective-permute-done((f32[4,32,768]{2,1,0:T(8,128)S(1)}, f32[4,32,768]{2,1,0:T(8,128)S(1)}, u32[]{:S(2)}, u32[]{:S(2)}) %collective-permute-start.4) | collective-permute-done | bytes 393248 | tf_op jit(solution)/shard_map/ppermute | solution.py:91
  35.0 3.7 %collective-permute-start.5 = (f32[4,32,768]{2,1,0:T(8,128)S(1)}, f32[4,32,768]{2,1,0:T(8,128)S(1)}, u32[]{:S(2)}, u32[]{:S(2)}) collective-permute-start(f32[4,32,768]{2,1,0:T(8,128)S(1)} %collective-permute-done.4), channel_id=1, source_target_pairs={{0,224},{4,228},{8,232},{12,236},{16,240},{20,244},{24,248},{28,25... | collective-permute-start | bytes 1179656 | tf_op jit(solution)/shard_map/ppermute | solution.py:91
  38.8 0.1 collective-permute-done.8
  38.8 0.0 collective-permute-start.9
  38.9 6.9 %collective-permute-done.5 = f32[4,32,768]{2,1,0:T(8,128)S(1)} collective-permute-done((f32[4,32,768]{2,1,0:T(8,128)S(1)}, f32[4,32,768]{2,1,0:T(8,128)S(1)}, u32[]{:S(2)}, u32[]{:S(2)}) %collective-permute-start.5) | collective-permute-done | bytes 393248 | tf_op jit(solution)/shard_map/ppermute | solution.py:91
  45.7 3.7 %collective-permute-start.6 = (f32[4,32,768]{2,1,0:T(8,128)S(1)}, f32[4,32,768]{2,1,0:T(8,128)S(1)}, u32[]{:S(2)}, u32[]{:S(2)}) collective-permute-start(f32[4,32,768]{2,1,0:T(8,128)S(1)} %collective-permute-done.5), channel_id=1, source_target_pairs={{0,224},{4,228},{8,232},{12,236},{16,240},{20,244},{24,248},{28,25... | collective-permute-start | bytes 1179656 | tf_op jit(solution)/shard_map/ppermute | solution.py:91
  49.5 5.2 %collective-permute-done.6 = f32[4,32,768]{2,1,0:T(8,128)S(1)} collective-permute-done((f32[4,32,768]{2,1,0:T(8,128)S(1)}, f32[4,32,768]{2,1,0:T(8,128)S(1)}, u32[]{:S(2)}, u32[]{:S(2)}) %collective-permute-start.6) | collective-permute-done | bytes 393248 | tf_op jit(solution)/shard_map/ppermute | solution.py:91
  54.7 0.0 collective-permute-done.9
  54.9 0.0 copy-start
  54.9 0.1 collective-permute-start.10
  55.0 0.6 broadcast.44
  55.7 0.0 copy-done.3
  55.7 0.7 reduce.3
  56.4 0.1 reshape.34
  56.5 0.0 copy-done.2
  56.5 0.1 reshape.35
  57.2 0.8 multiply_bitcast_fusion
  58.0 0.1 copy.15
  58.1 0.6 fusion.5.idx_ref
  58.7 2.1 %collective-permute-done.10 = f32[8,4,32,768]{3,2,1,0:T(8,128)} collective-permute-done((f32[8,4,32,768]{3,2,1,0:T(8,128)S(1)}, f32[8,4,32,768]{3,2,1,0:T(8,128)}, u32[]{:S(2)}, u32[]{:S(2)}) %collective-permute-start.10) | collective-permute-done | bytes 3145760 | tf_op jit(solution)/shard_map/ppermute | solution.py:100
  60.8 0.8 %broadcast_in_dim.2.w_ref = f32[36,16,128]{2,1,0:T(8,128)} broadcast(f32[36,16]{1,0:T(8,128)S(1)} %copy.15), dimensions={0,1} | broadcast | bytes 297216 | tf_op jit(solution)/shard_map/broadcast_in_dim | solution.py:140
  61.6 0.0 copy-done
  61.6 11.5 %shard_map.86 = f32[6,4096]{1,0:T(8,128)} custom-call(s32[512]{0:T(512)} %fusion.5.idx_ref, f32[1024,768]{1,0:T(8,128)} %bitcast.42, f32[1024,768]{1,0:T(8,128)} %bitcast.15.far_ref, f32[36,16,128]{2,1,0:T(8,128)} %broadcast_in_dim.2.w_ref, bf16[36,16,4096]{2,1,0:T(8,128)(2,1)} %bitcast.40, bf16[36,16,4096]{2,1,0:T(8,128)(2,1)} %bitcast.41, f32[6,4096]{1,0:T(8,128)} %occ_ref.1), custom_call_target="tpu_custom_call" | custom-call | tf_op jit(solution)/shard_map/pallas_call | solution.py:51
  73.1 4.3 %all-to-all-start = ((f32[4,6,1024]{2,1,0:T(8,128)}), f32[4,6,1024]{2,1,0:T(8,128)S(1)}, u32[]{:S(2)}, u32[]{:S(2)}) async-start(f32[4,6,1024]{2,1,0:T(8,128)} %bitcast.45), calls=%async_computation | async-start | bytes 262144 | tf_op jit(solution)/shard_map/all_to_all | solution.py:148
  77.4 6.0 %all-to-all-done = f32[4,6,1024]{2,1,0:T(8,128)S(1)} async-done(((f32[4,6,1024]{2,1,0:T(8,128)}), f32[4,6,1024]{2,1,0:T(8,128)S(1)}, u32[]{:S(2)}, u32[]{:S(2)}) %all-to-all-start) | async-done | bytes 98336 | tf_op jit(solution)/shard_map/all_to_all | solution.py:148
  83.4 0.0 copy-start.1
  83.4 1.4 %multiply_add_fusion = f32[6,1024]{1,0:T(8,128)} fusion(f32[6,1024]{1,0:T(8,128)S(1)} %reduce_sum.9, f32[6,4096]{1,0:T(8,128)} %occ_ref.1, s32[]{:T(128)S(6)} %select_n.57), kind=kLoop, calls=%fused_computation.10 | loop fusion | flops 12288 | bytes 73732 | tf_op jit(solution)/shard_map/add | solution.py:152
  84.8 0.0 copy-done.1
  (11 shorter events, 0.3 us)
Async XLA Ops:
  1.6 5.9 %collective-permute-start = (f32[32,768]{1,0:T(8,128)S(1)}, f32[32,768]{1,0:T(8,128)S(1)}, u32[]{:S(2)}, u32[]{:S(2)}) collective-permute-start(f32[32,768]{1,0:T(8,128)S(1)} %bitcast.52), channel_id=1, source_target_pairs={{0,24},{4,28},{8,0},{12,4},{16,8},{20,12},{24,16},{28,20},{32,56},... | collective-permute-start | bytes 294920 | tf_op jit(solution)/shard_map/ppermute | solution.py:91
  2.4 6.0 %collective-permute-start.2 = (f32[32,768]{1,0:T(8,128)S(1)}, f32[32,768]{1,0:T(8,128)S(1)}, u32[]{:S(2)}, u32[]{:S(2)}) collective-permute-start(f32[32,768]{1,0:T(8,128)S(1)} %bitcast.53), channel_id=1, source_target_pairs={{0,8},{4,12},{8,16},{12,20},{16,24},{20,28},{24,0},{28,4},{32,40},... | collective-permute-start | bytes 294920 | tf_op jit(solution)/shard_map/ppermute | solution.py:94
  7.5 5.8 %collective-permute-start.1 = (f32[32,768]{1,0:T(8,128)S(1)}, f32[32,768]{1,0:T(8,128)S(1)}, u32[]{:S(2)}, u32[]{:S(2)}) collective-permute-start(f32[32,768]{1,0:T(8,128)S(1)} %collective-permute-done), channel_id=1, source_target_pairs={{0,24},{4,28},{8,0},{12,4},{16,8},{20,12},{24,16},{28,20},{32,56},... | collective-permute-start | bytes 294920 | tf_op jit(solution)/shard_map/ppermute | solution.py:91
  13.3 42.3 %copy-start.3 = (s32[1,1,16,32,1]{3,4,2,1,0:T(1,128)S(1)}, s32[1,1,16,32,1]{3,4,2,1,0:T(1,128)}, u32[]{:S(2)}) copy-start(s32[1,1,16,32,1]{3,4,2,1,0:T(1,128)} %param.10) | copy-start | bytes 6148
  13.3 43.1 %copy-start.2 = (s32[1,1,16,32]{3,2,1,0:T(8,128)S(1)}, s32[1,1,16,32]{3,2,1,0:T(8,128)}, u32[]{:S(2)}) copy-start(s32[1,1,16,32]{3,2,1,0:T(8,128)} %param.11) | copy-start | bytes 6148
  13.3 12.0 %collective-permute-start.3 = (f32[4,32,768]{2,1,0:T(8,128)S(1)}, f32[4,32,768]{2,1,0:T(8,128)S(1)}, u32[]{:S(2)}, u32[]{:S(2)}) collective-permute-start(f32[4,32,768]{2,1,0:T(8,128)S(1)} %pad_maximum_fusion), channel_id=1, source_target_pairs={{0,224},{4,228},{8,232},{12,236},{16,240},{20,244},{24,248},{28,25... | collective-permute-start | bytes 1179656 | tf_op jit(solution)/shard_map/ppermute | solution.py:91
  19.3 9.8 %collective-permute-start.7 = (f32[4,32,768]{2,1,0:T(8,128)S(1)}, f32[4,32,768]{2,1,0:T(8,128)S(1)}, u32[]{:S(2)}, u32[]{:S(2)}) collective-permute-start(f32[4,32,768]{2,1,0:T(8,128)S(1)} %pad_maximum_fusion), channel_id=1, source_target_pairs={{0,32},{4,36},{8,40},{12,44},{16,48},{20,52},{24,56},{28,60},{32,6... | collective-permute-start | bytes 1179656 | tf_op jit(solution)/shard_map/ppermute | solution.py:94
  25.4 9.6 %collective-permute-start.4 = (f32[4,32,768]{2,1,0:T(8,128)S(1)}, f32[4,32,768]{2,1,0:T(8,128)S(1)}, u32[]{:S(2)}, u32[]{:S(2)}) collective-permute-start(f32[4,32,768]{2,1,0:T(8,128)S(1)} %collective-permute-done.3), channel_id=1, source_target_pairs={{0,224},{4,228},{8,232},{12,236},{16,240},{20,244},{24,248},{28,25... | collective-permute-start | bytes 1179656 | tf_op jit(solution)/shard_map/ppermute | solution.py:91
  29.0 9.8 %collective-permute-start.8 = (f32[4,32,768]{2,1,0:T(8,128)S(1)}, f32[4,32,768]{2,1,0:T(8,128)S(1)}, u32[]{:S(2)}, u32[]{:S(2)}) collective-permute-start(f32[4,32,768]{2,1,0:T(8,128)S(1)} %collective-permute-done.7), channel_id=1, source_target_pairs={{0,32},{4,36},{8,40},{12,44},{16,48},{20,52},{24,56},{28,60},{32,6... | collective-permute-start | bytes 1179656 | tf_op jit(solution)/shard_map/ppermute | solution.py:94
  35.0 10.7 %collective-permute-start.5 = (f32[4,32,768]{2,1,0:T(8,128)S(1)}, f32[4,32,768]{2,1,0:T(8,128)S(1)}, u32[]{:S(2)}, u32[]{:S(2)}) collective-permute-start(f32[4,32,768]{2,1,0:T(8,128)S(1)} %collective-permute-done.4), channel_id=1, source_target_pairs={{0,224},{4,228},{8,232},{12,236},{16,240},{20,244},{24,248},{28,25... | collective-permute-start | bytes 1179656 | tf_op jit(solution)/shard_map/ppermute | solution.py:91
  38.8 15.9 %collective-permute-start.9 = (f32[4,32,768]{2,1,0:T(8,128)S(1)}, f32[4,32,768]{2,1,0:T(8,128)S(1)}, u32[]{:S(2)}, u32[]{:S(2)}) collective-permute-start(f32[4,32,768]{2,1,0:T(8,128)S(1)} %collective-permute-done.8), channel_id=1, source_target_pairs={{0,32},{4,36},{8,40},{12,44},{16,48},{20,52},{24,56},{28,60},{32,6... | collective-permute-start | bytes 1179656 | tf_op jit(solution)/shard_map/ppermute | solution.py:94
  45.7 9.0 %collective-permute-start.6 = (f32[4,32,768]{2,1,0:T(8,128)S(1)}, f32[4,32,768]{2,1,0:T(8,128)S(1)}, u32[]{:S(2)}, u32[]{:S(2)}) collective-permute-start(f32[4,32,768]{2,1,0:T(8,128)S(1)} %collective-permute-done.5), channel_id=1, source_target_pairs={{0,224},{4,228},{8,232},{12,236},{16,240},{20,244},{24,248},{28,25... | collective-permute-start | bytes 1179656 | tf_op jit(solution)/shard_map/ppermute | solution.py:91
  54.9 6.7 %copy-start = (f32[8,4,32,768]{3,2,1,0:T(8,128)}, f32[8,4,32,768]{3,2,1,0:T(8,128)S(1)}, u32[]{:S(2)}) copy-start(f32[8,4,32,768]{3,2,1,0:T(8,128)S(1)} %bitcast_dynamic-update-slice_fusion) | copy-start | bytes 9437188
  54.9 5.9 %collective-permute-start.10 = (f32[8,4,32,768]{3,2,1,0:T(8,128)S(1)}, f32[8,4,32,768]{3,2,1,0:T(8,128)}, u32[]{:S(2)}, u32[]{:S(2)}) collective-permute-start(f32[8,4,32,768]{3,2,1,0:T(8,128)S(1)} %bitcast_dynamic-update-slice_fusion), channel_id=1, source_target_pairs={{0,4},{4,0},{8,12},{12,8},{16,20},{20,16},{24,28},{28,24},{32,36},... | collective-permute-start | bytes 9437192 | tf_op jit(solution)/shard_map/ppermute | solution.py:100
  73.1 10.3 %all-to-all-start = ((f32[4,6,1024]{2,1,0:T(8,128)}), f32[4,6,1024]{2,1,0:T(8,128)S(1)}, u32[]{:S(2)}, u32[]{:S(2)}) async-start(f32[4,6,1024]{2,1,0:T(8,128)} %bitcast.45), calls=%async_computation | async-start | bytes 262144 | tf_op jit(solution)/shard_map/all_to_all | solution.py:148
  83.4 1.4 %copy-start.1 = (f32[6,1024]{1,0:T(8,128)}, f32[6,1024]{1,0:T(8,128)S(1)}, u32[]{:S(2)}) copy-start(f32[6,1024]{1,0:T(8,128)S(1)} %reduce_sum.9) | copy-start | bytes 73732

commit v10 on v9

--- a/solution.py
+++ b/solution.py
@@ -88,11 +88,16 @@
         ahead = {0: x}
         fwd, back = x, x
         for d in range(1, count // 2 + 1):
-            back = lax.ppermute(back, "ka", step(-1))
-            ahead[d] = back
             if d < count - d:
+                back = lax.ppermute(back, "ka", step(-1))
                 fwd = lax.ppermute(fwd, "ka", step(1))
+                ahead[d] = back
                 ahead[count - d] = fwd
+            else:
+                cut = x.shape[0] // 2
+                low = lax.ppermute(back[:cut], "ka", step(-1))
+                high = lax.ppermute(fwd[cut:], "ka", step(1))
+                ahead[d] = jnp.concatenate([low, high])
         return jnp.stack([ahead[d] for d in range(count)])
 
     along_y = ring(block, y_step, y_count)

time: 85.3 us -> 89.8 us (1.053)
  the two profiles are of different devices: /device:TPU:24 before, /device:TPU:1 now
where the time goes in v10:
time: 89.8 us; the launch traced here: 89.4 us
  waiting for transfers between devices  36.5 us (41%)
  starting transfers between devices  33.3 us (37%)
  Pallas kernels  11.5 us (13%)
  local copies, waits for them, and re-layouts  3.7 us (4%)
  other arithmetic  2.85 us (3%)
  between operations  1.47 us (2%)
    ppermute x4, starting transfers between devices, ring(): back = lax.ppermute(back, 'ka', step(-1))  15.8 us
    pallas_call x1, Pallas kernels, collide(): pl.pallas_call(kern, out_shape=jax.ShapeDtypeStruct((bands, width), jnp.f...  11.5 us
    ppermute x4, waiting for transfers between devices, ring(): back = lax.ppermute(back, 'ka', step(-1))  11.4 us
    ppermute x4, waiting for transfers between devices, ring(): fwd = lax.ppermute(fwd, 'ka', step(1))  9.07 us
    ppermute x2, waiting for transfers between devices, ring(): high = lax.ppermute(fwd[cut:], 'ka', step(1))  8.44 us
    ppermute x1, starting transfers between devices, ring_gather(): other = lax.ppermute(along_z, 'ka', pairs(lambda j: j ^ 1))  7.57 us
    ppermute x2, starting transfers between devices, ring(): low = lax.ppermute(back[:cut], 'ka', step(-1))  5.76 us
    all_to_all x1, waiting for transfers between devices, body(): collision = jnp.sum(lax.all_to_all(parts, 'pb', 0, 0, tiled=True), axis=0)  4.83 us
  transfers between devices with their start and end apart: 14, of which 9 were waited for; matrix products, arithmetic and copies ran while one was open for 4% of the time, Pallas kernels for 0%

profile of v10, /device:TPU:1, one launch (start us, length us, event | category | flops | bytes accessed | tf_op | source)
XLA Modules:
  0.0 89.4 jit_solution(14475125235948647942)
XLA Ops:
  0.6 0.9 %copy.19 = f32[4,8,6,128]{3,1,2,0:T(8,128)S(1)} copy(f32[4,8,6,128]{3,2,1,0:T(8,128)} %bitcast.46) | data formatting | bytes 196608
  1.6 3.6 %collective-permute-start = (f32[32,768]{1,0:T(8,128)S(1)}, f32[32,768]{1,0:T(8,128)S(1)}, u32[]{:S(2)}, u32[]{:S(2)}) collective-permute-start(f32[32,768]{1,0:T(8,128)S(1)} %bitcast.53), channel_id=1, source_target_pairs={{0,24},{4,28},{8,0},{12,4},{16,8},{20,12},{24,16},{28,20},{32,56},... | collective-permute-start | bytes 294920 | tf_op jit(solution)/shard_map/ppermute | solution.py:92
  5.2 0.0 collective-permute-start.2
  5.2 1.6 %collective-permute-done = f32[32,768]{1,0:T(8,128)S(1)} collective-permute-done((f32[32,768]{1,0:T(8,128)S(1)}, f32[32,768]{1,0:T(8,128)S(1)}, u32[]{:S(2)}, u32[]{:S(2)}) %collective-permute-start) | collective-permute-done | bytes 98336 | tf_op jit(solution)/shard_map/ppermute | solution.py:92
  6.8 3.0 %collective-permute-start.1 = (f32[16,768]{1,0:T(8,128)S(1)}, f32[16,768]{1,0:T(8,128)S(1)}, u32[]{:S(2)}, u32[]{:S(2)}) collective-permute-start(f32[16,768]{1,0:T(8,128)S(1)} %slice.16), channel_id=1, source_target_pairs={{0,24},{4,28},{8,0},{12,4},{16,8},{20,12},{24,16},{28,20},{32,56},... | collective-permute-start | bytes 147464 | tf_op jit(solution)/shard_map/ppermute | solution.py:98
  9.9 0.0 collective-permute-done.2
  9.9 0.1 collective-permute-start.3
  10.0 0.9 %stack_reshape.3 = f32[1,32,768]{2,1,0:T(8,128)S(1)} reshape(f32[32,6,128]{2,1,0:T(8,128)} %bitcast.47) | data formatting | bytes 196608 | tf_op jit(solution)/shard_map/stack;reshape | solution.py:101
  10.9 0.2 collective-permute-done.1
  11.1 3.1 %collective-permute-done.3 = f32[16,768]{1,0:T(8,128)S(1)} collective-permute-done((f32[16,768]{1,0:T(8,128)S(1)}, f32[16,768]{1,0:T(8,128)S(1)}, u32[]{:S(2)}, u32[]{:S(2)}) %collective-permute-start.3) | collective-permute-done | bytes 49184 | tf_op jit(solution)/shard_map/ppermute | solution.py:99
  14.2 5.7 %collective-permute-start.4 = (f32[4,32,768]{2,1,0:T(8,128)S(1)}, f32[4,32,768]{2,1,0:T(8,128)S(1)}, u32[]{:S(2)}, u32[]{:S(2)}) collective-permute-start(f32[4,32,768]{2,1,0:T(8,128)S(1)} %pad_maximum_fusion), channel_id=1, source_target_pairs={{0,224},{4,228},{8,232},{12,236},{16,240},{20,244},{24,248},{28,25... | collective-permute-start | bytes 1179656 | tf_op jit(solution)/shard_map/ppermute | solution.py:92
  19.8 0.0 collective-permute-start.8
  19.8 5.1 %collective-permute-done.4 = f32[4,32,768]{2,1,0:T(8,128)S(1)} collective-permute-done((f32[4,32,768]{2,1,0:T(8,128)S(1)}, f32[4,32,768]{2,1,0:T(8,128)S(1)}, u32[]{:S(2)}, u32[]{:S(2)}) %collective-permute-start.4) | collective-permute-done | bytes 393248 | tf_op jit(solution)/shard_map/ppermute | solution.py:92
  25.0 3.4 %collective-permute-start.5 = (f32[4,32,768]{2,1,0:T(8,128)S(1)}, f32[4,32,768]{2,1,0:T(8,128)S(1)}, u32[]{:S(2)}, u32[]{:S(2)}) collective-permute-start(f32[4,32,768]{2,1,0:T(8,128)S(1)} %collective-permute-done.4), channel_id=1, source_target_pairs={{0,224},{4,228},{8,232},{12,236},{16,240},{20,244},{24,248},{28,25... | collective-permute-start | bytes 1179656 | tf_op jit(solution)/shard_map/ppermute | solution.py:92
  28.4 0.0 collective-permute-done.8
  28.4 0.0 collective-permute-start.9
  28.4 0.0 copy-start.3
  28.4 0.0 copy-start.2
  28.4 0.0 copy-start.4
  28.4 4.6 %collective-permute-done.5 = f32[4,32,768]{2,1,0:T(8,128)S(1)} collective-permute-done((f32[4,32,768]{2,1,0:T(8,128)S(1)}, f32[4,32,768]{2,1,0:T(8,128)S(1)}, u32[]{:S(2)}, u32[]{:S(2)}) %collective-permute-start.5) | collective-permute-done | bytes 393248 | tf_op jit(solution)/shard_map/ppermute | solution.py:92
  33.1 3.1 %collective-permute-start.6 = (f32[4,32,768]{2,1,0:T(8,128)S(1)}, f32[4,32,768]{2,1,0:T(8,128)S(1)}, u32[]{:S(2)}, u32[]{:S(2)}) collective-permute-start(f32[4,32,768]{2,1,0:T(8,128)S(1)} %collective-permute-done.5), channel_id=1, source_target_pairs={{0,224},{4,228},{8,232},{12,236},{16,240},{20,244},{24,248},{28,25... | collective-permute-start | bytes 1179656 | tf_op jit(solution)/shard_map/ppermute | solution.py:92
  36.2 0.0 collective-permute-done.9
  36.2 0.0 collective-permute-start.10
  36.3 9.1 %collective-permute-done.10 = f32[4,32,768]{2,1,0:T(8,128)S(1)} collective-permute-done((f32[4,32,768]{2,1,0:T(8,128)S(1)}, f32[4,32,768]{2,1,0:T(8,128)S(1)}, u32[]{:S(2)}, u32[]{:S(2)}) %collective-permute-start.10) | collective-permute-done | bytes 393248 | tf_op jit(solution)/shard_map/ppermute | solution.py:93
  45.4 0.1 collective-permute-start.11
  45.5 0.0 collective-permute-done.6
  45.5 2.7 %collective-permute-start.7 = (f32[2,32,768]{2,1,0:T(8,128)S(1)}, f32[2,32,768]{2,1,0:T(8,128)S(1)}, u32[]{:S(2)}, u32[]{:S(2)}) collective-permute-start(f32[2,32,768]{2,1,0:T(8,128)S(1)} %slice.18), channel_id=1, source_target_pairs={{0,224},{4,228},{8,232},{12,236},{16,240},{20,244},{24,248},{28,25... | collective-permute-start | bytes 589832 | tf_op jit(solution)/shard_map/ppermute | solution.py:98
  48.2 5.4 %collective-permute-done.11 = f32[2,32,768]{2,1,0:T(8,128)S(1)} collective-permute-done((f32[2,32,768]{2,1,0:T(8,128)S(1)}, f32[2,32,768]{2,1,0:T(8,128)S(1)}, u32[]{:S(2)}, u32[]{:S(2)}) %collective-permute-start.11) | collective-permute-done | bytes 196640 | tf_op jit(solution)/shard_map/ppermute | solution.py:99
  53.6 0.0 collective-permute-done.7
  53.8 0.0 copy-start
  53.8 7.6 %collective-permute-start.12 = (f32[8,4,32,768]{3,2,1,0:T(8,128)S(1)}, f32[8,4,32,768]{3,2,1,0:T(8,128)}, u32[]{:S(2)}, u32[]{:S(2)}) collective-permute-start(f32[8,4,32,768]{3,2,1,0:T(8,128)S(1)} %bitcast_dynamic-update-slice_fusion), channel_id=1, source_target_pairs={{0,4},{4,0},{8,12},{12,8},{16,20},{20,16},{24,28},{28,24},{32,36},... | collective-permute-start | bytes 9437192 | tf_op jit(solution)/shard_map/ppermute | solution.py:105
  61.4 0.5 broadcast.44
  61.9 0.0 copy-done.3
  61.9 0.7 reduce.3
  62.6 0.1 reshape.34
  62.6 0.0 copy-done.2
  62.6 0.1 reshape.35
  63.4 0.0 copy-done.4
  63.4 0.1 multiply_bitcast_fusion
  63.5 0.1 copy.15
  63.6 0.6 fusion.6.idx_ref
  64.2 2.6 %collective-permute-done.12 = f32[8,4,32,768]{3,2,1,0:T(8,128)} collective-permute-done((f32[8,4,32,768]{3,2,1,0:T(8,128)S(1)}, f32[8,4,32,768]{3,2,1,0:T(8,128)}, u32[]{:S(2)}, u32[]{:S(2)}) %collective-permute-start.12) | collective-permute-done | bytes 3145760 | tf_op jit(solution)/shard_map/ppermute | solution.py:105
  66.8 0.9 broadcast_in_dim.2.w_ref
  67.6 0.0 copy-done
  67.6 11.5 %shard_map.86 = f32[6,4096]{1,0:T(8,128)} custom-call(s32[512]{0:T(512)} %fusion.6.idx_ref, f32[1024,768]{1,0:T(8,128)} %bitcast.45, f32[1024,768]{1,0:T(8,128)} %bitcast.15.far_ref, f32[36,16,128]{2,1,0:T(8,128)} %broadcast_in_dim.2.w_ref, bf16[36,16,4096]{2,1,0:T(8,128)(2,1)} %bitcast.43, bf16[36,16,4096]{2,1,0:T(8,128)(2,1)} %bitcast.44, f32[6,4096]{1,0:T(8,128)} %occ_ref.1), custom_call_target="tpu_custom_call" | custom-call | tf_op jit(solution)/shard_map/pallas_call | solution.py:51
  79.1 4.0 %all-to-all-start = ((f32[4,6,1024]{2,1,0:T(8,128)}), f32[4,6,1024]{2,1,0:T(8,128)S(1)}, u32[]{:S(2)}, u32[]{:S(2)}) async-start(f32[4,6,1024]{2,1,0:T(8,128)} %bitcast.52), calls=%async_computation | async-start | bytes 262144 | tf_op jit(solution)/shard_map/all_to_all | solution.py:153
  83.1 4.8 %all-to-all-done = f32[4,6,1024]{2,1,0:T(8,128)S(1)} async-done(((f32[4,6,1024]{2,1,0:T(8,128)}), f32[4,6,1024]{2,1,0:T(8,128)S(1)}, u32[]{:S(2)}, u32[]{:S(2)}) %all-to-all-start) | async-done | bytes 98336 | tf_op jit(solution)/shard_map/all_to_all | solution.py:153
  88.0 0.0 copy-start.1
  88.0 1.4 %multiply_add_fusion = f32[6,1024]{1,0:T(8,128)} fusion(f32[6,1024]{1,0:T(8,128)S(1)} %reduce_sum.9, f32[6,4096]{1,0:T(8,128)} %occ_ref.1, s32[]{:T(128)S(6)} %select_n.57), kind=kLoop, calls=%fused_computation.12 | loop fusion | flops 12288 | bytes 73732 | tf_op jit(solution)/shard_map/add | solution.py:157
  89.4 0.0 copy-done.1
  (16 shorter events, 0.3 us)
Async XLA Ops:
  1.6 5.3 %collective-permute-start = (f32[32,768]{1,0:T(8,128)S(1)}, f32[32,768]{1,0:T(8,128)S(1)}, u32[]{:S(2)}, u32[]{:S(2)}) collective-permute-start(f32[32,768]{1,0:T(8,128)S(1)} %bitcast.53), channel_id=1, source_target_pairs={{0,24},{4,28},{8,0},{12,4},{16,8},{20,12},{24,16},{28,20},{32,56},... | collective-permute-start | bytes 294920 | tf_op jit(solution)/shard_map/ppermute | solution.py:92
  5.2 4.7 %collective-permute-start.2 = (f32[32,768]{1,0:T(8,128)S(1)}, f32[32,768]{1,0:T(8,128)S(1)}, u32[]{:S(2)}, u32[]{:S(2)}) collective-permute-start(f32[32,768]{1,0:T(8,128)S(1)} %bitcast.54), channel_id=1, source_target_pairs={{0,8},{4,12},{8,16},{12,20},{16,24},{20,28},{24,0},{28,4},{32,40},... | collective-permute-start | bytes 294920 | tf_op jit(solution)/shard_map/ppermute | solution.py:93
  6.8 4.2 %collective-permute-start.1 = (f32[16,768]{1,0:T(8,128)S(1)}, f32[16,768]{1,0:T(8,128)S(1)}, u32[]{:S(2)}, u32[]{:S(2)}) collective-permute-start(f32[16,768]{1,0:T(8,128)S(1)} %slice.16), channel_id=1, source_target_pairs={{0,24},{4,28},{8,0},{12,4},{16,8},{20,12},{24,16},{28,20},{32,56},... | collective-permute-start | bytes 147464 | tf_op jit(solution)/shard_map/ppermute | solution.py:98
  9.9 4.2 %collective-permute-start.3 = (f32[16,768]{1,0:T(8,128)S(1)}, f32[16,768]{1,0:T(8,128)S(1)}, u32[]{:S(2)}, u32[]{:S(2)}) collective-permute-start(f32[16,768]{1,0:T(8,128)S(1)} %slice.17), channel_id=1, source_target_pairs={{0,8},{4,12},{8,16},{12,20},{16,24},{20,28},{24,0},{28,4},{32,40},... | collective-permute-start | bytes 147464 | tf_op jit(solution)/shard_map/ppermute | solution.py:99
  14.2 10.8 %collective-permute-start.4 = (f32[4,32,768]{2,1,0:T(8,128)S(1)}, f32[4,32,768]{2,1,0:T(8,128)S(1)}, u32[]{:S(2)}, u32[]{:S(2)}) collective-permute-start(f32[4,32,768]{2,1,0:T(8,128)S(1)} %pad_maximum_fusion), channel_id=1, source_target_pairs={{0,224},{4,228},{8,232},{12,236},{16,240},{20,244},{24,248},{28,25... | collective-permute-start | bytes 1179656 | tf_op jit(solution)/shard_map/ppermute | solution.py:92
  19.8 8.6 %collective-permute-start.8 = (f32[4,32,768]{2,1,0:T(8,128)S(1)}, f32[4,32,768]{2,1,0:T(8,128)S(1)}, u32[]{:S(2)}, u32[]{:S(2)}) collective-permute-start(f32[4,32,768]{2,1,0:T(8,128)S(1)} %pad_maximum_fusion), channel_id=1, source_target_pairs={{0,32},{4,36},{8,40},{12,44},{16,48},{20,52},{24,56},{28,60},{32,6... | collective-permute-start | bytes 1179656 | tf_op jit(solution)/shard_map/ppermute | solution.py:93
  25.0 8.1 %collective-permute-start.5 = (f32[4,32,768]{2,1,0:T(8,128)S(1)}, f32[4,32,768]{2,1,0:T(8,128)S(1)}, u32[]{:S(2)}, u32[]{:S(2)}) collective-permute-start(f32[4,32,768]{2,1,0:T(8,128)S(1)} %collective-permute-done.4), channel_id=1, source_target_pairs={{0,224},{4,228},{8,232},{12,236},{16,240},{20,244},{24,248},{28,25... | collective-permute-start | bytes 1179656 | tf_op jit(solution)/shard_map/ppermute | solution.py:92
  28.4 7.8 %collective-permute-start.9 = (f32[4,32,768]{2,1,0:T(8,128)S(1)}, f32[4,32,768]{2,1,0:T(8,128)S(1)}, u32[]{:S(2)}, u32[]{:S(2)}) collective-permute-start(f32[4,32,768]{2,1,0:T(8,128)S(1)} %collective-permute-done.8), channel_id=1, source_target_pairs={{0,32},{4,36},{8,40},{12,44},{16,48},{20,52},{24,56},{28,60},{32,6... | collective-permute-start | bytes 1179656 | tf_op jit(solution)/shard_map/ppermute | solution.py:93
  28.4 33.5 %copy-start.3 = (s32[1,1,16,32,1]{3,4,2,1,0:T(1,128)S(1)}, s32[1,1,16,32,1]{3,4,2,1,0:T(1,128)}, u32[]{:S(2)}) copy-start(s32[1,1,16,32,1]{3,4,2,1,0:T(1,128)} %param.10) | copy-start | bytes 6148
  28.4 34.2 %copy-start.2 = (s32[1,1,16,32]{3,2,1,0:T(8,128)S(1)}, s32[1,1,16,32]{3,2,1,0:T(8,128)}, u32[]{:S(2)}) copy-start(s32[1,1,16,32]{3,2,1,0:T(8,128)} %param.11) | copy-start | bytes 6148
  28.4 34.9 %copy-start.4 = (s32[16,36]{1,0:T(8,128)S(1)}, s32[16,36]{1,0:T(8,128)}, u32[]{:S(2)}) copy-start(s32[16,36]{1,0:T(8,128)} %param.12) | copy-start | bytes 6916
  33.1 12.4 %collective-permute-start.6 = (f32[4,32,768]{2,1,0:T(8,128)S(1)}, f32[4,32,768]{2,1,0:T(8,128)S(1)}, u32[]{:S(2)}, u32[]{:S(2)}) collective-permute-start(f32[4,32,768]{2,1,0:T(8,128)S(1)} %collective-permute-done.5), channel_id=1, source_target_pairs={{0,224},{4,228},{8,232},{12,236},{16,240},{20,244},{24,248},{28,25... | collective-permute-start | bytes 1179656 | tf_op jit(solution)/shard_map/ppermute | solution.py:92
  36.2 9.1 %collective-permute-start.10 = (f32[4,32,768]{2,1,0:T(8,128)S(1)}, f32[4,32,768]{2,1,0:T(8,128)S(1)}, u32[]{:S(2)}, u32[]{:S(2)}) collective-permute-start(f32[4,32,768]{2,1,0:T(8,128)S(1)} %collective-permute-done.9), channel_id=1, source_target_pairs={{0,32},{4,36},{8,40},{12,44},{16,48},{20,52},{24,56},{28,60},{32,6... | collective-permute-start | bytes 1179656 | tf_op jit(solution)/shard_map/ppermute | solution.py:93
  45.4 8.3 %collective-permute-start.11 = (f32[2,32,768]{2,1,0:T(8,128)S(1)}, f32[2,32,768]{2,1,0:T(8,128)S(1)}, u32[]{:S(2)}, u32[]{:S(2)}) collective-permute-start(f32[2,32,768]{2,1,0:T(8,128)S(1)} %slice.19), channel_id=1, source_target_pairs={{0,32},{4,36},{8,40},{12,44},{16,48},{20,52},{24,56},{28,60},{32,6... | collective-permute-start | bytes 589832 | tf_op jit(solution)/shard_map/ppermute | solution.py:99
  45.5 8.2 %collective-permute-start.7 = (f32[2,32,768]{2,1,0:T(8,128)S(1)}, f32[2,32,768]{2,1,0:T(8,128)S(1)}, u32[]{:S(2)}, u32[]{:S(2)}) collective-permute-start(f32[2,32,768]{2,1,0:T(8,128)S(1)} %slice.18), channel_id=1, source_target_pairs={{0,224},{4,228},{8,232},{12,236},{16,240},{20,244},{24,248},{28,25... | collective-permute-start | bytes 589832 | tf_op jit(solution)/shard_map/ppermute | solution.py:98
  53.8 13.9 %copy-start = (f32[8,4,32,768]{3,2,1,0:T(8,128)}, f32[8,4,32,768]{3,2,1,0:T(8,128)S(1)}, u32[]{:S(2)}) copy-start(f32[8,4,32,768]{3,2,1,0:T(8,128)S(1)} %bitcast_dynamic-update-slice_fusion) | copy-start | bytes 9437188
  53.8 13.0 %collective-permute-start.12 = (f32[8,4,32,768]{3,2,1,0:T(8,128)S(1)}, f32[8,4,32,768]{3,2,1,0:T(8,128)}, u32[]{:S(2)}, u32[]{:S(2)}) collective-permute-start(f32[8,4,32,768]{3,2,1,0:T(8,128)S(1)} %bitcast_dynamic-update-slice_fusion), channel_id=1, source_target_pairs={{0,4},{4,0},{8,12},{12,8},{16,20},{20,16},{24,28},{28,24},{32,36},... | collective-permute-start | bytes 9437192 | tf_op jit(solution)/shard_map/ppermute | solution.py:105
  79.1 8.8 %all-to-all-start = ((f32[4,6,1024]{2,1,0:T(8,128)}), f32[4,6,1024]{2,1,0:T(8,128)S(1)}, u32[]{:S(2)}, u32[]{:S(2)}) async-start(f32[4,6,1024]{2,1,0:T(8,128)} %bitcast.52), calls=%async_computation | async-start | bytes 262144 | tf_op jit(solution)/shard_map/all_to_all | solution.py:153
  88.0 1.4 %copy-start.1 = (f32[6,1024]{1,0:T(8,128)}, f32[6,1024]{1,0:T(8,128)S(1)}, u32[]{:S(2)}) copy-start(f32[6,1024]{1,0:T(8,128)S(1)} %reduce_sum.9) | copy-start | bytes 73732

commit v11 on v9

--- a/solution.py
+++ b/solution.py
@@ -95,7 +95,10 @@
                 ahead[count - d] = fwd
         return jnp.stack([ahead[d] for d in range(count)])
 
-    along_y = ring(block, y_step, y_count)
+    def direct(x, step, count):
+        return jnp.stack([x] + [lax.ppermute(x, "ka", step(-d)) for d in range(1, count)])
+
+    along_y = direct(block, y_step, y_count)
     along_z = ring(along_y, z_step, z_count)
     other = lax.ppermute(along_z, "ka", pairs(lambda j: j ^ 1))
     return along_z, other

time: 85.3 us -> 86.4 us (1.013)
  the two profiles are of different devices: /device:TPU:24 before, /device:TPU:1 now
where the time goes in v11:
time: 86.4 us; the launch traced here: 86 us
  waiting for transfers between devices  36.5 us (42%)
  starting transfers between devices  29.4 us (34%)
  Pallas kernels  11.5 us (13%)
  local copies, waits for them, and re-layouts  3.68 us (4%)
  other arithmetic  3.51 us (4%)
  between operations  1.44 us (2%)
    ppermute x4, waiting for transfers between devices, ring(): back = lax.ppermute(back, 'ka', step(-1))  23.9 us
    ppermute x4, starting transfers between devices, ring(): back = lax.ppermute(back, 'ka', step(-1))  15.9 us
    pallas_call x1, Pallas kernels, collide(): pl.pallas_call(kern, out_shape=jax.ShapeDtypeStruct((bands, width), jnp.f...  11.5 us
    ppermute x3, waiting for transfers between devices, direct(): lax.ppermute(x, 'ka', step(-d))  5.82 us
    all_to_all x1, waiting for transfers between devices, body(): collision = jnp.sum(lax.all_to_all(parts, 'pb', 0, 0, tiled=True), axis=0)  4.83 us
    ppermute x1, starting transfers between devices, ring_gather(): other = lax.ppermute(along_z, 'ka', pairs(lambda j: j ^ 1))  4.73 us
    ppermute x3, starting transfers between devices, direct(): lax.ppermute(x, 'ka', step(-d))  4.68 us
    all_to_all x1, starting transfers between devices, body(): collision = jnp.sum(lax.all_to_all(parts, 'pb', 0, 0, tiled=True), axis=0)  4.01 us
  transfers between devices with their start and end apart: 12, of which 8 were waited for; matrix products, arithmetic and copies ran while one was open for 5% of the time, Pallas kernels for 0%

profile of v11, /device:TPU:1, one launch (start us, length us, event | category | flops | bytes accessed | tf_op | source)
XLA Modules:
  0.0 86.0 jit_solution(7565247936475897830)
XLA Ops:
  0.6 0.9 %copy.19 = f32[4,8,6,128]{3,1,2,0:T(8,128)S(1)} copy(f32[4,8,6,128]{3,2,1,0:T(8,128)} %bitcast.43) | data formatting | bytes 196608
  1.6 3.6 %collective-permute-start = (f32[32,768]{1,0:T(8,128)S(1)}, f32[32,768]{1,0:T(8,128)S(1)}, u32[]{:S(2)}, u32[]{:S(2)}) collective-permute-start(f32[32,768]{1,0:T(8,128)S(1)} %bitcast.52), channel_id=1, source_target_pairs={{0,24},{4,28},{8,0},{12,4},{16,8},{20,12},{24,16},{28,20},{32,56},... | collective-permute-start | bytes 294920 | tf_op jit(solution)/shard_map/ppermute | solution.py:99
  5.2 0.3 collective-permute-start.1
  5.5 0.7 collective-permute-start.2
  6.2 0.9 %stack_reshape.3 = f32[1,32,768]{2,1,0:T(8,128)S(1)} reshape(f32[32,6,128]{2,1,0:T(8,128)} %bitcast.44) | data formatting | bytes 196608 | tf_op jit(solution)/shard_map/stack;reshape | solution.py:99
  7.2 0.0 collective-permute-done
  7.2 3.1 %collective-permute-done.1 = f32[32,768]{1,0:T(8,128)S(1)} collective-permute-done((f32[32,768]{1,0:T(8,128)S(1)}, f32[32,768]{1,0:T(8,128)S(1)}, u32[]{:S(2)}, u32[]{:S(2)}) %collective-permute-start.1) | collective-permute-done | bytes 98336 | tf_op jit(solution)/shard_map/ppermute | solution.py:99
  10.3 2.7 %collective-permute-done.2 = f32[32,768]{1,0:T(8,128)S(1)} collective-permute-done((f32[32,768]{1,0:T(8,128)S(1)}, f32[32,768]{1,0:T(8,128)S(1)}, u32[]{:S(2)}, u32[]{:S(2)}) %collective-permute-start.2) | collective-permute-done | bytes 98336 | tf_op jit(solution)/shard_map/ppermute | solution.py:99
  13.0 0.0 copy-start.3
  13.0 0.0 copy-start.2
  13.1 5.7 %collective-permute-start.3 = (f32[4,32,768]{2,1,0:T(8,128)S(1)}, f32[4,32,768]{2,1,0:T(8,128)S(1)}, u32[]{:S(2)}, u32[]{:S(2)}) collective-permute-start(f32[4,32,768]{2,1,0:T(8,128)S(1)} %pad_maximum_fusion), channel_id=1, source_target_pairs={{0,224},{4,228},{8,232},{12,236},{16,240},{20,244},{24,248},{28,25... | collective-permute-start | bytes 1179656 | tf_op jit(solution)/shard_map/ppermute | solution.py:91
  18.7 0.0 collective-permute-start.7
  18.7 7.4 %collective-permute-done.3 = f32[4,32,768]{2,1,0:T(8,128)S(1)} collective-permute-done((f32[4,32,768]{2,1,0:T(8,128)S(1)}, f32[4,32,768]{2,1,0:T(8,128)S(1)}, u32[]{:S(2)}, u32[]{:S(2)}) %collective-permute-start.3) | collective-permute-done | bytes 393248 | tf_op jit(solution)/shard_map/ppermute | solution.py:91
  26.1 3.4 %collective-permute-start.4 = (f32[4,32,768]{2,1,0:T(8,128)S(1)}, f32[4,32,768]{2,1,0:T(8,128)S(1)}, u32[]{:S(2)}, u32[]{:S(2)}) collective-permute-start(f32[4,32,768]{2,1,0:T(8,128)S(1)} %collective-permute-done.3), channel_id=1, source_target_pairs={{0,224},{4,228},{8,232},{12,236},{16,240},{20,244},{24,248},{28,25... | collective-permute-start | bytes 1179656 | tf_op jit(solution)/shard_map/ppermute | solution.py:91
  29.5 0.0 collective-permute-done.7
  29.5 0.0 collective-permute-start.8
  29.5 6.5 %collective-permute-done.4 = f32[4,32,768]{2,1,0:T(8,128)S(1)} collective-permute-done((f32[4,32,768]{2,1,0:T(8,128)S(1)}, f32[4,32,768]{2,1,0:T(8,128)S(1)}, u32[]{:S(2)}, u32[]{:S(2)}) %collective-permute-start.4) | collective-permute-done | bytes 393248 | tf_op jit(solution)/shard_map/ppermute | solution.py:91
  36.0 3.4 %collective-permute-start.5 = (f32[4,32,768]{2,1,0:T(8,128)S(1)}, f32[4,32,768]{2,1,0:T(8,128)S(1)}, u32[]{:S(2)}, u32[]{:S(2)}) collective-permute-start(f32[4,32,768]{2,1,0:T(8,128)S(1)} %collective-permute-done.4), channel_id=1, source_target_pairs={{0,224},{4,228},{8,232},{12,236},{16,240},{20,244},{24,248},{28,25... | collective-permute-start | bytes 1179656 | tf_op jit(solution)/shard_map/ppermute | solution.py:91
  39.4 0.0 collective-permute-done.8
  39.5 0.1 collective-permute-start.9
  39.6 5.4 %collective-permute-done.5 = f32[4,32,768]{2,1,0:T(8,128)S(1)} collective-permute-done((f32[4,32,768]{2,1,0:T(8,128)S(1)}, f32[4,32,768]{2,1,0:T(8,128)S(1)}, u32[]{:S(2)}, u32[]{:S(2)}) %collective-permute-start.5) | collective-permute-done | bytes 393248 | tf_op jit(solution)/shard_map/ppermute | solution.py:91
  44.9 3.4 %collective-permute-start.6 = (f32[4,32,768]{2,1,0:T(8,128)S(1)}, f32[4,32,768]{2,1,0:T(8,128)S(1)}, u32[]{:S(2)}, u32[]{:S(2)}) collective-permute-start(f32[4,32,768]{2,1,0:T(8,128)S(1)} %collective-permute-done.5), channel_id=1, source_target_pairs={{0,224},{4,228},{8,232},{12,236},{16,240},{20,244},{24,248},{28,25... | collective-permute-start | bytes 1179656 | tf_op jit(solution)/shard_map/ppermute | solution.py:91
  48.4 4.7 %collective-permute-done.6 = f32[4,32,768]{2,1,0:T(8,128)S(1)} collective-permute-done((f32[4,32,768]{2,1,0:T(8,128)S(1)}, f32[4,32,768]{2,1,0:T(8,128)S(1)}, u32[]{:S(2)}, u32[]{:S(2)}) %collective-permute-start.6) | collective-permute-done | bytes 393248 | tf_op jit(solution)/shard_map/ppermute | solution.py:91
  53.1 0.0 collective-permute-done.9
  53.2 0.0 copy-start
  53.2 4.7 %collective-permute-start.10 = (f32[8,4,32,768]{3,2,1,0:T(8,128)S(1)}, f32[8,4,32,768]{3,2,1,0:T(8,128)}, u32[]{:S(2)}, u32[]{:S(2)}) collective-permute-start(f32[8,4,32,768]{3,2,1,0:T(8,128)S(1)} %bitcast_dynamic-update-slice_fusion), channel_id=1, source_target_pairs={{0,4},{4,0},{8,12},{12,8},{16,20},{20,16},{24,28},{28,24},{32,36},... | collective-permute-start | bytes 9437192 | tf_op jit(solution)/shard_map/ppermute | solution.py:103
  57.9 0.5 broadcast.44
  58.5 0.0 copy-done.3
  58.5 0.7 reduce.3
  59.1 0.1 reshape.34
  59.2 0.0 copy-done.2
  59.2 0.1 reshape.35
  60.0 0.8 multiply_bitcast_fusion
  60.7 0.1 copy.15
  60.8 0.6 fusion.5.idx_ref
  61.4 1.9 %collective-permute-done.10 = f32[8,4,32,768]{3,2,1,0:T(8,128)} collective-permute-done((f32[8,4,32,768]{3,2,1,0:T(8,128)S(1)}, f32[8,4,32,768]{3,2,1,0:T(8,128)}, u32[]{:S(2)}, u32[]{:S(2)}) %collective-permute-start.10) | collective-permute-done | bytes 3145760 | tf_op jit(solution)/shard_map/ppermute | solution.py:103
  63.4 0.8 broadcast_in_dim.2.w_ref
  64.2 0.0 copy-done
  64.2 11.5 %shard_map.86 = f32[6,4096]{1,0:T(8,128)} custom-call(s32[512]{0:T(512)} %fusion.5.idx_ref, f32[1024,768]{1,0:T(8,128)} %bitcast.42, f32[1024,768]{1,0:T(8,128)} %bitcast.15.far_ref, f32[36,16,128]{2,1,0:T(8,128)} %broadcast_in_dim.2.w_ref, bf16[36,16,4096]{2,1,0:T(8,128)(2,1)} %bitcast.40, bf16[36,16,4096]{2,1,0:T(8,128)(2,1)} %bitcast.41, f32[6,4096]{1,0:T(8,128)} %occ_ref.1), custom_call_target="tpu_custom_call" | custom-call | tf_op jit(solution)/shard_map/pallas_call | solution.py:51
  75.7 4.0 %all-to-all-start = ((f32[4,6,1024]{2,1,0:T(8,128)}), f32[4,6,1024]{2,1,0:T(8,128)S(1)}, u32[]{:S(2)}, u32[]{:S(2)}) async-start(f32[4,6,1024]{2,1,0:T(8,128)} %bitcast.45), calls=%async_computation | async-start | bytes 262144 | tf_op jit(solution)/shard_map/all_to_all | solution.py:151
  79.7 4.8 %all-to-all-done = f32[4,6,1024]{2,1,0:T(8,128)S(1)} async-done(((f32[4,6,1024]{2,1,0:T(8,128)}), f32[4,6,1024]{2,1,0:T(8,128)S(1)}, u32[]{:S(2)}, u32[]{:S(2)}) %all-to-all-start) | async-done | bytes 98336 | tf_op jit(solution)/shard_map/all_to_all | solution.py:151
  84.6 0.0 copy-start.1
  84.6 1.4 %multiply_add_fusion = f32[6,1024]{1,0:T(8,128)} fusion(f32[6,1024]{1,0:T(8,128)S(1)} %reduce_sum.9, f32[6,4096]{1,0:T(8,128)} %occ_ref.1, s32[]{:T(128)S(6)} %select_n.57), kind=kLoop, calls=%fused_computation.10 | loop fusion | flops 12288 | bytes 73732 | tf_op jit(solution)/shard_map/add | solution.py:155
  86.0 0.0 copy-done.1
  (11 shorter events, 0.3 us)
Async XLA Ops:
  1.6 5.6 %collective-permute-start = (f32[32,768]{1,0:T(8,128)S(1)}, f32[32,768]{1,0:T(8,128)S(1)}, u32[]{:S(2)}, u32[]{:S(2)}) collective-permute-start(f32[32,768]{1,0:T(8,128)S(1)} %bitcast.52), channel_id=1, source_target_pairs={{0,24},{4,28},{8,0},{12,4},{16,8},{20,12},{24,16},{28,20},{32,56},... | collective-permute-start | bytes 294920 | tf_op jit(solution)/shard_map/ppermute | solution.py:99
  5.2 5.1 %collective-permute-start.1 = (f32[32,768]{1,0:T(8,128)S(1)}, f32[32,768]{1,0:T(8,128)S(1)}, u32[]{:S(2)}, u32[]{:S(2)}) collective-permute-start(f32[32,768]{1,0:T(8,128)S(1)} %bitcast.53), channel_id=1, source_target_pairs={{0,16},{4,20},{8,24},{12,28},{16,0},{20,4},{24,8},{28,12},{32,48},... | collective-permute-start | bytes 294920 | tf_op jit(solution)/shard_map/ppermute | solution.py:99
  5.5 7.5 %collective-permute-start.2 = (f32[32,768]{1,0:T(8,128)S(1)}, f32[32,768]{1,0:T(8,128)S(1)}, u32[]{:S(2)}, u32[]{:S(2)}) collective-permute-start(f32[32,768]{1,0:T(8,128)S(1)} %bitcast.54), channel_id=1, source_target_pairs={{0,8},{4,12},{8,16},{12,20},{16,24},{20,28},{24,0},{28,4},{32,40},... | collective-permute-start | bytes 294920 | tf_op jit(solution)/shard_map/ppermute | solution.py:99
  13.0 45.4 %copy-start.3 = (s32[1,1,16,32,1]{3,4,2,1,0:T(1,128)S(1)}, s32[1,1,16,32,1]{3,4,2,1,0:T(1,128)}, u32[]{:S(2)}) copy-start(s32[1,1,16,32,1]{3,4,2,1,0:T(1,128)} %param.10) | copy-start | bytes 6148
  13.0 46.2 %copy-start.2 = (s32[1,1,16,32]{3,2,1,0:T(8,128)S(1)}, s32[1,1,16,32]{3,2,1,0:T(8,128)}, u32[]{:S(2)}) copy-start(s32[1,1,16,32]{3,2,1,0:T(8,128)} %param.11) | copy-start | bytes 6148
  13.1 13.0 %collective-permute-start.3 = (f32[4,32,768]{2,1,0:T(8,128)S(1)}, f32[4,32,768]{2,1,0:T(8,128)S(1)}, u32[]{:S(2)}, u32[]{:S(2)}) collective-permute-start(f32[4,32,768]{2,1,0:T(8,128)S(1)} %pad_maximum_fusion), channel_id=1, source_target_pairs={{0,224},{4,228},{8,232},{12,236},{16,240},{20,244},{24,248},{28,25... | collective-permute-start | bytes 1179656 | tf_op jit(solution)/shard_map/ppermute | solution.py:91
  18.7 10.8 %collective-permute-start.7 = (f32[4,32,768]{2,1,0:T(8,128)S(1)}, f32[4,32,768]{2,1,0:T(8,128)S(1)}, u32[]{:S(2)}, u32[]{:S(2)}) collective-permute-start(f32[4,32,768]{2,1,0:T(8,128)S(1)} %pad_maximum_fusion), channel_id=1, source_target_pairs={{0,32},{4,36},{8,40},{12,44},{16,48},{20,52},{24,56},{28,60},{32,6... | collective-permute-start | bytes 1179656 | tf_op jit(solution)/shard_map/ppermute | solution.py:94
  26.1 9.9 %collective-permute-start.4 = (f32[4,32,768]{2,1,0:T(8,128)S(1)}, f32[4,32,768]{2,1,0:T(8,128)S(1)}, u32[]{:S(2)}, u32[]{:S(2)}) collective-permute-start(f32[4,32,768]{2,1,0:T(8,128)S(1)} %collective-permute-done.3), channel_id=1, source_target_pairs={{0,224},{4,228},{8,232},{12,236},{16,240},{20,244},{24,248},{28,25... | collective-permute-start | bytes 1179656 | tf_op jit(solution)/shard_map/ppermute | solution.py:91
  29.5 9.9 %collective-permute-start.8 = (f32[4,32,768]{2,1,0:T(8,128)S(1)}, f32[4,32,768]{2,1,0:T(8,128)S(1)}, u32[]{:S(2)}, u32[]{:S(2)}) collective-permute-start(f32[4,32,768]{2,1,0:T(8,128)S(1)} %collective-permute-done.7), channel_id=1, source_target_pairs={{0,32},{4,36},{8,40},{12,44},{16,48},{20,52},{24,56},{28,60},{32,6... | collective-permute-start | bytes 1179656 | tf_op jit(solution)/shard_map/ppermute | solution.py:94
  36.0 9.0 %collective-permute-start.5 = (f32[4,32,768]{2,1,0:T(8,128)S(1)}, f32[4,32,768]{2,1,0:T(8,128)S(1)}, u32[]{:S(2)}, u32[]{:S(2)}) collective-permute-start(f32[4,32,768]{2,1,0:T(8,128)S(1)} %collective-permute-done.4), channel_id=1, source_target_pairs={{0,224},{4,228},{8,232},{12,236},{16,240},{20,244},{24,248},{28,25... | collective-permute-start | bytes 1179656 | tf_op jit(solution)/shard_map/ppermute | solution.py:91
  39.5 13.6 %collective-permute-start.9 = (f32[4,32,768]{2,1,0:T(8,128)S(1)}, f32[4,32,768]{2,1,0:T(8,128)S(1)}, u32[]{:S(2)}, u32[]{:S(2)}) collective-permute-start(f32[4,32,768]{2,1,0:T(8,128)S(1)} %collective-permute-done.8), channel_id=1, source_target_pairs={{0,32},{4,36},{8,40},{12,44},{16,48},{20,52},{24,56},{28,60},{32,6... | collective-permute-start | bytes 1179656 | tf_op jit(solution)/shard_map/ppermute | solution.py:94
  44.9 8.1 %collective-permute-start.6 = (f32[4,32,768]{2,1,0:T(8,128)S(1)}, f32[4,32,768]{2,1,0:T(8,128)S(1)}, u32[]{:S(2)}, u32[]{:S(2)}) collective-permute-start(f32[4,32,768]{2,1,0:T(8,128)S(1)} %collective-permute-done.5), channel_id=1, source_target_pairs={{0,224},{4,228},{8,232},{12,236},{16,240},{20,244},{24,248},{28,25... | collective-permute-start | bytes 1179656 | tf_op jit(solution)/shard_map/ppermute | solution.py:91
  53.2 11.0 %copy-start = (f32[8,4,32,768]{3,2,1,0:T(8,128)}, f32[8,4,32,768]{3,2,1,0:T(8,128)S(1)}, u32[]{:S(2)}) copy-start(f32[8,4,32,768]{3,2,1,0:T(8,128)S(1)} %bitcast_dynamic-update-slice_fusion) | copy-start | bytes 9437188
  53.2 10.1 %collective-permute-start.10 = (f32[8,4,32,768]{3,2,1,0:T(8,128)S(1)}, f32[8,4,32,768]{3,2,1,0:T(8,128)}, u32[]{:S(2)}, u32[]{:S(2)}) collective-permute-start(f32[8,4,32,768]{3,2,1,0:T(8,128)S(1)} %bitcast_dynamic-update-slice_fusion), channel_id=1, source_target_pairs={{0,4},{4,0},{8,12},{12,8},{16,20},{20,16},{24,28},{28,24},{32,36},... | collective-permute-start | bytes 9437192 | tf_op jit(solution)/shard_map/ppermute | solution.py:103
  75.7 8.8 %all-to-all-start = ((f32[4,6,1024]{2,1,0:T(8,128)}), f32[4,6,1024]{2,1,0:T(8,128)S(1)}, u32[]{:S(2)}, u32[]{:S(2)}) async-start(f32[4,6,1024]{2,1,0:T(8,128)} %bitcast.45), calls=%async_computation | async-start | bytes 262144 | tf_op jit(solution)/shard_map/all_to_all | solution.py:151
  84.6 1.4 %copy-start.1 = (f32[6,1024]{1,0:T(8,128)}, f32[6,1024]{1,0:T(8,128)S(1)}, u32[]{:S(2)}) copy-start(f32[6,1024]{1,0:T(8,128)S(1)} %reduce_sum.9) | copy-start | bytes 73732

commit v12 on v9

--- a/solution.py
+++ b/solution.py
@@ -10,16 +10,19 @@
 half_step = 0.5
 
 
-def collide_kernel(idx_ref, near_ref, far_ref, w_ref, gain_ref, loss_ref, occ_ref, out_ref, sh_ref, rest_ref,
+def collide_kernel(idx_ref, near_ref, far_ref, last_ref, w_ref, gain_ref, loss_ref, occ_ref, out_ref, sh_ref, rest_ref,
                    *, shifts, nsub, sub_count, sub_width, bands):
     t = pl.program_id(0)
     half = near_ref.shape[0]
+    early = far_ref.shape[0]
+    late = last_ref.shape[0]
     for s in range(shifts):
         for jj in range(nsub):
             at = idx_ref[s * sub_count + t * nsub + jj]
             near = near_ref[pl.ds(jnp.minimum(at, half - 1), 1), :]
-            far = far_ref[pl.ds(jnp.maximum(at - half, 0), 1), :]
-            row = jnp.where(at < half, near, far)
+            far = far_ref[pl.ds(jnp.clip(at - half, 0, early - 1), 1), :]
+            last = last_ref[pl.ds(jnp.clip(at - half - early, 0, late - 1), 1), :]
+            row = jnp.where(at < half, near, jnp.where(at < half + early, far, last))
             for n in range(bands):
                 piece = row[:, n * sub_width:(n + 1) * sub_width]
                 sh_ref[n, pl.ds(s, 1), pl.ds(jj * sub_width, sub_width)] = piece
@@ -41,7 +44,7 @@
         out_ref[pl.ds(m, 1), :] = (1.0 - occ[m:m + 1]) * inflow - occ[m:m + 1] * outflow
 
 
-def collide(idx, near, far, weight_t, gain_t, loss_t, occ, sub_width, lanes=1024):
+def collide(idx, near, far, last, weight_t, gain_t, loss_t, occ, sub_width, lanes=1024):
     pairs, shifts, width = gain_t.shape
     bands = occ.shape[0]
     sub_count = width // sub_width
@@ -57,6 +60,7 @@
             in_specs=[
                 pl.BlockSpec(near.shape, lambda t, i: (0, 0)),
                 pl.BlockSpec(far.shape, lambda t, i: (0, 0)),
+                pl.BlockSpec(last.shape, lambda t, i: (0, 0)),
                 pl.BlockSpec(weight_t.shape, lambda t, i: (0, 0, 0)),
                 pl.BlockSpec((pairs, shifts, lanes), lambda t, i: (0, 0, t)),
                 pl.BlockSpec((pairs, shifts, lanes), lambda t, i: (0, 0, t)),
@@ -68,7 +72,7 @@
                 pltpu.VMEM((bands, shifts, lanes), jnp.float32),
             ],
         ),
-    )(idx, near, far, weight_t, gain_t, loss_t, occ)
+    )(idx, near, far, last, weight_t, gain_t, loss_t, occ)
 
 
 def ring_gather(block, y_count, z_count):
@@ -96,9 +100,20 @@
         return jnp.stack([ahead[d] for d in range(count)])
 
     along_y = ring(block, y_step, y_count)
-    along_z = ring(along_y, z_step, z_count)
-    other = lax.ppermute(along_z, "ka", pairs(lambda j: j ^ 1))
-    return along_z, other
+    swap = pairs(lambda j: j ^ 1)
+    ahead = {0: along_y}
+    fwd, back = along_y, along_y
+    for d in range(1, z_count // 2):
+        back = lax.ppermute(back, "ka", z_step(-1))
+        fwd = lax.ppermute(fwd, "ka", z_step(1))
+        ahead[d] = back
+        ahead[z_count - d] = fwd
+    order = [d for d in range(z_count) if d != z_count // 2]
+    early = jnp.stack([ahead[d] for d in order])
+    early_other = lax.ppermute(early, "ka", swap)
+    last = lax.ppermute(back, "ka", z_step(-1))
+    last_other = lax.ppermute(last, "ka", swap)
+    return jnp.concatenate([early, last[None]]), early_other, last_other
 
 
 def body(occupation, gain_table, loss_table, owner, local_index, pair_mask, counts):
@@ -117,16 +132,20 @@
         .transpose(1, 0, 2)
         .reshape(sub_count, bands * sub_width)
     )
-    near, far = ring_gather(local_rows, y_count, z_count)
-    near = near.reshape(ka_count * sub_count // 2, bands * sub_width)
-    far = far.reshape(ka_count * sub_count // 2, bands * sub_width)
+    near, far, last = ring_gather(local_rows, y_count, z_count)
+    near = near.reshape(-1, bands * sub_width)
+    far = far.reshape(-1, bands * sub_width)
+    last = last.reshape(-1, bands * sub_width)
     me = lax.axis_index("ka")
     my_z, my_y, my_c = me // (2 * y_count), (me // 2) % y_count, me % 2
     owners = owner.reshape(total_requests)
     o_z, o_y, o_c = owners // (2 * y_count), (owners // 2) % y_count, owners % 2
+    dz = (o_z - my_z) % z_count
+    far_z = z_count // 2
+    z_slot = jnp.where(dz < far_z, dz, jnp.where(dz > far_z, dz - 1, z_count - 1))
     where = (
         (o_c ^ my_c) * (z_count * y_count)
-        + ((o_z - my_z) % z_count) * y_count
+        + z_slot * y_count
         + (o_y - my_y) % y_count
     )
     sources = local_index.reshape(total_requests)
@@ -137,6 +156,7 @@
         picks,
         near,
         far,
+        last,
         jnp.broadcast_to(weight.T[:, :, None], (bands * bands, shifts, sub_width)),
         gain_table.transpose(1, 0, 2),
         loss_table.transpose(1, 0, 2),

time: 85.3 us -> 93 us (1.090)
  local copies, waits for them, and re-layouts: 3.82 us -> 12.4 us
  starting transfers between devices: 24.7 us -> 22 us
  waiting for transfers between devices: 39.7 us -> 37.3 us
  other arithmetic: 3.55 us -> 5.69 us
  Pallas kernels: 11.5 us -> 13.6 us
    ppermute x6 -> x2, waiting for transfers between devices: 31.6 us -> 7.47 us  [ring(): back = lax.ppermute(back, 'ka', step(-1))]
    ppermute x1 -> x9, waiting for transfers between devices: 2.07 us -> 23.9 us  [the longest x3 14.8 us: ring_gather(): back = lax.ppermute(back, 'ka', z_step(-1))]
    ppermute x6 -> x2, starting transfers between devices: 17.8 us -> 0.82 us  [ring(): back = lax.ppermute(back, 'ka', step(-1))]
    ppermute x1 -> x9, starting transfers between devices: 0.09 us -> 14.4 us  [the longest x3 13.3 us: ring_gather(): back = lax.ppermute(back, 'ka', z_step(-1))]
    unnamed x16 -> x15, local copies, waits for them, and re-layouts: 1.77 us -> 7.66 us
    pallas_call x1, Pallas kernels: 11.5 us -> 13.6 us  [collide(): pl.pallas_call(kern, out_shape=jax.ShapeDtypeStruct((bands, width), jnp.f...]
    unnamed x2, other arithmetic: 0.74 us -> 2.19 us
    ppermute x4 -> x1, starting transfers between devices: 2.52 us -> 2.49 us  [ring(): fwd = lax.ppermute(fwd, 'ka', step(1))]
  transfers between devices with their start and end apart: 12 -> 13, of which waited for: 9 -> 9; matrix products, arithmetic and copies ran while one was open for 5% -> 11% of each run, Pallas kernels for 0% -> 0%
where the time goes in v12:
time: 93 us; the launch traced here: 92.4 us
  waiting for transfers between devices  37.3 us (40%)
  starting transfers between devices  22 us (24%)
  Pallas kernels  13.6 us (15%)
  local copies, waits for them, and re-layouts  12.4 us (13%)
  other arithmetic  5.69 us (6%)
  between operations  1.36 us (1%)
    ppermute x3, waiting for transfers between devices, ring_gather(): back = lax.ppermute(back, 'ka', z_step(-1))  14.8 us
    pallas_call x1, Pallas kernels, collide(): pl.pallas_call(kern, out_shape=jax.ShapeDtypeStruct((bands, width), jnp.f...  13.6 us
    ppermute x3, starting transfers between devices, ring_gather(): back = lax.ppermute(back, 'ka', z_step(-1))  13.3 us
    unnamed x15, local copies, waits for them, and re-layouts  7.66 us
    ppermute x2, waiting for transfers between devices, ring(): back = lax.ppermute(back, 'ka', step(-1))  7.47 us
    all_to_all x1, waiting for transfers between devices, body(): collision = jnp.sum(lax.all_to_all(parts, 'pb', 0, 0, tiled=True), axis=0)  5.98 us
    ppermute x1, waiting for transfers between devices, ring_gather(): last = lax.ppermute(back, 'ka', z_step(-1))  5.92 us
    all_to_all x1, starting transfers between devices, body(): collision = jnp.sum(lax.all_to_all(parts, 'pb', 0, 0, tiled=True), axis=0)  4.29 us
  transfers between devices with their start and end apart: 13, of which 9 were waited for; matrix products, arithmetic and copies ran while one was open for 11% of the time, Pallas kernels for 0%

profile of v12, /device:TPU:24, one launch (start us, length us, event | category | flops | bytes accessed | tf_op | source)
XLA Modules:
  0.0 92.4 jit_solution(16636514876657852913)
XLA Ops:
  0.6 0.9 %copy.19 = f32[4,8,6,128]{3,1,2,0:T(8,128)S(1)} copy(f32[4,8,6,128]{3,2,1,0:T(8,128)} %bitcast.51) | data formatting | bytes 196608
  1.6 0.8 collective-permute-start
  2.4 2.5 %collective-permute-start.2 = (f32[32,768]{1,0:T(8,128)S(1)}, f32[32,768]{1,0:T(8,128)S(1)}, u32[]{:S(2)}, u32[]{:S(2)}) collective-permute-start(f32[32,768]{1,0:T(8,128)S(1)} %bitcast.62), channel_id=1, source_target_pairs={{0,8},{4,12},{8,16},{12,20},{16,24},{20,28},{24,0},{28,4},{32,40},... | collective-permute-start | bytes 294920 | tf_op jit(solution)/shard_map/ppermute | solution.py:98
  4.9 2.6 %collective-permute-done = f32[32,768]{1,0:T(8,128)S(1)} collective-permute-done((f32[32,768]{1,0:T(8,128)S(1)}, f32[32,768]{1,0:T(8,128)S(1)}, u32[]{:S(2)}, u32[]{:S(2)}) %collective-permute-start) | collective-permute-done | bytes 98336 | tf_op jit(solution)/shard_map/ppermute | solution.py:95
  7.5 0.0 collective-permute-start.1
  7.5 0.9 %stack_reshape.3 = f32[1,32,768]{2,1,0:T(8,128)S(1)} reshape(f32[32,6,128]{2,1,0:T(8,128)} %bitcast.52) | data formatting | bytes 196608 | tf_op jit(solution)/shard_map/stack;reshape | solution.py:100
  8.4 0.0 collective-permute-done.2
  8.4 4.9 %collective-permute-done.1 = f32[32,768]{1,0:T(8,128)S(1)} collective-permute-done((f32[32,768]{1,0:T(8,128)S(1)}, f32[32,768]{1,0:T(8,128)S(1)}, u32[]{:S(2)}, u32[]{:S(2)}) %collective-permute-start.1) | collective-permute-done | bytes 98336 | tf_op jit(solution)/shard_map/ppermute | solution.py:95
  13.3 5.9 %collective-permute-start.3 = (f32[4,32,768]{2,1,0:T(8,128)S(1)}, f32[4,32,768]{2,1,0:T(8,128)S(1)}, u32[]{:S(2)}, u32[]{:S(2)}) collective-permute-start(f32[4,32,768]{2,1,0:T(8,128)S(1)} %pad_maximum_fusion), channel_id=1, source_target_pairs={{0,224},{4,228},{8,232},{12,236},{16,240},{20,244},{24,248},{28,25... | collective-permute-start | bytes 1179656 | tf_op jit(solution)/shard_map/ppermute | solution.py:107
  19.3 0.0 collective-permute-start.6
  19.3 6.1 %collective-permute-done.3 = f32[4,32,768]{2,1,0:T(8,128)S(1)} collective-permute-done((f32[4,32,768]{2,1,0:T(8,128)S(1)}, f32[4,32,768]{2,1,0:T(8,128)S(1)}, u32[]{:S(2)}, u32[]{:S(2)}) %collective-permute-start.3) | collective-permute-done | bytes 393248 | tf_op jit(solution)/shard_map/ppermute | solution.py:107
  25.3 3.7 %collective-permute-start.4 = (f32[4,32,768]{2,1,0:T(8,128)S(1)}, f32[4,32,768]{2,1,0:T(8,128)S(1)}, u32[]{:S(2)}, u32[]{:S(2)}) collective-permute-start(f32[4,32,768]{2,1,0:T(8,128)S(1)} %collective-permute-done.3), channel_id=1, source_target_pairs={{0,224},{4,228},{8,232},{12,236},{16,240},{20,244},{24,248},{28,25... | collective-permute-start | bytes 1179656 | tf_op jit(solution)/shard_map/ppermute | solution.py:107
  29.0 0.0 collective-permute-done.6
  29.0 0.0 collective-permute-start.7
  29.0 0.8 bitcast_dynamic-update-slice_fusion.13
  29.9 5.1 %collective-permute-done.4 = f32[4,32,768]{2,1,0:T(8,128)S(1)} collective-permute-done((f32[4,32,768]{2,1,0:T(8,128)S(1)}, f32[4,32,768]{2,1,0:T(8,128)S(1)}, u32[]{:S(2)}, u32[]{:S(2)}) %collective-permute-start.4) | collective-permute-done | bytes 393248 | tf_op jit(solution)/shard_map/ppermute | solution.py:107
  35.0 3.7 %collective-permute-start.5 = (f32[4,32,768]{2,1,0:T(8,128)S(1)}, f32[4,32,768]{2,1,0:T(8,128)}, u32[]{:S(2)}, u32[]{:S(2)}) collective-permute-start(f32[4,32,768]{2,1,0:T(8,128)S(1)} %collective-permute-done.4), channel_id=1, source_target_pairs={{0,224},{4,228},{8,232},{12,236},{16,240},{20,244},{24,248},{28,25... | collective-permute-start | bytes 1179656 | tf_op jit(solution)/shard_map/ppermute | solution.py:107
  38.7 0.8 bitcast_dynamic-update-slice_fusion.11
  39.5 0.0 copy-start.3
  39.5 0.0 collective-permute-done.7
  39.5 0.0 collective-permute-start.8
  39.5 0.8 bitcast_dynamic-update-slice_fusion.9
  40.3 3.6 %collective-permute-done.5 = f32[4,32,768]{2,1,0:T(8,128)} collective-permute-done((f32[4,32,768]{2,1,0:T(8,128)S(1)}, f32[4,32,768]{2,1,0:T(8,128)}, u32[]{:S(2)}, u32[]{:S(2)}) %collective-permute-start.5) | collective-permute-done | bytes 393248 | tf_op jit(solution)/shard_map/ppermute | solution.py:107
  44.0 1.8 %bitcast_dynamic-update-slice_fusion.7 = (f32[7,4,32,768]{3,2,1,0:T(8,128)}, f32[8,4,32,768]{3,2,1,0:T(8,128)S(1)}) fusion(f32[7,4,32,768]{3,2,1,0:T(8,128)} %get-tuple-element.10, f32[4,32,768]{2,1,0:T(8,128)} %collective-permute-done.5, f32[8,4,32,768]{3,2,1,0:T(8,128)S(1)} %get-tuple-element.11), kind=kLoop, calls=%fused_computation.8 | loop fusion | bytes 1179648
  45.7 2.7 %collective-permute-done.8 = f32[4,32,768]{2,1,0:T(8,128)S(1)} collective-permute-done((f32[4,32,768]{2,1,0:T(8,128)S(1)}, f32[4,32,768]{2,1,0:T(8,128)S(1)}, u32[]{:S(2)}, u32[]{:S(2)}) %collective-permute-start.8) | collective-permute-done | bytes 393248 | tf_op jit(solution)/shard_map/ppermute | solution.py:108
  48.5 0.8 bitcast_dynamic-update-slice_fusion.5
  49.3 0.9 bitcast_dynamic-update-slice_fusion.3
  50.2 0.8 bitcast_dynamic-update-slice_fusion.1
  51.0 0.0 collective-permute-start.10
  51.0 1.1 %collective-permute-start.9 = (f32[4,32,768]{2,1,0:T(8,128)}, f32[4,32,768]{2,1,0:T(8,128)S(1)}, u32[]{:S(2)}, u32[]{:S(2)}) collective-permute-start(f32[4,32,768]{2,1,0:T(8,128)} %collective-permute-done.5), channel_id=1, source_target_pairs={{0,224},{4,228},{8,232},{12,236},{16,240},{20,244},{24,248},{28,25... | collective-permute-start | bytes 1179656 | tf_op jit(solution)/shard_map/ppermute | solution.py:114
  52.0 0.5 broadcast.54
  52.6 1.4 %reduce.3 = s32[16,32]{1,0:T(8,128)S(1)} reduce(s32[1,1,16,32,1]{3,4,2,1,0:T(1,128)} %param.10, s32[]{:T(128)} %broadcast.54), dimensions={0,1,4}, to_apply=%param.10.reduce_sub_computation.3 | reduce | bytes 4100 | tf_op args[3]
  53.9 0.7 reshape.37
  54.6 0.0 copy-done.3
  54.6 0.1 reshape.38
  55.3 0.8 multiply_bitcast_fusion
  56.1 0.7 copy.15
  56.8 5.9 %collective-permute-done.9 = f32[4,32,768]{2,1,0:T(8,128)S(1)} collective-permute-done((f32[4,32,768]{2,1,0:T(8,128)}, f32[4,32,768]{2,1,0:T(8,128)S(1)}, u32[]{:S(2)}, u32[]{:S(2)}) %collective-permute-start.9) | collective-permute-done | bytes 393248 | tf_op jit(solution)/shard_map/ppermute | solution.py:114
  62.7 0.0 collective-permute-start.11
  62.7 1.3 %fusion.5.idx_ref = s32[512]{0:T(512)} fusion(s32[512]{0:T(512)S(1)} %reshape.38, s32[512]{0:T(512)} %reshape.37, s32[]{:T(128)S(6)} %select_n.64, s32[]{:T(128)S(6)} %select_n.57, s32[]{:T(128)S(6)} %select_n.55), kind=kLoop, calls=%fused_computation.42 | loop fusion | flops 38912 | bytes 6156 | tf_op jit(solution)/shard_map/add | solution.py:152
  64.0 0.0 copy-start
  64.0 0.4 collective-permute-done.11
  64.4 0.0 copy-start.1
  64.4 1.1 %copy-done.1 = f32[4,32,768]{2,1,0:T(8,128)} copy-done((f32[4,32,768]{2,1,0:T(8,128)}, f32[4,32,768]{2,1,0:T(8,128)S(1)}, u32[]{:S(2)}) %copy-start.1) | copy-done | bytes 393240
  65.5 0.0 collective-permute-done.10
  65.5 1.6 %broadcast_in_dim.7.w_ref = f32[36,16,128]{2,1,0:T(8,128)} broadcast(f32[36,16]{1,0:T(8,128)} %copy.15), dimensions={0,1} | broadcast | bytes 297216 | tf_op jit(solution)/shard_map/broadcast_in_dim | solution.py:160
  67.1 0.0 copy-done
  67.1 13.6 %shard_map.86 = f32[6,4096]{1,0:T(8,128)} custom-call(s32[512]{0:T(512)} %fusion.5.idx_ref, f32[1024,768]{1,0:T(8,128)} %bitcast.50, f32[896,768]{1,0:T(8,128)} %bitcast.15.far_ref, f32[128,768]{1,0:T(8,128)} %bitcast.60, f32[36,16,128]{2,1,0:T(8,128)} %broadcast_in_dim.7.w_ref, bf16[36,16,4096]{2,1,0:T(8,128)(2,1)} %bitcast.48, ...), custom_call_target="tpu_custom_call" | custom-call | tf_op jit(solution)/shard_map/pallas_call | solution.py:54
  80.7 4.3 %all-to-all-start = ((f32[4,6,1024]{2,1,0:T(8,128)}), f32[4,6,1024]{2,1,0:T(8,128)S(1)}, u32[]{:S(2)}, u32[]{:S(2)}) async-start(f32[4,6,1024]{2,1,0:T(8,128)} %bitcast.53), calls=%async_computation | async-start | bytes 262144 | tf_op jit(solution)/shard_map/all_to_all | solution.py:168
  85.0 6.0 %all-to-all-done = f32[4,6,1024]{2,1,0:T(8,128)S(1)} async-done(((f32[4,6,1024]{2,1,0:T(8,128)}), f32[4,6,1024]{2,1,0:T(8,128)S(1)}, u32[]{:S(2)}, u32[]{:S(2)}) %all-to-all-start) | async-done | bytes 98336 | tf_op jit(solution)/shard_map/all_to_all | solution.py:168
  91.0 0.0 copy-start.2
  91.0 1.4 %multiply_add_fusion = f32[6,1024]{1,0:T(8,128)} fusion(f32[6,1024]{1,0:T(8,128)S(1)} %reduce_sum.9, f32[6,4096]{1,0:T(8,128)} %occ_ref.1, s32[]{:T(128)S(6)} %select_n.66), kind=kLoop, calls=%fused_computation.17 | loop fusion | flops 12288 | bytes 73732 | tf_op jit(solution)/shard_map/add | solution.py:172
  92.4 0.0 copy-done.2
  (4 shorter events, 0.1 us)
Async XLA Ops:
  1.6 5.9 %collective-permute-start = (f32[32,768]{1,0:T(8,128)S(1)}, f32[32,768]{1,0:T(8,128)S(1)}, u32[]{:S(2)}, u32[]{:S(2)}) collective-permute-start(f32[32,768]{1,0:T(8,128)S(1)} %bitcast.61), channel_id=1, source_target_pairs={{0,24},{4,28},{8,0},{12,4},{16,8},{20,12},{24,16},{28,20},{32,56},... | collective-permute-start | bytes 294920 | tf_op jit(solution)/shard_map/ppermute | solution.py:95
  2.4 6.0 %collective-permute-start.2 = (f32[32,768]{1,0:T(8,128)S(1)}, f32[32,768]{1,0:T(8,128)S(1)}, u32[]{:S(2)}, u32[]{:S(2)}) collective-permute-start(f32[32,768]{1,0:T(8,128)S(1)} %bitcast.62), channel_id=1, source_target_pairs={{0,8},{4,12},{8,16},{12,20},{16,24},{20,28},{24,0},{28,4},{32,40},... | collective-permute-start | bytes 294920 | tf_op jit(solution)/shard_map/ppermute | solution.py:98
  7.5 5.8 %collective-permute-start.1 = (f32[32,768]{1,0:T(8,128)S(1)}, f32[32,768]{1,0:T(8,128)S(1)}, u32[]{:S(2)}, u32[]{:S(2)}) collective-permute-start(f32[32,768]{1,0:T(8,128)S(1)} %collective-permute-done), channel_id=1, source_target_pairs={{0,24},{4,28},{8,0},{12,4},{16,8},{20,12},{24,16},{28,20},{32,56},... | collective-permute-start | bytes 294920 | tf_op jit(solution)/shard_map/ppermute | solution.py:95
  13.3 12.0 %collective-permute-start.3 = (f32[4,32,768]{2,1,0:T(8,128)S(1)}, f32[4,32,768]{2,1,0:T(8,128)S(1)}, u32[]{:S(2)}, u32[]{:S(2)}) collective-permute-start(f32[4,32,768]{2,1,0:T(8,128)S(1)} %pad_maximum_fusion), channel_id=1, source_target_pairs={{0,224},{4,228},{8,232},{12,236},{16,240},{20,244},{24,248},{28,25... | collective-permute-start | bytes 1179656 | tf_op jit(solution)/shard_map/ppermute | solution.py:107
  19.3 9.8 %collective-permute-start.6 = (f32[4,32,768]{2,1,0:T(8,128)S(1)}, f32[4,32,768]{2,1,0:T(8,128)S(1)}, u32[]{:S(2)}, u32[]{:S(2)}) collective-permute-start(f32[4,32,768]{2,1,0:T(8,128)S(1)} %pad_maximum_fusion), channel_id=1, source_target_pairs={{0,32},{4,36},{8,40},{12,44},{16,48},{20,52},{24,56},{28,60},{32,6... | collective-permute-start | bytes 1179656 | tf_op jit(solution)/shard_map/ppermute | solution.py:108
  25.3 9.6 %collective-permute-start.4 = (f32[4,32,768]{2,1,0:T(8,128)S(1)}, f32[4,32,768]{2,1,0:T(8,128)S(1)}, u32[]{:S(2)}, u32[]{:S(2)}) collective-permute-start(f32[4,32,768]{2,1,0:T(8,128)S(1)} %collective-permute-done.3), channel_id=1, source_target_pairs={{0,224},{4,228},{8,232},{12,236},{16,240},{20,244},{24,248},{28,25... | collective-permute-start | bytes 1179656 | tf_op jit(solution)/shard_map/ppermute | solution.py:107
  29.0 10.5 %collective-permute-start.7 = (f32[4,32,768]{2,1,0:T(8,128)S(1)}, f32[4,32,768]{2,1,0:T(8,128)S(1)}, u32[]{:S(2)}, u32[]{:S(2)}) collective-permute-start(f32[4,32,768]{2,1,0:T(8,128)S(1)} %collective-permute-done.6), channel_id=1, source_target_pairs={{0,32},{4,36},{8,40},{12,44},{16,48},{20,52},{24,56},{28,60},{32,6... | collective-permute-start | bytes 1179656 | tf_op jit(solution)/shard_map/ppermute | solution.py:108
  35.0 9.0 %collective-permute-start.5 = (f32[4,32,768]{2,1,0:T(8,128)S(1)}, f32[4,32,768]{2,1,0:T(8,128)}, u32[]{:S(2)}, u32[]{:S(2)}) collective-permute-start(f32[4,32,768]{2,1,0:T(8,128)S(1)} %collective-permute-done.4), channel_id=1, source_target_pairs={{0,224},{4,228},{8,232},{12,236},{16,240},{20,244},{24,248},{28,25... | collective-permute-start | bytes 1179656 | tf_op jit(solution)/shard_map/ppermute | solution.py:107
  39.5 15.1 %copy-start.3 = (s32[1,1,16,32]{3,2,1,0:T(8,128)S(1)}, s32[1,1,16,32]{3,2,1,0:T(8,128)}, u32[]{:S(2)}) copy-start(s32[1,1,16,32]{3,2,1,0:T(8,128)} %param.11) | copy-start | bytes 6148
  39.5 9.0 %collective-permute-start.8 = (f32[4,32,768]{2,1,0:T(8,128)S(1)}, f32[4,32,768]{2,1,0:T(8,128)S(1)}, u32[]{:S(2)}, u32[]{:S(2)}) collective-permute-start(f32[4,32,768]{2,1,0:T(8,128)S(1)} %collective-permute-done.7), channel_id=1, source_target_pairs={{0,32},{4,36},{8,40},{12,44},{16,48},{20,52},{24,56},{28,60},{32,6... | collective-permute-start | bytes 1179656 | tf_op jit(solution)/shard_map/ppermute | solution.py:108
  51.0 14.6 %collective-permute-start.10 = (f32[7,4,32,768]{3,2,1,0:T(8,128)}, f32[7,4,32,768]{3,2,1,0:T(8,128)}, u32[]{:S(2)}, u32[]{:S(2)}) collective-permute-start(f32[7,4,32,768]{3,2,1,0:T(8,128)} %get-tuple-element.2), channel_id=1, source_target_pairs={{0,4},{4,0},{8,12},{12,8},{16,20},{20,16},{24,28},{28,24},{32,36},... | collective-permute-start | bytes 8257544 | tf_op jit(solution)/shard_map/ppermute | solution.py:113
  51.0 11.7 %collective-permute-start.9 = (f32[4,32,768]{2,1,0:T(8,128)}, f32[4,32,768]{2,1,0:T(8,128)S(1)}, u32[]{:S(2)}, u32[]{:S(2)}) collective-permute-start(f32[4,32,768]{2,1,0:T(8,128)} %collective-permute-done.5), channel_id=1, source_target_pairs={{0,224},{4,228},{8,232},{12,236},{16,240},{20,244},{24,248},{28,25... | collective-permute-start | bytes 1179656 | tf_op jit(solution)/shard_map/ppermute | solution.py:114
  62.7 1.7 %collective-permute-start.11 = (f32[4,32,768]{2,1,0:T(8,128)S(1)}, f32[4,32,768]{2,1,0:T(8,128)S(1)}, u32[]{:S(2)}, u32[]{:S(2)}) collective-permute-start(f32[4,32,768]{2,1,0:T(8,128)S(1)} %collective-permute-done.9), channel_id=1, source_target_pairs={{0,4},{4,0},{8,12},{12,8},{16,20},{20,16},{24,28},{28,24},{32,36},... | collective-permute-start | bytes 1179656 | tf_op jit(solution)/shard_map/ppermute | solution.py:115
  64.0 3.1 %copy-start = (f32[8,4,32,768]{3,2,1,0:T(8,128)}, f32[8,4,32,768]{3,2,1,0:T(8,128)S(1)}, u32[]{:S(2)}) copy-start(f32[8,4,32,768]{3,2,1,0:T(8,128)S(1)} %bitcast_dynamic-update-slice_fusion) | copy-start | bytes 9437188
  64.4 1.1 %copy-start.1 = (f32[4,32,768]{2,1,0:T(8,128)}, f32[4,32,768]{2,1,0:T(8,128)S(1)}, u32[]{:S(2)}) copy-start(f32[4,32,768]{2,1,0:T(8,128)S(1)} %collective-permute-done.11) | copy-start | bytes 1179652
  80.7 10.3 %all-to-all-start = ((f32[4,6,1024]{2,1,0:T(8,128)}), f32[4,6,1024]{2,1,0:T(8,128)S(1)}, u32[]{:S(2)}, u32[]{:S(2)}) async-start(f32[4,6,1024]{2,1,0:T(8,128)} %bitcast.53), calls=%async_computation | async-start | bytes 262144 | tf_op jit(solution)/shard_map/all_to_all | solution.py:168
  91.0 1.4 %copy-start.2 = (f32[6,1024]{1,0:T(8,128)}, f32[6,1024]{1,0:T(8,128)S(1)}, u32[]{:S(2)}) copy-start(f32[6,1024]{1,0:T(8,128)S(1)} %reduce_sum.9) | copy-start | bytes 73732

commit v13 on v8

--- a/solution.py
+++ b/solution.py
@@ -23,14 +23,15 @@
             for n in range(bands):
                 piece = row[:, n * sub_width:(n + 1) * sub_width]
                 sh_ref[n, pl.ds(s, 1), pl.ds(jj * sub_width, sub_width)] = piece
-                rest_ref[n, pl.ds(s, 1), pl.ds(jj * sub_width, sub_width)] = 1.0 - piece
+    for n in range(bands):
+        rest_ref[n] = 1.0 - sh_ref[n]
     occ = occ_ref[...]
     for m in range(bands):
         acc_i = None
         acc_o = None
         for n in range(bands):
             p = m * bands + n
-            w = w_ref[p]
+            w = jnp.tile(w_ref[p], (1, gain_ref.shape[2] // w_ref.shape[2]))
             term_i = gain_ref[p].astype(jnp.float32) * w * sh_ref[n]
             term_o = loss_ref[p].astype(jnp.float32) * w * rest_ref[n]
             acc_i = term_i if acc_i is None else acc_i + term_i
@@ -133,7 +134,7 @@
     picks = where * sub_count + sources
     active = (jnp.arange(shifts, dtype=jnp.int32) < counts.reshape(())).astype(jnp.float32)
     weight = pair_mask.astype(jnp.float32) * active[:, None]
-    lanes = 512
+    lanes = 1024
     share_width = width // pb_count
     per_share = share_width // lanes
     me_pb = lax.axis_index("pb")
@@ -142,16 +143,16 @@
         [((me_pb + d) % pb_count) * per_share + step for d in range(1, pb_count)]
     )
     own = me_pb * per_share + step
-    tables = (picks, near, far, weight.T[:, :, None],
-              gain_table.transpose(1, 0, 2), loss_table.transpose(1, 0, 2), occupation)
-    sent = collide(tables[0], remote, *tables[1:], sub_width, lanes)
+    operands = (near, far, jnp.broadcast_to(weight.T[:, :, None], (bands * bands, shifts, sub_width)),
+                gain_table.transpose(1, 0, 2), loss_table.transpose(1, 0, 2), occupation)
+    sent = collide(picks, remote, *operands, sub_width, lanes)
     slots = jnp.concatenate([jnp.zeros((bands, share_width), jnp.float32), sent], axis=1)
     slots = slots.reshape(bands, pb_count, share_width).transpose(1, 0, 2)
     by_target = lax.dynamic_slice_in_dim(
         jnp.concatenate([slots, slots]), (pb_count - me_pb) % pb_count, pb_count, 0
     )
     received = lax.all_to_all(by_target, "pb", 0, 0, tiled=True)
-    kept = collide(tables[0], own, *tables[1:], sub_width, lanes)
+    kept = collide(picks, own, *operands, sub_width, lanes)
     collision = kept + jnp.sum(received, axis=0)
     own_share = lax.dynamic_slice_in_dim(
         occupation, lax.axis_index("pb") * share_width, share_width, 1

time: 87 us -> 85.8 us (0.986)
  Pallas kernels: 17.3 us -> 15.9 us
    pallas_call x2, Pallas kernels: 17.3 us -> 15.9 us  [collide(): pl.pallas_call(kern, out_shape=jax.ShapeDtypeStruct((bands, count * lanes...]
    ppermute x1, waiting for transfers between devices: 0.58 us -> 1.47 us  [ring_gather(): other = lax.ppermute(along_z, 'ka', pairs(lambda j: j ^ 1))]
  transfers between devices with their start and end apart: 12 -> 12, of which waited for: 8 -> 8; matrix products, arithmetic and copies ran while one was open for 7% -> 5% of each run, Pallas kernels for 8% -> 7%
where the time goes in v13:
time: 85.8 us; the launch traced here: 84.8 us
  waiting for transfers between devices  33.1 us (39%)
  starting transfers between devices  24.7 us (29%)
  Pallas kernels  15.9 us (19%)
  other arithmetic  4.83 us (6%)
  local copies, waits for them, and re-layouts  4.72 us (6%)
  between operations  1.51 us (2%)
    ppermute x6, waiting for transfers between devices, ring(): back = lax.ppermute(back, 'ka', step(-1))  31.6 us
    ppermute x6, starting transfers between devices, ring(): back = lax.ppermute(back, 'ka', step(-1))  17.8 us
    pallas_call x2, Pallas kernels, collide(): pl.pallas_call(kern, out_shape=jax.ShapeDtypeStruct((bands, count * lanes...  15.9 us
    all_to_all x1, starting transfers between devices, body(): received = lax.all_to_all(by_target, 'pb', 0, 0, tiled=True)  4.3 us
    ppermute x4, starting transfers between devices, ring(): fwd = lax.ppermute(fwd, 'ka', step(1))  2.52 us
    unnamed x14, local copies, waits for them, and re-layouts  1.77 us
  transfers between devices with their start and end apart: 12, of which 8 were waited for; matrix products, arithmetic and copies ran while one was open for 5% of the time, Pallas kernels for 7%

profile of v13, /device:TPU:24, one launch (start us, length us, event | category | flops | bytes accessed | tf_op | source)
XLA Modules:
  0.0 84.8 jit_solution(4093640881917051553)
XLA Ops:
  0.6 0.9 %copy.19 = f32[4,8,6,128]{3,1,2,0:T(8,128)S(1)} copy(f32[4,8,6,128]{3,2,1,0:T(8,128)} %bitcast.50) | data formatting | bytes 196608
  1.6 0.8 collective-permute-start
  2.4 2.5 %collective-permute-start.2 = (f32[32,768]{1,0:T(8,128)S(1)}, f32[32,768]{1,0:T(8,128)S(1)}, u32[]{:S(2)}, u32[]{:S(2)}) collective-permute-start(f32[32,768]{1,0:T(8,128)S(1)} %bitcast.60), channel_id=1, source_target_pairs={{0,8},{4,12},{8,16},{12,20},{16,24},{20,28},{24,0},{28,4},{32,40},... | collective-permute-start | bytes 294920 | tf_op jit(solution)/shard_map/ppermute | solution.py:95
  4.9 2.6 %collective-permute-done = f32[32,768]{1,0:T(8,128)S(1)} collective-permute-done((f32[32,768]{1,0:T(8,128)S(1)}, f32[32,768]{1,0:T(8,128)S(1)}, u32[]{:S(2)}, u32[]{:S(2)}) %collective-permute-start) | collective-permute-done | bytes 98336 | tf_op jit(solution)/shard_map/ppermute | solution.py:92
  7.5 0.0 collective-permute-start.1
  7.5 0.9 %stack_reshape.3 = f32[1,32,768]{2,1,0:T(8,128)S(1)} reshape(f32[32,6,128]{2,1,0:T(8,128)} %bitcast.51) | data formatting | bytes 196608 | tf_op jit(solution)/shard_map/stack;reshape | solution.py:97
  8.4 0.0 collective-permute-done.2
  8.4 4.9 %collective-permute-done.1 = f32[32,768]{1,0:T(8,128)S(1)} collective-permute-done((f32[32,768]{1,0:T(8,128)S(1)}, f32[32,768]{1,0:T(8,128)S(1)}, u32[]{:S(2)}, u32[]{:S(2)}) %collective-permute-start.1) | collective-permute-done | bytes 98336 | tf_op jit(solution)/shard_map/ppermute | solution.py:92
  13.3 0.0 copy-start.2
  13.3 0.0 copy-start.1
  13.3 5.9 %collective-permute-start.3 = (f32[4,32,768]{2,1,0:T(8,128)S(1)}, f32[4,32,768]{2,1,0:T(8,128)S(1)}, u32[]{:S(2)}, u32[]{:S(2)}) collective-permute-start(f32[4,32,768]{2,1,0:T(8,128)S(1)} %pad_maximum_fusion), channel_id=1, source_target_pairs={{0,224},{4,228},{8,232},{12,236},{16,240},{20,244},{24,248},{28,25... | collective-permute-start | bytes 1179656 | tf_op jit(solution)/shard_map/ppermute | solution.py:92
  19.3 0.0 collective-permute-start.7
  19.3 6.1 %collective-permute-done.3 = f32[4,32,768]{2,1,0:T(8,128)S(1)} collective-permute-done((f32[4,32,768]{2,1,0:T(8,128)S(1)}, f32[4,32,768]{2,1,0:T(8,128)S(1)}, u32[]{:S(2)}, u32[]{:S(2)}) %collective-permute-start.3) | collective-permute-done | bytes 393248 | tf_op jit(solution)/shard_map/ppermute | solution.py:92
  25.4 3.7 %collective-permute-start.4 = (f32[4,32,768]{2,1,0:T(8,128)S(1)}, f32[4,32,768]{2,1,0:T(8,128)S(1)}, u32[]{:S(2)}, u32[]{:S(2)}) collective-permute-start(f32[4,32,768]{2,1,0:T(8,128)S(1)} %collective-permute-done.3), channel_id=1, source_target_pairs={{0,224},{4,228},{8,232},{12,236},{16,240},{20,244},{24,248},{28,25... | collective-permute-start | bytes 1179656 | tf_op jit(solution)/shard_map/ppermute | solution.py:92
  29.0 0.0 collective-permute-done.7
  29.0 0.0 collective-permute-start.8
  29.0 5.9 %collective-permute-done.4 = f32[4,32,768]{2,1,0:T(8,128)S(1)} collective-permute-done((f32[4,32,768]{2,1,0:T(8,128)S(1)}, f32[4,32,768]{2,1,0:T(8,128)S(1)}, u32[]{:S(2)}, u32[]{:S(2)}) %collective-permute-start.4) | collective-permute-done | bytes 393248 | tf_op jit(solution)/shard_map/ppermute | solution.py:92
  35.0 3.7 %collective-permute-start.5 = (f32[4,32,768]{2,1,0:T(8,128)S(1)}, f32[4,32,768]{2,1,0:T(8,128)S(1)}, u32[]{:S(2)}, u32[]{:S(2)}) collective-permute-start(f32[4,32,768]{2,1,0:T(8,128)S(1)} %collective-permute-done.4), channel_id=1, source_target_pairs={{0,224},{4,228},{8,232},{12,236},{16,240},{20,244},{24,248},{28,25... | collective-permute-start | bytes 1179656 | tf_op jit(solution)/shard_map/ppermute | solution.py:92
  38.8 0.1 collective-permute-done.8
  38.8 0.0 collective-permute-start.9
  38.9 6.9 %collective-permute-done.5 = f32[4,32,768]{2,1,0:T(8,128)S(1)} collective-permute-done((f32[4,32,768]{2,1,0:T(8,128)S(1)}, f32[4,32,768]{2,1,0:T(8,128)S(1)}, u32[]{:S(2)}, u32[]{:S(2)}) %collective-permute-start.5) | collective-permute-done | bytes 393248 | tf_op jit(solution)/shard_map/ppermute | solution.py:92
  45.7 3.7 %collective-permute-start.6 = (f32[4,32,768]{2,1,0:T(8,128)S(1)}, f32[4,32,768]{2,1,0:T(8,128)S(1)}, u32[]{:S(2)}, u32[]{:S(2)}) collective-permute-start(f32[4,32,768]{2,1,0:T(8,128)S(1)} %collective-permute-done.5), channel_id=1, source_target_pairs={{0,224},{4,228},{8,232},{12,236},{16,240},{20,244},{24,248},{28,25... | collective-permute-start | bytes 1179656 | tf_op jit(solution)/shard_map/ppermute | solution.py:92
  49.5 5.2 %collective-permute-done.6 = f32[4,32,768]{2,1,0:T(8,128)S(1)} collective-permute-done((f32[4,32,768]{2,1,0:T(8,128)S(1)}, f32[4,32,768]{2,1,0:T(8,128)S(1)}, u32[]{:S(2)}, u32[]{:S(2)}) %collective-permute-start.6) | collective-permute-done | bytes 393248 | tf_op jit(solution)/shard_map/ppermute | solution.py:92
  54.7 0.0 collective-permute-done.9
  54.9 0.0 copy-start
  54.9 0.1 collective-permute-start.10
  55.0 0.7 broadcast.54
  55.7 0.0 copy-done.2
  55.7 0.7 reduce.3
  56.4 0.1 reshape.34
  56.5 0.0 copy-done.1
  56.5 0.1 reshape.35
  57.2 0.8 multiply_bitcast_fusion
  58.0 0.1 copy.15
  58.1 0.6 pad_add_fusion.tiles_ref
  58.7 0.6 fusion.6.idx_ref
  59.3 1.5 %collective-permute-done.10 = f32[8,4,32,768]{3,2,1,0:T(8,128)} collective-permute-done((f32[8,4,32,768]{3,2,1,0:T(8,128)S(1)}, f32[8,4,32,768]{3,2,1,0:T(8,128)}, u32[]{:S(2)}, u32[]{:S(2)}) %collective-permute-start.10) | collective-permute-done | bytes 3145760 | tf_op jit(solution)/shard_map/ppermute | solution.py:101
  60.8 0.8 %broadcast_in_dim.2.w_ref = f32[36,16,128]{2,1,0:T(8,128)} broadcast(f32[36,16]{1,0:T(8,128)S(1)} %copy.15), dimensions={0,1} | broadcast | bytes 297216 | tf_op jit(solution)/shard_map/broadcast_in_dim | solution.py:146
  61.6 0.0 copy-done
  61.6 9.5 %shard_map.87 = f32[6,3072]{1,0:T(8,128)} custom-call(s32[512]{0:T(512)} %fusion.6.idx_ref, s32[3]{0:T(128)} %pad_add_fusion.tiles_ref, f32[1024,768]{1,0:T(8,128)} %bitcast.48, f32[1024,768]{1,0:T(8,128)} %bitcast.16.far_ref, f32[36,16,128]{2,1,0:T(8,128)} %broadcast_in_dim.2.w_ref, bf16[36,16,4096]{2,1,0:T(8,128)(2,1)} %bitcast.44, ...), custom_call_target="tpu_custom_call" | custom-call | tf_op jit(solution)/shard_map/pallas_call | solution.py:52
  71.2 0.9 %concatenate.10 = f32[6,4096]{1,0:T(8,128)S(1)} pad(f32[6,3072]{1,0:T(8,128)} %shard_map.87, f32[]{:T(128)} %constant.123.clone.1), padding=0_0x1024_0 | pad | bytes 172036 | tf_op jit(solution)/shard_map/concatenate | solution.py:149
  72.1 0.7 fusion
  72.7 4.3 %all-to-all-start = ((f32[4,6,1024]{2,1,0:T(8,128)}), f32[4,6,1024]{2,1,0:T(8,128)S(1)}, u32[]{:S(2)}, u32[]{:S(2)}) async-start(f32[4,6,1024]{2,1,0:T(8,128)} %fusion), calls=%async_computation | async-start | bytes 262144 | tf_op jit(solution)/shard_map/all_to_all | solution.py:154
  77.0 6.3 %shard_map.86 = f32[6,1024]{1,0:T(8,128)} custom-call(s32[512]{0:T(512)} %fusion.6.idx_ref, s32[1]{0:T(128)} %bitcast.tiles_ref, f32[1024,768]{1,0:T(8,128)} %bitcast.49, f32[1024,768]{1,0:T(8,128)} %bitcast.16.far_ref, f32[36,16,128]{2,1,0:T(8,128)} %broadcast_in_dim.2.w_ref, bf16[36,16,4096]{2,1,0:T(8,128)(2,1)} %bitcast.45, ...), custom_call_target="tpu_custom_call" | custom-call | tf_op jit(solution)/shard_map/pallas_call | solution.py:52
  83.4 0.0 all-to-all-done
  83.4 1.4 %multiply_add_fusion = (f32[6,1024]{1,0:T(8,128)}, f32[6,1024]{1,0:T(8,128)}) fusion(f32[6,4096]{1,0:T(8,128)} %occ_ref.3, s32[]{:T(128)S(6)} %select_n.81, f32[6,1024]{1,0:T(8,128)} %shard_map.86, f32[6,1024]{1,0:T(8,128)S(1)} %reduce_sum.9), kind=kLoop, calls=%fused_computation.13 | loop fusion | flops 18432 | bytes 122884 | tf_op jit(solution)/shard_map/add | solution.py:160
  (11 shorter events, 0.3 us)
Async XLA Ops:
  1.6 5.9 %collective-permute-start = (f32[32,768]{1,0:T(8,128)S(1)}, f32[32,768]{1,0:T(8,128)S(1)}, u32[]{:S(2)}, u32[]{:S(2)}) collective-permute-start(f32[32,768]{1,0:T(8,128)S(1)} %bitcast.59), channel_id=1, source_target_pairs={{0,24},{4,28},{8,0},{12,4},{16,8},{20,12},{24,16},{28,20},{32,56},... | collective-permute-start | bytes 294920 | tf_op jit(solution)/shard_map/ppermute | solution.py:92
  2.4 6.0 %collective-permute-start.2 = (f32[32,768]{1,0:T(8,128)S(1)}, f32[32,768]{1,0:T(8,128)S(1)}, u32[]{:S(2)}, u32[]{:S(2)}) collective-permute-start(f32[32,768]{1,0:T(8,128)S(1)} %bitcast.60), channel_id=1, source_target_pairs={{0,8},{4,12},{8,16},{12,20},{16,24},{20,28},{24,0},{28,4},{32,40},... | collective-permute-start | bytes 294920 | tf_op jit(solution)/shard_map/ppermute | solution.py:95
  7.5 5.8 %collective-permute-start.1 = (f32[32,768]{1,0:T(8,128)S(1)}, f32[32,768]{1,0:T(8,128)S(1)}, u32[]{:S(2)}, u32[]{:S(2)}) collective-permute-start(f32[32,768]{1,0:T(8,128)S(1)} %collective-permute-done), channel_id=1, source_target_pairs={{0,24},{4,28},{8,0},{12,4},{16,8},{20,12},{24,16},{28,20},{32,56},... | collective-permute-start | bytes 294920 | tf_op jit(solution)/shard_map/ppermute | solution.py:92
  13.3 42.4 %copy-start.2 = (s32[1,1,16,32,1]{3,4,2,1,0:T(1,128)S(1)}, s32[1,1,16,32,1]{3,4,2,1,0:T(1,128)}, u32[]{:S(2)}) copy-start(s32[1,1,16,32,1]{3,4,2,1,0:T(1,128)} %param.10) | copy-start | bytes 6148
  13.3 43.2 %copy-start.1 = (s32[1,1,16,32]{3,2,1,0:T(8,128)S(1)}, s32[1,1,16,32]{3,2,1,0:T(8,128)}, u32[]{:S(2)}) copy-start(s32[1,1,16,32]{3,2,1,0:T(8,128)} %param.11) | copy-start | bytes 6148
  13.3 12.0 %collective-permute-start.3 = (f32[4,32,768]{2,1,0:T(8,128)S(1)}, f32[4,32,768]{2,1,0:T(8,128)S(1)}, u32[]{:S(2)}, u32[]{:S(2)}) collective-permute-start(f32[4,32,768]{2,1,0:T(8,128)S(1)} %pad_maximum_fusion), channel_id=1, source_target_pairs={{0,224},{4,228},{8,232},{12,236},{16,240},{20,244},{24,248},{28,25... | collective-permute-start | bytes 1179656 | tf_op jit(solution)/shard_map/ppermute | solution.py:92
  19.3 9.8 %collective-permute-start.7 = (f32[4,32,768]{2,1,0:T(8,128)S(1)}, f32[4,32,768]{2,1,0:T(8,128)S(1)}, u32[]{:S(2)}, u32[]{:S(2)}) collective-permute-start(f32[4,32,768]{2,1,0:T(8,128)S(1)} %pad_maximum_fusion), channel_id=1, source_target_pairs={{0,32},{4,36},{8,40},{12,44},{16,48},{20,52},{24,56},{28,60},{32,6... | collective-permute-start | bytes 1179656 | tf_op jit(solution)/shard_map/ppermute | solution.py:95
  25.4 9.6 %collective-permute-start.4 = (f32[4,32,768]{2,1,0:T(8,128)S(1)}, f32[4,32,768]{2,1,0:T(8,128)S(1)}, u32[]{:S(2)}, u32[]{:S(2)}) collective-permute-start(f32[4,32,768]{2,1,0:T(8,128)S(1)} %collective-permute-done.3), channel_id=1, source_target_pairs={{0,224},{4,228},{8,232},{12,236},{16,240},{20,244},{24,248},{28,25... | collective-permute-start | bytes 1179656 | tf_op jit(solution)/shard_map/ppermute | solution.py:92
  29.0 9.8 %collective-permute-start.8 = (f32[4,32,768]{2,1,0:T(8,128)S(1)}, f32[4,32,768]{2,1,0:T(8,128)S(1)}, u32[]{:S(2)}, u32[]{:S(2)}) collective-permute-start(f32[4,32,768]{2,1,0:T(8,128)S(1)} %collective-permute-done.7), channel_id=1, source_target_pairs={{0,32},{4,36},{8,40},{12,44},{16,48},{20,52},{24,56},{28,60},{32,6... | collective-permute-start | bytes 1179656 | tf_op jit(solution)/shard_map/ppermute | solution.py:95
  35.0 10.7 %collective-permute-start.5 = (f32[4,32,768]{2,1,0:T(8,128)S(1)}, f32[4,32,768]{2,1,0:T(8,128)S(1)}, u32[]{:S(2)}, u32[]{:S(2)}) collective-permute-start(f32[4,32,768]{2,1,0:T(8,128)S(1)} %collective-permute-done.4), channel_id=1, source_target_pairs={{0,224},{4,228},{8,232},{12,236},{16,240},{20,244},{24,248},{28,25... | collective-permute-start | bytes 1179656 | tf_op jit(solution)/shard_map/ppermute | solution.py:92
  38.8 15.9 %collective-permute-start.9 = (f32[4,32,768]{2,1,0:T(8,128)S(1)}, f32[4,32,768]{2,1,0:T(8,128)S(1)}, u32[]{:S(2)}, u32[]{:S(2)}) collective-permute-start(f32[4,32,768]{2,1,0:T(8,128)S(1)} %collective-permute-done.8), channel_id=1, source_target_pairs={{0,32},{4,36},{8,40},{12,44},{16,48},{20,52},{24,56},{28,60},{32,6... | collective-permute-start | bytes 1179656 | tf_op jit(solution)/shard_map/ppermute | solution.py:95
  45.7 9.0 %collective-permute-start.6 = (f32[4,32,768]{2,1,0:T(8,128)S(1)}, f32[4,32,768]{2,1,0:T(8,128)S(1)}, u32[]{:S(2)}, u32[]{:S(2)}) collective-permute-start(f32[4,32,768]{2,1,0:T(8,128)S(1)} %collective-permute-done.5), channel_id=1, source_target_pairs={{0,224},{4,228},{8,232},{12,236},{16,240},{20,244},{24,248},{28,25... | collective-permute-start | bytes 1179656 | tf_op jit(solution)/shard_map/ppermute | solution.py:92
  54.9 6.7 %copy-start = (f32[8,4,32,768]{3,2,1,0:T(8,128)}, f32[8,4,32,768]{3,2,1,0:T(8,128)S(1)}, u32[]{:S(2)}) copy-start(f32[8,4,32,768]{3,2,1,0:T(8,128)S(1)} %bitcast_dynamic-update-slice_fusion) | copy-start | bytes 9437188
  54.9 5.9 %collective-permute-start.10 = (f32[8,4,32,768]{3,2,1,0:T(8,128)S(1)}, f32[8,4,32,768]{3,2,1,0:T(8,128)}, u32[]{:S(2)}, u32[]{:S(2)}) collective-permute-start(f32[8,4,32,768]{3,2,1,0:T(8,128)S(1)} %bitcast_dynamic-update-slice_fusion), channel_id=1, source_target_pairs={{0,4},{4,0},{8,12},{12,8},{16,20},{20,16},{24,28},{28,24},{32,36},... | collective-permute-start | bytes 9437192 | tf_op jit(solution)/shard_map/ppermute | solution.py:101
  72.7 10.6 %all-to-all-start = ((f32[4,6,1024]{2,1,0:T(8,128)}), f32[4,6,1024]{2,1,0:T(8,128)S(1)}, u32[]{:S(2)}, u32[]{:S(2)}) async-start(f32[4,6,1024]{2,1,0:T(8,128)} %fusion), calls=%async_computation | async-start | bytes 262144 | tf_op jit(solution)/shard_map/all_to_all | solution.py:154

commit v14 on v9

--- a/solution.py
+++ b/solution.py
@@ -144,8 +144,15 @@
         sub_width,
     )
     share_width = width // pb_count
-    parts = partial_terms.reshape(bands, pb_count, share_width).transpose(1, 0, 2)
-    collision = jnp.sum(lax.all_to_all(parts, "pb", 0, 0, tiled=True), axis=0)
+    me_pb = lax.axis_index("pb")
+    collision = lax.dynamic_slice_in_dim(partial_terms, me_pb * share_width, share_width, 1)
+    for d in range(1, pb_count):
+        share = lax.dynamic_slice_in_dim(
+            partial_terms, ((me_pb + d) % pb_count) * share_width, share_width, 1
+        )
+        collision = collision + lax.ppermute(
+            share, "pb", [(j, (j + d) % pb_count) for j in range(pb_count)]
+        )
     own_share = lax.dynamic_slice_in_dim(
         occupation, lax.axis_index("pb") * share_width, share_width, 1
     )

time: 85.3 us -> 83.9 us (0.984)
  waiting for transfers between devices: 39.7 us -> 36.2 us
  starting transfers between devices: 24.7 us -> 26.2 us
    all_to_all x1 -> x0, waiting for transfers between devices: 5.98 us -> none  [body(): collision = jnp.sum(lax.all_to_all(parts, 'pb', 0, 0, tiled=True), axis=0)]
    ppermute x0 -> x3, starting transfers between devices: none -> 5.72 us  [body(): lax.ppermute(share, 'pb', [(j, (j + d) % pb_count) for j in range(pb_coun...]
    all_to_all x1 -> x0, starting transfers between devices: 4.29 us -> none  [body(): collision = jnp.sum(lax.all_to_all(parts, 'pb', 0, 0, tiled=True), axis=0)]
    ppermute x0 -> x3, waiting for transfers between devices: none -> 2.48 us  [body(): lax.ppermute(share, 'pb', [(j, (j + d) % pb_count) for j in range(pb_coun...]
    unnamed x16 -> x14, local copies, waits for them, and re-layouts: 1.77 us -> 1.77 us
  transfers between devices with their start and end apart: 12 -> 14, of which waited for: 9 -> 10; matrix products, arithmetic and copies ran while one was open for 5% -> 5% of each run, Pallas kernels for 0% -> 0%
where the time goes in v14:
time: 83.9 us; the launch traced here: 83.5 us
  waiting for transfers between devices  36.2 us (43%)
  starting transfers between devices  26.2 us (31%)
  Pallas kernels  11.5 us (14%)
  local copies, waits for them, and re-layouts  4.63 us (6%)
  other arithmetic  3.55 us (4%)
  between operations  1.51 us (2%)
    ppermute x6, waiting for transfers between devices, ring(): back = lax.ppermute(back, 'ka', step(-1))  31.6 us
    ppermute x6, starting transfers between devices, ring(): back = lax.ppermute(back, 'ka', step(-1))  17.8 us
    pallas_call x1, Pallas kernels, collide(): pl.pallas_call(kern, out_shape=jax.ShapeDtypeStruct((bands, width), jnp.f...  11.5 us
    ppermute x3, starting transfers between devices, body(): lax.ppermute(share, 'pb', [(j, (j + d) % pb_count) for j in range(pb_coun...  5.72 us
    ppermute x4, starting transfers between devices, ring(): fwd = lax.ppermute(fwd, 'ka', step(1))  2.52 us
    ppermute x3, waiting for transfers between devices, body(): lax.ppermute(share, 'pb', [(j, (j + d) % pb_count) for j in range(pb_coun...  2.48 us
    ppermute x1, waiting for transfers between devices, ring_gather(): other = lax.ppermute(along_z, 'ka', pairs(lambda j: j ^ 1))  2.03 us
    unnamed x14, local copies, waits for them, and re-layouts  1.77 us
  transfers between devices with their start and end apart: 14, of which 10 were waited for; matrix products, arithmetic and copies ran while one was open for 5% of the time, Pallas kernels for 0%

profile of v14, /device:TPU:24, one launch (start us, length us, event | category | flops | bytes accessed | tf_op | source)
XLA Modules:
  0.0 83.5 jit_solution(8841449843489650879)
XLA Ops:
  0.6 0.9 %copy.16 = f32[4,8,6,128]{3,1,2,0:T(8,128)S(1)} copy(f32[4,8,6,128]{3,2,1,0:T(8,128)} %bitcast.40) | data formatting | bytes 196608
  1.6 0.8 collective-permute-start
  2.4 2.5 %collective-permute-start.2 = (f32[32,768]{1,0:T(8,128)S(1)}, f32[32,768]{1,0:T(8,128)S(1)}, u32[]{:S(2)}, u32[]{:S(2)}) collective-permute-start(f32[32,768]{1,0:T(8,128)S(1)} %bitcast.49), channel_id=1, source_target_pairs={{0,8},{4,12},{8,16},{12,20},{16,24},{20,28},{24,0},{28,4},{32,40},... | collective-permute-start | bytes 294920 | tf_op jit(solution)/shard_map/ppermute | solution.py:94
  4.9 2.6 %collective-permute-done = f32[32,768]{1,0:T(8,128)S(1)} collective-permute-done((f32[32,768]{1,0:T(8,128)S(1)}, f32[32,768]{1,0:T(8,128)S(1)}, u32[]{:S(2)}, u32[]{:S(2)}) %collective-permute-start) | collective-permute-done | bytes 98336 | tf_op jit(solution)/shard_map/ppermute | solution.py:91
  7.5 0.0 collective-permute-start.1
  7.5 0.9 %stack_reshape.3 = f32[1,32,768]{2,1,0:T(8,128)S(1)} reshape(f32[32,6,128]{2,1,0:T(8,128)} %bitcast.41) | data formatting | bytes 196608 | tf_op jit(solution)/shard_map/stack;reshape | solution.py:96
  8.4 0.0 collective-permute-done.2
  8.4 4.9 %collective-permute-done.1 = f32[32,768]{1,0:T(8,128)S(1)} collective-permute-done((f32[32,768]{1,0:T(8,128)S(1)}, f32[32,768]{1,0:T(8,128)S(1)}, u32[]{:S(2)}, u32[]{:S(2)}) %collective-permute-start.1) | collective-permute-done | bytes 98336 | tf_op jit(solution)/shard_map/ppermute | solution.py:91
  13.3 0.0 copy-start.2
  13.3 0.0 copy-start.1
  13.3 5.9 %collective-permute-start.3 = (f32[4,32,768]{2,1,0:T(8,128)S(1)}, f32[4,32,768]{2,1,0:T(8,128)S(1)}, u32[]{:S(2)}, u32[]{:S(2)}) collective-permute-start(f32[4,32,768]{2,1,0:T(8,128)S(1)} %pad_maximum_fusion), channel_id=1, source_target_pairs={{0,224},{4,228},{8,232},{12,236},{16,240},{20,244},{24,248},{28,25... | collective-permute-start | bytes 1179656 | tf_op jit(solution)/shard_map/ppermute | solution.py:91
  19.3 0.0 collective-permute-start.7
  19.3 6.1 %collective-permute-done.3 = f32[4,32,768]{2,1,0:T(8,128)S(1)} collective-permute-done((f32[4,32,768]{2,1,0:T(8,128)S(1)}, f32[4,32,768]{2,1,0:T(8,128)S(1)}, u32[]{:S(2)}, u32[]{:S(2)}) %collective-permute-start.3) | collective-permute-done | bytes 393248 | tf_op jit(solution)/shard_map/ppermute | solution.py:91
  25.4 3.7 %collective-permute-start.4 = (f32[4,32,768]{2,1,0:T(8,128)S(1)}, f32[4,32,768]{2,1,0:T(8,128)S(1)}, u32[]{:S(2)}, u32[]{:S(2)}) collective-permute-start(f32[4,32,768]{2,1,0:T(8,128)S(1)} %collective-permute-done.3), channel_id=1, source_target_pairs={{0,224},{4,228},{8,232},{12,236},{16,240},{20,244},{24,248},{28,25... | collective-permute-start | bytes 1179656 | tf_op jit(solution)/shard_map/ppermute | solution.py:91
  29.0 0.0 collective-permute-done.7
  29.0 0.0 collective-permute-start.8
  29.0 5.9 %collective-permute-done.4 = f32[4,32,768]{2,1,0:T(8,128)S(1)} collective-permute-done((f32[4,32,768]{2,1,0:T(8,128)S(1)}, f32[4,32,768]{2,1,0:T(8,128)S(1)}, u32[]{:S(2)}, u32[]{:S(2)}) %collective-permute-start.4) | collective-permute-done | bytes 393248 | tf_op jit(solution)/shard_map/ppermute | solution.py:91
  35.0 3.7 %collective-permute-start.5 = (f32[4,32,768]{2,1,0:T(8,128)S(1)}, f32[4,32,768]{2,1,0:T(8,128)S(1)}, u32[]{:S(2)}, u32[]{:S(2)}) collective-permute-start(f32[4,32,768]{2,1,0:T(8,128)S(1)} %collective-permute-done.4), channel_id=1, source_target_pairs={{0,224},{4,228},{8,232},{12,236},{16,240},{20,244},{24,248},{28,25... | collective-permute-start | bytes 1179656 | tf_op jit(solution)/shard_map/ppermute | solution.py:91
  38.8 0.1 collective-permute-done.8
  38.8 0.0 collective-permute-start.9
  38.9 6.9 %collective-permute-done.5 = f32[4,32,768]{2,1,0:T(8,128)S(1)} collective-permute-done((f32[4,32,768]{2,1,0:T(8,128)S(1)}, f32[4,32,768]{2,1,0:T(8,128)S(1)}, u32[]{:S(2)}, u32[]{:S(2)}) %collective-permute-start.5) | collective-permute-done | bytes 393248 | tf_op jit(solution)/shard_map/ppermute | solution.py:91
  45.7 3.7 %collective-permute-start.6 = (f32[4,32,768]{2,1,0:T(8,128)S(1)}, f32[4,32,768]{2,1,0:T(8,128)S(1)}, u32[]{:S(2)}, u32[]{:S(2)}) collective-permute-start(f32[4,32,768]{2,1,0:T(8,128)S(1)} %collective-permute-done.5), channel_id=1, source_target_pairs={{0,224},{4,228},{8,232},{12,236},{16,240},{20,244},{24,248},{28,25... | collective-permute-start | bytes 1179656 | tf_op jit(solution)/shard_map/ppermute | solution.py:91
  49.5 5.2 %collective-permute-done.6 = f32[4,32,768]{2,1,0:T(8,128)S(1)} collective-permute-done((f32[4,32,768]{2,1,0:T(8,128)S(1)}, f32[4,32,768]{2,1,0:T(8,128)S(1)}, u32[]{:S(2)}, u32[]{:S(2)}) %collective-permute-start.6) | collective-permute-done | bytes 393248 | tf_op jit(solution)/shard_map/ppermute | solution.py:91
  54.7 0.0 collective-permute-done.9
  54.9 0.0 copy-start
  54.9 0.1 collective-permute-start.10
  55.1 0.7 broadcast.51
  55.7 0.0 copy-done.2
  55.7 0.7 reduce.3
  56.4 0.1 reshape.31
  56.5 0.0 copy-done.1
  56.5 0.1 reshape.32
  57.3 0.8 multiply_bitcast_fusion
  58.0 0.1 copy.13
  58.1 0.6 fusion.5.idx_ref
  58.7 2.0 %collective-permute-done.10 = f32[8,4,32,768]{3,2,1,0:T(8,128)} collective-permute-done((f32[8,4,32,768]{3,2,1,0:T(8,128)S(1)}, f32[8,4,32,768]{3,2,1,0:T(8,128)}, u32[]{:S(2)}, u32[]{:S(2)}) %collective-permute-start.10) | collective-permute-done | bytes 3145760 | tf_op jit(solution)/shard_map/ppermute | solution.py:100
  60.8 0.9 %broadcast_in_dim.2.w_ref = f32[36,16,128]{2,1,0:T(8,128)} broadcast(f32[36,16]{1,0:T(8,128)S(1)} %copy.13), dimensions={0,1} | broadcast | bytes 297216 | tf_op jit(solution)/shard_map/broadcast_in_dim | solution.py:140
  61.6 0.0 copy-done
  61.6 11.5 %shard_map.86 = f32[6,4096]{1,0:T(8,128)} custom-call(s32[512]{0:T(512)} %fusion.5.idx_ref, f32[1024,768]{1,0:T(8,128)} %bitcast.39, f32[1024,768]{1,0:T(8,128)} %bitcast.15.far_ref, f32[36,16,128]{2,1,0:T(8,128)} %broadcast_in_dim.2.w_ref, bf16[36,16,4096]{2,1,0:T(8,128)(2,1)} %bitcast.37, bf16[36,16,4096]{2,1,0:T(8,128)(2,1)} %bitcast.38, f32[6,4096]{1,0:T(8,128)} %occ_ref.1), custom_call_target="tpu_custom_call" | custom-call | tf_op jit(solution)/shard_map/pallas_call | solution.py:51
  73.1 0.8 constant_dynamic-slice_fusion.2
  73.9 1.6 %collective-permute-start.11 = (f32[6,1024]{1,0:T(8,128)S(1)}, f32[6,1024]{1,0:T(8,128)S(1)}, u32[]{:S(2)}, u32[]{:S(2)}) collective-permute-start(f32[6,1024]{1,0:T(8,128)S(1)} %get-tuple-element.4), channel_id=1, source_target_pairs={{0,1},{1,2},{2,3},{3,0},{4,5},{5,6},{6,7},{7,4},{8,9},{9,10},{10,1... | collective-permute-start | bytes 73736 | tf_op jit(solution)/shard_map/ppermute | solution.py:153
  75.5 2.7 %collective-permute-start.12 = (f32[6,1024]{1,0:T(8,128)S(1)}, f32[6,1024]{1,0:T(8,128)S(1)}, u32[]{:S(2)}, u32[]{:S(2)}) collective-permute-start(f32[6,1024]{1,0:T(8,128)S(1)} %get-tuple-element.6), channel_id=1, source_target_pairs={{0,2},{1,3},{2,0},{3,1},{4,6},{5,7},{6,4},{7,5},{8,10},{9,11},{10,... | collective-permute-start | bytes 73736 | tf_op jit(solution)/shard_map/ppermute | solution.py:153
  78.2 1.4 %collective-permute-start.13 = (f32[6,1024]{1,0:T(8,128)S(1)}, f32[6,1024]{1,0:T(8,128)S(1)}, u32[]{:S(2)}, u32[]{:S(2)}) collective-permute-start(f32[6,1024]{1,0:T(8,128)S(1)} %get-tuple-element.5), channel_id=1, source_target_pairs={{0,3},{1,0},{2,1},{3,2},{4,7},{5,4},{6,5},{7,6},{8,11},{9,8},{10,9... | collective-permute-start | bytes 73736 | tf_op jit(solution)/shard_map/ppermute | solution.py:153
  79.6 0.0 collective-permute-done.11
  79.6 1.3 %collective-permute-done.12 = f32[6,1024]{1,0:T(8,128)S(1)} collective-permute-done((f32[6,1024]{1,0:T(8,128)S(1)}, f32[6,1024]{1,0:T(8,128)S(1)}, u32[]{:S(2)}, u32[]{:S(2)}) %collective-permute-start.12) | collective-permute-done | bytes 24608 | tf_op jit(solution)/shard_map/ppermute | solution.py:153
  80.9 1.2 %collective-permute-done.13 = f32[6,1024]{1,0:T(8,128)S(1)} collective-permute-done((f32[6,1024]{1,0:T(8,128)S(1)}, f32[6,1024]{1,0:T(8,128)S(1)}, u32[]{:S(2)}, u32[]{:S(2)}) %collective-permute-start.13) | collective-permute-done | bytes 24608 | tf_op jit(solution)/shard_map/ppermute | solution.py:153
  82.1 1.4 %multiply_add_fusion = (f32[6,1024]{1,0:T(8,128)}, f32[6,1024]{1,0:T(8,128)}) fusion(f32[6,4096]{1,0:T(8,128)} %occ_ref.1, s32[]{:T(128)S(6)} %select_n.79, f32[6,1024]{1,0:T(8,128)S(1)} %collective-permute-done.13, f32[6,1024]{1,0:T(8,128)S(1)} %collective-permute-done.12, f32[6,1024]{1,0:T(8,128)S(1)} %collective-permute-done.11, f32[6,4096]{1,0:T(8,128)} %shard_map.86), kind=kLoop, calls=%fused_computation.10 | loop fusion | flops 30720 | bytes 172036 | tf_op jit(solution)/shard_map/add | solution.py:159
  (10 shorter events, 0.3 us)
Async XLA Ops:
  1.6 5.9 %collective-permute-start = (f32[32,768]{1,0:T(8,128)S(1)}, f32[32,768]{1,0:T(8,128)S(1)}, u32[]{:S(2)}, u32[]{:S(2)}) collective-permute-start(f32[32,768]{1,0:T(8,128)S(1)} %bitcast.48), channel_id=1, source_target_pairs={{0,24},{4,28},{8,0},{12,4},{16,8},{20,12},{24,16},{28,20},{32,56},... | collective-permute-start | bytes 294920 | tf_op jit(solution)/shard_map/ppermute | solution.py:91
  2.4 6.0 %collective-permute-start.2 = (f32[32,768]{1,0:T(8,128)S(1)}, f32[32,768]{1,0:T(8,128)S(1)}, u32[]{:S(2)}, u32[]{:S(2)}) collective-permute-start(f32[32,768]{1,0:T(8,128)S(1)} %bitcast.49), channel_id=1, source_target_pairs={{0,8},{4,12},{8,16},{12,20},{16,24},{20,28},{24,0},{28,4},{32,40},... | collective-permute-start | bytes 294920 | tf_op jit(solution)/shard_map/ppermute | solution.py:94
  7.5 5.8 %collective-permute-start.1 = (f32[32,768]{1,0:T(8,128)S(1)}, f32[32,768]{1,0:T(8,128)S(1)}, u32[]{:S(2)}, u32[]{:S(2)}) collective-permute-start(f32[32,768]{1,0:T(8,128)S(1)} %collective-permute-done), channel_id=1, source_target_pairs={{0,24},{4,28},{8,0},{12,4},{16,8},{20,12},{24,16},{28,20},{32,56},... | collective-permute-start | bytes 294920 | tf_op jit(solution)/shard_map/ppermute | solution.py:91
  13.3 42.4 %copy-start.2 = (s32[1,1,16,32,1]{3,4,2,1,0:T(1,128)S(1)}, s32[1,1,16,32,1]{3,4,2,1,0:T(1,128)}, u32[]{:S(2)}) copy-start(s32[1,1,16,32,1]{3,4,2,1,0:T(1,128)} %param.10) | copy-start | bytes 6148
  13.3 43.2 %copy-start.1 = (s32[1,1,16,32]{3,2,1,0:T(8,128)S(1)}, s32[1,1,16,32]{3,2,1,0:T(8,128)}, u32[]{:S(2)}) copy-start(s32[1,1,16,32]{3,2,1,0:T(8,128)} %param.11) | copy-start | bytes 6148
  13.3 12.0 %collective-permute-start.3 = (f32[4,32,768]{2,1,0:T(8,128)S(1)}, f32[4,32,768]{2,1,0:T(8,128)S(1)}, u32[]{:S(2)}, u32[]{:S(2)}) collective-permute-start(f32[4,32,768]{2,1,0:T(8,128)S(1)} %pad_maximum_fusion), channel_id=1, source_target_pairs={{0,224},{4,228},{8,232},{12,236},{16,240},{20,244},{24,248},{28,25... | collective-permute-start | bytes 1179656 | tf_op jit(solution)/shard_map/ppermute | solution.py:91
  19.3 9.8 %collective-permute-start.7 = (f32[4,32,768]{2,1,0:T(8,128)S(1)}, f32[4,32,768]{2,1,0:T(8,128)S(1)}, u32[]{:S(2)}, u32[]{:S(2)}) collective-permute-start(f32[4,32,768]{2,1,0:T(8,128)S(1)} %pad_maximum_fusion), channel_id=1, source_target_pairs={{0,32},{4,36},{8,40},{12,44},{16,48},{20,52},{24,56},{28,60},{32,6... | collective-permute-start | bytes 1179656 | tf_op jit(solution)/shard_map/ppermute | solution.py:94
  25.4 9.6 %collective-permute-start.4 = (f32[4,32,768]{2,1,0:T(8,128)S(1)}, f32[4,32,768]{2,1,0:T(8,128)S(1)}, u32[]{:S(2)}, u32[]{:S(2)}) collective-permute-start(f32[4,32,768]{2,1,0:T(8,128)S(1)} %collective-permute-done.3), channel_id=1, source_target_pairs={{0,224},{4,228},{8,232},{12,236},{16,240},{20,244},{24,248},{28,25... | collective-permute-start | bytes 1179656 | tf_op jit(solution)/shard_map/ppermute | solution.py:91
  29.0 9.8 %collective-permute-start.8 = (f32[4,32,768]{2,1,0:T(8,128)S(1)}, f32[4,32,768]{2,1,0:T(8,128)S(1)}, u32[]{:S(2)}, u32[]{:S(2)}) collective-permute-start(f32[4,32,768]{2,1,0:T(8,128)S(1)} %collective-permute-done.7), channel_id=1, source_target_pairs={{0,32},{4,36},{8,40},{12,44},{16,48},{20,52},{24,56},{28,60},{32,6... | collective-permute-start | bytes 1179656 | tf_op jit(solution)/shard_map/ppermute | solution.py:94
  35.0 10.7 %collective-permute-start.5 = (f32[4,32,768]{2,1,0:T(8,128)S(1)}, f32[4,32,768]{2,1,0:T(8,128)S(1)}, u32[]{:S(2)}, u32[]{:S(2)}) collective-permute-start(f32[4,32,768]{2,1,0:T(8,128)S(1)} %collective-permute-done.4), channel_id=1, source_target_pairs={{0,224},{4,228},{8,232},{12,236},{16,240},{20,244},{24,248},{28,25... | collective-permute-start | bytes 1179656 | tf_op jit(solution)/shard_map/ppermute | solution.py:91
  38.8 15.9 %collective-permute-start.9 = (f32[4,32,768]{2,1,0:T(8,128)S(1)}, f32[4,32,768]{2,1,0:T(8,128)S(1)}, u32[]{:S(2)}, u32[]{:S(2)}) collective-permute-start(f32[4,32,768]{2,1,0:T(8,128)S(1)} %collective-permute-done.8), channel_id=1, source_target_pairs={{0,32},{4,36},{8,40},{12,44},{16,48},{20,52},{24,56},{28,60},{32,6... | collective-permute-start | bytes 1179656 | tf_op jit(solution)/shard_map/ppermute | solution.py:94
  45.7 9.0 %collective-permute-start.6 = (f32[4,32,768]{2,1,0:T(8,128)S(1)}, f32[4,32,768]{2,1,0:T(8,128)S(1)}, u32[]{:S(2)}, u32[]{:S(2)}) collective-permute-start(f32[4,32,768]{2,1,0:T(8,128)S(1)} %collective-permute-done.5), channel_id=1, source_target_pairs={{0,224},{4,228},{8,232},{12,236},{16,240},{20,244},{24,248},{28,25... | collective-permute-start | bytes 1179656 | tf_op jit(solution)/shard_map/ppermute | solution.py:91
  54.9 6.8 %copy-start = (f32[8,4,32,768]{3,2,1,0:T(8,128)}, f32[8,4,32,768]{3,2,1,0:T(8,128)S(1)}, u32[]{:S(2)}) copy-start(f32[8,4,32,768]{3,2,1,0:T(8,128)S(1)} %bitcast_dynamic-update-slice_fusion) | copy-start | bytes 9437188
  54.9 5.9 %collective-permute-start.10 = (f32[8,4,32,768]{3,2,1,0:T(8,128)S(1)}, f32[8,4,32,768]{3,2,1,0:T(8,128)}, u32[]{:S(2)}, u32[]{:S(2)}) collective-permute-start(f32[8,4,32,768]{3,2,1,0:T(8,128)S(1)} %bitcast_dynamic-update-slice_fusion), channel_id=1, source_target_pairs={{0,4},{4,0},{8,12},{12,8},{16,20},{20,16},{24,28},{28,24},{32,36},... | collective-permute-start | bytes 9437192 | tf_op jit(solution)/shard_map/ppermute | solution.py:100
  73.9 5.7 %collective-permute-start.11 = (f32[6,1024]{1,0:T(8,128)S(1)}, f32[6,1024]{1,0:T(8,128)S(1)}, u32[]{:S(2)}, u32[]{:S(2)}) collective-permute-start(f32[6,1024]{1,0:T(8,128)S(1)} %get-tuple-element.4), channel_id=1, source_target_pairs={{0,1},{1,2},{2,3},{3,0},{4,5},{5,6},{6,7},{7,4},{8,9},{9,10},{10,1... | collective-permute-start | bytes 73736 | tf_op jit(solution)/shard_map/ppermute | solution.py:153
  75.5 5.4 %collective-permute-start.12 = (f32[6,1024]{1,0:T(8,128)S(1)}, f32[6,1024]{1,0:T(8,128)S(1)}, u32[]{:S(2)}, u32[]{:S(2)}) collective-permute-start(f32[6,1024]{1,0:T(8,128)S(1)} %get-tuple-element.6), channel_id=1, source_target_pairs={{0,2},{1,3},{2,0},{3,1},{4,6},{5,7},{6,4},{7,5},{8,10},{9,11},{10,... | collective-permute-start | bytes 73736 | tf_op jit(solution)/shard_map/ppermute | solution.py:153
  78.2 3.9 %collective-permute-start.13 = (f32[6,1024]{1,0:T(8,128)S(1)}, f32[6,1024]{1,0:T(8,128)S(1)}, u32[]{:S(2)}, u32[]{:S(2)}) collective-permute-start(f32[6,1024]{1,0:T(8,128)S(1)} %get-tuple-element.5), channel_id=1, source_target_pairs={{0,3},{1,0},{2,1},{3,2},{4,7},{5,4},{6,5},{7,6},{8,11},{9,8},{10,9... | collective-permute-start | bytes 73736 | tf_op jit(solution)/shard_map/ppermute | solution.py:153

commit v15 on v14

--- a/solution.py
+++ b/solution.py
@@ -146,7 +146,7 @@
     share_width = width // pb_count
     me_pb = lax.axis_index("pb")
     collision = lax.dynamic_slice_in_dim(partial_terms, me_pb * share_width, share_width, 1)
-    for d in range(1, pb_count):
+    for d in sorted(range(1, pb_count), key=lambda d: -min(d, pb_count - d)):
         share = lax.dynamic_slice_in_dim(
             partial_terms, ((me_pb + d) % pb_count) * share_width, share_width, 1
         )

time: 83.9 us -> 84.4 us (level)
  transfers between devices with their start and end apart: 14 -> 14, of which waited for: 10 -> 9; matrix products, arithmetic and copies ran while one was open for 5% -> 5% of each run, Pallas kernels for 0% -> 0%
where the time goes in v15:
time: 84.4 us; the launch traced here: 83.5 us
  waiting for transfers between devices  35.6 us (42%)
  starting transfers between devices  26.8 us (32%)
  Pallas kernels  11.5 us (14%)
  local copies, waits for them, and re-layouts  4.63 us (5%)
  other arithmetic  3.55 us (4%)
  between operations  1.51 us (2%)
    ppermute x6, waiting for transfers between devices, ring(): back = lax.ppermute(back, 'ka', step(-1))  31.6 us
    ppermute x6, starting transfers between devices, ring(): back = lax.ppermute(back, 'ka', step(-1))  17.8 us
    pallas_call x1, Pallas kernels, collide(): pl.pallas_call(kern, out_shape=jax.ShapeDtypeStruct((bands, width), jnp.f...  11.5 us
    ppermute x3, starting transfers between devices, body(): lax.ppermute(share, 'pb', [(j, (j + d) % pb_count) for j in range(pb_coun...  6.33 us
    ppermute x4, starting transfers between devices, ring(): fwd = lax.ppermute(fwd, 'ka', step(1))  2.52 us
    ppermute x1, waiting for transfers between devices, ring_gather(): other = lax.ppermute(along_z, 'ka', pairs(lambda j: j ^ 1))  2.03 us
    ppermute x3, waiting for transfers between devices, body(): lax.ppermute(share, 'pb', [(j, (j + d) % pb_count) for j in range(pb_coun...  1.89 us
    unnamed x14, local copies, waits for them, and re-layouts  1.77 us
  transfers between devices with their start and end apart: 14, of which 9 were waited for; matrix products, arithmetic and copies ran while one was open for 5% of the time, Pallas kernels for 0%

profile of v15, /device:TPU:24, one launch (start us, length us, event | category | flops | bytes accessed | tf_op | source)
XLA Modules:
  0.0 83.5 jit_solution(2360087509434029488)
XLA Ops:
  0.6 0.9 %copy.16 = f32[4,8,6,128]{3,1,2,0:T(8,128)S(1)} copy(f32[4,8,6,128]{3,2,1,0:T(8,128)} %bitcast.40) | data formatting | bytes 196608
  1.6 0.8 collective-permute-start
  2.4 2.5 %collective-permute-start.2 = (f32[32,768]{1,0:T(8,128)S(1)}, f32[32,768]{1,0:T(8,128)S(1)}, u32[]{:S(2)}, u32[]{:S(2)}) collective-permute-start(f32[32,768]{1,0:T(8,128)S(1)} %bitcast.49), channel_id=1, source_target_pairs={{0,8},{4,12},{8,16},{12,20},{16,24},{20,28},{24,0},{28,4},{32,40},... | collective-permute-start | bytes 294920 | tf_op jit(solution)/shard_map/ppermute | solution.py:94
  4.9 2.6 %collective-permute-done = f32[32,768]{1,0:T(8,128)S(1)} collective-permute-done((f32[32,768]{1,0:T(8,128)S(1)}, f32[32,768]{1,0:T(8,128)S(1)}, u32[]{:S(2)}, u32[]{:S(2)}) %collective-permute-start) | collective-permute-done | bytes 98336 | tf_op jit(solution)/shard_map/ppermute | solution.py:91
  7.5 0.0 collective-permute-start.1
  7.5 0.9 %stack_reshape.3 = f32[1,32,768]{2,1,0:T(8,128)S(1)} reshape(f32[32,6,128]{2,1,0:T(8,128)} %bitcast.41) | data formatting | bytes 196608 | tf_op jit(solution)/shard_map/stack;reshape | solution.py:96
  8.4 0.0 collective-permute-done.2
  8.4 4.9 %collective-permute-done.1 = f32[32,768]{1,0:T(8,128)S(1)} collective-permute-done((f32[32,768]{1,0:T(8,128)S(1)}, f32[32,768]{1,0:T(8,128)S(1)}, u32[]{:S(2)}, u32[]{:S(2)}) %collective-permute-start.1) | collective-permute-done | bytes 98336 | tf_op jit(solution)/shard_map/ppermute | solution.py:91
  13.3 0.0 copy-start.2
  13.3 0.0 copy-start.1
  13.3 5.9 %collective-permute-start.3 = (f32[4,32,768]{2,1,0:T(8,128)S(1)}, f32[4,32,768]{2,1,0:T(8,128)S(1)}, u32[]{:S(2)}, u32[]{:S(2)}) collective-permute-start(f32[4,32,768]{2,1,0:T(8,128)S(1)} %pad_maximum_fusion), channel_id=1, source_target_pairs={{0,224},{4,228},{8,232},{12,236},{16,240},{20,244},{24,248},{28,25... | collective-permute-start | bytes 1179656 | tf_op jit(solution)/shard_map/ppermute | solution.py:91
  19.3 0.0 collective-permute-start.7
  19.3 6.1 %collective-permute-done.3 = f32[4,32,768]{2,1,0:T(8,128)S(1)} collective-permute-done((f32[4,32,768]{2,1,0:T(8,128)S(1)}, f32[4,32,768]{2,1,0:T(8,128)S(1)}, u32[]{:S(2)}, u32[]{:S(2)}) %collective-permute-start.3) | collective-permute-done | bytes 393248 | tf_op jit(solution)/shard_map/ppermute | solution.py:91
  25.4 3.7 %collective-permute-start.4 = (f32[4,32,768]{2,1,0:T(8,128)S(1)}, f32[4,32,768]{2,1,0:T(8,128)S(1)}, u32[]{:S(2)}, u32[]{:S(2)}) collective-permute-start(f32[4,32,768]{2,1,0:T(8,128)S(1)} %collective-permute-done.3), channel_id=1, source_target_pairs={{0,224},{4,228},{8,232},{12,236},{16,240},{20,244},{24,248},{28,25... | collective-permute-start | bytes 1179656 | tf_op jit(solution)/shard_map/ppermute | solution.py:91
  29.0 0.0 collective-permute-done.7
  29.0 0.0 collective-permute-start.8
  29.0 5.9 %collective-permute-done.4 = f32[4,32,768]{2,1,0:T(8,128)S(1)} collective-permute-done((f32[4,32,768]{2,1,0:T(8,128)S(1)}, f32[4,32,768]{2,1,0:T(8,128)S(1)}, u32[]{:S(2)}, u32[]{:S(2)}) %collective-permute-start.4) | collective-permute-done | bytes 393248 | tf_op jit(solution)/shard_map/ppermute | solution.py:91
  35.0 3.7 %collective-permute-start.5 = (f32[4,32,768]{2,1,0:T(8,128)S(1)}, f32[4,32,768]{2,1,0:T(8,128)S(1)}, u32[]{:S(2)}, u32[]{:S(2)}) collective-permute-start(f32[4,32,768]{2,1,0:T(8,128)S(1)} %collective-permute-done.4), channel_id=1, source_target_pairs={{0,224},{4,228},{8,232},{12,236},{16,240},{20,244},{24,248},{28,25... | collective-permute-start | bytes 1179656 | tf_op jit(solution)/shard_map/ppermute | solution.py:91
  38.8 0.1 collective-permute-done.8
  38.8 0.0 collective-permute-start.9
  38.9 6.9 %collective-permute-done.5 = f32[4,32,768]{2,1,0:T(8,128)S(1)} collective-permute-done((f32[4,32,768]{2,1,0:T(8,128)S(1)}, f32[4,32,768]{2,1,0:T(8,128)S(1)}, u32[]{:S(2)}, u32[]{:S(2)}) %collective-permute-start.5) | collective-permute-done | bytes 393248 | tf_op jit(solution)/shard_map/ppermute | solution.py:91
  45.7 3.7 %collective-permute-start.6 = (f32[4,32,768]{2,1,0:T(8,128)S(1)}, f32[4,32,768]{2,1,0:T(8,128)S(1)}, u32[]{:S(2)}, u32[]{:S(2)}) collective-permute-start(f32[4,32,768]{2,1,0:T(8,128)S(1)} %collective-permute-done.5), channel_id=1, source_target_pairs={{0,224},{4,228},{8,232},{12,236},{16,240},{20,244},{24,248},{28,25... | collective-permute-start | bytes 1179656 | tf_op jit(solution)/shard_map/ppermute | solution.py:91
  49.5 5.2 %collective-permute-done.6 = f32[4,32,768]{2,1,0:T(8,128)S(1)} collective-permute-done((f32[4,32,768]{2,1,0:T(8,128)S(1)}, f32[4,32,768]{2,1,0:T(8,128)S(1)}, u32[]{:S(2)}, u32[]{:S(2)}) %collective-permute-start.6) | collective-permute-done | bytes 393248 | tf_op jit(solution)/shard_map/ppermute | solution.py:91
  54.7 0.0 collective-permute-done.9
  54.9 0.0 copy-start
  54.9 0.1 collective-permute-start.10
  55.1 0.7 broadcast.51
  55.7 0.0 copy-done.2
  55.7 0.7 reduce.3
  56.4 0.1 reshape.31
  56.5 0.0 copy-done.1
  56.5 0.1 reshape.32
  57.3 0.8 multiply_bitcast_fusion
  58.0 0.1 copy.13
  58.1 0.6 fusion.5.idx_ref
  58.7 2.0 %collective-permute-done.10 = f32[8,4,32,768]{3,2,1,0:T(8,128)} collective-permute-done((f32[8,4,32,768]{3,2,1,0:T(8,128)S(1)}, f32[8,4,32,768]{3,2,1,0:T(8,128)}, u32[]{:S(2)}, u32[]{:S(2)}) %collective-permute-start.10) | collective-permute-done | bytes 3145760 | tf_op jit(solution)/shard_map/ppermute | solution.py:100
  60.8 0.9 %broadcast_in_dim.2.w_ref = f32[36,16,128]{2,1,0:T(8,128)} broadcast(f32[36,16]{1,0:T(8,128)S(1)} %copy.13), dimensions={0,1} | broadcast | bytes 297216 | tf_op jit(solution)/shard_map/broadcast_in_dim | solution.py:140
  61.6 0.0 copy-done
  61.6 11.5 %shard_map.86 = f32[6,4096]{1,0:T(8,128)} custom-call(s32[512]{0:T(512)} %fusion.5.idx_ref, f32[1024,768]{1,0:T(8,128)} %bitcast.39, f32[1024,768]{1,0:T(8,128)} %bitcast.15.far_ref, f32[36,16,128]{2,1,0:T(8,128)} %broadcast_in_dim.2.w_ref, bf16[36,16,4096]{2,1,0:T(8,128)(2,1)} %bitcast.37, bf16[36,16,4096]{2,1,0:T(8,128)(2,1)} %bitcast.38, f32[6,4096]{1,0:T(8,128)} %occ_ref.1), custom_call_target="tpu_custom_call" | custom-call | tf_op jit(solution)/shard_map/pallas_call | solution.py:51
  73.1 0.8 constant_dynamic-slice_fusion.2
  73.9 3.1 %collective-permute-start.11 = (f32[6,1024]{1,0:T(8,128)S(1)}, f32[6,1024]{1,0:T(8,128)S(1)}, u32[]{:S(2)}, u32[]{:S(2)}) collective-permute-start(f32[6,1024]{1,0:T(8,128)S(1)} %get-tuple-element.4), channel_id=1, source_target_pairs={{0,2},{1,3},{2,0},{3,1},{4,6},{5,7},{6,4},{7,5},{8,10},{9,11},{10,... | collective-permute-start | bytes 73736 | tf_op jit(solution)/shard_map/ppermute | solution.py:153
  77.0 0.6 collective-permute-start.12
  77.6 2.6 %collective-permute-start.13 = (f32[6,1024]{1,0:T(8,128)S(1)}, f32[6,1024]{1,0:T(8,128)S(1)}, u32[]{:S(2)}, u32[]{:S(2)}) collective-permute-start(f32[6,1024]{1,0:T(8,128)S(1)} %get-tuple-element.5), channel_id=1, source_target_pairs={{0,3},{1,0},{2,1},{3,2},{4,7},{5,4},{6,5},{7,6},{8,11},{9,8},{10,9... | collective-permute-start | bytes 73736 | tf_op jit(solution)/shard_map/ppermute | solution.py:153
  80.2 0.0 collective-permute-done.11
  80.2 1.9 %collective-permute-done.12 = f32[6,1024]{1,0:T(8,128)S(1)} collective-permute-done((f32[6,1024]{1,0:T(8,128)S(1)}, f32[6,1024]{1,0:T(8,128)S(1)}, u32[]{:S(2)}, u32[]{:S(2)}) %collective-permute-start.12) | collective-permute-done | bytes 24608 | tf_op jit(solution)/shard_map/ppermute | solution.py:153
  82.1 0.0 collective-permute-done.13
  82.1 1.4 %multiply_add_fusion = (f32[6,1024]{1,0:T(8,128)}, f32[6,1024]{1,0:T(8,128)}) fusion(f32[6,4096]{1,0:T(8,128)} %occ_ref.1, s32[]{:T(128)S(6)} %select_n.79, f32[6,1024]{1,0:T(8,128)S(1)} %collective-permute-done.13, f32[6,1024]{1,0:T(8,128)S(1)} %collective-permute-done.12, f32[6,1024]{1,0:T(8,128)S(1)} %collective-permute-done.11, f32[6,4096]{1,0:T(8,128)} %shard_map.86), kind=kLoop, calls=%fused_computation.10 | loop fusion | flops 30720 | bytes 172036 | tf_op jit(solution)/shard_map/add | solution.py:159
  (10 shorter events, 0.3 us)
Async XLA Ops:
  1.6 5.9 %collective-permute-start = (f32[32,768]{1,0:T(8,128)S(1)}, f32[32,768]{1,0:T(8,128)S(1)}, u32[]{:S(2)}, u32[]{:S(2)}) collective-permute-start(f32[32,768]{1,0:T(8,128)S(1)} %bitcast.48), channel_id=1, source_target_pairs={{0,24},{4,28},{8,0},{12,4},{16,8},{20,12},{24,16},{28,20},{32,56},... | collective-permute-start | bytes 294920 | tf_op jit(solution)/shard_map/ppermute | solution.py:91
  2.4 6.0 %collective-permute-start.2 = (f32[32,768]{1,0:T(8,128)S(1)}, f32[32,768]{1,0:T(8,128)S(1)}, u32[]{:S(2)}, u32[]{:S(2)}) collective-permute-start(f32[32,768]{1,0:T(8,128)S(1)} %bitcast.49), channel_id=1, source_target_pairs={{0,8},{4,12},{8,16},{12,20},{16,24},{20,28},{24,0},{28,4},{32,40},... | collective-permute-start | bytes 294920 | tf_op jit(solution)/shard_map/ppermute | solution.py:94
  7.5 5.8 %collective-permute-start.1 = (f32[32,768]{1,0:T(8,128)S(1)}, f32[32,768]{1,0:T(8,128)S(1)}, u32[]{:S(2)}, u32[]{:S(2)}) collective-permute-start(f32[32,768]{1,0:T(8,128)S(1)} %collective-permute-done), channel_id=1, source_target_pairs={{0,24},{4,28},{8,0},{12,4},{16,8},{20,12},{24,16},{28,20},{32,56},... | collective-permute-start | bytes 294920 | tf_op jit(solution)/shard_map/ppermute | solution.py:91
  13.3 42.4 %copy-start.2 = (s32[1,1,16,32,1]{3,4,2,1,0:T(1,128)S(1)}, s32[1,1,16,32,1]{3,4,2,1,0:T(1,128)}, u32[]{:S(2)}) copy-start(s32[1,1,16,32,1]{3,4,2,1,0:T(1,128)} %param.10) | copy-start | bytes 6148
  13.3 43.2 %copy-start.1 = (s32[1,1,16,32]{3,2,1,0:T(8,128)S(1)}, s32[1,1,16,32]{3,2,1,0:T(8,128)}, u32[]{:S(2)}) copy-start(s32[1,1,16,32]{3,2,1,0:T(8,128)} %param.11) | copy-start | bytes 6148
  13.3 12.0 %collective-permute-start.3 = (f32[4,32,768]{2,1,0:T(8,128)S(1)}, f32[4,32,768]{2,1,0:T(8,128)S(1)}, u32[]{:S(2)}, u32[]{:S(2)}) collective-permute-start(f32[4,32,768]{2,1,0:T(8,128)S(1)} %pad_maximum_fusion), channel_id=1, source_target_pairs={{0,224},{4,228},{8,232},{12,236},{16,240},{20,244},{24,248},{28,25... | collective-permute-start | bytes 1179656 | tf_op jit(solution)/shard_map/ppermute | solution.py:91
  19.3 9.8 %collective-permute-start.7 = (f32[4,32,768]{2,1,0:T(8,128)S(1)}, f32[4,32,768]{2,1,0:T(8,128)S(1)}, u32[]{:S(2)}, u32[]{:S(2)}) collective-permute-start(f32[4,32,768]{2,1,0:T(8,128)S(1)} %pad_maximum_fusion), channel_id=1, source_target_pairs={{0,32},{4,36},{8,40},{12,44},{16,48},{20,52},{24,56},{28,60},{32,6... | collective-permute-start | bytes 1179656 | tf_op jit(solution)/shard_map/ppermute | solution.py:94
  25.4 9.6 %collective-permute-start.4 = (f32[4,32,768]{2,1,0:T(8,128)S(1)}, f32[4,32,768]{2,1,0:T(8,128)S(1)}, u32[]{:S(2)}, u32[]{:S(2)}) collective-permute-start(f32[4,32,768]{2,1,0:T(8,128)S(1)} %collective-permute-done.3), channel_id=1, source_target_pairs={{0,224},{4,228},{8,232},{12,236},{16,240},{20,244},{24,248},{28,25... | collective-permute-start | bytes 1179656 | tf_op jit(solution)/shard_map/ppermute | solution.py:91
  29.0 9.8 %collective-permute-start.8 = (f32[4,32,768]{2,1,0:T(8,128)S(1)}, f32[4,32,768]{2,1,0:T(8,128)S(1)}, u32[]{:S(2)}, u32[]{:S(2)}) collective-permute-start(f32[4,32,768]{2,1,0:T(8,128)S(1)} %collective-permute-done.7), channel_id=1, source_target_pairs={{0,32},{4,36},{8,40},{12,44},{16,48},{20,52},{24,56},{28,60},{32,6... | collective-permute-start | bytes 1179656 | tf_op jit(solution)/shard_map/ppermute | solution.py:94
  35.0 10.7 %collective-permute-start.5 = (f32[4,32,768]{2,1,0:T(8,128)S(1)}, f32[4,32,768]{2,1,0:T(8,128)S(1)}, u32[]{:S(2)}, u32[]{:S(2)}) collective-permute-start(f32[4,32,768]{2,1,0:T(8,128)S(1)} %collective-permute-done.4), channel_id=1, source_target_pairs={{0,224},{4,228},{8,232},{12,236},{16,240},{20,244},{24,248},{28,25... | collective-permute-start | bytes 1179656 | tf_op jit(solution)/shard_map/ppermute | solution.py:91
  38.8 15.9 %collective-permute-start.9 = (f32[4,32,768]{2,1,0:T(8,128)S(1)}, f32[4,32,768]{2,1,0:T(8,128)S(1)}, u32[]{:S(2)}, u32[]{:S(2)}) collective-permute-start(f32[4,32,768]{2,1,0:T(8,128)S(1)} %collective-permute-done.8), channel_id=1, source_target_pairs={{0,32},{4,36},{8,40},{12,44},{16,48},{20,52},{24,56},{28,60},{32,6... | collective-permute-start | bytes 1179656 | tf_op jit(solution)/shard_map/ppermute | solution.py:94
  45.7 9.0 %collective-permute-start.6 = (f32[4,32,768]{2,1,0:T(8,128)S(1)}, f32[4,32,768]{2,1,0:T(8,128)S(1)}, u32[]{:S(2)}, u32[]{:S(2)}) collective-permute-start(f32[4,32,768]{2,1,0:T(8,128)S(1)} %collective-permute-done.5), channel_id=1, source_target_pairs={{0,224},{4,228},{8,232},{12,236},{16,240},{20,244},{24,248},{28,25... | collective-permute-start | bytes 1179656 | tf_op jit(solution)/shard_map/ppermute | solution.py:91
  54.9 6.8 %copy-start = (f32[8,4,32,768]{3,2,1,0:T(8,128)}, f32[8,4,32,768]{3,2,1,0:T(8,128)S(1)}, u32[]{:S(2)}) copy-start(f32[8,4,32,768]{3,2,1,0:T(8,128)S(1)} %bitcast_dynamic-update-slice_fusion) | copy-start | bytes 9437188
  54.9 5.9 %collective-permute-start.10 = (f32[8,4,32,768]{3,2,1,0:T(8,128)S(1)}, f32[8,4,32,768]{3,2,1,0:T(8,128)}, u32[]{:S(2)}, u32[]{:S(2)}) collective-permute-start(f32[8,4,32,768]{3,2,1,0:T(8,128)S(1)} %bitcast_dynamic-update-slice_fusion), channel_id=1, source_target_pairs={{0,4},{4,0},{8,12},{12,8},{16,20},{20,16},{24,28},{28,24},{32,36},... | collective-permute-start | bytes 9437192 | tf_op jit(solution)/shard_map/ppermute | solution.py:100
  73.9 6.3 %collective-permute-start.11 = (f32[6,1024]{1,0:T(8,128)S(1)}, f32[6,1024]{1,0:T(8,128)S(1)}, u32[]{:S(2)}, u32[]{:S(2)}) collective-permute-start(f32[6,1024]{1,0:T(8,128)S(1)} %get-tuple-element.4), channel_id=1, source_target_pairs={{0,2},{1,3},{2,0},{3,1},{4,6},{5,7},{6,4},{7,5},{8,10},{9,11},{10,... | collective-permute-start | bytes 73736 | tf_op jit(solution)/shard_map/ppermute | solution.py:153
  77.0 5.1 %collective-permute-start.12 = (f32[6,1024]{1,0:T(8,128)S(1)}, f32[6,1024]{1,0:T(8,128)S(1)}, u32[]{:S(2)}, u32[]{:S(2)}) collective-permute-start(f32[6,1024]{1,0:T(8,128)S(1)} %get-tuple-element.6), channel_id=1, source_target_pairs={{0,1},{1,2},{2,3},{3,0},{4,5},{5,6},{6,7},{7,4},{8,9},{9,10},{10,1... | collective-permute-start | bytes 73736 | tf_op jit(solution)/shard_map/ppermute | solution.py:153
  77.6 4.5 %collective-permute-start.13 = (f32[6,1024]{1,0:T(8,128)S(1)}, f32[6,1024]{1,0:T(8,128)S(1)}, u32[]{:S(2)}, u32[]{:S(2)}) collective-permute-start(f32[6,1024]{1,0:T(8,128)S(1)} %get-tuple-element.5), channel_id=1, source_target_pairs={{0,3},{1,0},{2,1},{3,2},{4,7},{5,4},{6,5},{7,6},{8,11},{9,8},{10,9... | collective-permute-start | bytes 73736 | tf_op jit(solution)/shard_map/ppermute | solution.py:153

commit v16 on v14

--- a/solution.py
+++ b/solution.py
@@ -38,19 +38,20 @@
             acc_o = term_o if acc_o is None else acc_o + term_o
         inflow = jnp.sum(acc_i, axis=0, keepdims=True)
         outflow = jnp.sum(acc_o, axis=0, keepdims=True)
-        out_ref[pl.ds(m, 1), :] = (1.0 - occ[m:m + 1]) * inflow - occ[m:m + 1] * outflow
+        out_ref[0, pl.ds(m, 1), :] = (1.0 - occ[m:m + 1]) * inflow - occ[m:m + 1] * outflow
 
 
-def collide(idx, near, far, weight_t, gain_t, loss_t, occ, sub_width, lanes=1024):
+def collide(idx, near, far, weight_t, gain_t, loss_t, occ, sub_width, parts, lanes=1024):
     pairs, shifts, width = gain_t.shape
     bands = occ.shape[0]
     sub_count = width // sub_width
     nsub = lanes // sub_width
+    per_part = width // parts // lanes
     kern = functools.partial(collide_kernel, shifts=shifts, nsub=nsub, sub_count=sub_count,
                              sub_width=sub_width, bands=bands)
     return pl.pallas_call(
         kern,
-        out_shape=jax.ShapeDtypeStruct((bands, width), jnp.float32),
+        out_shape=jax.ShapeDtypeStruct((parts, bands, width // parts), jnp.float32),
         grid_spec=pltpu.PrefetchScalarGridSpec(
             num_scalar_prefetch=1,
             grid=(width // lanes,),
@@ -62,7 +63,9 @@
                 pl.BlockSpec((pairs, shifts, lanes), lambda t, i: (0, 0, t)),
                 pl.BlockSpec((bands, lanes), lambda t, i: (0, t)),
             ],
-            out_specs=pl.BlockSpec((bands, lanes), lambda t, i: (0, t)),
+            out_specs=pl.BlockSpec(
+                (1, bands, lanes), lambda t, i: (t // per_part, 0, t % per_part)
+            ),
             scratch_shapes=[
                 pltpu.VMEM((bands, shifts, lanes), jnp.float32),
                 pltpu.VMEM((bands, shifts, lanes), jnp.float32),
@@ -142,14 +145,13 @@
         loss_table.transpose(1, 0, 2),
         occupation,
         sub_width,
+        pb_count,
     )
     share_width = width // pb_count
     me_pb = lax.axis_index("pb")
-    collision = lax.dynamic_slice_in_dim(partial_terms, me_pb * share_width, share_width, 1)
+    collision = partial_terms[me_pb]
     for d in range(1, pb_count):
-        share = lax.dynamic_slice_in_dim(
-            partial_terms, ((me_pb + d) % pb_count) * share_width, share_width, 1
-        )
+        share = partial_terms[(me_pb + d) % pb_count]
         collision = collision + lax.ppermute(
             share, "pb", [(j, (j + d) % pb_count) for j in range(pb_count)]
         )

time: 83.9 us -> 83.9 us (level)
  no operation moved by 1% of the time
where the time goes in v16:
time: 83.9 us; the launch traced here: 83.5 us
  waiting for transfers between devices  36.2 us (43%)
  starting transfers between devices  26.2 us (31%)
  Pallas kernels  11.5 us (14%)
  local copies, waits for them, and re-layouts  4.63 us (6%)
  other arithmetic  3.56 us (4%)
  between operations  1.51 us (2%)
    ppermute x6, waiting for transfers between devices, ring(): back = lax.ppermute(back, 'ka', step(-1))  31.6 us
    ppermute x6, starting transfers between devices, ring(): back = lax.ppermute(back, 'ka', step(-1))  17.8 us
    pallas_call x1, Pallas kernels, collide(): pl.pallas_call(kern, out_shape=jax.ShapeDtypeStruct((parts, bands, width...  11.5 us
    ppermute x3, starting transfers between devices, body(): lax.ppermute(share, 'pb', [(j, (j + d) % pb_count) for j in range(pb_coun...  5.72 us
    ppermute x4, starting transfers between devices, ring(): fwd = lax.ppermute(fwd, 'ka', step(1))  2.52 us
    ppermute x3, waiting for transfers between devices, body(): lax.ppermute(share, 'pb', [(j, (j + d) % pb_count) for j in range(pb_coun...  2.48 us
    ppermute x1, waiting for transfers between devices, ring_gather(): other = lax.ppermute(along_z, 'ka', pairs(lambda j: j ^ 1))  2.03 us
    unnamed x14, local copies, waits for them, and re-layouts  1.77 us
  transfers between devices with their start and end apart: 14, of which 10 were waited for; matrix products, arithmetic and copies ran while one was open for 5% of the time, Pallas kernels for 0%

profile of v16, /device:TPU:24, one launch (start us, length us, event | category | flops | bytes accessed | tf_op | source)
XLA Modules:
  0.0 83.5 jit_solution(924294229743051674)
XLA Ops:
  0.6 0.9 %copy.16 = f32[4,8,6,128]{3,1,2,0:T(8,128)S(1)} copy(f32[4,8,6,128]{3,2,1,0:T(8,128)} %bitcast.53) | data formatting | bytes 196608
  1.6 0.8 collective-permute-start
  2.4 2.5 %collective-permute-start.2 = (f32[32,768]{1,0:T(8,128)S(1)}, f32[32,768]{1,0:T(8,128)S(1)}, u32[]{:S(2)}, u32[]{:S(2)}) collective-permute-start(f32[32,768]{1,0:T(8,128)S(1)} %bitcast.62), channel_id=1, source_target_pairs={{0,8},{4,12},{8,16},{12,20},{16,24},{20,28},{24,0},{28,4},{32,40},... | collective-permute-start | bytes 294920 | tf_op jit(solution)/shard_map/ppermute | solution.py:97
  4.9 2.6 %collective-permute-done = f32[32,768]{1,0:T(8,128)S(1)} collective-permute-done((f32[32,768]{1,0:T(8,128)S(1)}, f32[32,768]{1,0:T(8,128)S(1)}, u32[]{:S(2)}, u32[]{:S(2)}) %collective-permute-start) | collective-permute-done | bytes 98336 | tf_op jit(solution)/shard_map/ppermute | solution.py:94
  7.5 0.0 collective-permute-start.1
  7.5 0.9 %stack_reshape.3 = f32[1,32,768]{2,1,0:T(8,128)S(1)} reshape(f32[32,6,128]{2,1,0:T(8,128)} %bitcast.54) | data formatting | bytes 196608 | tf_op jit(solution)/shard_map/stack;reshape | solution.py:99
  8.4 0.0 collective-permute-done.2
  8.4 4.9 %collective-permute-done.1 = f32[32,768]{1,0:T(8,128)S(1)} collective-permute-done((f32[32,768]{1,0:T(8,128)S(1)}, f32[32,768]{1,0:T(8,128)S(1)}, u32[]{:S(2)}, u32[]{:S(2)}) %collective-permute-start.1) | collective-permute-done | bytes 98336 | tf_op jit(solution)/shard_map/ppermute | solution.py:94
  13.3 0.0 copy-start.2
  13.3 0.0 copy-start.1
  13.3 5.9 %collective-permute-start.3 = (f32[4,32,768]{2,1,0:T(8,128)S(1)}, f32[4,32,768]{2,1,0:T(8,128)S(1)}, u32[]{:S(2)}, u32[]{:S(2)}) collective-permute-start(f32[4,32,768]{2,1,0:T(8,128)S(1)} %pad_maximum_fusion), channel_id=1, source_target_pairs={{0,224},{4,228},{8,232},{12,236},{16,240},{20,244},{24,248},{28,25... | collective-permute-start | bytes 1179656 | tf_op jit(solution)/shard_map/ppermute | solution.py:94
  19.3 0.0 collective-permute-start.7
  19.3 6.1 %collective-permute-done.3 = f32[4,32,768]{2,1,0:T(8,128)S(1)} collective-permute-done((f32[4,32,768]{2,1,0:T(8,128)S(1)}, f32[4,32,768]{2,1,0:T(8,128)S(1)}, u32[]{:S(2)}, u32[]{:S(2)}) %collective-permute-start.3) | collective-permute-done | bytes 393248 | tf_op jit(solution)/shard_map/ppermute | solution.py:94
  25.4 3.7 %collective-permute-start.4 = (f32[4,32,768]{2,1,0:T(8,128)S(1)}, f32[4,32,768]{2,1,0:T(8,128)S(1)}, u32[]{:S(2)}, u32[]{:S(2)}) collective-permute-start(f32[4,32,768]{2,1,0:T(8,128)S(1)} %collective-permute-done.3), channel_id=1, source_target_pairs={{0,224},{4,228},{8,232},{12,236},{16,240},{20,244},{24,248},{28,25... | collective-permute-start | bytes 1179656 | tf_op jit(solution)/shard_map/ppermute | solution.py:94
  29.0 0.0 collective-permute-done.7
  29.0 0.0 collective-permute-start.8
  29.0 5.9 %collective-permute-done.4 = f32[4,32,768]{2,1,0:T(8,128)S(1)} collective-permute-done((f32[4,32,768]{2,1,0:T(8,128)S(1)}, f32[4,32,768]{2,1,0:T(8,128)S(1)}, u32[]{:S(2)}, u32[]{:S(2)}) %collective-permute-start.4) | collective-permute-done | bytes 393248 | tf_op jit(solution)/shard_map/ppermute | solution.py:94
  35.0 3.7 %collective-permute-start.5 = (f32[4,32,768]{2,1,0:T(8,128)S(1)}, f32[4,32,768]{2,1,0:T(8,128)S(1)}, u32[]{:S(2)}, u32[]{:S(2)}) collective-permute-start(f32[4,32,768]{2,1,0:T(8,128)S(1)} %collective-permute-done.4), channel_id=1, source_target_pairs={{0,224},{4,228},{8,232},{12,236},{16,240},{20,244},{24,248},{28,25... | collective-permute-start | bytes 1179656 | tf_op jit(solution)/shard_map/ppermute | solution.py:94
  38.8 0.1 collective-permute-done.8
  38.8 0.0 collective-permute-start.9
  38.9 6.9 %collective-permute-done.5 = f32[4,32,768]{2,1,0:T(8,128)S(1)} collective-permute-done((f32[4,32,768]{2,1,0:T(8,128)S(1)}, f32[4,32,768]{2,1,0:T(8,128)S(1)}, u32[]{:S(2)}, u32[]{:S(2)}) %collective-permute-start.5) | collective-permute-done | bytes 393248 | tf_op jit(solution)/shard_map/ppermute | solution.py:94
  45.7 3.7 %collective-permute-start.6 = (f32[4,32,768]{2,1,0:T(8,128)S(1)}, f32[4,32,768]{2,1,0:T(8,128)S(1)}, u32[]{:S(2)}, u32[]{:S(2)}) collective-permute-start(f32[4,32,768]{2,1,0:T(8,128)S(1)} %collective-permute-done.5), channel_id=1, source_target_pairs={{0,224},{4,228},{8,232},{12,236},{16,240},{20,244},{24,248},{28,25... | collective-permute-start | bytes 1179656 | tf_op jit(solution)/shard_map/ppermute | solution.py:94
  49.5 5.2 %collective-permute-done.6 = f32[4,32,768]{2,1,0:T(8,128)S(1)} collective-permute-done((f32[4,32,768]{2,1,0:T(8,128)S(1)}, f32[4,32,768]{2,1,0:T(8,128)S(1)}, u32[]{:S(2)}, u32[]{:S(2)}) %collective-permute-start.6) | collective-permute-done | bytes 393248 | tf_op jit(solution)/shard_map/ppermute | solution.py:94
  54.7 0.0 collective-permute-done.9
  54.9 0.0 copy-start
  54.9 0.1 collective-permute-start.10
  55.1 0.7 broadcast.51
  55.7 0.0 copy-done.2
  55.7 0.7 reduce.3
  56.4 0.1 reshape.31
  56.5 0.0 copy-done.1
  56.5 0.1 reshape.32
  57.3 0.8 multiply_bitcast_fusion
  58.0 0.1 copy.13
  58.1 0.6 fusion.7.idx_ref
  58.7 2.0 %collective-permute-done.10 = f32[8,4,32,768]{3,2,1,0:T(8,128)} collective-permute-done((f32[8,4,32,768]{3,2,1,0:T(8,128)S(1)}, f32[8,4,32,768]{3,2,1,0:T(8,128)}, u32[]{:S(2)}, u32[]{:S(2)}) %collective-permute-start.10) | collective-permute-done | bytes 3145760 | tf_op jit(solution)/shard_map/ppermute | solution.py:103
  60.8 0.9 %broadcast_in_dim.2.w_ref = f32[36,16,128]{2,1,0:T(8,128)} broadcast(f32[36,16]{1,0:T(8,128)S(1)} %copy.13), dimensions={0,1} | broadcast | bytes 297216 | tf_op jit(solution)/shard_map/broadcast_in_dim | solution.py:143
  61.6 0.0 copy-done
  61.6 11.5 %shard_map.86 = f32[4,6,1024]{2,1,0:T(8,128)} custom-call(s32[512]{0:T(512)} %fusion.7.idx_ref, f32[1024,768]{1,0:T(8,128)} %bitcast.52, f32[1024,768]{1,0:T(8,128)} %bitcast.15.far_ref, f32[36,16,128]{2,1,0:T(8,128)} %broadcast_in_dim.2.w_ref, bf16[36,16,4096]{2,1,0:T(8,128)(2,1)} %bitcast.50, bf16[36,16,4096]{2,1,0:T(8,128)(2,1)} %bitcast.51, ...), custom_call_target="tpu_custom_call" | custom-call | tf_op jit(solution)/shard_map/pallas_call | solution.py:52
  73.1 0.8 dynamic-slice_bitcast_fusion.2
  73.9 1.6 %collective-permute-start.11 = (f32[6,1024]{1,0:T(8,128)S(1)}, f32[6,1024]{1,0:T(8,128)S(1)}, u32[]{:S(2)}, u32[]{:S(2)}) collective-permute-start(f32[6,1024]{1,0:T(8,128)S(1)} %get-tuple-element.4), channel_id=1, source_target_pairs={{0,1},{1,2},{2,3},{3,0},{4,5},{5,6},{6,7},{7,4},{8,9},{9,10},{10,1... | collective-permute-start | bytes 73736 | tf_op jit(solution)/shard_map/ppermute | solution.py:155
  75.5 2.7 %collective-permute-start.12 = (f32[6,1024]{1,0:T(8,128)S(1)}, f32[6,1024]{1,0:T(8,128)S(1)}, u32[]{:S(2)}, u32[]{:S(2)}) collective-permute-start(f32[6,1024]{1,0:T(8,128)S(1)} %get-tuple-element.6), channel_id=1, source_target_pairs={{0,2},{1,3},{2,0},{3,1},{4,6},{5,7},{6,4},{7,5},{8,10},{9,11},{10,... | collective-permute-start | bytes 73736 | tf_op jit(solution)/shard_map/ppermute | solution.py:155
  78.2 1.4 %collective-permute-start.13 = (f32[6,1024]{1,0:T(8,128)S(1)}, f32[6,1024]{1,0:T(8,128)S(1)}, u32[]{:S(2)}, u32[]{:S(2)}) collective-permute-start(f32[6,1024]{1,0:T(8,128)S(1)} %get-tuple-element.5), channel_id=1, source_target_pairs={{0,3},{1,0},{2,1},{3,2},{4,7},{5,4},{6,5},{7,6},{8,11},{9,8},{10,9... | collective-permute-start | bytes 73736 | tf_op jit(solution)/shard_map/ppermute | solution.py:155
  79.6 0.0 collective-permute-done.11
  79.6 1.3 %collective-permute-done.12 = f32[6,1024]{1,0:T(8,128)S(1)} collective-permute-done((f32[6,1024]{1,0:T(8,128)S(1)}, f32[6,1024]{1,0:T(8,128)S(1)}, u32[]{:S(2)}, u32[]{:S(2)}) %collective-permute-start.12) | collective-permute-done | bytes 24608 | tf_op jit(solution)/shard_map/ppermute | solution.py:155
  80.9 1.2 %collective-permute-done.13 = f32[6,1024]{1,0:T(8,128)S(1)} collective-permute-done((f32[6,1024]{1,0:T(8,128)S(1)}, f32[6,1024]{1,0:T(8,128)S(1)}, u32[]{:S(2)}, u32[]{:S(2)}) %collective-permute-start.13) | collective-permute-done | bytes 24608 | tf_op jit(solution)/shard_map/ppermute | solution.py:155
  82.1 1.4 %multiply_add_fusion = (f32[6,1024]{1,0:T(8,128)}, f32[6,1024]{1,0:T(8,128)}) fusion(f32[6,4096]{1,0:T(8,128)} %occ_ref.1, s32[]{:T(128)S(6)} %select_n.88, f32[6,1024]{1,0:T(8,128)S(1)} %collective-permute-done.13, f32[6,1024]{1,0:T(8,128)S(1)} %collective-permute-done.12, f32[6,1024]{1,0:T(8,128)S(1)} %collective-permute-done.11, ...), kind=kLoop, calls=%fused_computation.13 | loop fusion | flops 30720 | bytes 172040 | tf_op jit(solution)/shard_map/add | solution.py:161
  (10 shorter events, 0.3 us)
Async XLA Ops:
  1.6 5.9 %collective-permute-start = (f32[32,768]{1,0:T(8,128)S(1)}, f32[32,768]{1,0:T(8,128)S(1)}, u32[]{:S(2)}, u32[]{:S(2)}) collective-permute-start(f32[32,768]{1,0:T(8,128)S(1)} %bitcast.61), channel_id=1, source_target_pairs={{0,24},{4,28},{8,0},{12,4},{16,8},{20,12},{24,16},{28,20},{32,56},... | collective-permute-start | bytes 294920 | tf_op jit(solution)/shard_map/ppermute | solution.py:94
  2.4 6.0 %collective-permute-start.2 = (f32[32,768]{1,0:T(8,128)S(1)}, f32[32,768]{1,0:T(8,128)S(1)}, u32[]{:S(2)}, u32[]{:S(2)}) collective-permute-start(f32[32,768]{1,0:T(8,128)S(1)} %bitcast.62), channel_id=1, source_target_pairs={{0,8},{4,12},{8,16},{12,20},{16,24},{20,28},{24,0},{28,4},{32,40},... | collective-permute-start | bytes 294920 | tf_op jit(solution)/shard_map/ppermute | solution.py:97
  7.5 5.8 %collective-permute-start.1 = (f32[32,768]{1,0:T(8,128)S(1)}, f32[32,768]{1,0:T(8,128)S(1)}, u32[]{:S(2)}, u32[]{:S(2)}) collective-permute-start(f32[32,768]{1,0:T(8,128)S(1)} %collective-permute-done), channel_id=1, source_target_pairs={{0,24},{4,28},{8,0},{12,4},{16,8},{20,12},{24,16},{28,20},{32,56},... | collective-permute-start | bytes 294920 | tf_op jit(solution)/shard_map/ppermute | solution.py:94
  13.3 42.4 %copy-start.2 = (s32[1,1,16,32,1]{3,4,2,1,0:T(1,128)S(1)}, s32[1,1,16,32,1]{3,4,2,1,0:T(1,128)}, u32[]{:S(2)}) copy-start(s32[1,1,16,32,1]{3,4,2,1,0:T(1,128)} %param.10) | copy-start | bytes 6148
  13.3 43.2 %copy-start.1 = (s32[1,1,16,32]{3,2,1,0:T(8,128)S(1)}, s32[1,1,16,32]{3,2,1,0:T(8,128)}, u32[]{:S(2)}) copy-start(s32[1,1,16,32]{3,2,1,0:T(8,128)} %param.11) | copy-start | bytes 6148
  13.3 12.0 %collective-permute-start.3 = (f32[4,32,768]{2,1,0:T(8,128)S(1)}, f32[4,32,768]{2,1,0:T(8,128)S(1)}, u32[]{:S(2)}, u32[]{:S(2)}) collective-permute-start(f32[4,32,768]{2,1,0:T(8,128)S(1)} %pad_maximum_fusion), channel_id=1, source_target_pairs={{0,224},{4,228},{8,232},{12,236},{16,240},{20,244},{24,248},{28,25... | collective-permute-start | bytes 1179656 | tf_op jit(solution)/shard_map/ppermute | solution.py:94
  19.3 9.8 %collective-permute-start.7 = (f32[4,32,768]{2,1,0:T(8,128)S(1)}, f32[4,32,768]{2,1,0:T(8,128)S(1)}, u32[]{:S(2)}, u32[]{:S(2)}) collective-permute-start(f32[4,32,768]{2,1,0:T(8,128)S(1)} %pad_maximum_fusion), channel_id=1, source_target_pairs={{0,32},{4,36},{8,40},{12,44},{16,48},{20,52},{24,56},{28,60},{32,6... | collective-permute-start | bytes 1179656 | tf_op jit(solution)/shard_map/ppermute | solution.py:97
  25.4 9.6 %collective-permute-start.4 = (f32[4,32,768]{2,1,0:T(8,128)S(1)}, f32[4,32,768]{2,1,0:T(8,128)S(1)}, u32[]{:S(2)}, u32[]{:S(2)}) collective-permute-start(f32[4,32,768]{2,1,0:T(8,128)S(1)} %collective-permute-done.3), channel_id=1, source_target_pairs={{0,224},{4,228},{8,232},{12,236},{16,240},{20,244},{24,248},{28,25... | collective-permute-start | bytes 1179656 | tf_op jit(solution)/shard_map/ppermute | solution.py:94
  29.0 9.8 %collective-permute-start.8 = (f32[4,32,768]{2,1,0:T(8,128)S(1)}, f32[4,32,768]{2,1,0:T(8,128)S(1)}, u32[]{:S(2)}, u32[]{:S(2)}) collective-permute-start(f32[4,32,768]{2,1,0:T(8,128)S(1)} %collective-permute-done.7), channel_id=1, source_target_pairs={{0,32},{4,36},{8,40},{12,44},{16,48},{20,52},{24,56},{28,60},{32,6... | collective-permute-start | bytes 1179656 | tf_op jit(solution)/shard_map/ppermute | solution.py:97
  35.0 10.7 %collective-permute-start.5 = (f32[4,32,768]{2,1,0:T(8,128)S(1)}, f32[4,32,768]{2,1,0:T(8,128)S(1)}, u32[]{:S(2)}, u32[]{:S(2)}) collective-permute-start(f32[4,32,768]{2,1,0:T(8,128)S(1)} %collective-permute-done.4), channel_id=1, source_target_pairs={{0,224},{4,228},{8,232},{12,236},{16,240},{20,244},{24,248},{28,25... | collective-permute-start | bytes 1179656 | tf_op jit(solution)/shard_map/ppermute | solution.py:94
  38.8 15.9 %collective-permute-start.9 = (f32[4,32,768]{2,1,0:T(8,128)S(1)}, f32[4,32,768]{2,1,0:T(8,128)S(1)}, u32[]{:S(2)}, u32[]{:S(2)}) collective-permute-start(f32[4,32,768]{2,1,0:T(8,128)S(1)} %collective-permute-done.8), channel_id=1, source_target_pairs={{0,32},{4,36},{8,40},{12,44},{16,48},{20,52},{24,56},{28,60},{32,6... | collective-permute-start | bytes 1179656 | tf_op jit(solution)/shard_map/ppermute | solution.py:97
  45.7 9.0 %collective-permute-start.6 = (f32[4,32,768]{2,1,0:T(8,128)S(1)}, f32[4,32,768]{2,1,0:T(8,128)S(1)}, u32[]{:S(2)}, u32[]{:S(2)}) collective-permute-start(f32[4,32,768]{2,1,0:T(8,128)S(1)} %collective-permute-done.5), channel_id=1, source_target_pairs={{0,224},{4,228},{8,232},{12,236},{16,240},{20,244},{24,248},{28,25... | collective-permute-start | bytes 1179656 | tf_op jit(solution)/shard_map/ppermute | solution.py:94
  54.9 6.8 %copy-start = (f32[8,4,32,768]{3,2,1,0:T(8,128)}, f32[8,4,32,768]{3,2,1,0:T(8,128)S(1)}, u32[]{:S(2)}) copy-start(f32[8,4,32,768]{3,2,1,0:T(8,128)S(1)} %bitcast_dynamic-update-slice_fusion) | copy-start | bytes 9437188
  54.9 5.9 %collective-permute-start.10 = (f32[8,4,32,768]{3,2,1,0:T(8,128)S(1)}, f32[8,4,32,768]{3,2,1,0:T(8,128)}, u32[]{:S(2)}, u32[]{:S(2)}) collective-permute-start(f32[8,4,32,768]{3,2,1,0:T(8,128)S(1)} %bitcast_dynamic-update-slice_fusion), channel_id=1, source_target_pairs={{0,4},{4,0},{8,12},{12,8},{16,20},{20,16},{24,28},{28,24},{32,36},... | collective-permute-start | bytes 9437192 | tf_op jit(solution)/shard_map/ppermute | solution.py:103
  73.9 5.7 %collective-permute-start.11 = (f32[6,1024]{1,0:T(8,128)S(1)}, f32[6,1024]{1,0:T(8,128)S(1)}, u32[]{:S(2)}, u32[]{:S(2)}) collective-permute-start(f32[6,1024]{1,0:T(8,128)S(1)} %get-tuple-element.4), channel_id=1, source_target_pairs={{0,1},{1,2},{2,3},{3,0},{4,5},{5,6},{6,7},{7,4},{8,9},{9,10},{10,1... | collective-permute-start | bytes 73736 | tf_op jit(solution)/shard_map/ppermute | solution.py:155
  75.5 5.4 %collective-permute-start.12 = (f32[6,1024]{1,0:T(8,128)S(1)}, f32[6,1024]{1,0:T(8,128)S(1)}, u32[]{:S(2)}, u32[]{:S(2)}) collective-permute-start(f32[6,1024]{1,0:T(8,128)S(1)} %get-tuple-element.6), channel_id=1, source_target_pairs={{0,2},{1,3},{2,0},{3,1},{4,6},{5,7},{6,4},{7,5},{8,10},{9,11},{10,... | collective-permute-start | bytes 73736 | tf_op jit(solution)/shard_map/ppermute | solution.py:155
  78.2 3.9 %collective-permute-start.13 = (f32[6,1024]{1,0:T(8,128)S(1)}, f32[6,1024]{1,0:T(8,128)S(1)}, u32[]{:S(2)}, u32[]{:S(2)}) collective-permute-start(f32[6,1024]{1,0:T(8,128)S(1)} %get-tuple-element.5), channel_id=1, source_target_pairs={{0,3},{1,0},{2,1},{3,2},{4,7},{5,4},{6,5},{7,6},{8,11},{9,8},{10,9... | collective-permute-start | bytes 73736 | tf_op jit(solution)/shard_map/ppermute | solution.py:155
